TPU v7x, 32 devices: a whole 2x2x4 slice. The times are simulated.
32 devices in a mesh: seq: 8 (over z, core), chan: 4 (over y, x).
Axes of the slice: x: 2, y: 2, z: 4, core: 2. Of those that a mesh axis runs over, the one named last changes fastest.
Arguments:
- grad_out: bfloat16 [4096, 8192], P('seq', 'chan'), may hold values from -6 to 6
- qkv_saved: bfloat16 [4096, 3, 8192], P('seq', None, 'chan'), may hold values from -6 to 6
- conv_saved: bfloat16 [4096, 8192], P('seq', 'chan'), may hold values from -6 to 6
- long_taps: bfloat16 [4096, 512], P('seq', 'chan'), may hold values from -1 to 1
- short_taps: float32 [3, 3, 8192], P(None, None, 'chan'), may hold values from -3 to 3
Outputs:
- grad_proj: bfloat16 [4096, 3, 8192], P(('seq', 'chan'))
All inputs are finite; a program needn't handle non-finite values.
Results may differ from a plain program's by a relative error of at most 0.0042.
Values may be sent and summed in bfloat16 or wider, within the bound.
No kernel may reach another device: no remote copies, remote signals or barrier semaphores. Data moves between devices by JAX's collectives and lax.ppermute only.
A program may use at most 128 MiB of HBM per device.

v0:
```python
import jax
import jax.numpy as jnp
from jax import lax
from jax.sharding import PartitionSpec as P

tile_rows = 128


def shifted(value, axis, steps):
    count = lax.axis_size(axis)
    leading, last = (max(0, -steps), min(count, count - steps))
    return lax.ppermute(value, axis, [(source, source + steps) for source in range(leading, last)])


def band_matrix(window):
    groups = window.shape[0]
    rolled = jnp.concatenate(
        [
            window[:, tile_rows - 1 :],
            jnp.zeros((groups, 1), window.dtype),
            window[:, : tile_rows - 1],
        ],
        1,
    )
    spread = jnp.broadcast_to(rolled[:, None, :], (groups, tile_rows, 2 * tile_rows))
    flat = spread.reshape(groups, 2 * tile_rows * tile_rows)[:, : tile_rows * (2 * tile_rows - 1)]
    return flat.reshape(groups, tile_rows, 2 * tile_rows - 1)[:, :, :tile_rows]


def correlate(gradients, filters, first_row, out_rows, span):
    groups = gradients.shape[0]
    per_group = gradients.shape[1]
    tiles_out = out_rows // tile_rows
    padded_grads = jnp.concatenate(
        [gradients, jnp.zeros((groups, per_group, out_rows), gradients.dtype)], 2
    )
    padded_taps = jnp.concatenate(
        [
            jnp.zeros((groups, tile_rows), filters.dtype),
            filters,
            jnp.zeros((groups, tile_rows), filters.dtype),
        ],
        1,
    )

    def advance(offset, running):
        lag_start = offset * tile_rows
        window = lax.dynamic_slice_in_dim(padded_taps, lag_start + 1, 2 * tile_rows - 1, 1)
        band = band_matrix(window)
        source = lax.dynamic_slice_in_dim(padded_grads, first_row + lag_start, out_rows, 2)
        source = source.reshape(groups, per_group * tiles_out, tile_rows)
        product = lax.dot_general(
            source, band, (((2,), (2,)), ((0,), (0,))), preferred_element_type=jnp.float32
        )
        return running + product

    start = jnp.zeros((groups, per_group * tiles_out, tile_rows), jnp.float32)
    summed = lax.fori_loop(0, span // tile_rows, advance, start)
    return summed.reshape(groups * per_group, out_rows)


def on_device(grad_out, qkv_saved, conv_saved, long_taps, short_taps):
    block_rows = grad_out.shape[0]
    channels = grad_out.shape[1]
    shards = lax.axis_size("seq")
    position = lax.axis_index("seq")
    total_rows = shards * block_rows
    out_wide = grad_out.astype(jnp.float32)
    query = qkv_saved[:, 0, :]
    key_part = qkv_saved[:, 1, :]
    value_part = qkv_saved[:, 2, :]
    grad_query = out_wide * conv_saved.astype(jnp.float32)
    grad_mixed = (out_wide * query.astype(jnp.float32)).astype(jnp.bfloat16)
    mixed_lanes = grad_mixed.T
    taps_lanes = long_taps.T
    local_groups = long_taps.shape[1]
    per_group = channels // local_groups
    all_grads, all_filters = (
        lax.all_gather(mixed_lanes, "seq", axis=1, tiled=True),
        lax.all_gather(taps_lanes, "seq", axis=1, tiled=True),
    )
    shaped = all_grads.reshape(local_groups, per_group, total_rows)
    first_row = position * block_rows
    grad_lanes = correlate(shaped, all_filters, first_row, block_rows, total_rows - first_row)
    grad_z = grad_lanes.T
    grad_key = grad_z * value_part.astype(jnp.float32)
    grad_value = grad_z * key_part.astype(jnp.float32)
    stacked = jnp.stack([grad_query, grad_key, grad_value], 1)
    short_len = short_taps.shape[1]
    borrowed = shifted(stacked[: short_len - 1], "seq", -1)
    extended = jnp.concatenate([stacked, borrowed], 0)
    result = jnp.zeros_like(stacked)
    for lag_index in range(short_len):
        result = (
            result
            + short_taps[:, lag_index, :][None] * extended[lag_index : lag_index + block_rows]
        )
    mixed = result.astype(jnp.bfloat16)
    return lax.all_to_all(mixed, "chan", split_axis=0, concat_axis=2, tiled=True)


def solution(mesh):
    in_specs = (
        P("seq", "chan"),
        P("seq", None, "chan"),
        P("seq", "chan"),
        P("seq", "chan"),
        P(None, None, "chan"),
    )
    out_specs = P(("seq", "chan"), None, None)
    return jax.shard_map(
        on_device, mesh=mesh, in_specs=in_specs, out_specs=out_specs, check_vma=False
    )
```

profile of v0, /device:TPU:0, one launch (start us, length us, event | category | flops | bytes accessed | tf_op | source)
XLA Modules:
  0.0 2563.1 jit_solution(16474790631052970217)
XLA Ops:
  40.4 146.1 %all-gather.3.cloned.1.call-done = bf16[2048,4096]{1,0:T(8,128)(2,1)} async-done(((bf16[2048,512]{1,0:T(8,128)(2,1)}), bf16[2048,4096]{1,0:T(8,128)(2,1)}) %all-gather.3.cloned.1.call-update) | async-done | bytes 16777232 | tf_op jit(solution)/shard_map/all_gather | solution.py:79
  186.5 16.5 concatenate.15
  205.5 2171.4 %while.12 = (s32[]{:T(128)}, f32[128,64,128]{2,1,0:T(8,128)}, s32[]{:T(128)}, s32[]{:T(128)}, bf16[128,16,4608]{2,1,0:T(8,128)(2,1)}, /*index=5*/bf16[128,4352]{...) while((s32[]{:T(128)}, f32[128,64,128]{2,1,0:T(8,128)}, ...), condition=%wide.region_1.2_spmd, body=%wide.region_0.1_spmd.sunk | while | flops 269680640 | bytes 81986056 | solution.py:58
  209.5 12.5 copy.48
  229.2 29.5 %reshape.43 = bf16[128,128,255]{2,1,0:T(8,128)(2,1)} reshape(bf16[128,32640]{1,0:T(8,128)(2,1)} %slice.88) | data formatting | bytes 16711680 | tf_op jit(solution)/shard_map/while/body/reshape | solution.py:27
  277.4 12.5 copy.48
  297.1 29.5 %reshape.43 = bf16[128,128,255]{2,1,0:T(8,128)(2,1)} reshape(bf16[128,32640]{1,0:T(8,128)(2,1)} %slice.88) | data formatting | bytes 16711680 | tf_op jit(solution)/shard_map/while/body/reshape | solution.py:27
  345.2 12.5 copy.48
  364.9 29.5 %reshape.43 = bf16[128,128,255]{2,1,0:T(8,128)(2,1)} reshape(bf16[128,32640]{1,0:T(8,128)(2,1)} %slice.88) | data formatting | bytes 16711680 | tf_op jit(solution)/shard_map/while/body/reshape | solution.py:27
  413.1 12.5 copy.48
  432.8 29.5 %reshape.43 = bf16[128,128,255]{2,1,0:T(8,128)(2,1)} reshape(bf16[128,32640]{1,0:T(8,128)(2,1)} %slice.88) | data formatting | bytes 16711680 | tf_op jit(solution)/shard_map/while/body/reshape | solution.py:27
  480.9 12.5 copy.48
  500.6 29.5 %reshape.43 = bf16[128,128,255]{2,1,0:T(8,128)(2,1)} reshape(bf16[128,32640]{1,0:T(8,128)(2,1)} %slice.88) | data formatting | bytes 16711680 | tf_op jit(solution)/shard_map/while/body/reshape | solution.py:27
  548.8 12.5 copy.48
  568.5 29.5 %reshape.43 = bf16[128,128,255]{2,1,0:T(8,128)(2,1)} reshape(bf16[128,32640]{1,0:T(8,128)(2,1)} %slice.88) | data formatting | bytes 16711680 | tf_op jit(solution)/shard_map/while/body/reshape | solution.py:27
  616.7 12.5 copy.48
  636.4 29.5 %reshape.43 = bf16[128,128,255]{2,1,0:T(8,128)(2,1)} reshape(bf16[128,32640]{1,0:T(8,128)(2,1)} %slice.88) | data formatting | bytes 16711680 | tf_op jit(solution)/shard_map/while/body/reshape | solution.py:27
  684.5 12.5 copy.48
  704.2 29.5 %reshape.43 = bf16[128,128,255]{2,1,0:T(8,128)(2,1)} reshape(bf16[128,32640]{1,0:T(8,128)(2,1)} %slice.88) | data formatting | bytes 16711680 | tf_op jit(solution)/shard_map/while/body/reshape | solution.py:27
  772.1 29.5 %reshape.43 = bf16[128,128,255]{2,1,0:T(8,128)(2,1)} reshape(bf16[128,32640]{1,0:T(8,128)(2,1)} %slice.88) | data formatting | bytes 16711680 | tf_op jit(solution)/shard_map/while/body/reshape | solution.py:27
  820.2 12.5 copy.48
  839.9 29.5 %reshape.43 = bf16[128,128,255]{2,1,0:T(8,128)(2,1)} reshape(bf16[128,32640]{1,0:T(8,128)(2,1)} %slice.88) | data formatting | bytes 16711680 | tf_op jit(solution)/shard_map/while/body/reshape | solution.py:27
  888.1 12.5 copy.48
  907.8 29.5 %reshape.43 = bf16[128,128,255]{2,1,0:T(8,128)(2,1)} reshape(bf16[128,32640]{1,0:T(8,128)(2,1)} %slice.88) | data formatting | bytes 16711680 | tf_op jit(solution)/shard_map/while/body/reshape | solution.py:27
  955.9 12.5 copy.48
  975.6 29.5 %reshape.43 = bf16[128,128,255]{2,1,0:T(8,128)(2,1)} reshape(bf16[128,32640]{1,0:T(8,128)(2,1)} %slice.88) | data formatting | bytes 16711680 | tf_op jit(solution)/shard_map/while/body/reshape | solution.py:27
  1023.8 12.5 copy.48
  1043.5 29.5 %reshape.43 = bf16[128,128,255]{2,1,0:T(8,128)(2,1)} reshape(bf16[128,32640]{1,0:T(8,128)(2,1)} %slice.88) | data formatting | bytes 16711680 | tf_op jit(solution)/shard_map/while/body/reshape | solution.py:27
  1091.7 12.5 copy.48
  1111.4 29.5 %reshape.43 = bf16[128,128,255]{2,1,0:T(8,128)(2,1)} reshape(bf16[128,32640]{1,0:T(8,128)(2,1)} %slice.88) | data formatting | bytes 16711680 | tf_op jit(solution)/shard_map/while/body/reshape | solution.py:27
  1159.5 12.5 copy.48
  1179.2 29.5 %reshape.43 = bf16[128,128,255]{2,1,0:T(8,128)(2,1)} reshape(bf16[128,32640]{1,0:T(8,128)(2,1)} %slice.88) | data formatting | bytes 16711680 | tf_op jit(solution)/shard_map/while/body/reshape | solution.py:27
  1227.4 12.5 copy.48
  1247.1 29.5 %reshape.43 = bf16[128,128,255]{2,1,0:T(8,128)(2,1)} reshape(bf16[128,32640]{1,0:T(8,128)(2,1)} %slice.88) | data formatting | bytes 16711680 | tf_op jit(solution)/shard_map/while/body/reshape | solution.py:27
  1314.9 29.5 %reshape.43 = bf16[128,128,255]{2,1,0:T(8,128)(2,1)} reshape(bf16[128,32640]{1,0:T(8,128)(2,1)} %slice.88) | data formatting | bytes 16711680 | tf_op jit(solution)/shard_map/while/body/reshape | solution.py:27
  1382.8 29.5 %reshape.43 = bf16[128,128,255]{2,1,0:T(8,128)(2,1)} reshape(bf16[128,32640]{1,0:T(8,128)(2,1)} %slice.88) | data formatting | bytes 16711680 | tf_op jit(solution)/shard_map/while/body/reshape | solution.py:27
  1430.9 12.5 copy.48
  1450.6 29.5 %reshape.43 = bf16[128,128,255]{2,1,0:T(8,128)(2,1)} reshape(bf16[128,32640]{1,0:T(8,128)(2,1)} %slice.88) | data formatting | bytes 16711680 | tf_op jit(solution)/shard_map/while/body/reshape | solution.py:27
  1498.8 12.5 copy.48
  1518.5 29.5 %reshape.43 = bf16[128,128,255]{2,1,0:T(8,128)(2,1)} reshape(bf16[128,32640]{1,0:T(8,128)(2,1)} %slice.88) | data formatting | bytes 16711680 | tf_op jit(solution)/shard_map/while/body/reshape | solution.py:27
  1566.7 12.5 copy.48
  1586.4 29.5 %reshape.43 = bf16[128,128,255]{2,1,0:T(8,128)(2,1)} reshape(bf16[128,32640]{1,0:T(8,128)(2,1)} %slice.88) | data formatting | bytes 16711680 | tf_op jit(solution)/shard_map/while/body/reshape | solution.py:27
  1634.5 12.5 copy.48
  1654.2 29.5 %reshape.43 = bf16[128,128,255]{2,1,0:T(8,128)(2,1)} reshape(bf16[128,32640]{1,0:T(8,128)(2,1)} %slice.88) | data formatting | bytes 16711680 | tf_op jit(solution)/shard_map/while/body/reshape | solution.py:27
  1702.4 12.5 copy.48
  1722.1 29.5 %reshape.43 = bf16[128,128,255]{2,1,0:T(8,128)(2,1)} reshape(bf16[128,32640]{1,0:T(8,128)(2,1)} %slice.88) | data formatting | bytes 16711680 | tf_op jit(solution)/shard_map/while/body/reshape | solution.py:27
  1770.2 12.5 copy.48
  1789.9 29.5 %reshape.43 = bf16[128,128,255]{2,1,0:T(8,128)(2,1)} reshape(bf16[128,32640]{1,0:T(8,128)(2,1)} %slice.88) | data formatting | bytes 16711680 | tf_op jit(solution)/shard_map/while/body/reshape | solution.py:27
  1838.1 12.5 copy.48
  1857.8 29.5 %reshape.43 = bf16[128,128,255]{2,1,0:T(8,128)(2,1)} reshape(bf16[128,32640]{1,0:T(8,128)(2,1)} %slice.88) | data formatting | bytes 16711680 | tf_op jit(solution)/shard_map/while/body/reshape | solution.py:27
  1925.6 29.5 %reshape.43 = bf16[128,128,255]{2,1,0:T(8,128)(2,1)} reshape(bf16[128,32640]{1,0:T(8,128)(2,1)} %slice.88) | data formatting | bytes 16711680 | tf_op jit(solution)/shard_map/while/body/reshape | solution.py:27
  1993.5 29.5 %reshape.43 = bf16[128,128,255]{2,1,0:T(8,128)(2,1)} reshape(bf16[128,32640]{1,0:T(8,128)(2,1)} %slice.88) | data formatting | bytes 16711680 | tf_op jit(solution)/shard_map/while/body/reshape | solution.py:27
  2061.4 29.5 %reshape.43 = bf16[128,128,255]{2,1,0:T(8,128)(2,1)} reshape(bf16[128,32640]{1,0:T(8,128)(2,1)} %slice.88) | data formatting | bytes 16711680 | tf_op jit(solution)/shard_map/while/body/reshape | solution.py:27
  2109.5 12.5 copy.48
  2129.2 29.5 %reshape.43 = bf16[128,128,255]{2,1,0:T(8,128)(2,1)} reshape(bf16[128,32640]{1,0:T(8,128)(2,1)} %slice.88) | data formatting | bytes 16711680 | tf_op jit(solution)/shard_map/while/body/reshape | solution.py:27
  2177.4 12.5 copy.48
  2197.1 29.5 %reshape.43 = bf16[128,128,255]{2,1,0:T(8,128)(2,1)} reshape(bf16[128,32640]{1,0:T(8,128)(2,1)} %slice.88) | data formatting | bytes 16711680 | tf_op jit(solution)/shard_map/while/body/reshape | solution.py:27
  2245.2 12.5 copy.48
  2264.9 29.5 %reshape.43 = bf16[128,128,255]{2,1,0:T(8,128)(2,1)} reshape(bf16[128,32640]{1,0:T(8,128)(2,1)} %slice.88) | data formatting | bytes 16711680 | tf_op jit(solution)/shard_map/while/body/reshape | solution.py:27
  2313.1 12.5 copy.48
  2332.8 29.5 %reshape.43 = bf16[128,128,255]{2,1,0:T(8,128)(2,1)} reshape(bf16[128,32640]{1,0:T(8,128)(2,1)} %slice.88) | data formatting | bytes 16711680 | tf_op jit(solution)/shard_map/while/body/reshape | solution.py:27
  2404.7 13.3 fusion.6
  2418.0 14.4 copy.34
  2432.4 100.9 %all_to_all.18 = bf16[512,3,2048]{2,1,0:T(4,128)(2,1)} all-to-all(bf16[512,3,2048]{2,1,0:T(4,128)(2,1)} %copy.34), channel_id=1, replica_groups=mesh['seq'=8,'chan'=4] {'chan'}, dimensions={0} | all-to-all | bytes 12582912 | tf_op jit(solution)/shard_map/all_to_all | solution.py:99
  (338 shorter events, 990.2 us)
Async XLA Ops:
  6.5 32.5 %all-gather.5.cloned.1.call-start = ((), (), s32[]{:S(2)}) async-start(), calls=%async_computation.2 | async-start | bytes 1179648 | tf_op jit(solution)/shard_map/all_gather | solution.py:80
  8.2 178.3 %all-gather.3.cloned.1.call-start = ((), (), s32[]{:S(2)}) async-start(), calls=%async_computation.1 | async-start | bytes 18874368 | tf_op jit(solution)/shard_map/all_gather | solution.py:79
  32.5 6.5 copy-start.6
  2376.9 5.1 copy-start.5
  2382.0 4.3 copy-start
  2386.3 2.2 copy-start.2
  2386.3 3.3 copy-start.4
  2391.2 3.1 collective-permute-start
  2396.5 8.2 copy-start.1
  2396.5 8.2 copy-start.3
Sparse Core Ops, SparseCore 0:
  8.9 24.9 all-gather.4
  35.5 150.8 all-gather.2
where the time goes:
time: 2570 us; the launch traced here: 2560 us
  local copies, waits for them, and re-layouts  1990 us (77%)
  matrix products  271 us (11%)
  waiting for transfers between devices  148 us (6%)
  blocking collectives  101 us (4%)
  other arithmetic  37.9 us (1%)
    reshape x32, local copies, waits for them, and re-layouts, band_matrix(): return flat.reshape(groups, tile_rows, 2 * tile_rows - 1)[:, :, :tile_rows]  943 us
    while x32, local copies, waits for them, and re-layouts  400 us
    dot_general x32, matrix products, advance(): lax.dot_general(source, band, (((2,), (2,)), ((0,), (0,))), preferred_ele...  271 us
    slice x32, local copies, waits for them, and re-layouts, band_matrix(): spread.reshape(groups, 2 * tile_rows * tile_rows)  231 us
    all_gather x1, waiting for transfers between devices, on_device(): lax.all_gather(mixed_lanes, 'seq', axis=1, tiled=True)  146 us
    broadcast_in_dim x32, local copies, waits for them, and re-layouts, band_matrix(): jnp.broadcast_to(rolled[:, None, :], (groups, tile_rows, 2 * tile_rows))  123 us
    all_to_all x1, blocking collectives, on_device(): lax.all_to_all(mixed, 'chan', split_axis=0, concat_axis=2, tiled=True)  101 us
    dynamic_slice x32, local copies, waits for them, and re-layouts, advance(): lax.dynamic_slice_in_dim(padded_grads, first_row + lag_start, out_rows, 2)  99.2 us
  transfers between devices with their start and end apart: 3, of which 2 were waited for; matrix products, arithmetic and copies ran while one was open for 1% of the time, Pallas kernels for 0%

commit v1 on v0

v1 whole, which is shorter than its diff:
```python
import functools

import jax
import jax.numpy as jnp
from jax import lax
from jax.experimental import pallas as pl
from jax.experimental.pallas import tpu as pltpu
from jax.sharding import PartitionSpec as P

block = 256
per_group = 16


def shifted(value, axis, steps):
    count = lax.axis_size(axis)
    leading, last = (max(0, -steps), min(count, count - steps))
    return lax.ppermute(value, axis, [(source, source + steps) for source in range(leading, last)])


def correlate_kernel(x_ref, h_ref, o_ref):
    rows_all = x_ref.shape[1]
    blocks = rows_all // per_group
    tokens = blocks * block
    o_ref[...] = jnp.zeros(o_ref.shape, o_ref.dtype)
    for lag_block in range(blocks):
        start = tokens - block * (lag_block + 1)
        window = h_ref[0, :, start : start + 2 * block]
        spread = jnp.broadcast_to(window, (block, 2 * block))
        rolled = pltpu.roll(spread, block + 1, 1, stride=1, stride_axis=0)
        band = rolled[:, :block].astype(jnp.bfloat16)
        rows = per_group * (blocks - lag_block)
        source = x_ref[0, per_group * lag_block :, :]
        o_ref[0, :rows, :] += jnp.dot(source, band, preferred_element_type=jnp.float32)


def correlate(grads, taps):
    tokens, channels = grads.shape
    groups = taps.shape[1]
    blocks = tokens // block
    shaped = grads.reshape(blocks, block, groups, per_group).transpose(2, 0, 3, 1)
    shaped = shaped.reshape(groups, blocks * per_group, block)
    reversed_taps = taps.astype(jnp.float32).T[:, ::-1]
    padded = jnp.concatenate([reversed_taps, jnp.zeros((groups, block), jnp.float32)], 1)
    padded = padded.reshape(groups, 1, tokens + block)
    flops = 2 * groups * per_group * block * block * blocks * (blocks + 1) // 2
    out = pl.pallas_call(
        correlate_kernel,
        out_shape=jax.ShapeDtypeStruct((groups, blocks * per_group, block), jnp.float32),
        grid=(groups,),
        in_specs=[
            pl.BlockSpec((1, blocks * per_group, block), lambda g: (g, 0, 0)),
            pl.BlockSpec((1, 1, tokens + block), lambda g: (g, 0, 0)),
        ],
        out_specs=pl.BlockSpec((1, blocks * per_group, block), lambda g: (g, 0, 0)),
        cost_estimate=pl.CostEstimate(
            flops=flops, bytes_accessed=grads.size * 6 + padded.size * 4, transcendentals=0
        ),
    )(shaped, padded)
    out = out.reshape(groups, blocks, per_group, block).transpose(1, 3, 0, 2)
    return out.reshape(tokens, channels)


def on_device(grad_out, qkv_saved, conv_saved, long_taps, short_taps):
    block_rows = grad_out.shape[0]
    out_wide = grad_out.astype(jnp.float32)
    query = qkv_saved[:, 0, :]
    key_part = qkv_saved[:, 1, :]
    value_part = qkv_saved[:, 2, :]
    grad_query = out_wide * conv_saved.astype(jnp.float32)
    grad_mixed = (out_wide * query.astype(jnp.float32)).astype(jnp.bfloat16)
    mixed_cols = lax.all_to_all(grad_mixed, "seq", split_axis=1, concat_axis=0, tiled=True)
    taps_cols = lax.all_to_all(long_taps, "seq", split_axis=1, concat_axis=0, tiled=True)
    z_cols = correlate(mixed_cols, taps_cols)
    grad_z = lax.all_to_all(z_cols, "seq", split_axis=0, concat_axis=1, tiled=True)
    grad_key = grad_z * value_part.astype(jnp.float32)
    grad_value = grad_z * key_part.astype(jnp.float32)
    stacked = jnp.stack([grad_query, grad_key, grad_value], 1)
    short_len = short_taps.shape[1]
    borrowed = shifted(stacked[: short_len - 1], "seq", -1)
    extended = jnp.concatenate([stacked, borrowed], 0)
    result = jnp.zeros_like(stacked)
    for lag_index in range(short_len):
        result = (
            result
            + short_taps[:, lag_index, :][None] * extended[lag_index : lag_index + block_rows]
        )
    mixed = result.astype(jnp.bfloat16)
    return lax.all_to_all(mixed, "chan", split_axis=0, concat_axis=2, tiled=True)


def solution(mesh):
    in_specs = (
        P("seq", "chan"),
        P("seq", None, "chan"),
        P("seq", "chan"),
        P("seq", "chan"),
        P(None, None, "chan"),
    )
    out_specs = P(("seq", "chan"), None, None)
    return jax.shard_map(
        on_device, mesh=mesh, in_specs=in_specs, out_specs=out_specs, check_vma=False
    )
```

time: 2570 us -> 402 us (0.16)
  the two profiles are of different devices: /device:TPU:0 before, /device:TPU:18 now
where the time goes in v1:
time: 402 us; the launch traced here: 395 us
  waiting for transfers between devices  128 us (32%)
  blocking collectives  99.7 us (25%)
  local copies, waits for them, and re-layouts  97.6 us (24%)
  other arithmetic  33.8 us (8%)
  starting transfers between devices  20 us (5%)
  Pallas kernels  15.7 us (4%)
    all_to_all x1, blocking collectives, on_device(): lax.all_to_all(mixed, 'chan', split_axis=0, concat_axis=2, tiled=True)  99.7 us
    all_to_all x1, waiting for transfers between devices, on_device(): lax.all_to_all(z_cols, 'seq', split_axis=0, concat_axis=1, tiled=True)  84 us
    all_to_all x1, waiting for transfers between devices, on_device(): lax.all_to_all(grad_mixed, 'seq', split_axis=1, concat_axis=0, tiled=True)  42.5 us
    all_to_all x2, local copies, waits for them, and re-layouts, on_device(): lax.all_to_all(mixed, 'chan', split_axis=0, concat_axis=2, tiled=True)  23.1 us
    unnamed x22, local copies, waits for them, and re-layouts  20.7 us
    pallas_call x1, Pallas kernels, correlate(): pl.pallas_call(correlate_kernel, out_shape=jax.ShapeDtypeStruct((groups,...  15.7 us
    convert_element_type x1, local copies, waits for them, and re-layouts, on_device(): mixed = result.astype(jnp.bfloat16)  14.4 us
    convert_element_type x1, other arithmetic, on_device(): mixed = result.astype(jnp.bfloat16)  13.3 us
  transfers between devices with their start and end apart: 4, of which 3 were waited for; matrix products, arithmetic and copies ran while one was open for 8% of the time, Pallas kernels for 0%

profile of v1, /device:TPU:18, one launch (start us, length us, event | category | flops | bytes accessed | tf_op | source)
XLA Modules:
  0.0 395.2 jit_solution(17245781761734176318)
XLA Ops:
  0.0 1.7 copy.31
  1.7 5.2 %all-to-all-start.1 = ((bf16[512,8,16]{0,2,1:T(8,128)(2,1)}), bf16[512,8,16]{0,2,1:T(8,128)(2,1)S(1)}, u32[]{:S(2)}, u32[]{:S(2)}) async-start(bf16[512,8,16]{0,2,1:T(8,128)(2,1)} %bitcast.6), calls=%async_computation.1 | async-start | bytes 262144 | tf_op jit(solution)/shard_map/all_to_all | solution.py:72
  6.9 2.9 copy.26
  9.7 3.9 copy.27
  13.7 5.8 %fusion.5 = (bf16[512,1,2048]{2,0,1:T(8,128)(2,1)}, bf16[512,1,2048]{2,0,1:T(8,128)(2,1)}, bf16[512,1,2048]{2,0,1:T(8,128)(2,1)}) fusion(bf16[512,3,2048]{2,0,1:T(8,128)(2,1)} %param.6), kind=kLoop, calls=%fused_computation.18 | loop fusion | bytes 12582912 | tf_op jit(solution)/shard_map/slice | solution.py:68
  19.5 3.9 copy.44
  23.4 5.9 %fusion.3 = (f32[512,1,2048]{0,2,1:T(8,128)}, bf16[512,2048]{0,1:T(8,128)(2,1)}) fusion(bf16[512,2048]{0,1:T(8,128)(2,1)S(1)} %copy.26, bf16[512,2048]{0,1:T(8,128)(2,1)} %copy.27, bf16[512,1,2048]{0,2,1:T(8,128)(2,1)} %copy.44), kind=kLoop, calls=%fused_computation.9 | loop fusion | flops 6291456 | bytes 12582912 | tf_op jit(solution)/shard_map/stack | solution.py:77
  29.3 0.0 all-to-all-done.1
  29.3 5.1 %all-to-all-start = ((bf16[512,8,256]{0,2,1:T(8,128)(2,1)}), bf16[512,8,256]{0,2,1:T(8,128)(2,1)S(1)}, u32[]{:S(2)}, u32[]{:S(2)}) async-start(bf16[512,8,256]{0,2,1:T(8,128)(2,1)} %bitcast.47), calls=%async_computation | async-start | bytes 4194304 | tf_op jit(solution)/shard_map/all_to_all | solution.py:71
  34.5 2.3 rev.3
  36.8 0.1 concatenate.6
  36.8 0.9 reshape.35.h_ref
  37.7 42.5 %all-to-all-done = bf16[512,8,256]{0,2,1:T(8,128)(2,1)S(1)} async-done(((bf16[512,8,256]{0,2,1:T(8,128)(2,1)}), bf16[512,8,256]{0,2,1:T(8,128)(2,1)S(1)}, u32[]{:S(2)}, u32[]{:S(2)}) %all-to-all-start) | async-done | bytes 2097184 | tf_op jit(solution)/shard_map/all_to_all | solution.py:71
  80.2 2.5 copy.29
  82.7 2.7 reshape.33
  85.4 2.2 copy.30
  87.6 15.7 %shard_map.55 = f32[16,256,256]{2,1,0:T(8,128)} custom-call(bf16[16,256,256]{2,1,0:T(8,128)(2,1)} %bitcast.49, f32[16,1,4352]{2,1,0:T(1,128)} %reshape.35.h_ref), custom_call_target="tpu_custom_call" | custom-call | flops 4563402752 | bytes 6569984 | tf_op jit(solution)/shard_map/pallas_call | solution.py:46
  103.3 7.4 %copy.52 = f32[16,16,16,256]{3,1,2,0:T(8,128)} copy(f32[16,16,16,256]{3,2,1,0:T(8,128)} %bitcast.48) | data formatting | bytes 8388608 | tf_op jit(solution)/shard_map/reshape | solution.py:59
  110.7 5.2 %all_to_all.54 = f32[8,512,256]{1,0,2:T(8,128)} reshape(f32[16,256,16,16]{1,0,3,2:T(8,128)} %bitcast.44) | data formatting | bytes 8388608 | tf_op jit(solution)/shard_map/all_to_all | solution.py:74
  115.9 6.6 %copy.34 = f32[8,512,256]{1,2,0:T(8,128)} copy(f32[8,512,256]{1,0,2:T(8,128)} %all_to_all.54) | data formatting | bytes 8388608 | tf_op jit(solution)/shard_map/all_to_all | solution.py:74
  122.5 7.7 %all-to-all-start.2 = ((f32[8,512,256]{1,2,0:T(8,128)}), f32[8,512,256]{1,2,0:T(8,128)}, u32[]{:S(2)}, u32[]{:S(2)}) async-start(f32[8,512,256]{1,2,0:T(8,128)} %copy.34), calls=%async_computation.2 | async-start | bytes 8388608 | tf_op jit(solution)/shard_map/all_to_all | solution.py:74
  130.2 0.0 copy-start.5
  130.2 0.0 copy-start.6
  130.2 4.1 %copy.45 = bf16[512,1,2048]{0,2,1:T(8,128)(2,1)} copy(bf16[512,1,2048]{2,0,1:T(8,128)(2,1)} %get-tuple-element.5) | data formatting | bytes 4194304
  134.3 0.0 copy-done.5
  134.3 2.5 copy.46
  136.9 0.0 copy-done.6
  136.9 0.1 fusion.6
  136.9 84.0 %all-to-all-done.2 = f32[8,512,256]{1,2,0:T(8,128)} async-done(((f32[8,512,256]{1,2,0:T(8,128)}), f32[8,512,256]{1,2,0:T(8,128)}, u32[]{:S(2)}, u32[]{:S(2)}) %all-to-all-start.2) | async-done | bytes 4194336 | tf_op jit(solution)/shard_map/all_to_all | solution.py:74
  221.0 0.0 copy-start
  221.0 4.9 %bitcast_multiply_fusion.1 = (f32[512,1,2048]{0,2,1:T(8,128)S(1)}, f32[512,1,2048]{0,2,1:T(8,128)S(1)}) fusion(f32[8,512,256]{1,2,0:T(8,128)} %all-to-all-done.2, bf16[512,1,2048]{0,2,1:T(8,128)(2,1)} %copy.45, bf16[512,1,2048]{0,2,1:T(8,128)(2,1)} %copy.46), kind=kLoop, calls=%fused_computation.12 | loop fusion | flops 4194304 | bytes 16777216 | tf_op jit(solution)/shard_map/mul | solution.py:75
  225.8 0.0 copy-start.2
  225.8 0.0 copy-start.4
  225.9 0.0 copy-done
  225.9 1.5 pad_maximum_fusion.1
  227.4 0.5 copy-done.2
  227.9 1.1 copy-done.4
  229.0 0.4 slice.36
  229.5 1.2 copy.37
  230.6 1.9 collective-permute-start
  232.6 1.7 collective-permute-done
  234.3 2.2 copy.38
  236.5 0.0 copy-start.1
  236.5 0.0 copy-start.3
  236.5 8.1 %pad_maximum_fusion = f32[514,3,2048]{0,2,1:T(8,128)S(1)} fusion(f32[2,3,2048]{0,2,1:T(8,128)} %copy.38, f32[512,1,2048]{0,2,1:T(8,128)} %copy-done.4, f32[512,1,2048]{0,2,1:T(8,128)} %copy-done.2, f32[512,1,2048]{0,2,1:T(8,128)} %get-tuple-element.10), kind=kLoop, calls=%fused_computation | loop fusion | flops 9474048 | bytes 25264128 | tf_op jit(solution)/shard_map/concatenate | solution.py:80
  244.7 0.0 copy-done.1
  244.7 0.0 copy-done.3
  244.7 13.3 %fusion.1 = bf16[512,3,2048]{0,2,1:T(8,128)(2,1)} fusion(f32[514,3,2048]{0,2,1:T(8,128)S(1)} %pad_maximum_fusion, f32[3,2048]{1,0:T(4,128)S(1)} %get-tuple-element.15, f32[3,2048]{1,0:T(4,128)S(1)} %get-tuple-element.16, f32[3,2048]{1,0:T(4,128)S(1)} %bitcast.51, f32[512,1,2048]{0,2,1:T(8,128)} %copy-done.4, f32[512,1,2048]{0,2,1:T(8,128)S(1)} %copy-done.3, ...), kind=kLoop, calls=%fused_computation.3 | loop fusion | flops 25165824 | bytes 44113920 | tf_op jit(solution)/shard_map/convert_element_type | solution.py:87
  258.0 14.4 %copy.39 = bf16[512,3,2048]{2,1,0:T(4,128)(2,1)} copy(bf16[512,3,2048]{0,2,1:T(8,128)(2,1)} %fusion.1) | data formatting | bytes 12582912 | tf_op jit(solution)/shard_map/convert_element_type | solution.py:87
  272.4 99.7 %all_to_all.66 = bf16[512,3,2048]{2,1,0:T(4,128)(2,1)} all-to-all(bf16[512,3,2048]{2,1,0:T(4,128)(2,1)} %copy.39), channel_id=1, replica_groups=mesh['seq'=8,'chan'=4] {'chan'}, dimensions={0} | all-to-all | bytes 12582912 | tf_op jit(solution)/shard_map/all_to_all | solution.py:88
  372.1 12.0 %copy.40 = bf16[128,3,4,2048]{3,2,0,1:T(4,128)(2,1)} copy(bf16[128,3,4,2048]{3,1,0,2:T(4,128)(2,1)} %bitcast.43) | data formatting | bytes 12582912 | tf_op jit(solution)/shard_map/all_to_all | solution.py:88
  384.1 11.0 %all_to_all.61 = bf16[128,3,8192]{2,0,1:T(8,128)(2,1)} reshape(bf16[128,3,4,2048]{3,2,0,1:T(4,128)(2,1)} %copy.40) | data formatting | bytes 12582912 | tf_op jit(solution)/shard_map/all_to_all | solution.py:88
  (4 shorter events, 0.1 us)
Async XLA Ops:
  1.7 27.7 %all-to-all-start.1 = ((bf16[512,8,16]{0,2,1:T(8,128)(2,1)}), bf16[512,8,16]{0,2,1:T(8,128)(2,1)S(1)}, u32[]{:S(2)}, u32[]{:S(2)}) async-start(bf16[512,8,16]{0,2,1:T(8,128)(2,1)} %bitcast.6), calls=%async_computation.1 | async-start | bytes 262144 | tf_op jit(solution)/shard_map/all_to_all | solution.py:72
  29.3 50.9 %all-to-all-start = ((bf16[512,8,256]{0,2,1:T(8,128)(2,1)}), bf16[512,8,256]{0,2,1:T(8,128)(2,1)S(1)}, u32[]{:S(2)}, u32[]{:S(2)}) async-start(bf16[512,8,256]{0,2,1:T(8,128)(2,1)} %bitcast.47), calls=%async_computation | async-start | bytes 4194304 | tf_op jit(solution)/shard_map/all_to_all | solution.py:71
  122.5 98.4 %all-to-all-start.2 = ((f32[8,512,256]{1,2,0:T(8,128)}), f32[8,512,256]{1,2,0:T(8,128)}, u32[]{:S(2)}, u32[]{:S(2)}) async-start(f32[8,512,256]{1,2,0:T(8,128)} %copy.34), calls=%async_computation.2 | async-start | bytes 8388608 | tf_op jit(solution)/shard_map/all_to_all | solution.py:74
  130.2 4.1 %copy-start.5 = (bf16[512,1,2048]{2,0,1:T(8,128)(2,1)S(1)}, bf16[512,1,2048]{2,0,1:T(8,128)(2,1)}, u32[]{:S(2)}) copy-start(bf16[512,1,2048]{2,0,1:T(8,128)(2,1)} %get-tuple-element.7) | copy-start | bytes 6291460
  130.2 6.6 %copy-start.6 = (f32[3,3,2048]{2,1,0:T(4,128)S(1)}, f32[3,3,2048]{2,1,0:T(4,128)}, u32[]{:S(2)}) copy-start(f32[3,3,2048]{2,1,0:T(4,128)} %param.9) | copy-start | bytes 221188
  221.0 4.9 %copy-start = (f32[512,1,2048]{0,2,1:T(8,128)S(1)}, f32[512,1,2048]{0,2,1:T(8,128)}, u32[]{:S(2)}) copy-start(f32[512,1,2048]{0,2,1:T(8,128)} %get-tuple-element.10) | copy-start | bytes 12582916
  225.8 2.1 copy-start.2
  225.8 3.2 copy-start.4
  230.6 3.7 collective-permute-start
  236.5 8.2 %copy-start.1 = (f32[512,1,2048]{0,2,1:T(8,128)S(1)}, f32[512,1,2048]{0,2,1:T(8,128)}, u32[]{:S(2)}) copy-start(f32[512,1,2048]{0,2,1:T(8,128)} %get-tuple-element.10) | copy-start | bytes 12582916
  236.5 8.2 %copy-start.3 = (f32[512,1,2048]{0,2,1:T(8,128)S(1)}, f32[512,1,2048]{0,2,1:T(8,128)}, u32[]{:S(2)}) copy-start(f32[512,1,2048]{0,2,1:T(8,128)} %copy-done.2) | copy-start | bytes 12582916

commit v2 on v1

--- a/solution.py
+++ b/solution.py
@@ -70,22 +70,27 @@
     grad_mixed = (out_wide * query.astype(jnp.float32)).astype(jnp.bfloat16)
     mixed_cols = lax.all_to_all(grad_mixed, "seq", split_axis=1, concat_axis=0, tiled=True)
     taps_cols = lax.all_to_all(long_taps, "seq", split_axis=1, concat_axis=0, tiled=True)
+    short_len = short_taps.shape[1]
+    query_proj = short_filter(grad_query[:, None], short_taps[:1], block_rows)
+    query_rows = lax.all_to_all(query_proj, "chan", split_axis=0, concat_axis=2, tiled=True)
     z_cols = correlate(mixed_cols, taps_cols)
     grad_z = lax.all_to_all(z_cols, "seq", split_axis=0, concat_axis=1, tiled=True)
     grad_key = grad_z * value_part.astype(jnp.float32)
     grad_value = grad_z * key_part.astype(jnp.float32)
-    stacked = jnp.stack([grad_query, grad_key, grad_value], 1)
-    short_len = short_taps.shape[1]
+    stacked = jnp.stack([grad_key, grad_value], 1)
+    pair_proj = short_filter(stacked, short_taps[1:], block_rows)
+    pair_rows = lax.all_to_all(pair_proj, "chan", split_axis=0, concat_axis=2, tiled=True)
+    return jnp.concatenate([query_rows, pair_rows], 1)
+
+
+def short_filter(stacked, taps, block_rows):
+    short_len = taps.shape[1]
     borrowed = shifted(stacked[: short_len - 1], "seq", -1)
     extended = jnp.concatenate([stacked, borrowed], 0)
     result = jnp.zeros_like(stacked)
     for lag_index in range(short_len):
-        result = (
-            result
-            + short_taps[:, lag_index, :][None] * extended[lag_index : lag_index + block_rows]
-        )
-    mixed = result.astype(jnp.bfloat16)
-    return lax.all_to_all(mixed, "chan", split_axis=0, concat_axis=2, tiled=True)
+        result = result + taps[:, lag_index, :][None] * extended[lag_index : lag_index + block_rows]
+    return result.astype(jnp.bfloat16)
 
 
 def solution(mesh):

time: 402 us -> 365 us (0.908)
  blocking collectives: 99.7 us -> 0 us
  other arithmetic: 33.8 us -> 60.8 us
  waiting for transfers between devices: 128 us -> 147 us
  starting transfers between devices: 20 us -> 33.8 us
  local copies, waits for them, and re-layouts: 97.6 us -> 103 us
    all_to_all x1 -> x0, blocking collectives: 99.7 us -> none  [on_device(): lax.all_to_all(mixed, 'chan', split_axis=0, concat_axis=2, tiled=True)]
    all_to_all x1, waiting for transfers between devices: 84 us -> 0.01 us  [on_device(): lax.all_to_all(z_cols, 'seq', split_axis=0, concat_axis=1, tiled=True)]
    ppermute x1 -> x2, waiting for transfers between devices: 1.67 us -> 71.6 us  [shifted(): lax.ppermute(value, axis, [(source, source + steps) for source in range(l...]
    all_to_all x0 -> x2, waiting for transfers between devices: none -> 33.3 us  [the longest x1 33.3 us: on_device(): lax.all_to_all(pair_proj, 'chan', split_axis=0, concat_axis=2, tiled=True)]
    convert_element_type x1 -> x3, other arithmetic: 13.3 us -> 34.5 us  [short_filter(): return result.astype(jnp.bfloat16)]
    mul x0 -> x1, other arithmetic: none -> 9.39 us  [short_filter(): taps[:, lag_index, :][None] * extended[lag_index:lag_index + block_rows]]
    all_to_all x0 -> x2, starting transfers between devices: none -> 9.38 us  [the longest x1 5.13 us: on_device(): lax.all_to_all(pair_proj, 'chan', split_axis=0, concat_axis=2, tiled=True)]
    unnamed x22 -> x17, local copies, waits for them, and re-layouts: 20.7 us -> 27.6 us
  transfers between devices with their start and end apart: 4 -> 7, of which waited for: 3 -> 4; matrix products, arithmetic and copies ran while one was open for 8% -> 31% of each run, Pallas kernels for 0% -> 0%
where the time goes in v2:
time: 365 us; the launch traced here: 361 us
  waiting for transfers between devices  147 us (40%)
  local copies, waits for them, and re-layouts  103 us (28%)
  other arithmetic  60.8 us (17%)
  starting transfers between devices  33.8 us (9%)
  Pallas kernels  15.7 us (4%)
    ppermute x2, waiting for transfers between devices, shifted(): lax.ppermute(value, axis, [(source, source + steps) for source in range(l...  71.6 us
    all_to_all x1, waiting for transfers between devices, on_device(): lax.all_to_all(grad_mixed, 'seq', split_axis=1, concat_axis=0, tiled=True)  42.4 us
    convert_element_type x3, other arithmetic, short_filter(): return result.astype(jnp.bfloat16)  34.5 us
    all_to_all x1, waiting for transfers between devices, on_device(): lax.all_to_all(pair_proj, 'chan', split_axis=0, concat_axis=2, tiled=True)  33.3 us
    unnamed x17, local copies, waits for them, and re-layouts  27.6 us
    pallas_call x1, Pallas kernels, correlate(): pl.pallas_call(correlate_kernel, out_shape=jax.ShapeDtypeStruct((groups,...  15.7 us
    all_to_all x2, local copies, waits for them, and re-layouts, on_device(): lax.all_to_all(pair_proj, 'chan', split_axis=0, concat_axis=2, tiled=True)  15.2 us
    all_to_all x2, local copies, waits for them, and re-layouts, on_device(): lax.all_to_all(z_cols, 'seq', split_axis=0, concat_axis=1, tiled=True)  11.8 us
  transfers between devices with their start and end apart: 7, of which 4 were waited for; matrix products, arithmetic and copies ran while one was open for 31% of the time, Pallas kernels for 0%

profile of v2, /device:TPU:18, one launch (start us, length us, event | category | flops | bytes accessed | tf_op | source)
XLA Modules:
  0.0 360.8 jit_solution(16238679817791525381)
XLA Ops:
  0.0 1.7 copy.63
  1.7 5.2 %all-to-all-start.2 = ((bf16[512,8,16]{0,2,1:T(8,128)(2,1)}), bf16[512,8,16]{0,2,1:T(8,128)(2,1)S(1)}, u32[]{:S(2)}, u32[]{:S(2)}) async-start(bf16[512,8,16]{0,2,1:T(8,128)(2,1)} %bitcast.12), calls=%async_computation.2 | async-start | bytes 262144 | tf_op jit(solution)/shard_map/all_to_all | solution.py:72
  6.9 0.9 fusion.11
  7.8 9.4 %broadcast_multiply_fusion = (f32[512,2048]{1,0:T(8,128)}, f32[512,1,2048]{2,0,1:T(8,128)}, f32[512,2048]{1,0:T(8,128)}, bf16[512,2048]{1,0:T(8,128)(2,1)S(1)}) fusion(f32[2048]{0:T(1024)S(1)} %bitcast.64, bf16[512,2048]{1,0:T(8,128)(2,1)} %param.7, bf16[512,2048]{1,0:T(8,128)(2,1)} %param.5, bf16[512,3,2048]{2,0,1:T(8,128)(2,1)} %param.6), kind=kLoop, calls=%fused_computation.24 | loop fusion | flops 7340032 | bytes 20979712 | tf_op jit(solution)/shard_map/mul | solution.py:92
  17.2 2.6 copy.74
  19.7 0.0 all-to-all-done.2
  19.7 5.1 %all-to-all-start.1 = ((bf16[512,8,256]{0,2,1:T(8,128)(2,1)}), bf16[512,8,256]{0,2,1:T(8,128)(2,1)S(1)}, u32[]{:S(2)}, u32[]{:S(2)}) async-start(bf16[512,8,256]{0,2,1:T(8,128)(2,1)} %bitcast.54), calls=%async_computation.1 | async-start | bytes 4194304 | tf_op jit(solution)/shard_map/all_to_all | solution.py:71
  24.9 2.3 rev.3
  27.2 0.1 concatenate.13
  27.2 0.9 reshape.43.h_ref
  28.1 42.4 %all-to-all-done.1 = bf16[512,8,256]{0,2,1:T(8,128)(2,1)S(1)} async-done(((bf16[512,8,256]{0,2,1:T(8,128)(2,1)}), bf16[512,8,256]{0,2,1:T(8,128)(2,1)S(1)}, u32[]{:S(2)}, u32[]{:S(2)}) %all-to-all-start.1) | async-done | bytes 2097184 | tf_op jit(solution)/shard_map/all_to_all | solution.py:71
  70.6 2.5 copy.61
  73.1 2.7 reshape.41
  75.8 2.2 copy.62
  78.0 15.7 %shard_map.55 = f32[16,256,256]{2,1,0:T(8,128)} custom-call(bf16[16,256,256]{2,1,0:T(8,128)(2,1)} %bitcast.59, f32[16,1,4352]{2,1,0:T(1,128)} %reshape.43.h_ref), custom_call_target="tpu_custom_call" | custom-call | flops 4563402752 | bytes 6569984 | tf_op jit(solution)/shard_map/pallas_call | solution.py:46
  93.7 7.4 %copy.88 = f32[16,16,16,256]{3,1,2,0:T(8,128)} copy(f32[16,16,16,256]{3,2,1,0:T(8,128)} %bitcast.58) | data formatting | bytes 8388608 | tf_op jit(solution)/shard_map/reshape | solution.py:59
  101.1 5.2 %all_to_all.71 = f32[8,512,256]{1,0,2:T(8,128)} reshape(f32[16,256,16,16]{1,0,3,2:T(8,128)} %bitcast.52) | data formatting | bytes 8388608 | tf_op jit(solution)/shard_map/all_to_all | solution.py:77
  106.3 6.6 %copy.66 = f32[8,512,256]{1,2,0:T(8,128)} copy(f32[8,512,256]{1,0,2:T(8,128)} %all_to_all.71) | data formatting | bytes 8388608 | tf_op jit(solution)/shard_map/all_to_all | solution.py:77
  112.9 7.8 %all-to-all-start.3 = ((f32[8,512,256]{1,2,0:T(8,128)}), f32[8,512,256]{1,2,0:T(8,128)}, u32[]{:S(2)}, u32[]{:S(2)}) async-start(f32[8,512,256]{1,2,0:T(8,128)} %copy.66), calls=%async_computation.3 | async-start | bytes 8388608 | tf_op jit(solution)/shard_map/all_to_all | solution.py:77
  120.6 0.8 slice_bitcast_fusion
  121.5 0.0 copy-start.2
  121.5 2.7 collective-permute-start
  124.1 4.0 %fusion.10 = (bf16[512,1,2048]{2,0,1:T(8,128)(2,1)}, bf16[512,1,2048]{2,0,1:T(8,128)(2,1)S(1)}) fusion(bf16[512,3,2048]{2,0,1:T(8,128)(2,1)} %param.6), kind=kLoop, calls=%fused_computation.32 | loop fusion | bytes 8388608 | tf_op jit(solution)/shard_map/slice | solution.py:68
  128.2 0.0 copy-done.2
  128.2 0.0 copy-start.3
  128.2 6.3 %copy_dynamic-update-slice_fusion = f32[514,1,2048]{2,1,0:T(1,128)} fusion(f32[512,1,2048]{2,0,1:T(8,128)S(1)} %copy-done.2), kind=kLoop, calls=%fused_computation.21 | loop fusion | bytes 8388608
  134.5 0.0 copy-done.3
  134.5 3.9 %copy.79 = bf16[512,1,2048]{0,2,1:T(8,128)(2,1)} copy(bf16[512,1,2048]{2,0,1:T(8,128)(2,1)} %get-tuple-element.5) | data formatting | bytes 4194304
  138.5 2.6 copy.80
  141.0 70.4 %collective-permute-done = f32[2,1,2048]{2,0,1:T(2,128)S(1)} collective-permute-done((f32[2,1,2048]{2,0,1:T(2,128)S(1)}, f32[2,1,2048]{2,0,1:T(2,128)S(1)}, u32[]{:S(2)}, u32[]{:S(2)}) %collective-permute-start) | collective-permute-done | bytes 16416 | tf_op jit(solution)/shard_map/ppermute | solution.py:17
  211.4 0.6 copy_dynamic-update-slice_fusion.1
  212.0 11.2 %fusion.7 = bf16[512,1,2048]{2,1,0:T(2,128)(2,1)} fusion(f32[514,1,2048]{2,1,0:T(1,128)} %copy_dynamic-update-slice_fusion.1, f32[512,2048]{1,0:T(8,128)} %get-tuple-element.7, f32[2048]{0:T(1024)S(1)} %bitcast.63, f32[2048]{0:T(1024)S(1)} %bitcast.62), kind=kLoop, calls=%fused_computation.22 | loop fusion | flops 5242880 | bytes 14696448 | tf_op jit(solution)/shard_map/convert_element_type | solution.py:93
  223.2 0.5 broadcast.6
  223.7 13.2 %reduce = bf16[512,2048]{1,0:T(8,128)(2,1)S(1)} reduce(bf16[512,1,2048]{2,1,0:T(2,128)(2,1)} %fusion.7, bf16[]{:T(256)} %broadcast.6), dimensions={1}, to_apply=%fusion.7.reduce_sub_computation | reduce | bytes 4194306 | tf_op jit(solution)/shard_map/convert_element_type | solution.py:93
  236.9 2.8 reshape.47
  239.7 0.0 all-to-all-done.3
  239.7 4.3 %all-to-all-start = ((bf16[4,2,131072]{2,1,0:T(2,128)(2,1)}), bf16[4,2,131072]{2,1,0:T(2,128)(2,1)S(1)}, u32[]{:S(2)}, u32[]{:S(2)}) async-start(bf16[4,2,131072]{2,1,0:T(2,128)(2,1)} %reshape.47), calls=%async_computation | async-start | bytes 4194304 | tf_op jit(solution)/shard_map/all_to_all | solution.py:75
  243.9 4.7 %bitcast_multiply_fusion.1 = (f32[512,1,2048]{0,2,1:T(8,128)S(1)}, f32[512,1,2048]{0,2,1:T(8,128)S(1)}) fusion(f32[8,512,256]{1,2,0:T(8,128)} %all-to-all-done.3, bf16[512,1,2048]{0,2,1:T(8,128)(2,1)} %copy.79, bf16[512,1,2048]{0,2,1:T(8,128)(2,1)} %copy.80), kind=kLoop, calls=%fused_computation.19 | loop fusion | flops 4194304 | bytes 16777216 | tf_op jit(solution)/shard_map/mul | solution.py:78
  248.7 0.0 copy-start
  248.7 0.0 copy-start.1
  248.7 2.0 copy-done
  250.7 1.3 copy-done.1
  252.0 1.6 fusion.8
  253.7 2.2 copy.69
  255.9 3.7 %collective-permute-start.1 = (f32[2,2,2048]{2,1,0:T(2,128)S(1)}, f32[2,2,2048]{2,1,0:T(2,128)S(1)}, u32[]{:S(2)}, u32[]{:S(2)}) collective-permute-start(f32[2,2,2048]{2,1,0:T(2,128)S(1)} %copy.69), channel_id=1, source_target_pairs={{4,0},{8,4},{12,8},{16,12},{20,16},{24,20},{28,24},{5,1},{9,5},{13... | collective-permute-start | bytes 98312 | tf_op jit(solution)/shard_map/ppermute | solution.py:17
  259.6 1.3 collective-permute-done.1
  260.9 2.0 copy.70
  262.9 5.1 %pad_maximum_fusion = f32[514,2,2048]{0,2,1:T(8,128)S(1)} fusion(f32[2,2,2048]{0,2,1:T(8,128)} %copy.70, f32[512,1,2048]{0,2,1:T(8,128)} %copy-done.1, f32[512,1,2048]{0,2,1:T(8,128)} %copy-done), kind=kLoop, calls=%fused_computation | loop fusion | flops 4210688 | bytes 16842752 | tf_op jit(solution)/shard_map/concatenate | solution.py:89
  268.0 10.1 %fusion.3 = bf16[512,2,2048]{0,2,1:T(8,128)(2,1)} fusion(f32[512,1,2048]{0,2,1:T(8,128)} %copy-done.1, f32[512,1,2048]{0,2,1:T(8,128)} %copy-done, f32[514,2,2048]{0,2,1:T(8,128)S(1)} %pad_maximum_fusion, f32[2,2048]{1,0:T(2,128)S(1)} %get-tuple-element.19, f32[2,2048]{1,0:T(2,128)S(1)} %get-tuple-element.20, f32[2,2048]{1,0:T(2,128)S(1)} %bitcast.61), kind=kLoop, calls=%fused_computation.7 | loop fusion | flops 14680064 | bytes 29409280 | tf_op jit(solution)/shard_map/convert_element_type | solution.py:93
  278.1 11.3 %copy.71 = bf16[512,2,2048]{2,1,0:T(2,128)(2,1)} copy(bf16[512,2,2048]{0,2,1:T(8,128)(2,1)} %fusion.3) | data formatting | bytes 8388608 | tf_op jit(solution)/shard_map/convert_element_type | solution.py:93
  289.4 0.0 all-to-all-done
  289.4 5.1 %all-to-all-start.4 = ((bf16[512,2,2048]{2,1,0:T(2,128)(2,1)}), bf16[512,2,2048]{2,1,0:T(2,128)(2,1)}, u32[]{:S(2)}, u32[]{:S(2)}) async-start(bf16[512,2,2048]{2,1,0:T(2,128)(2,1)} %copy.71), calls=%async_computation.4 | async-start | bytes 8388608 | tf_op jit(solution)/shard_map/all_to_all | solution.py:82
  294.5 3.4 reshape.48
  297.9 3.5 copy.75
  301.4 2.6 copy.59
  303.9 2.9 copy.73
  306.9 33.3 %all-to-all-done.4 = bf16[512,2,2048]{2,1,0:T(2,128)(2,1)} async-done(((bf16[512,2,2048]{2,1,0:T(2,128)(2,1)}), bf16[512,2,2048]{2,1,0:T(2,128)(2,1)}, u32[]{:S(2)}, u32[]{:S(2)}) %all-to-all-start.4) | async-done | bytes 4194336 | tf_op jit(solution)/shard_map/all_to_all | solution.py:82
  340.1 7.5 %copy.72 = bf16[128,2,4,2048]{3,2,0,1:T(4,128)(2,1)} copy(bf16[128,2,4,2048]{3,1,0,2:T(2,128)(2,1)} %bitcast.21) | data formatting | bytes 8388608 | tf_op jit(solution)/shard_map/all_to_all | solution.py:82
  347.6 7.7 %all_to_all.78 = bf16[128,2,8192]{2,0,1:T(8,128)(2,1)} reshape(bf16[128,2,4,2048]{3,2,0,1:T(4,128)(2,1)} %copy.72) | data formatting | bytes 8388608 | tf_op jit(solution)/shard_map/all_to_all | solution.py:82
  355.3 5.4 %pad_maximum_fusion.2 = bf16[128,3,8192]{2,0,1:T(8,128)(2,1)} fusion(bf16[128,2,8192]{2,0,1:T(8,128)(2,1)} %all_to_all.78, bf16[128,1,8192]{2,0,1:T(8,128)(2,1)S(1)} %copy.73), kind=kLoop, calls=%fused_computation.10 | loop fusion | flops 3145728 | bytes 12582912 | tf_op jit(solution)/shard_map/concatenate | solution.py:83
  (5 shorter events, 0.1 us)
Async XLA Ops:
  1.7 18.1 %all-to-all-start.2 = ((bf16[512,8,16]{0,2,1:T(8,128)(2,1)}), bf16[512,8,16]{0,2,1:T(8,128)(2,1)S(1)}, u32[]{:S(2)}, u32[]{:S(2)}) async-start(bf16[512,8,16]{0,2,1:T(8,128)(2,1)} %bitcast.12), calls=%async_computation.2 | async-start | bytes 262144 | tf_op jit(solution)/shard_map/all_to_all | solution.py:72
  19.7 50.9 %all-to-all-start.1 = ((bf16[512,8,256]{0,2,1:T(8,128)(2,1)}), bf16[512,8,256]{0,2,1:T(8,128)(2,1)S(1)}, u32[]{:S(2)}, u32[]{:S(2)}) async-start(bf16[512,8,256]{0,2,1:T(8,128)(2,1)} %bitcast.54), calls=%async_computation.1 | async-start | bytes 4194304 | tf_op jit(solution)/shard_map/all_to_all | solution.py:71
  112.9 126.8 %all-to-all-start.3 = ((f32[8,512,256]{1,2,0:T(8,128)}), f32[8,512,256]{1,2,0:T(8,128)}, u32[]{:S(2)}, u32[]{:S(2)}) async-start(f32[8,512,256]{1,2,0:T(8,128)} %copy.66), calls=%async_computation.3 | async-start | bytes 8388608 | tf_op jit(solution)/shard_map/all_to_all | solution.py:77
  121.5 6.7 %copy-start.2 = (f32[512,1,2048]{2,0,1:T(8,128)S(1)}, f32[512,1,2048]{2,0,1:T(8,128)}, u32[]{:S(2)}) copy-start(f32[512,1,2048]{2,0,1:T(8,128)} %get-tuple-element.8) | copy-start | bytes 12582916
  121.5 89.9 %collective-permute-start = (f32[2,1,2048]{2,0,1:T(2,128)S(1)}, f32[2,1,2048]{2,0,1:T(2,128)S(1)}, u32[]{:S(2)}, u32[]{:S(2)}) collective-permute-start(f32[2,1,2048]{2,0,1:T(2,128)S(1)} %slice_bitcast_fusion), channel_id=1, source_target_pairs={{4,0},{8,4},{12,8},{16,12},{20,16},{24,20},{28,24},{5,1},{9,5},{13... | collective-permute-start | bytes 49160 | tf_op jit(solution)/shard_map/ppermute | solution.py:17
  128.2 6.3 %copy-start.3 = (f32[3,3,2048]{2,1,0:T(4,128)S(1)}, f32[3,3,2048]{2,1,0:T(4,128)}, u32[]{:S(2)}) copy-start(f32[3,3,2048]{2,1,0:T(4,128)} %param.9) | copy-start | bytes 221188
  239.7 49.7 %all-to-all-start = ((bf16[4,2,131072]{2,1,0:T(2,128)(2,1)}), bf16[4,2,131072]{2,1,0:T(2,128)(2,1)S(1)}, u32[]{:S(2)}, u32[]{:S(2)}) async-start(bf16[4,2,131072]{2,1,0:T(2,128)(2,1)} %reshape.47), calls=%async_computation | async-start | bytes 4194304 | tf_op jit(solution)/shard_map/all_to_all | solution.py:75
  248.7 2.0 copy-start
  248.7 3.4 copy-start.1
  255.9 5.0 %collective-permute-start.1 = (f32[2,2,2048]{2,1,0:T(2,128)S(1)}, f32[2,2,2048]{2,1,0:T(2,128)S(1)}, u32[]{:S(2)}, u32[]{:S(2)}) collective-permute-start(f32[2,2,2048]{2,1,0:T(2,128)S(1)} %copy.69), channel_id=1, source_target_pairs={{4,0},{8,4},{12,8},{16,12},{20,16},{24,20},{28,24},{5,1},{9,5},{13... | collective-permute-start | bytes 98312 | tf_op jit(solution)/shard_map/ppermute | solution.py:17
  289.4 50.7 %all-to-all-start.4 = ((bf16[512,2,2048]{2,1,0:T(2,128)(2,1)}), bf16[512,2,2048]{2,1,0:T(2,128)(2,1)}, u32[]{:S(2)}, u32[]{:S(2)}) async-start(bf16[512,2,2048]{2,1,0:T(2,128)(2,1)} %copy.71), calls=%async_computation.4 | async-start | bytes 8388608 | tf_op jit(solution)/shard_map/all_to_all | solution.py:82

commit v3 on v2

--- a/solution.py
+++ b/solution.py
@@ -72,15 +72,31 @@
     taps_cols = lax.all_to_all(long_taps, "seq", split_axis=1, concat_axis=0, tiled=True)
     short_len = short_taps.shape[1]
     query_proj = short_filter(grad_query[:, None], short_taps[:1], block_rows)
-    query_rows = lax.all_to_all(query_proj, "chan", split_axis=0, concat_axis=2, tiled=True)
+    query_rows = spread_rows(query_proj, "chan")
     z_cols = correlate(mixed_cols, taps_cols)
     grad_z = lax.all_to_all(z_cols, "seq", split_axis=0, concat_axis=1, tiled=True)
     grad_key = grad_z * value_part.astype(jnp.float32)
     grad_value = grad_z * key_part.astype(jnp.float32)
     stacked = jnp.stack([grad_key, grad_value], 1)
     pair_proj = short_filter(stacked, short_taps[1:], block_rows)
-    pair_rows = lax.all_to_all(pair_proj, "chan", split_axis=0, concat_axis=2, tiled=True)
+    pair_rows = spread_rows(pair_proj, "chan")
     return jnp.concatenate([query_rows, pair_rows], 1)
+
+
+def spread_rows(value, axis):
+    count = lax.axis_size(axis)
+    me = lax.axis_index(axis)
+    rows, planes, channels = value.shape
+    chunks = value.reshape(count, rows // count, planes, channels)
+    pieces = [lax.dynamic_index_in_dim(chunks, me, 0, keepdims=False)]
+    for step in range(1, count):
+        outgoing = lax.dynamic_index_in_dim(chunks, (me + step) % count, 0, keepdims=False)
+        pairs = [(source, (source + step) % count) for source in range(count)]
+        pieces.append(lax.ppermute(outgoing, axis, pairs))
+    gathered = jnp.stack(pieces)
+    order = (me - jnp.arange(count)) % count
+    placed = jnp.take(gathered, order, axis=0)
+    return placed.transpose(1, 2, 0, 3).reshape(rows // count, planes, count * channels)
 
 
 def short_filter(stacked, taps, block_rows):

time: 365 us -> 344 us (0.942)
  local copies, waits for them, and re-layouts: 103 us -> 87.8 us
  other arithmetic: 60.8 us -> 51 us
  waiting for transfers between devices: 147 us -> 154 us
    ppermute x0 -> x6, waiting for transfers between devices: none -> 34.2 us  [spread_rows(): pieces.append(lax.ppermute(outgoing, axis, pairs))]
    all_to_all x2 -> x0, waiting for transfers between devices: 33.3 us -> none  [the longest x1 33.3 us: on_device(): lax.all_to_all(pair_proj, 'chan', split_axis=0, concat_axis=2, tiled=True)]
    all_to_all x4 -> x0, local copies, waits for them, and re-layouts: 20.7 us -> none  [the longest x2 15.2 us: on_device(): lax.all_to_all(pair_proj, 'chan', split_axis=0, concat_axis=2, tiled=True)]
    convert_element_type x3 -> x2, other arithmetic: 34.5 us -> 17 us  [short_filter(): return result.astype(jnp.bfloat16)]
    unnamed x17 -> x18, local copies, waits for them, and re-layouts: 27.6 us -> 15.5 us
    all_to_all x2 -> x0, starting transfers between devices: 9.38 us -> none  [the longest x1 5.13 us: on_device(): lax.all_to_all(pair_proj, 'chan', split_axis=0, concat_axis=2, tiled=True)]
    concatenate x1, local copies, waits for them, and re-layouts: 0.62 us -> 8.62 us  [on_device(): return jnp.concatenate([query_rows, pair_rows], 1)]
    ppermute x0 -> x6, starting transfers between devices: none -> 7.88 us  [spread_rows(): pieces.append(lax.ppermute(outgoing, axis, pairs))]
  transfers between devices with their start and end apart: 7 -> 11, of which waited for: 4 -> 4; matrix products, arithmetic and copies ran while one was open for 31% -> 20% of each run, Pallas kernels for 0% -> 0%
where the time goes in v3:
time: 344 us; the launch traced here: 341 us
  waiting for transfers between devices  154 us (45%)
  local copies, waits for them, and re-layouts  87.8 us (26%)
  other arithmetic  51 us (15%)
  starting transfers between devices  32.2 us (9%)
  Pallas kernels  15.7 us (5%)
    ppermute x2, waiting for transfers between devices, shifted(): lax.ppermute(value, axis, [(source, source + steps) for source in range(l...  77 us
    all_to_all x1, waiting for transfers between devices, on_device(): lax.all_to_all(grad_mixed, 'seq', split_axis=1, concat_axis=0, tiled=True)  42.4 us
    ppermute x6, waiting for transfers between devices, spread_rows(): pieces.append(lax.ppermute(outgoing, axis, pairs))  34.2 us
    convert_element_type x2, other arithmetic, short_filter(): return result.astype(jnp.bfloat16)  17 us
    pallas_call x1, Pallas kernels, correlate(): pl.pallas_call(correlate_kernel, out_shape=jax.ShapeDtypeStruct((groups,...  15.7 us
    unnamed x18, local copies, waits for them, and re-layouts  15.5 us
    all_to_all x2, local copies, waits for them, and re-layouts, on_device(): lax.all_to_all(z_cols, 'seq', split_axis=0, concat_axis=1, tiled=True)  11.9 us
    concatenate x1, local copies, waits for them, and re-layouts, on_device(): return jnp.concatenate([query_rows, pair_rows], 1)  8.62 us
  transfers between devices with their start and end apart: 11, of which 4 were waited for; matrix products, arithmetic and copies ran while one was open for 20% of the time, Pallas kernels for 0%

profile of v3, /device:TPU:18, one launch (start us, length us, event | category | flops | bytes accessed | tf_op | source)
XLA Modules:
  0.0 340.5 jit_solution(7569270979688712432)
XLA Ops:
  0.0 1.7 copy.29
  1.7 5.2 %all-to-all-start.1 = ((bf16[512,8,16]{0,2,1:T(8,128)(2,1)}), bf16[512,8,16]{0,2,1:T(8,128)(2,1)S(1)}, u32[]{:S(2)}, u32[]{:S(2)}) async-start(bf16[512,8,16]{0,2,1:T(8,128)(2,1)} %bitcast.23), calls=%async_computation.1 | async-start | bytes 262144 | tf_op jit(solution)/shard_map/all_to_all | solution.py:72
  6.9 7.8 %convert_multiply_fusion.1 = (f32[512,2048]{1,0:T(8,128)}, f32[512,1,2048]{2,0,1:T(8,128)}, bf16[512,2048]{1,0:T(8,128)(2,1)S(1)}) fusion(bf16[512,2048]{1,0:T(8,128)(2,1)} %param.5, bf16[512,2048]{1,0:T(8,128)(2,1)} %param.7, bf16[512,3,2048]{2,0,1:T(8,128)(2,1)} %param.6), kind=kLoop, calls=%fused_computation.14 | loop fusion | flops 6291456 | bytes 16777216 | tf_op jit(solution)/shard_map/mul | solution.py:69
  14.7 2.5 copy.26
  17.2 0.0 all-to-all-done.1
  17.2 5.1 %all-to-all-start = ((bf16[512,8,256]{0,2,1:T(8,128)(2,1)}), bf16[512,8,256]{0,2,1:T(8,128)(2,1)S(1)}, u32[]{:S(2)}, u32[]{:S(2)}) async-start(bf16[512,8,256]{0,2,1:T(8,128)(2,1)} %bitcast.19), calls=%async_computation | async-start | bytes 4194304 | tf_op jit(solution)/shard_map/all_to_all | solution.py:71
  22.4 2.3 rev.3
  24.6 0.1 concatenate.13
  24.7 0.9 reshape.119.h_ref
  25.6 42.4 %all-to-all-done = bf16[512,8,256]{0,2,1:T(8,128)(2,1)S(1)} async-done(((bf16[512,8,256]{0,2,1:T(8,128)(2,1)}), bf16[512,8,256]{0,2,1:T(8,128)(2,1)S(1)}, u32[]{:S(2)}, u32[]{:S(2)}) %all-to-all-start) | async-done | bytes 2097184 | tf_op jit(solution)/shard_map/all_to_all | solution.py:71
  68.1 2.5 copy.27
  70.6 2.7 reshape.117
  73.3 2.3 copy.28
  75.5 15.7 %shard_map.55 = f32[16,256,256]{2,1,0:T(8,128)} custom-call(bf16[16,256,256]{2,1,0:T(8,128)(2,1)} %bitcast.89, f32[16,1,4352]{2,1,0:T(1,128)} %reshape.119.h_ref), custom_call_target="tpu_custom_call" | custom-call | flops 4563402752 | bytes 6569984 | tf_op jit(solution)/shard_map/pallas_call | solution.py:46
  91.2 7.4 %copy.52 = f32[16,16,16,256]{3,1,2,0:T(8,128)} copy(f32[16,16,16,256]{3,2,1,0:T(8,128)} %bitcast.88) | data formatting | bytes 8388608 | tf_op jit(solution)/shard_map/reshape | solution.py:59
  98.7 5.3 %all_to_all.41 = f32[8,512,256]{1,0,2:T(8,128)} reshape(f32[16,256,16,16]{1,0,3,2:T(8,128)} %bitcast.83) | data formatting | bytes 8388608 | tf_op jit(solution)/shard_map/all_to_all | solution.py:77
  104.0 6.6 %copy.32 = f32[8,512,256]{1,2,0:T(8,128)} copy(f32[8,512,256]{1,0,2:T(8,128)} %all_to_all.41) | data formatting | bytes 8388608 | tf_op jit(solution)/shard_map/all_to_all | solution.py:77
  110.5 7.9 %all-to-all-start.2 = ((f32[8,512,256]{1,2,0:T(8,128)}), f32[8,512,256]{1,2,0:T(8,128)}, u32[]{:S(2)}, u32[]{:S(2)}) async-start(f32[8,512,256]{1,2,0:T(8,128)} %copy.32), calls=%async_computation.2 | async-start | bytes 8388608 | tf_op jit(solution)/shard_map/all_to_all | solution.py:77
  118.4 0.8 slice_bitcast_fusion
  119.2 2.4 collective-permute-start
  121.7 4.0 %fusion.17 = (bf16[512,1,2048]{2,0,1:T(8,128)(2,1)}, bf16[512,1,2048]{2,0,1:T(8,128)(2,1)S(1)}) fusion(bf16[512,3,2048]{2,0,1:T(8,128)(2,1)} %param.6), kind=kLoop, calls=%fused_computation.61 | loop fusion | bytes 8388608 | tf_op jit(solution)/shard_map/slice | solution.py:68
  125.8 3.9 %copy.44 = bf16[512,1,2048]{0,2,1:T(8,128)(2,1)} copy(bf16[512,1,2048]{2,0,1:T(8,128)(2,1)} %get-tuple-element.5) | data formatting | bytes 4194304
  129.7 2.5 copy.45
  132.2 77.0 %collective-permute-done = f32[2,1,2048]{2,0,1:T(2,128)S(1)} collective-permute-done((f32[2,1,2048]{2,0,1:T(2,128)S(1)}, f32[2,1,2048]{2,0,1:T(2,128)S(1)}, u32[]{:S(2)}, u32[]{:S(2)}) %collective-permute-start) | collective-permute-done | bytes 16416 | tf_op jit(solution)/shard_map/ppermute | solution.py:17
  209.2 6.8 %fusion.8 = bf16[512,1,2048]{2,0,1:T(8,128)(2,1)} fusion(f32[512,1,2048]{2,0,1:T(8,128)} %get-tuple-element.8, f32[2,1,2048]{2,0,1:T(2,128)S(1)} %collective-permute-done, f32[2048]{0:T(1024)S(1)} %bitcast.93, f32[2048]{0:T(1024)S(1)} %bitcast.94, f32[2048]{0:T(1024)S(1)} %bitcast.92, bf16[512,2048]{1,0:T(8,128)(2,1)} %param.7, bf16[512,2048]{1,0:T(8,128)(2,1)} %param.5), kind=kLoop, calls=%fused_computation.21 | loop fusion | flops 11534336 | bytes 10526720 | tf_op jit(solution)/shard_map/convert_element_type | solution.py:109
  216.0 0.0 all-to-all-done.2
  216.0 4.2 %bitcast_multiply_fusion.1 = (f32[512,1,2048]{0,2,1:T(8,128)S(1)}, f32[512,1,2048]{0,2,1:T(8,128)S(1)}) fusion(f32[8,512,256]{1,2,0:T(8,128)} %all-to-all-done.2, bf16[512,1,2048]{0,2,1:T(8,128)(2,1)S(1)} %copy-done.3, bf16[512,1,2048]{0,2,1:T(8,128)(2,1)} %copy.45), kind=kLoop, calls=%fused_computation.27 | loop fusion | flops 4194304 | bytes 16777216 | tf_op jit(solution)/shard_map/mul | solution.py:78
  220.1 0.0 copy-start.1
  220.2 1.9 copy-done
  222.1 1.4 copy-done.1
  223.5 0.3 fusion.11
  223.8 0.6 copy.35
  224.4 3.8 %collective-permute-start.4 = (f32[2,2,2048]{2,1,0:T(2,128)S(1)}, f32[2,2,2048]{2,1,0:T(2,128)S(1)}, u32[]{:S(2)}, u32[]{:S(2)}) collective-permute-start(f32[2,2,2048]{2,1,0:T(2,128)S(1)} %copy.35), channel_id=1, source_target_pairs={{4,0},{8,4},{12,8},{16,12},{20,16},{24,20},{28,24},{5,1},{9,5},{13... | collective-permute-start | bytes 98312 | tf_op jit(solution)/shard_map/ppermute | solution.py:17
  228.3 3.0 constant_dynamic-slice_fusion
  231.2 0.5 collective-permute-start.3
  231.8 1.5 collective-permute-start.2
  233.3 2.4 collective-permute-start.1
  235.7 0.0 collective-permute-done.4
  235.7 0.6 copy.36
  236.3 4.5 %pad_maximum_fusion = f32[514,2,2048]{0,2,1:T(8,128)S(1)} fusion(f32[2,2,2048]{0,2,1:T(8,128)S(1)} %copy.36, f32[512,1,2048]{0,2,1:T(8,128)} %copy-done.1, f32[512,1,2048]{0,2,1:T(8,128)} %copy-done), kind=kLoop, calls=%fused_computation.2 | loop fusion | flops 4210688 | bytes 16842752 | tf_op jit(solution)/shard_map/concatenate | solution.py:105
  240.8 10.2 %fusion.3 = bf16[512,2,2048]{0,2,1:T(8,128)(2,1)} fusion(f32[512,1,2048]{0,2,1:T(8,128)} %copy-done.1, f32[512,1,2048]{0,2,1:T(8,128)} %copy-done, f32[514,2,2048]{0,2,1:T(8,128)S(1)} %pad_maximum_fusion, f32[2,2048]{1,0:T(2,128)S(1)} %get-tuple-element.26, f32[2,2048]{1,0:T(2,128)S(1)} %get-tuple-element.27, f32[2,2048]{1,0:T(2,128)S(1)} %bitcast.91), kind=kLoop, calls=%fused_computation.9 | loop fusion | flops 14680064 | bytes 29409280 | tf_op jit(solution)/shard_map/convert_element_type | solution.py:109
  251.0 6.2 %copy.37 = bf16[512,2,2048]{2,0,1:T(8,128)(2,1)} copy(bf16[512,2,2048]{0,2,1:T(8,128)(2,1)} %fusion.3) | data formatting | bytes 8388608 | tf_op jit(solution)/shard_map/convert_element_type | solution.py:109
  257.2 4.0 %dynamic-slice_bitcast_fusion.3 = (bf16[1,128,2,2048]{3,1,2,0:T(8,128)(2,1)S(1)}, bf16[128,2,2048]{2,0,1:T(8,128)(2,1)}, bf16[128,2,2048]{2,0,1:T(8,128)(2,1)}, bf16[128,2,2048]{2,0,1:T(8,128)(2,1)}) fusion(bf16[4,128,2,2048]{3,1,0,2:T(8,128)(2,1)} %bitcast.82, s32[]{:T(128)S(6)} %select_n.98, s32[]{:T(128)S(6)} %select_n.104, s32[]{:T(128)S(6)} %select_n.102, ...), kind=kLoop, calls=%fused_computation.37 | loop fusion | bytes 8388624
  261.3 0.0 collective-permute-start.7
  261.3 0.6 collective-permute-start.6
  261.8 0.0 collective-permute-done.3
  261.8 2.9 collective-permute-start.5
  264.7 0.0 collective-permute-done.2
  264.7 0.0 collective-permute-done.1
  264.7 0.0 copy-done.4
  264.8 1.6 maximum_bitcast_fusion
  266.4 2.0 gather_fusion
  268.4 1.9 fusion.12
  270.2 2.5 copy.25
  272.7 15.8 %collective-permute-done.7 = bf16[128,2,2048]{2,0,1:T(8,128)(2,1)} collective-permute-done((bf16[128,2,2048]{2,0,1:T(8,128)(2,1)}, bf16[128,2,2048]{2,0,1:T(8,128)(2,1)}, u32[]{:S(2)}, u32[]{:S(2)}) %collective-permute-start.7) | collective-permute-done | bytes 1048608 | tf_op jit(solution)/shard_map/ppermute | solution.py:95
  288.5 18.4 %collective-permute-done.6 = bf16[128,2,2048]{2,0,1:T(8,128)(2,1)} collective-permute-done((bf16[128,2,2048]{2,0,1:T(8,128)(2,1)}, bf16[128,2,2048]{2,0,1:T(8,128)(2,1)}, u32[]{:S(2)}, u32[]{:S(2)}) %collective-permute-start.6) | collective-permute-done | bytes 1048608 | tf_op jit(solution)/shard_map/ppermute | solution.py:95
  306.9 0.0 collective-permute-done.5
  306.9 3.6 %pad_maximum_fusion.4 = bf16[4,128,2,2048]{3,1,2,0:T(8,128)(2,1)} fusion(bf16[1,128,2,2048]{3,1,2,0:T(8,128)(2,1)} %bitcast.37, bf16[1,128,2,2048]{3,1,2,0:T(8,128)(2,1)} %bitcast.35, bf16[1,128,2,2048]{3,1,2,0:T(8,128)(2,1)} %bitcast.33, bf16[1,128,2,2048]{3,1,2,0:T(8,128)(2,1)S(1)} %get-tuple-element.9), kind=kLoop, calls=%fused_computation.25 | loop fusion | flops 6291456 | bytes 8388608 | tf_op jit(solution)/shard_map/stack | solution.py:96
  310.5 5.0 %gather_fusion.1 = bf16[4,128,2,2048]{3,1,2,0:T(8,128)(2,1)} fusion(bf16[4,128,2,2048]{3,1,2,0:T(8,128)(2,1)} %pad_maximum_fusion.4, s32[1024]{0:T(1024)S(1)} %pad_clamp_fusion), kind=kCustom, calls=%fused_computation.1 | custom fusion | bytes 8388624 | tf_op jit(solution)/shard_map/jit(_take)/gather | solution.py:98
  315.5 4.7 %select_bitcast_fusion = bf16[128,2,4,2048]{3,0,1,2:T(8,128)(2,1)} fusion(bf16[4,128,2,2048]{3,1,2,0:T(8,128)(2,1)} %gather_fusion.1, pred[4]{0:T(512)(128)(4,1)S(1)} %compare_and_fusion), kind=kLoop, calls=%fused_computation.29 | loop fusion | flops 2097152 | bytes 8388612 | tf_op jit(solution)/shard_map/jit(_take)/select_n | solution.py:98
  320.1 6.4 %copy.39 = bf16[128,2,4,2048]{0,3,2,1:T(8,128)(2,1)} copy(bf16[128,2,4,2048]{3,0,1,2:T(8,128)(2,1)} %select_bitcast_fusion) | data formatting | bytes 8388608 | tf_op jit(solution)/shard_map/jit(_take)/select_n | solution.py:98
  326.5 0.0 copy-done.2
  326.5 5.4 %pad_maximum_fusion.2 = bf16[128,3,8192]{0,2,1:T(8,128)(2,1)} fusion(bf16[128,2,8192]{0,2,1:T(8,128)(2,1)} %bitcast.81, bf16[128,1,8192]{0,2,1:T(8,128)(2,1)S(1)} %bitcast.86), kind=kLoop, calls=%fused_computation.12 | loop fusion | flops 3145728 | bytes 12582912 | tf_op jit(solution)/shard_map/concatenate | solution.py:83
  331.9 8.6 %copy.40 = bf16[128,3,8192]{2,0,1:T(8,128)(2,1)} copy(bf16[128,3,8192]{0,2,1:T(8,128)(2,1)} %pad_maximum_fusion.2) | data formatting | bytes 12582912 | tf_op jit(solution)/shard_map/concatenate | solution.py:83
  (16 shorter events, 0.2 us)
Async XLA Ops:
  1.7 15.6 %all-to-all-start.1 = ((bf16[512,8,16]{0,2,1:T(8,128)(2,1)}), bf16[512,8,16]{0,2,1:T(8,128)(2,1)S(1)}, u32[]{:S(2)}, u32[]{:S(2)}) async-start(bf16[512,8,16]{0,2,1:T(8,128)(2,1)} %bitcast.23), calls=%async_computation.1 | async-start | bytes 262144 | tf_op jit(solution)/shard_map/all_to_all | solution.py:72
  17.2 50.9 %all-to-all-start = ((bf16[512,8,256]{0,2,1:T(8,128)(2,1)}), bf16[512,8,256]{0,2,1:T(8,128)(2,1)S(1)}, u32[]{:S(2)}, u32[]{:S(2)}) async-start(bf16[512,8,256]{0,2,1:T(8,128)(2,1)} %bitcast.19), calls=%async_computation | async-start | bytes 4194304 | tf_op jit(solution)/shard_map/all_to_all | solution.py:71
  110.5 11.1 %copy-start.5 = (f32[3,3,2048]{2,1,0:T(4,128)S(1)}, f32[3,3,2048]{2,1,0:T(4,128)}, u32[]{:S(2)}) copy-start(f32[3,3,2048]{2,1,0:T(4,128)} %param.9) | copy-start | bytes 221188
  110.5 105.4 %all-to-all-start.2 = ((f32[8,512,256]{1,2,0:T(8,128)}), f32[8,512,256]{1,2,0:T(8,128)}, u32[]{:S(2)}, u32[]{:S(2)}) async-start(f32[8,512,256]{1,2,0:T(8,128)} %copy.32), calls=%async_computation.2 | async-start | bytes 8388608 | tf_op jit(solution)/shard_map/all_to_all | solution.py:77
  119.2 89.9 %collective-permute-start = (f32[2,1,2048]{2,0,1:T(2,128)S(1)}, f32[2,1,2048]{2,0,1:T(2,128)S(1)}, u32[]{:S(2)}, u32[]{:S(2)}) collective-permute-start(f32[2,1,2048]{2,0,1:T(2,128)S(1)} %slice_bitcast_fusion), channel_id=1, source_target_pairs={{4,0},{8,4},{12,8},{16,12},{20,16},{24,20},{28,24},{5,1},{9,5},{13... | collective-permute-start | bytes 49160 | tf_op jit(solution)/shard_map/ppermute | solution.py:17
  209.2 6.8 %copy-start.3 = (bf16[512,1,2048]{0,2,1:T(8,128)(2,1)S(1)}, bf16[512,1,2048]{0,2,1:T(8,128)(2,1)}, u32[]{:S(2)}) copy-start(bf16[512,1,2048]{0,2,1:T(8,128)(2,1)} %copy.44) | copy-start | bytes 6291460
  220.1 2.0 copy-start
  220.1 3.4 copy-start.1
  224.4 11.2 %collective-permute-start.4 = (f32[2,2,2048]{2,1,0:T(2,128)S(1)}, f32[2,2,2048]{2,1,0:T(2,128)S(1)}, u32[]{:S(2)}, u32[]{:S(2)}) collective-permute-start(f32[2,2,2048]{2,1,0:T(2,128)S(1)} %copy.35), channel_id=1, source_target_pairs={{4,0},{8,4},{12,8},{16,12},{20,16},{24,20},{28,24},{5,1},{9,5},{13... | collective-permute-start | bytes 98312 | tf_op jit(solution)/shard_map/ppermute | solution.py:17
  231.2 30.6 %collective-permute-start.3 = (bf16[128,1,2048]{2,0,1:T(8,128)(2,1)}, bf16[128,1,2048]{2,0,1:T(8,128)(2,1)}, u32[]{:S(2)}, u32[]{:S(2)}) collective-permute-start(bf16[128,1,2048]{2,0,1:T(8,128)(2,1)} %get-tuple-element.16), channel_id=1, source_target_pairs={{0,3},{1,0},{2,1},{3,2},{4,7},{5,4},{6,5},{7,6},{8,11},{9,8},{10,9... | collective-permute-start | bytes 1572872 | tf_op jit(solution)/shard_map/ppermute | solution.py:95
  231.8 33.0 %collective-permute-start.2 = (bf16[128,1,2048]{2,0,1:T(8,128)(2,1)}, bf16[128,1,2048]{2,0,1:T(8,128)(2,1)}, u32[]{:S(2)}, u32[]{:S(2)}) collective-permute-start(bf16[128,1,2048]{2,0,1:T(8,128)(2,1)} %get-tuple-element.17), channel_id=1, source_target_pairs={{0,2},{1,3},{2,0},{3,1},{4,6},{5,7},{6,4},{7,5},{8,10},{9,11},{10,... | collective-permute-start | bytes 1572872 | tf_op jit(solution)/shard_map/ppermute | solution.py:95
  233.3 31.5 %collective-permute-start.1 = (bf16[128,1,2048]{2,0,1:T(8,128)(2,1)}, bf16[128,1,2048]{2,0,1:T(8,128)(2,1)}, u32[]{:S(2)}, u32[]{:S(2)}) collective-permute-start(bf16[128,1,2048]{2,0,1:T(8,128)(2,1)} %get-tuple-element.18), channel_id=1, source_target_pairs={{0,1},{1,2},{2,3},{3,0},{4,5},{5,6},{6,7},{7,4},{8,9},{9,10},{10,1... | collective-permute-start | bytes 1572872 | tf_op jit(solution)/shard_map/ppermute | solution.py:95
  257.2 7.5 %copy-start.4 = (bf16[1,128,1,2048]{3,1,0,2:T(8,128)(2,1)S(1)}, bf16[1,128,1,2048]{3,1,0,2:T(8,128)(2,1)}, u32[]{:S(2)}) copy-start(bf16[1,128,1,2048]{3,1,0,2:T(8,128)(2,1)} %get-tuple-element.15) | copy-start | bytes 1572868
  261.3 27.2 %collective-permute-start.7 = (bf16[128,2,2048]{2,0,1:T(8,128)(2,1)}, bf16[128,2,2048]{2,0,1:T(8,128)(2,1)}, u32[]{:S(2)}, u32[]{:S(2)}) collective-permute-start(bf16[128,2,2048]{2,0,1:T(8,128)(2,1)} %get-tuple-element.10), channel_id=1, source_target_pairs={{0,3},{1,0},{2,1},{3,2},{4,7},{5,4},{6,5},{7,6},{8,11},{9,8},{10,9... | collective-permute-start | bytes 3145736 | tf_op jit(solution)/shard_map/ppermute | solution.py:95
  261.3 45.6 %collective-permute-start.6 = (bf16[128,2,2048]{2,0,1:T(8,128)(2,1)}, bf16[128,2,2048]{2,0,1:T(8,128)(2,1)}, u32[]{:S(2)}, u32[]{:S(2)}) collective-permute-start(bf16[128,2,2048]{2,0,1:T(8,128)(2,1)} %get-tuple-element.11), channel_id=1, source_target_pairs={{0,2},{1,3},{2,0},{3,1},{4,6},{5,7},{6,4},{7,5},{8,10},{9,11},{10,... | collective-permute-start | bytes 3145736 | tf_op jit(solution)/shard_map/ppermute | solution.py:95
  261.8 45.0 %collective-permute-start.5 = (bf16[128,2,2048]{2,0,1:T(8,128)(2,1)}, bf16[128,2,2048]{2,0,1:T(8,128)(2,1)}, u32[]{:S(2)}, u32[]{:S(2)}) collective-permute-start(bf16[128,2,2048]{2,0,1:T(8,128)(2,1)} %get-tuple-element.12), channel_id=1, source_target_pairs={{0,1},{1,2},{2,3},{3,0},{4,5},{5,6},{6,7},{7,4},{8,9},{9,10},{10,1... | collective-permute-start | bytes 3145736 | tf_op jit(solution)/shard_map/ppermute | solution.py:95
  320.1 6.4 %copy-start.2 = (bf16[128,1,4,2048]{0,3,2,1:T(8,128)(2,1)S(1)}, bf16[128,1,4,2048]{0,3,2,1:T(8,128)(2,1)}, u32[]{:S(2)}) copy-start(bf16[128,1,4,2048]{0,3,2,1:T(8,128)(2,1)} %copy.25) | copy-start | bytes 6291460

commit v4 on v3

--- a/solution.py
+++ b/solution.py
@@ -74,6 +74,7 @@
     query_proj = short_filter(grad_query[:, None], short_taps[:1], block_rows)
     query_rows = spread_rows(query_proj, "chan")
     z_cols = correlate(mixed_cols, taps_cols)
+    z_cols, query_rows = lax.optimization_barrier((z_cols, query_rows))
     grad_z = lax.all_to_all(z_cols, "seq", split_axis=0, concat_axis=1, tiled=True)
     grad_key = grad_z * value_part.astype(jnp.float32)
     grad_value = grad_z * key_part.astype(jnp.float32)

time: 344 us -> 371 us (1.078)
  waiting for transfers between devices: 154 us -> 179 us
  starting transfers between devices: 32.2 us -> 27.3 us
    all_to_all x1, waiting for transfers between devices: 0.01 us -> 79.8 us  [on_device(): lax.all_to_all(z_cols, 'seq', split_axis=0, concat_axis=1, tiled=True)]
    all_to_all x1, waiting for transfers between devices: 42.4 us -> 0.01 us  [on_device(): lax.all_to_all(grad_mixed, 'seq', split_axis=1, concat_axis=0, tiled=True)]
    ppermute x2, waiting for transfers between devices: 77 us -> 44.2 us  [shifted(): lax.ppermute(value, axis, [(source, source + steps) for source in range(l...]
    ppermute x6, waiting for transfers between devices: 34.2 us -> 55 us  [spread_rows(): pieces.append(lax.ppermute(outgoing, axis, pairs))]
    all_to_all x2 -> x1, local copies, waits for them, and re-layouts: 11.9 us -> 5.49 us  [on_device(): lax.all_to_all(z_cols, 'seq', split_axis=0, concat_axis=1, tiled=True)]
    optimization_barrier x0 -> x1, local copies, waits for them, and re-layouts: none -> 5.7 us  [on_device(): z_cols, query_rows = lax.optimization_barrier((z_cols, query_rows))]
    unnamed x18 -> x17, local copies, waits for them, and re-layouts: 15.5 us -> 20.2 us
  transfers between devices with their start and end apart: 11 -> 11, of which waited for: 4 -> 8; matrix products, arithmetic and copies ran while one was open for 20% -> 13% of each run, Pallas kernels for 0% -> 0%
where the time goes in v4:
time: 371 us; the launch traced here: 365 us
  waiting for transfers between devices  179 us (48%)
  local copies, waits for them, and re-layouts  91.2 us (25%)
  other arithmetic  51.2 us (14%)
  starting transfers between devices  27.3 us (7%)
  Pallas kernels  15.7 us (4%)
    all_to_all x1, waiting for transfers between devices, on_device(): lax.all_to_all(z_cols, 'seq', split_axis=0, concat_axis=1, tiled=True)  79.8 us
    ppermute x6, waiting for transfers between devices, spread_rows(): pieces.append(lax.ppermute(outgoing, axis, pairs))  55 us
    ppermute x2, waiting for transfers between devices, shifted(): lax.ppermute(value, axis, [(source, source + steps) for source in range(l...  44.2 us
    unnamed x17, local copies, waits for them, and re-layouts  20.2 us
    convert_element_type x2, other arithmetic, short_filter(): return result.astype(jnp.bfloat16)  16 us
    pallas_call x1, Pallas kernels, correlate(): pl.pallas_call(correlate_kernel, out_shape=jax.ShapeDtypeStruct((groups,...  15.7 us
    concatenate x1, local copies, waits for them, and re-layouts, on_device(): return jnp.concatenate([query_rows, pair_rows], 1)  8.62 us
    gather x2, local copies, waits for them, and re-layouts, spread_rows(): placed = jnp.take(gathered, order, axis=0)  8.54 us
  transfers between devices with their start and end apart: 11, of which 8 were waited for; matrix products, arithmetic and copies ran while one was open for 13% of the time, Pallas kernels for 0%

profile of v4, /device:TPU:18, one launch (start us, length us, event | category | flops | bytes accessed | tf_op | source)
XLA Modules:
  0.0 364.6 jit_solution(4863586571192898562)
XLA Ops:
  0.0 1.7 copy.30
  1.7 5.2 %all-to-all-start.1 = ((bf16[512,8,16]{0,2,1:T(8,128)(2,1)}), bf16[512,8,16]{0,2,1:T(8,128)(2,1)S(1)}, u32[]{:S(2)}, u32[]{:S(2)}) async-start(bf16[512,8,16]{0,2,1:T(8,128)(2,1)} %bitcast.5), calls=%async_computation.1 | async-start | bytes 262144 | tf_op jit(solution)/shard_map/all_to_all | solution.py:72
  6.9 7.8 %convert_multiply_fusion = (f32[512,2048]{1,0:T(8,128)}, f32[512,1,2048]{2,0,1:T(8,128)}, bf16[512,2048]{1,0:T(8,128)(2,1)S(1)}) fusion(bf16[512,2048]{1,0:T(8,128)(2,1)} %param.5, bf16[512,2048]{1,0:T(8,128)(2,1)} %param.7, bf16[512,3,2048]{2,0,1:T(8,128)(2,1)} %param.6), kind=kLoop, calls=%fused_computation.13 | loop fusion | flops 6291456 | bytes 16777216 | tf_op jit(solution)/shard_map/mul | solution.py:69
  14.7 2.5 copy.27
  17.2 0.0 all-to-all-done.1
  17.2 5.1 %all-to-all-start = ((bf16[512,8,256]{0,2,1:T(8,128)(2,1)}), bf16[512,8,256]{0,2,1:T(8,128)(2,1)S(1)}, u32[]{:S(2)}, u32[]{:S(2)}) async-start(bf16[512,8,256]{0,2,1:T(8,128)(2,1)} %bitcast.1), calls=%async_computation | async-start | bytes 4194304 | tf_op jit(solution)/shard_map/all_to_all | solution.py:71
  22.3 0.8 slice_bitcast_fusion
  23.1 2.2 collective-permute-start
  25.4 42.7 %collective-permute-done = f32[2,1,2048]{2,0,1:T(2,128)S(1)} collective-permute-done((f32[2,1,2048]{2,0,1:T(2,128)S(1)}, f32[2,1,2048]{2,0,1:T(2,128)S(1)}, u32[]{:S(2)}, u32[]{:S(2)}) %collective-permute-start) | collective-permute-done | bytes 16416 | tf_op jit(solution)/shard_map/ppermute | solution.py:17
  68.1 5.8 %fusion.8 = bf16[512,1,2048]{2,0,1:T(8,128)(2,1)S(1)} fusion(f32[512,1,2048]{2,0,1:T(8,128)} %get-tuple-element.18, f32[2,1,2048]{2,0,1:T(2,128)S(1)} %collective-permute-done, f32[2048]{0:T(1024)S(1)} %bitcast.99, f32[2048]{0:T(1024)S(1)} %bitcast.100, f32[2048]{0:T(1024)S(1)} %bitcast.98, bf16[512,2048]{1,0:T(8,128)(2,1)} %param.7, bf16[512,2048]{1,0:T(8,128)(2,1)} %param.5), kind=kLoop, calls=%fused_computation.21 | loop fusion | flops 11534336 | bytes 10526720 | tf_op jit(solution)/shard_map/convert_element_type | solution.py:110
  73.9 1.2 constant_dynamic-slice_fusion
  75.1 0.5 collective-permute-start.3
  75.7 1.5 collective-permute-start.2
  77.2 2.4 collective-permute-start.1
  79.7 2.5 rev.3
  82.1 0.1 concatenate.12
  82.2 0.9 reshape.118.h_ref
  83.1 3.7 %collective-permute-done.3 = bf16[128,1,2048]{2,0,1:T(8,128)(2,1)} collective-permute-done((bf16[128,1,2048]{2,0,1:T(8,128)(2,1)}, bf16[128,1,2048]{2,0,1:T(8,128)(2,1)}, u32[]{:S(2)}, u32[]{:S(2)}) %collective-permute-start.3) | collective-permute-done | bytes 524320 | tf_op jit(solution)/shard_map/ppermute | solution.py:96
  86.8 4.8 %collective-permute-done.2 = bf16[128,1,2048]{2,0,1:T(8,128)(2,1)} collective-permute-done((bf16[128,1,2048]{2,0,1:T(8,128)(2,1)}, bf16[128,1,2048]{2,0,1:T(8,128)(2,1)}, u32[]{:S(2)}, u32[]{:S(2)}) %collective-permute-start.2) | collective-permute-done | bytes 524320 | tf_op jit(solution)/shard_map/ppermute | solution.py:96
  91.7 0.8 collective-permute-done.1
  92.4 2.9 maximum_bitcast_fusion
  95.4 3.6 gather_fusion
  99.0 3.2 fusion.12
  102.1 3.9 %copy.33 = bf16[128,1,4,2048]{0,3,2,1:T(8,128)(2,1)} copy(bf16[128,1,4,2048]{3,0,2,1:T(8,128)(2,1)} %fusion.12) | data formatting | bytes 4194304 | tf_op jit(solution)/shard_map/transpose | solution.py:100
  106.1 0.0 all-to-all-done
  106.1 2.5 copy.28
  108.6 2.7 reshape.116
  111.3 2.2 copy.29
  113.4 15.7 %shard_map.55 = f32[16,256,256]{2,1,0:T(8,128)} custom-call(bf16[16,256,256]{2,1,0:T(8,128)(2,1)} %bitcast.92, f32[16,1,4352]{2,1,0:T(1,128)} %reshape.118.h_ref), custom_call_target="tpu_custom_call" | custom-call | flops 4563402752 | bytes 6569984 | tf_op jit(solution)/shard_map/pallas_call | solution.py:46
  129.1 5.4 %copy.32 = f32[16,16,16,256]{3,1,2,0:T(8,128)S(1)} copy(f32[16,16,16,256]{3,2,1,0:T(8,128)} %bitcast.91) | data formatting | bytes 8388608 | tf_op jit(solution)/shard_map/reshape | solution.py:59
  134.6 5.8 %copy.51 = f32[32,8,16,256]{3,1,2,0:T(8,128)} copy(f32[32,8,16,256]{3,2,1,0:T(8,128)S(1)} %bitcast.84) | data formatting | bytes 8388608
  140.4 5.7 %copy.34 = f32[4096,256]{1,0:T(8,128)} copy(f32[4096,256]{0,1:T(8,128)} %bitcast.85) | data formatting | bytes 8388608 | tf_op jit(solution)/shard_map/optimization_barrier | solution.py:77
  146.1 4.7 %all-to-all-start.2 = ((f32[8,512,256]{2,1,0:T(8,128)}), f32[8,512,256]{2,1,0:T(8,128)}, u32[]{:S(2)}, u32[]{:S(2)}) async-start(f32[8,512,256]{2,1,0:T(8,128)} %bitcast.83), calls=%async_computation.2 | async-start | bytes 8388608 | tf_op jit(solution)/shard_map/all_to_all | solution.py:78
  150.8 4.0 %fusion.17 = (bf16[512,1,2048]{2,0,1:T(8,128)(2,1)}, bf16[512,1,2048]{2,0,1:T(8,128)(2,1)S(1)}) fusion(bf16[512,3,2048]{2,0,1:T(8,128)(2,1)} %param.6), kind=kLoop, calls=%fused_computation.60 | loop fusion | bytes 8388608 | tf_op jit(solution)/shard_map/slice | solution.py:68
  154.8 4.0 %copy.47 = bf16[512,1,2048]{0,2,1:T(8,128)(2,1)} copy(bf16[512,1,2048]{2,0,1:T(8,128)(2,1)} %get-tuple-element.9) | data formatting | bytes 4194304
  158.8 2.6 copy.48
  161.4 79.8 %all-to-all-done.2 = f32[8,512,256]{2,1,0:T(8,128)} async-done(((f32[8,512,256]{2,1,0:T(8,128)}), f32[8,512,256]{2,1,0:T(8,128)}, u32[]{:S(2)}, u32[]{:S(2)}) %all-to-all-start.2) | async-done | bytes 4194336 | tf_op jit(solution)/shard_map/all_to_all | solution.py:78
  241.2 5.5 %copy.35 = f32[512,8,256]{0,2,1:T(8,128)} copy(f32[512,8,256]{2,0,1:T(8,128)} %bitcast.29) | data formatting | bytes 8388608 | tf_op jit(solution)/shard_map/all_to_all | solution.py:78
  246.7 4.1 %bitcast_multiply_fusion.1 = (f32[512,1,2048]{0,2,1:T(8,128)S(1)}, f32[512,1,2048]{0,2,1:T(8,128)S(1)}) fusion(bf16[512,1,2048]{0,2,1:T(8,128)(2,1)S(1)} %copy-done.3, bf16[512,1,2048]{0,2,1:T(8,128)(2,1)} %copy.48, f32[512,1,2048]{0,2,1:T(8,128)} %bitcast.86), kind=kLoop, calls=%fused_computation.27 | loop fusion | flops 4194304 | bytes 16777216 | tf_op jit(solution)/shard_map/mul | solution.py:79
  250.8 0.0 copy-start
  250.8 0.0 copy-start.1
  250.9 1.9 copy-done
  252.8 1.5 copy-done.1
  254.2 0.3 fusion.11
  254.5 0.6 copy.38
  255.1 2.0 collective-permute-start.4
  257.1 1.5 collective-permute-done.4
  258.7 0.6 copy.39
  259.3 4.5 %pad_maximum_fusion = f32[514,2,2048]{0,2,1:T(8,128)S(1)} fusion(f32[2,2,2048]{0,2,1:T(8,128)S(1)} %copy.39, f32[512,1,2048]{0,2,1:T(8,128)} %copy-done.1, f32[512,1,2048]{0,2,1:T(8,128)} %copy-done), kind=kLoop, calls=%fused_computation.2 | loop fusion | flops 4210688 | bytes 16842752 | tf_op jit(solution)/shard_map/concatenate | solution.py:106
  263.8 10.2 %fusion.3 = bf16[512,2,2048]{0,2,1:T(8,128)(2,1)} fusion(f32[512,1,2048]{0,2,1:T(8,128)} %copy-done.1, f32[512,1,2048]{0,2,1:T(8,128)} %copy-done, f32[514,2,2048]{0,2,1:T(8,128)S(1)} %pad_maximum_fusion, f32[2,2048]{1,0:T(2,128)S(1)} %get-tuple-element.30, f32[2,2048]{1,0:T(2,128)S(1)} %get-tuple-element.31, f32[2,2048]{1,0:T(2,128)S(1)} %bitcast.97), kind=kLoop, calls=%fused_computation.9 | loop fusion | flops 14680064 | bytes 29409280 | tf_op jit(solution)/shard_map/convert_element_type | solution.py:110
  274.0 6.2 %copy.40 = bf16[512,2,2048]{2,0,1:T(8,128)(2,1)} copy(bf16[512,2,2048]{0,2,1:T(8,128)(2,1)} %fusion.3) | data formatting | bytes 8388608 | tf_op jit(solution)/shard_map/convert_element_type | solution.py:110
  280.2 2.7 dynamic-slice_bitcast_fusion.3
  283.0 1.7 collective-permute-start.7
  284.7 0.5 collective-permute-start.6
  285.2 1.5 collective-permute-start.5
  286.7 22.0 %collective-permute-done.7 = bf16[128,2,2048]{2,0,1:T(8,128)(2,1)S(1)} collective-permute-done((bf16[128,2,2048]{2,0,1:T(8,128)(2,1)S(1)}, bf16[128,2,2048]{2,0,1:T(8,128)(2,1)S(1)}, u32[]{:S(2)}, u32[]{:S(2)}) %collective-permute-start.7) | collective-permute-done | bytes 1048608 | tf_op jit(solution)/shard_map/ppermute | solution.py:96
  308.7 23.7 %collective-permute-done.6 = bf16[128,2,2048]{2,0,1:T(8,128)(2,1)S(1)} collective-permute-done((bf16[128,2,2048]{2,0,1:T(8,128)(2,1)S(1)}, bf16[128,2,2048]{2,0,1:T(8,128)(2,1)S(1)}, u32[]{:S(2)}, u32[]{:S(2)}) %collective-permute-start.6) | collective-permute-done | bytes 1048608 | tf_op jit(solution)/shard_map/ppermute | solution.py:96
  332.3 0.0 collective-permute-done.5
  332.3 2.3 pad_maximum_fusion.4
  334.6 4.9 %gather_fusion.1 = bf16[4,128,2,2048]{3,1,2,0:T(8,128)(2,1)} fusion(bf16[4,128,2,2048]{3,1,2,0:T(8,128)(2,1)} %pad_maximum_fusion.4, s32[1024]{0:T(1024)S(1)} %pad_clamp_fusion), kind=kCustom, calls=%fused_computation.1 | custom fusion | bytes 8388624 | tf_op jit(solution)/shard_map/jit(_take)/gather | solution.py:99
  339.6 4.7 %select_bitcast_fusion = bf16[128,2,4,2048]{3,0,1,2:T(8,128)(2,1)} fusion(bf16[4,128,2,2048]{3,1,2,0:T(8,128)(2,1)} %gather_fusion.1, pred[4]{0:T(512)(128)(4,1)S(1)} %compare_and_fusion), kind=kLoop, calls=%fused_computation.28 | loop fusion | flops 2097152 | bytes 8388612 | tf_op jit(solution)/shard_map/jit(_take)/select_n | solution.py:99
  344.2 6.4 %copy.42 = bf16[128,2,4,2048]{0,3,2,1:T(8,128)(2,1)} copy(bf16[128,2,4,2048]{3,0,1,2:T(8,128)(2,1)} %select_bitcast_fusion) | data formatting | bytes 8388608 | tf_op jit(solution)/shard_map/jit(_take)/select_n | solution.py:99
  350.6 5.4 %pad_maximum_fusion.2 = bf16[128,3,8192]{0,2,1:T(8,128)(2,1)} fusion(bf16[128,2,8192]{0,2,1:T(8,128)(2,1)} %bitcast.81, bf16[128,1,8192]{0,2,1:T(8,128)(2,1)S(1)} %bitcast.89), kind=kLoop, calls=%fused_computation.12 | loop fusion | flops 3145728 | bytes 12582912 | tf_op jit(solution)/shard_map/concatenate | solution.py:84
  356.0 8.6 %copy.43 = bf16[128,3,8192]{2,0,1:T(8,128)(2,1)} copy(bf16[128,3,8192]{0,2,1:T(8,128)(2,1)} %pad_maximum_fusion.2) | data formatting | bytes 12582912 | tf_op jit(solution)/shard_map/concatenate | solution.py:84
  (15 shorter events, 0.2 us)
Async XLA Ops:
  1.7 15.5 %all-to-all-start.1 = ((bf16[512,8,16]{0,2,1:T(8,128)(2,1)}), bf16[512,8,16]{0,2,1:T(8,128)(2,1)S(1)}, u32[]{:S(2)}, u32[]{:S(2)}) async-start(bf16[512,8,16]{0,2,1:T(8,128)(2,1)} %bitcast.5), calls=%async_computation.1 | async-start | bytes 262144 | tf_op jit(solution)/shard_map/all_to_all | solution.py:72
  14.7 10.6 %copy-start.4 = (f32[3,3,2048]{2,1,0:T(4,128)S(1)}, f32[3,3,2048]{2,1,0:T(4,128)}, u32[]{:S(2)}) copy-start(f32[3,3,2048]{2,1,0:T(4,128)} %param.9) | copy-start | bytes 221188
  17.2 88.9 %all-to-all-start = ((bf16[512,8,256]{0,2,1:T(8,128)(2,1)}), bf16[512,8,256]{0,2,1:T(8,128)(2,1)S(1)}, u32[]{:S(2)}, u32[]{:S(2)}) async-start(bf16[512,8,256]{0,2,1:T(8,128)(2,1)} %bitcast.1), calls=%async_computation | async-start | bytes 4194304 | tf_op jit(solution)/shard_map/all_to_all | solution.py:71
  23.1 45.0 %collective-permute-start = (f32[2,1,2048]{2,0,1:T(2,128)S(1)}, f32[2,1,2048]{2,0,1:T(2,128)S(1)}, u32[]{:S(2)}, u32[]{:S(2)}) collective-permute-start(f32[2,1,2048]{2,0,1:T(2,128)S(1)} %slice_bitcast_fusion), channel_id=1, source_target_pairs={{4,0},{8,4},{12,8},{16,12},{20,16},{24,20},{28,24},{5,1},{9,5},{13... | collective-permute-start | bytes 49160 | tf_op jit(solution)/shard_map/ppermute | solution.py:17
  75.1 11.7 %collective-permute-start.3 = (bf16[128,1,2048]{2,0,1:T(8,128)(2,1)}, bf16[128,1,2048]{2,0,1:T(8,128)(2,1)}, u32[]{:S(2)}, u32[]{:S(2)}) collective-permute-start(bf16[128,1,2048]{2,0,1:T(8,128)(2,1)} %get-tuple-element.20), channel_id=1, source_target_pairs={{0,3},{1,0},{2,1},{3,2},{4,7},{5,4},{6,5},{7,6},{8,11},{9,8},{10,9... | collective-permute-start | bytes 1572872 | tf_op jit(solution)/shard_map/ppermute | solution.py:96
  75.7 16.0 %collective-permute-start.2 = (bf16[128,1,2048]{2,0,1:T(8,128)(2,1)}, bf16[128,1,2048]{2,0,1:T(8,128)(2,1)}, u32[]{:S(2)}, u32[]{:S(2)}) collective-permute-start(bf16[128,1,2048]{2,0,1:T(8,128)(2,1)} %get-tuple-element.21), channel_id=1, source_target_pairs={{0,2},{1,3},{2,0},{3,1},{4,6},{5,7},{6,4},{7,5},{8,10},{9,11},{10,... | collective-permute-start | bytes 1572872 | tf_op jit(solution)/shard_map/ppermute | solution.py:96
  77.2 15.3 %collective-permute-start.1 = (bf16[128,1,2048]{2,0,1:T(8,128)(2,1)}, bf16[128,1,2048]{2,0,1:T(8,128)(2,1)}, u32[]{:S(2)}, u32[]{:S(2)}) collective-permute-start(bf16[128,1,2048]{2,0,1:T(8,128)(2,1)} %get-tuple-element.22), channel_id=1, source_target_pairs={{0,1},{1,2},{2,3},{3,0},{4,5},{5,6},{6,7},{7,4},{8,9},{9,10},{10,1... | collective-permute-start | bytes 1572872 | tf_op jit(solution)/shard_map/ppermute | solution.py:96
  146.1 95.1 %all-to-all-start.2 = ((f32[8,512,256]{2,1,0:T(8,128)}), f32[8,512,256]{2,1,0:T(8,128)}, u32[]{:S(2)}, u32[]{:S(2)}) async-start(f32[8,512,256]{2,1,0:T(8,128)} %bitcast.83), calls=%async_computation.2 | async-start | bytes 8388608 | tf_op jit(solution)/shard_map/all_to_all | solution.py:78
  241.2 5.5 %copy-start.3 = (bf16[512,1,2048]{0,2,1:T(8,128)(2,1)S(1)}, bf16[512,1,2048]{0,2,1:T(8,128)(2,1)}, u32[]{:S(2)}) copy-start(bf16[512,1,2048]{0,2,1:T(8,128)(2,1)} %copy.47) | copy-start | bytes 6291460
  250.8 1.9 copy-start
  250.8 3.4 copy-start.1
  255.1 3.6 collective-permute-start.4
  283.0 25.7 %collective-permute-start.7 = (bf16[128,2,2048]{2,0,1:T(8,128)(2,1)S(1)}, bf16[128,2,2048]{2,0,1:T(8,128)(2,1)S(1)}, u32[]{:S(2)}, u32[]{:S(2)}) collective-permute-start(bf16[128,2,2048]{2,0,1:T(8,128)(2,1)S(1)} %get-tuple-element.12), channel_id=1, source_target_pairs={{0,3},{1,0},{2,1},{3,2},{4,7},{5,4},{6,5},{7,6},{8,11},{9,8},{10,9... | collective-permute-start | bytes 3145736 | tf_op jit(solution)/shard_map/ppermute | solution.py:96
  284.7 47.6 %collective-permute-start.6 = (bf16[128,2,2048]{2,0,1:T(8,128)(2,1)S(1)}, bf16[128,2,2048]{2,0,1:T(8,128)(2,1)S(1)}, u32[]{:S(2)}, u32[]{:S(2)}) collective-permute-start(bf16[128,2,2048]{2,0,1:T(8,128)(2,1)S(1)} %get-tuple-element.13), channel_id=1, source_target_pairs={{0,2},{1,3},{2,0},{3,1},{4,6},{5,7},{6,4},{7,5},{8,10},{9,11},{10,... | collective-permute-start | bytes 3145736 | tf_op jit(solution)/shard_map/ppermute | solution.py:96
  285.2 47.1 %collective-permute-start.5 = (bf16[128,2,2048]{2,0,1:T(8,128)(2,1)S(1)}, bf16[128,2,2048]{2,0,1:T(8,128)(2,1)S(1)}, u32[]{:S(2)}, u32[]{:S(2)}) collective-permute-start(bf16[128,2,2048]{2,0,1:T(8,128)(2,1)S(1)} %get-tuple-element.14), channel_id=1, source_target_pairs={{0,1},{1,2},{2,3},{3,0},{4,5},{5,6},{6,7},{7,4},{8,9},{9,10},{10,1... | collective-permute-start | bytes 3145736 | tf_op jit(solution)/shard_map/ppermute | solution.py:96
  344.2 6.4 %copy-start.2 = (bf16[128,1,4,2048]{0,3,2,1:T(8,128)(2,1)S(1)}, bf16[128,1,4,2048]{0,3,2,1:T(8,128)(2,1)}, u32[]{:S(2)}) copy-start(bf16[128,1,4,2048]{0,3,2,1:T(8,128)(2,1)} %copy.33) | copy-start | bytes 6291460

commit v5 on v3

--- a/solution.py
+++ b/solution.py
@@ -74,7 +74,9 @@
     query_proj = short_filter(grad_query[:, None], short_taps[:1], block_rows)
     query_rows = spread_rows(query_proj, "chan")
     z_cols = correlate(mixed_cols, taps_cols)
-    grad_z = lax.all_to_all(z_cols, "seq", split_axis=0, concat_axis=1, tiled=True)
+    z_narrow = z_cols.astype(jnp.bfloat16)
+    grad_z = lax.all_to_all(z_narrow, "seq", split_axis=0, concat_axis=1, tiled=True)
+    grad_z = grad_z.astype(jnp.float32)
     grad_key = grad_z * value_part.astype(jnp.float32)
     grad_value = grad_z * key_part.astype(jnp.float32)
     stacked = jnp.stack([grad_key, grad_value], 1)

time: 344 us -> 287 us (0.83)
  waiting for transfers between devices: 154 us -> 106 us
  local copies, waits for them, and re-layouts: 87.8 us -> 77.6 us
    ppermute x2, waiting for transfers between devices: 77 us -> 29.9 us  [shifted(): lax.ppermute(value, axis, [(source, source + steps) for source in range(l...]
    all_to_all x2 -> x0, local copies, waits for them, and re-layouts: 11.9 us -> none  [on_device(): lax.all_to_all(z_cols, 'seq', split_axis=0, concat_axis=1, tiled=True)]
    reshape x1 -> x0, local copies, waits for them, and re-layouts: 7.41 us -> none  [correlate(): out = out.reshape(groups, blocks, per_group, block).transpose(1, 3, 0, 2)]
    convert_element_type x0 -> x3, local copies, waits for them, and re-layouts: none -> 6.74 us  [on_device(): z_narrow = z_cols.astype(jnp.bfloat16)]
    unnamed x18 -> x16, local copies, waits for them, and re-layouts: 15.5 us -> 17 us
  transfers between devices with their start and end apart: 11 -> 11, of which waited for: 4 -> 4; matrix products, arithmetic and copies ran while one was open for 20% -> 25% of each run, Pallas kernels for 0% -> 0%
where the time goes in v5:
time: 287 us; the launch traced here: 284 us
  waiting for transfers between devices  106 us (37%)
  local copies, waits for them, and re-layouts  77.6 us (27%)
  other arithmetic  52.8 us (18%)
  starting transfers between devices  31 us (11%)
  Pallas kernels  15.7 us (5%)
    all_to_all x1, waiting for transfers between devices, on_device(): lax.all_to_all(grad_mixed, 'seq', split_axis=1, concat_axis=0, tiled=True)  42.4 us
    ppermute x6, waiting for transfers between devices, spread_rows(): pieces.append(lax.ppermute(outgoing, axis, pairs))  34.1 us
    ppermute x2, waiting for transfers between devices, shifted(): lax.ppermute(value, axis, [(source, source + steps) for source in range(l...  29.9 us
    convert_element_type x2, other arithmetic, short_filter(): return result.astype(jnp.bfloat16)  17 us
    unnamed x16, local copies, waits for them, and re-layouts  17 us
    pallas_call x1, Pallas kernels, correlate(): pl.pallas_call(correlate_kernel, out_shape=jax.ShapeDtypeStruct((groups,...  15.7 us
    concatenate x1, local copies, waits for them, and re-layouts, on_device(): return jnp.concatenate([query_rows, pair_rows], 1)  8.62 us
    ppermute x6, starting transfers between devices, spread_rows(): pieces.append(lax.ppermute(outgoing, axis, pairs))  7.88 us
  transfers between devices with their start and end apart: 11, of which 4 were waited for; matrix products, arithmetic and copies ran while one was open for 25% of the time, Pallas kernels for 0%

profile of v5, /device:TPU:18, one launch (start us, length us, event | category | flops | bytes accessed | tf_op | source)
XLA Modules:
  0.0 283.8 jit_solution(6613863899200741090)
XLA Ops:
  0.0 1.7 copy.29
  1.7 5.2 %all-to-all-start.1 = ((bf16[512,8,16]{0,2,1:T(8,128)(2,1)}), bf16[512,8,16]{0,2,1:T(8,128)(2,1)S(1)}, u32[]{:S(2)}, u32[]{:S(2)}) async-start(bf16[512,8,16]{0,2,1:T(8,128)(2,1)} %bitcast.23), calls=%async_computation.1 | async-start | bytes 262144 | tf_op jit(solution)/shard_map/all_to_all | solution.py:72
  6.9 7.8 %convert_multiply_fusion.1 = (f32[512,2048]{1,0:T(8,128)}, f32[512,1,2048]{2,0,1:T(8,128)}, bf16[512,2048]{1,0:T(8,128)(2,1)S(1)}) fusion(bf16[512,2048]{1,0:T(8,128)(2,1)} %param.5, bf16[512,2048]{1,0:T(8,128)(2,1)} %param.7, bf16[512,3,2048]{2,0,1:T(8,128)(2,1)} %param.6), kind=kLoop, calls=%fused_computation.14 | loop fusion | flops 6291456 | bytes 16777216 | tf_op jit(solution)/shard_map/mul | solution.py:69
  14.7 2.5 copy.26
  17.2 0.0 all-to-all-done.1
  17.2 5.1 %all-to-all-start = ((bf16[512,8,256]{0,2,1:T(8,128)(2,1)}), bf16[512,8,256]{0,2,1:T(8,128)(2,1)S(1)}, u32[]{:S(2)}, u32[]{:S(2)}) async-start(bf16[512,8,256]{0,2,1:T(8,128)(2,1)} %bitcast.19), calls=%async_computation | async-start | bytes 4194304 | tf_op jit(solution)/shard_map/all_to_all | solution.py:71
  22.4 2.3 rev.3
  24.6 0.1 concatenate.13
  24.7 0.9 reshape.130.h_ref
  25.6 42.4 %all-to-all-done = bf16[512,8,256]{0,2,1:T(8,128)(2,1)S(1)} async-done(((bf16[512,8,256]{0,2,1:T(8,128)(2,1)}), bf16[512,8,256]{0,2,1:T(8,128)(2,1)S(1)}, u32[]{:S(2)}, u32[]{:S(2)}) %all-to-all-start) | async-done | bytes 2097184 | tf_op jit(solution)/shard_map/all_to_all | solution.py:71
  68.1 2.5 copy.27
  70.6 2.7 reshape.128
  73.3 2.3 copy.28
  75.5 15.7 %shard_map.55 = f32[16,256,256]{2,1,0:T(8,128)} custom-call(bf16[16,256,256]{2,1,0:T(8,128)(2,1)} %bitcast.89, f32[16,1,4352]{2,1,0:T(1,128)} %reshape.130.h_ref), custom_call_target="tpu_custom_call" | custom-call | flops 4563402752 | bytes 6569984 | tf_op jit(solution)/shard_map/pallas_call | solution.py:46
  91.3 2.4 convert_element_type.74
  93.7 0.9 copy.52
  94.6 2.2 convert_element_type.77
  96.8 3.7 %copy.32 = bf16[8,512,256]{1,2,0:T(8,128)(2,1)} copy(bf16[8,512,256]{1,0,2:T(8,128)(2,1)} %convert_element_type.77) | data formatting | bytes 4194304 | tf_op jit(solution)/shard_map/convert_element_type | solution.py:77
  100.5 6.8 %all-to-all-start.2 = ((bf16[8,512,256]{1,2,0:T(8,128)(2,1)}), bf16[8,512,256]{1,2,0:T(8,128)(2,1)S(1)}, u32[]{:S(2)}, u32[]{:S(2)}) async-start(bf16[8,512,256]{1,2,0:T(8,128)(2,1)} %copy.32), calls=%async_computation.2 | async-start | bytes 4194304 | tf_op jit(solution)/shard_map/all_to_all | solution.py:78
  107.3 0.8 slice_bitcast_fusion
  108.1 2.2 collective-permute-start
  110.4 4.9 %fusion.17 = (bf16[512,1,2048]{2,0,1:T(8,128)(2,1)}, bf16[512,1,2048]{2,0,1:T(8,128)(2,1)}) fusion(bf16[512,3,2048]{2,0,1:T(8,128)(2,1)} %param.6), kind=kLoop, calls=%fused_computation.61 | loop fusion | bytes 8388608 | tf_op jit(solution)/shard_map/slice | solution.py:68
  115.3 4.0 %copy.44 = bf16[512,1,2048]{0,2,1:T(8,128)(2,1)} copy(bf16[512,1,2048]{2,0,1:T(8,128)(2,1)} %get-tuple-element.5) | data formatting | bytes 4194304
  119.3 3.9 %copy.45 = bf16[512,1,2048]{0,2,1:T(8,128)(2,1)} copy(bf16[512,1,2048]{2,0,1:T(8,128)(2,1)} %get-tuple-element.6) | data formatting | bytes 4194304
  123.2 29.9 %collective-permute-done = f32[2,1,2048]{2,0,1:T(2,128)S(1)} collective-permute-done((f32[2,1,2048]{2,0,1:T(2,128)S(1)}, f32[2,1,2048]{2,0,1:T(2,128)S(1)}, u32[]{:S(2)}, u32[]{:S(2)}) %collective-permute-start) | collective-permute-done | bytes 16416 | tf_op jit(solution)/shard_map/ppermute | solution.py:17
  153.1 6.8 %fusion.8 = bf16[512,1,2048]{2,0,1:T(8,128)(2,1)} fusion(f32[512,1,2048]{2,0,1:T(8,128)} %get-tuple-element.8, f32[2,1,2048]{2,0,1:T(2,128)S(1)} %collective-permute-done, f32[2048]{0:T(1024)S(1)} %bitcast.93, f32[2048]{0:T(1024)S(1)} %bitcast.94, f32[2048]{0:T(1024)S(1)} %bitcast.92, bf16[512,2048]{1,0:T(8,128)(2,1)} %param.7, bf16[512,2048]{1,0:T(8,128)(2,1)} %param.5), kind=kLoop, calls=%fused_computation.21 | loop fusion | flops 11534336 | bytes 10526720 | tf_op jit(solution)/shard_map/convert_element_type | solution.py:111
  159.9 0.0 all-to-all-done.2
  159.9 3.5 %bitcast_multiply_fusion.1 = (f32[512,1,2048]{0,2,1:T(8,128)S(1)}, f32[512,1,2048]{0,2,1:T(8,128)S(1)}) fusion(bf16[8,512,256]{1,2,0:T(8,128)(2,1)S(1)} %all-to-all-done.2, bf16[512,1,2048]{0,2,1:T(8,128)(2,1)} %copy.44, bf16[512,1,2048]{0,2,1:T(8,128)(2,1)} %copy.45), kind=kLoop, calls=%fused_computation.27 | loop fusion | flops 5242880 | bytes 14680064 | tf_op jit(solution)/shard_map/mul | solution.py:80
  163.4 0.0 copy-start.1
  163.4 1.9 copy-done
  165.4 1.5 copy-done.1
  166.8 0.3 fusion.11
  167.1 0.6 copy.35
  167.7 3.8 %collective-permute-start.4 = (f32[2,2,2048]{2,1,0:T(2,128)S(1)}, f32[2,2,2048]{2,1,0:T(2,128)S(1)}, u32[]{:S(2)}, u32[]{:S(2)}) collective-permute-start(f32[2,2,2048]{2,1,0:T(2,128)S(1)} %copy.35), channel_id=1, source_target_pairs={{4,0},{8,4},{12,8},{16,12},{20,16},{24,20},{28,24},{5,1},{9,5},{13... | collective-permute-start | bytes 98312 | tf_op jit(solution)/shard_map/ppermute | solution.py:17
  171.5 3.0 %constant_dynamic-slice_fusion = (bf16[1,128,1,2048]{3,1,0,2:T(8,128)(2,1)}, bf16[128,1,2048]{2,0,1:T(8,128)(2,1)}, bf16[128,1,2048]{2,0,1:T(8,128)(2,1)}, bf16[128,1,2048]{2,0,1:T(8,128)(2,1)}) fusion(bf16[4,128,1,2048]{3,1,0,2:T(8,128)(2,1)} %bitcast.88, s32[]{:T(128)S(6)} %select_n.98, s32[]{:T(128)S(6)} %select_n.104, s32[]{:T(128)S(6)} %select_n.102, ...), kind=kLoop, calls=%fused_computation.53 | loop fusion | bytes 4194320 | tf_op jit(solution)/shard_map/jit(dynamic_index_in_dim)/dynamic_slice | solution.py:93
  174.5 0.5 collective-permute-start.3
  175.0 1.5 collective-permute-start.2
  176.6 2.4 collective-permute-start.1
  179.0 0.0 collective-permute-done.4
  179.0 0.6 copy.36
  179.6 4.5 %pad_maximum_fusion = f32[514,2,2048]{0,2,1:T(8,128)S(1)} fusion(f32[2,2,2048]{0,2,1:T(8,128)S(1)} %copy.36, f32[512,1,2048]{0,2,1:T(8,128)} %copy-done.1, f32[512,1,2048]{0,2,1:T(8,128)} %copy-done), kind=kLoop, calls=%fused_computation.2 | loop fusion | flops 4210688 | bytes 16842752 | tf_op jit(solution)/shard_map/concatenate | solution.py:107
  184.1 10.2 %fusion.3 = bf16[512,2,2048]{0,2,1:T(8,128)(2,1)} fusion(f32[512,1,2048]{0,2,1:T(8,128)} %copy-done.1, f32[512,1,2048]{0,2,1:T(8,128)} %copy-done, f32[514,2,2048]{0,2,1:T(8,128)S(1)} %pad_maximum_fusion, f32[2,2048]{1,0:T(2,128)S(1)} %get-tuple-element.26, f32[2,2048]{1,0:T(2,128)S(1)} %get-tuple-element.27, f32[2,2048]{1,0:T(2,128)S(1)} %bitcast.91), kind=kLoop, calls=%fused_computation.9 | loop fusion | flops 14680064 | bytes 29409280 | tf_op jit(solution)/shard_map/convert_element_type | solution.py:111
  194.3 6.2 %copy.37 = bf16[512,2,2048]{2,0,1:T(8,128)(2,1)} copy(bf16[512,2,2048]{0,2,1:T(8,128)(2,1)} %fusion.3) | data formatting | bytes 8388608 | tf_op jit(solution)/shard_map/convert_element_type | solution.py:111
  200.5 4.0 %dynamic-slice_bitcast_fusion.3 = (bf16[1,128,2,2048]{3,1,2,0:T(8,128)(2,1)S(1)}, bf16[128,2,2048]{2,0,1:T(8,128)(2,1)}, bf16[128,2,2048]{2,0,1:T(8,128)(2,1)}, bf16[128,2,2048]{2,0,1:T(8,128)(2,1)}) fusion(bf16[4,128,2,2048]{3,1,0,2:T(8,128)(2,1)} %bitcast.82, s32[]{:T(128)S(6)} %select_n.98, s32[]{:T(128)S(6)} %select_n.104, s32[]{:T(128)S(6)} %select_n.102, ...), kind=kLoop, calls=%fused_computation.37 | loop fusion | bytes 8388624
  204.5 0.0 collective-permute-start.7
  204.5 0.6 collective-permute-start.6
  205.1 0.0 collective-permute-done.3
  205.1 2.9 %collective-permute-start.5 = (bf16[128,2,2048]{2,0,1:T(8,128)(2,1)}, bf16[128,2,2048]{2,0,1:T(8,128)(2,1)}, u32[]{:S(2)}, u32[]{:S(2)}) collective-permute-start(bf16[128,2,2048]{2,0,1:T(8,128)(2,1)} %get-tuple-element.12), channel_id=1, source_target_pairs={{0,1},{1,2},{2,3},{3,0},{4,5},{5,6},{6,7},{7,4},{8,9},{9,10},{10,1... | collective-permute-start | bytes 3145736 | tf_op jit(solution)/shard_map/ppermute | solution.py:97
  208.0 0.0 collective-permute-done.2
  208.0 0.0 collective-permute-done.1
  208.0 1.6 maximum_bitcast_fusion
  209.6 2.0 gather_fusion
  211.6 1.9 fusion.12
  213.5 2.5 copy.25
  216.0 15.7 %collective-permute-done.7 = bf16[128,2,2048]{2,0,1:T(8,128)(2,1)} collective-permute-done((bf16[128,2,2048]{2,0,1:T(8,128)(2,1)}, bf16[128,2,2048]{2,0,1:T(8,128)(2,1)}, u32[]{:S(2)}, u32[]{:S(2)}) %collective-permute-start.7) | collective-permute-done | bytes 1048608 | tf_op jit(solution)/shard_map/ppermute | solution.py:97
  231.8 18.4 %collective-permute-done.6 = bf16[128,2,2048]{2,0,1:T(8,128)(2,1)} collective-permute-done((bf16[128,2,2048]{2,0,1:T(8,128)(2,1)}, bf16[128,2,2048]{2,0,1:T(8,128)(2,1)}, u32[]{:S(2)}, u32[]{:S(2)}) %collective-permute-start.6) | collective-permute-done | bytes 1048608 | tf_op jit(solution)/shard_map/ppermute | solution.py:97
  250.1 0.0 collective-permute-done.5
  250.1 3.6 %pad_maximum_fusion.4 = bf16[4,128,2,2048]{3,1,2,0:T(8,128)(2,1)} fusion(bf16[1,128,2,2048]{3,1,2,0:T(8,128)(2,1)} %bitcast.37, bf16[1,128,2,2048]{3,1,2,0:T(8,128)(2,1)} %bitcast.35, bf16[1,128,2,2048]{3,1,2,0:T(8,128)(2,1)} %bitcast.33, bf16[1,128,2,2048]{3,1,2,0:T(8,128)(2,1)S(1)} %get-tuple-element.9), kind=kLoop, calls=%fused_computation.25 | loop fusion | flops 6291456 | bytes 8388608 | tf_op jit(solution)/shard_map/stack | solution.py:98
  253.8 4.9 %gather_fusion.1 = bf16[4,128,2,2048]{3,1,2,0:T(8,128)(2,1)} fusion(bf16[4,128,2,2048]{3,1,2,0:T(8,128)(2,1)} %pad_maximum_fusion.4, s32[1024]{0:T(1024)S(1)} %pad_clamp_fusion), kind=kCustom, calls=%fused_computation.1 | custom fusion | bytes 8388624 | tf_op jit(solution)/shard_map/jit(_take)/gather | solution.py:100
  258.7 4.7 %select_bitcast_fusion = bf16[128,2,4,2048]{3,0,1,2:T(8,128)(2,1)} fusion(bf16[4,128,2,2048]{3,1,2,0:T(8,128)(2,1)} %gather_fusion.1, pred[4]{0:T(512)(128)(4,1)S(1)} %compare_and_fusion), kind=kLoop, calls=%fused_computation.28 | loop fusion | flops 2097152 | bytes 8388612 | tf_op jit(solution)/shard_map/jit(_take)/select_n | solution.py:100
  263.4 6.4 %copy.39 = bf16[128,2,4,2048]{0,3,2,1:T(8,128)(2,1)} copy(bf16[128,2,4,2048]{3,0,1,2:T(8,128)(2,1)} %select_bitcast_fusion) | data formatting | bytes 8388608 | tf_op jit(solution)/shard_map/jit(_take)/select_n | solution.py:100
  269.8 0.0 copy-done.2
  269.8 5.4 %pad_maximum_fusion.2 = bf16[128,3,8192]{0,2,1:T(8,128)(2,1)} fusion(bf16[128,2,8192]{0,2,1:T(8,128)(2,1)} %bitcast.81, bf16[128,1,8192]{0,2,1:T(8,128)(2,1)S(1)} %bitcast.87), kind=kLoop, calls=%fused_computation.12 | loop fusion | flops 3145728 | bytes 12582912 | tf_op jit(solution)/shard_map/concatenate | solution.py:85
  275.2 8.6 %copy.40 = bf16[128,3,8192]{2,0,1:T(8,128)(2,1)} copy(bf16[128,3,8192]{0,2,1:T(8,128)(2,1)} %pad_maximum_fusion.2) | data formatting | bytes 12582912 | tf_op jit(solution)/shard_map/concatenate | solution.py:85
  (15 shorter events, 0.2 us)
Async XLA Ops:
  1.7 15.5 %all-to-all-start.1 = ((bf16[512,8,16]{0,2,1:T(8,128)(2,1)}), bf16[512,8,16]{0,2,1:T(8,128)(2,1)S(1)}, u32[]{:S(2)}, u32[]{:S(2)}) async-start(bf16[512,8,16]{0,2,1:T(8,128)(2,1)} %bitcast.23), calls=%async_computation.1 | async-start | bytes 262144 | tf_op jit(solution)/shard_map/all_to_all | solution.py:72
  17.2 50.9 %all-to-all-start = ((bf16[512,8,256]{0,2,1:T(8,128)(2,1)}), bf16[512,8,256]{0,2,1:T(8,128)(2,1)S(1)}, u32[]{:S(2)}, u32[]{:S(2)}) async-start(bf16[512,8,256]{0,2,1:T(8,128)(2,1)} %bitcast.19), calls=%async_computation | async-start | bytes 4194304 | tf_op jit(solution)/shard_map/all_to_all | solution.py:71
  96.8 13.5 %copy-start.4 = (f32[3,3,2048]{2,1,0:T(4,128)S(1)}, f32[3,3,2048]{2,1,0:T(4,128)}, u32[]{:S(2)}) copy-start(f32[3,3,2048]{2,1,0:T(4,128)} %param.9) | copy-start | bytes 221188
  100.5 59.4 %all-to-all-start.2 = ((bf16[8,512,256]{1,2,0:T(8,128)(2,1)}), bf16[8,512,256]{1,2,0:T(8,128)(2,1)S(1)}, u32[]{:S(2)}, u32[]{:S(2)}) async-start(bf16[8,512,256]{1,2,0:T(8,128)(2,1)} %copy.32), calls=%async_computation.2 | async-start | bytes 4194304 | tf_op jit(solution)/shard_map/all_to_all | solution.py:78
  108.1 45.0 %collective-permute-start = (f32[2,1,2048]{2,0,1:T(2,128)S(1)}, f32[2,1,2048]{2,0,1:T(2,128)S(1)}, u32[]{:S(2)}, u32[]{:S(2)}) collective-permute-start(f32[2,1,2048]{2,0,1:T(2,128)S(1)} %slice_bitcast_fusion), channel_id=1, source_target_pairs={{4,0},{8,4},{12,8},{16,12},{20,16},{24,20},{28,24},{5,1},{9,5},{13... | collective-permute-start | bytes 49160 | tf_op jit(solution)/shard_map/ppermute | solution.py:17
  163.4 1.9 copy-start
  163.4 3.4 %copy-start.1 = (f32[512,1,2048]{0,2,1:T(8,128)}, f32[512,1,2048]{0,2,1:T(8,128)S(1)}, u32[]{:S(2)}) copy-start(f32[512,1,2048]{0,2,1:T(8,128)S(1)} %get-tuple-element.19) | copy-start | bytes 12582916
  167.7 11.2 %collective-permute-start.4 = (f32[2,2,2048]{2,1,0:T(2,128)S(1)}, f32[2,2,2048]{2,1,0:T(2,128)S(1)}, u32[]{:S(2)}, u32[]{:S(2)}) collective-permute-start(f32[2,2,2048]{2,1,0:T(2,128)S(1)} %copy.35), channel_id=1, source_target_pairs={{4,0},{8,4},{12,8},{16,12},{20,16},{24,20},{28,24},{5,1},{9,5},{13... | collective-permute-start | bytes 98312 | tf_op jit(solution)/shard_map/ppermute | solution.py:17
  174.5 30.6 %collective-permute-start.3 = (bf16[128,1,2048]{2,0,1:T(8,128)(2,1)}, bf16[128,1,2048]{2,0,1:T(8,128)(2,1)}, u32[]{:S(2)}, u32[]{:S(2)}) collective-permute-start(bf16[128,1,2048]{2,0,1:T(8,128)(2,1)} %get-tuple-element.14), channel_id=1, source_target_pairs={{0,3},{1,0},{2,1},{3,2},{4,7},{5,4},{6,5},{7,6},{8,11},{9,8},{10,9... | collective-permute-start | bytes 1572872 | tf_op jit(solution)/shard_map/ppermute | solution.py:97
  175.0 32.9 %collective-permute-start.2 = (bf16[128,1,2048]{2,0,1:T(8,128)(2,1)}, bf16[128,1,2048]{2,0,1:T(8,128)(2,1)}, u32[]{:S(2)}, u32[]{:S(2)}) collective-permute-start(bf16[128,1,2048]{2,0,1:T(8,128)(2,1)} %get-tuple-element.15), channel_id=1, source_target_pairs={{0,2},{1,3},{2,0},{3,1},{4,6},{5,7},{6,4},{7,5},{8,10},{9,11},{10,... | collective-permute-start | bytes 1572872 | tf_op jit(solution)/shard_map/ppermute | solution.py:97
  176.6 31.4 %collective-permute-start.1 = (bf16[128,1,2048]{2,0,1:T(8,128)(2,1)}, bf16[128,1,2048]{2,0,1:T(8,128)(2,1)}, u32[]{:S(2)}, u32[]{:S(2)}) collective-permute-start(bf16[128,1,2048]{2,0,1:T(8,128)(2,1)} %get-tuple-element.16), channel_id=1, source_target_pairs={{0,1},{1,2},{2,3},{3,0},{4,5},{5,6},{6,7},{7,4},{8,9},{9,10},{10,1... | collective-permute-start | bytes 1572872 | tf_op jit(solution)/shard_map/ppermute | solution.py:97
  200.5 7.5 %copy-start.3 = (bf16[1,128,1,2048]{3,1,0,2:T(8,128)(2,1)S(1)}, bf16[1,128,1,2048]{3,1,0,2:T(8,128)(2,1)}, u32[]{:S(2)}) copy-start(bf16[1,128,1,2048]{3,1,0,2:T(8,128)(2,1)} %get-tuple-element.13) | copy-start | bytes 1572868
  204.5 27.2 %collective-permute-start.7 = (bf16[128,2,2048]{2,0,1:T(8,128)(2,1)}, bf16[128,2,2048]{2,0,1:T(8,128)(2,1)}, u32[]{:S(2)}, u32[]{:S(2)}) collective-permute-start(bf16[128,2,2048]{2,0,1:T(8,128)(2,1)} %get-tuple-element.10), channel_id=1, source_target_pairs={{0,3},{1,0},{2,1},{3,2},{4,7},{5,4},{6,5},{7,6},{8,11},{9,8},{10,9... | collective-permute-start | bytes 3145736 | tf_op jit(solution)/shard_map/ppermute | solution.py:97
  204.5 45.6 %collective-permute-start.6 = (bf16[128,2,2048]{2,0,1:T(8,128)(2,1)}, bf16[128,2,2048]{2,0,1:T(8,128)(2,1)}, u32[]{:S(2)}, u32[]{:S(2)}) collective-permute-start(bf16[128,2,2048]{2,0,1:T(8,128)(2,1)} %get-tuple-element.11), channel_id=1, source_target_pairs={{0,2},{1,3},{2,0},{3,1},{4,6},{5,7},{6,4},{7,5},{8,10},{9,11},{10,... | collective-permute-start | bytes 3145736 | tf_op jit(solution)/shard_map/ppermute | solution.py:97
  205.1 45.0 %collective-permute-start.5 = (bf16[128,2,2048]{2,0,1:T(8,128)(2,1)}, bf16[128,2,2048]{2,0,1:T(8,128)(2,1)}, u32[]{:S(2)}, u32[]{:S(2)}) collective-permute-start(bf16[128,2,2048]{2,0,1:T(8,128)(2,1)} %get-tuple-element.12), channel_id=1, source_target_pairs={{0,1},{1,2},{2,3},{3,0},{4,5},{5,6},{6,7},{7,4},{8,9},{9,10},{10,1... | collective-permute-start | bytes 3145736 | tf_op jit(solution)/shard_map/ppermute | solution.py:97
  263.4 6.4 %copy-start.2 = (bf16[128,1,4,2048]{0,3,2,1:T(8,128)(2,1)S(1)}, bf16[128,1,4,2048]{0,3,2,1:T(8,128)(2,1)}, u32[]{:S(2)}) copy-start(bf16[128,1,4,2048]{0,3,2,1:T(8,128)(2,1)} %copy.25) | copy-start | bytes 6291460

commit v6 on v5

--- a/solution.py
+++ b/solution.py
@@ -82,7 +82,8 @@
     stacked = jnp.stack([grad_key, grad_value], 1)
     pair_proj = short_filter(stacked, short_taps[1:], block_rows)
     pair_rows = spread_rows(pair_proj, "chan")
-    return jnp.concatenate([query_rows, pair_rows], 1)
+    count = lax.axis_size("chan")
+    return place_rows([query_rows, pair_rows], count, block_rows // count, grad_out.shape[1])
 
 
 def spread_rows(value, axis):
@@ -90,15 +91,23 @@
     me = lax.axis_index(axis)
     rows, planes, channels = value.shape
     chunks = value.reshape(count, rows // count, planes, channels)
-    pieces = [lax.dynamic_index_in_dim(chunks, me, 0, keepdims=False)]
+    pieces = [(me, lax.dynamic_index_in_dim(chunks, me, 0, keepdims=False))]
     for step in range(1, count):
         outgoing = lax.dynamic_index_in_dim(chunks, (me + step) % count, 0, keepdims=False)
         pairs = [(source, (source + step) % count) for source in range(count)]
-        pieces.append(lax.ppermute(outgoing, axis, pairs))
-    gathered = jnp.stack(pieces)
-    order = (me - jnp.arange(count)) % count
-    placed = jnp.take(gathered, order, axis=0)
-    return placed.transpose(1, 2, 0, 3).reshape(rows // count, planes, count * channels)
+        pieces.append(((me + count - step) % count, lax.ppermute(outgoing, axis, pairs)))
+    return pieces
+
+
+def place_rows(parts, count, rows, channels):
+    planes = sum(pieces[0][1].shape[1] for pieces in parts)
+    out = jnp.zeros((rows, planes, count * channels), parts[0][0][1].dtype)
+    plane = 0
+    for pieces in parts:
+        for source, piece in pieces:
+            out = lax.dynamic_update_slice(out, piece, (0, plane, source * channels))
+        plane += pieces[0][1].shape[1]
+    return out
 
 
 def short_filter(stacked, taps, block_rows):

time: 287 us -> 285 us (level)
  local copies, waits for them, and re-layouts: 77.6 us -> 99.9 us
  other arithmetic: 52.8 us -> 34.6 us
  waiting for transfers between devices: 106 us -> 103 us
    dynamic_slice x1 -> x5, local copies, waits for them, and re-layouts: 2.97 us -> 33.9 us  [the longest x4 32.6 us: spread_rows(): lax.dynamic_index_in_dim(chunks, (me + step) % count, 0, keepdims=False)]
    dynamic_update_slice x0 -> x8, local copies, waits for them, and re-layouts: none -> 14.7 us  [place_rows(): out = lax.dynamic_update_slice(out, piece, (0, plane, source * channels))]
    concatenate x1 -> x0, local copies, waits for them, and re-layouts: 8.62 us -> none  [on_device(): return jnp.concatenate([query_rows, pair_rows], 1)]
    gather x2 -> x0, local copies, waits for them, and re-layouts: 6.94 us -> none  [spread_rows(): placed = jnp.take(gathered, order, axis=0)]
    reshape x0 -> x1, local copies, waits for them, and re-layouts: none -> 6.9 us  [spread_rows(): chunks = value.reshape(count, rows // count, planes, channels)]
    select_n x1 -> x0, local copies, waits for them, and re-layouts: 6.42 us -> none  [spread_rows(): placed = jnp.take(gathered, order, axis=0)]
    convert_element_type x1 -> x0, local copies, waits for them, and re-layouts: 6.19 us -> none  [short_filter(): return result.astype(jnp.bfloat16)]
    concatenate x1 -> x0, other arithmetic: 5.38 us -> none  [on_device(): return jnp.concatenate([query_rows, pair_rows], 1)]
  transfers between devices with their start and end apart: 11 -> 11, of which waited for: 4 -> 4; matrix products, arithmetic and copies ran while one was open for 25% -> 38% of each run, Pallas kernels for 0% -> 0%
where the time goes in v6:
time: 285 us; the launch traced here: 283 us
  waiting for transfers between devices  103 us (36%)
  local copies, waits for them, and re-layouts  99.9 us (35%)
  other arithmetic  34.6 us (12%)
  starting transfers between devices  29.2 us (10%)
  Pallas kernels  15.7 us (6%)
    all_to_all x1, waiting for transfers between devices, on_device(): lax.all_to_all(grad_mixed, 'seq', split_axis=1, concat_axis=0, tiled=True)  42.4 us
    dynamic_slice x4, local copies, waits for them, and re-layouts, spread_rows(): lax.dynamic_index_in_dim(chunks, (me + step) % count, 0, keepdims=False)  32.6 us
    ppermute x6, waiting for transfers between devices, spread_rows(): lax.ppermute(outgoing, axis, pairs)  30.5 us
    ppermute x2, waiting for transfers between devices, shifted(): lax.ppermute(value, axis, [(source, source + steps) for source in range(l...  29.8 us
    convert_element_type x2, other arithmetic, short_filter(): return result.astype(jnp.bfloat16)  16 us
    pallas_call x1, Pallas kernels, correlate(): pl.pallas_call(correlate_kernel, out_shape=jax.ShapeDtypeStruct((groups,...  15.7 us
    unnamed x15, local copies, waits for them, and re-layouts  15.6 us
    dynamic_update_slice x8, local copies, waits for them, and re-layouts, place_rows(): out = lax.dynamic_update_slice(out, piece, (0, plane, source * channels))  14.7 us
  transfers between devices with their start and end apart: 11, of which 4 were waited for; matrix products, arithmetic and copies ran while one was open for 38% of the time, Pallas kernels for 0%

profile of v6, /device:TPU:18, one launch (start us, length us, event | category | flops | bytes accessed | tf_op | source)
XLA Modules:
  0.0 282.6 jit_solution(380854466798655767)
XLA Ops:
  0.0 1.7 copy.51
  1.7 5.2 %all-to-all-start.1 = ((bf16[512,8,16]{0,2,1:T(8,128)(2,1)}), bf16[512,8,16]{0,2,1:T(8,128)(2,1)S(1)}, u32[]{:S(2)}, u32[]{:S(2)}) async-start(bf16[512,8,16]{0,2,1:T(8,128)(2,1)} %bitcast.18), calls=%async_computation.1 | async-start | bytes 262144 | tf_op jit(solution)/shard_map/all_to_all | solution.py:72
  6.9 7.8 %convert_multiply_fusion.1 = (f32[512,2048]{1,0:T(8,128)}, f32[512,1,2048]{2,0,1:T(8,128)}, bf16[512,2048]{1,0:T(8,128)(2,1)S(1)}) fusion(bf16[512,2048]{1,0:T(8,128)(2,1)} %param.5, bf16[512,2048]{1,0:T(8,128)(2,1)} %param.7, bf16[512,3,2048]{2,0,1:T(8,128)(2,1)} %param.6), kind=kLoop, calls=%fused_computation.11 | loop fusion | flops 6291456 | bytes 16777216 | tf_op jit(solution)/shard_map/mul | solution.py:69
  14.7 2.5 copy.48
  17.2 0.0 all-to-all-done.1
  17.2 5.1 %all-to-all-start = ((bf16[512,8,256]{0,2,1:T(8,128)(2,1)}), bf16[512,8,256]{0,2,1:T(8,128)(2,1)S(1)}, u32[]{:S(2)}, u32[]{:S(2)}) async-start(bf16[512,8,256]{0,2,1:T(8,128)(2,1)} %bitcast.14), calls=%async_computation | async-start | bytes 4194304 | tf_op jit(solution)/shard_map/all_to_all | solution.py:71
  22.4 2.3 rev.3
  24.6 0.1 concatenate.10
  24.7 0.9 reshape.61.h_ref
  25.6 42.4 %all-to-all-done = bf16[512,8,256]{0,2,1:T(8,128)(2,1)S(1)} async-done(((bf16[512,8,256]{0,2,1:T(8,128)(2,1)}), bf16[512,8,256]{0,2,1:T(8,128)(2,1)S(1)}, u32[]{:S(2)}, u32[]{:S(2)}) %all-to-all-start) | async-done | bytes 2097184 | tf_op jit(solution)/shard_map/all_to_all | solution.py:71
  68.1 2.5 copy.49
  70.6 2.7 reshape.59
  73.3 2.3 copy.50
  75.5 15.7 %shard_map.55 = f32[16,256,256]{2,1,0:T(8,128)} custom-call(bf16[16,256,256]{2,1,0:T(8,128)(2,1)} %bitcast.69, f32[16,1,4352]{2,1,0:T(1,128)} %reshape.61.h_ref), custom_call_target="tpu_custom_call" | custom-call | flops 4563402752 | bytes 6569984 | tf_op jit(solution)/shard_map/pallas_call | solution.py:46
  91.3 2.4 convert_element_type.74
  93.7 0.9 copy.73
  94.6 2.2 convert_element_type.77
  96.9 3.7 %copy.54 = bf16[8,512,256]{1,2,0:T(8,128)(2,1)} copy(bf16[8,512,256]{1,0,2:T(8,128)(2,1)} %convert_element_type.77) | data formatting | bytes 4194304 | tf_op jit(solution)/shard_map/convert_element_type | solution.py:77
  100.5 6.8 %all-to-all-start.2 = ((bf16[8,512,256]{1,2,0:T(8,128)(2,1)}), bf16[8,512,256]{1,2,0:T(8,128)(2,1)S(1)}, u32[]{:S(2)}, u32[]{:S(2)}) async-start(bf16[8,512,256]{1,2,0:T(8,128)(2,1)} %copy.54), calls=%async_computation.2 | async-start | bytes 4194304 | tf_op jit(solution)/shard_map/all_to_all | solution.py:78
  107.3 0.8 slice_bitcast_fusion
  108.2 2.2 collective-permute-start
  110.4 4.8 %fusion.13 = (bf16[512,1,2048]{2,0,1:T(8,128)(2,1)}, bf16[512,1,2048]{2,0,1:T(8,128)(2,1)}) fusion(bf16[512,3,2048]{2,0,1:T(8,128)(2,1)} %param.6), kind=kLoop, calls=%fused_computation.47 | loop fusion | bytes 8388608 | tf_op jit(solution)/shard_map/slice | solution.py:68
  115.3 4.0 %copy.66 = bf16[512,1,2048]{0,2,1:T(8,128)(2,1)} copy(bf16[512,1,2048]{2,0,1:T(8,128)(2,1)} %get-tuple-element.5) | data formatting | bytes 4194304
  119.3 4.0 %copy.67 = bf16[512,1,2048]{0,2,1:T(8,128)(2,1)} copy(bf16[512,1,2048]{2,0,1:T(8,128)(2,1)} %get-tuple-element.6) | data formatting | bytes 4194304
  123.3 29.8 %collective-permute-done = f32[2,1,2048]{2,0,1:T(2,128)S(1)} collective-permute-done((f32[2,1,2048]{2,0,1:T(2,128)S(1)}, f32[2,1,2048]{2,0,1:T(2,128)S(1)}, u32[]{:S(2)}, u32[]{:S(2)}) %collective-permute-start) | collective-permute-done | bytes 16416 | tf_op jit(solution)/shard_map/ppermute | solution.py:17
  153.1 5.8 %fusion.8 = bf16[512,1,2048]{2,0,1:T(8,128)(2,1)S(1)} fusion(f32[512,1,2048]{2,0,1:T(8,128)} %get-tuple-element.12, f32[2,1,2048]{2,0,1:T(2,128)S(1)} %collective-permute-done, f32[2048]{0:T(1024)S(1)} %bitcast.73, f32[2048]{0:T(1024)S(1)} %bitcast.74, f32[2048]{0:T(1024)S(1)} %bitcast.72, bf16[512,2048]{1,0:T(8,128)(2,1)} %param.7, bf16[512,2048]{1,0:T(8,128)(2,1)} %param.5), kind=kLoop, calls=%fused_computation.18 | loop fusion | flops 11534336 | bytes 10526720 | tf_op jit(solution)/shard_map/convert_element_type | solution.py:120
  158.9 0.0 copy-start.2
  158.9 1.1 dynamic-slice_bitcast_fusion
  160.1 0.5 collective-permute-start.3
  160.6 1.5 collective-permute-start.2
  162.2 2.4 collective-permute-start.1
  164.5 0.0 all-to-all-done.2
  164.6 3.5 %bitcast_multiply_fusion.1 = (f32[512,1,2048]{0,2,1:T(8,128)S(1)}, f32[512,1,2048]{0,2,1:T(8,128)S(1)}) fusion(bf16[8,512,256]{1,2,0:T(8,128)(2,1)S(1)} %all-to-all-done.2, bf16[512,1,2048]{0,2,1:T(8,128)(2,1)} %copy.66, bf16[512,1,2048]{0,2,1:T(8,128)(2,1)} %copy.67), kind=kLoop, calls=%fused_computation.23 | loop fusion | flops 5242880 | bytes 14680064 | tf_op jit(solution)/shard_map/mul | solution.py:80
  168.1 2.0 copy-done
  170.1 1.3 copy-done.1
  171.3 0.3 fusion.11
  171.6 0.6 copy.57
  172.2 3.0 %collective-permute-start.4 = (f32[2,2,2048]{2,1,0:T(2,128)S(1)}, f32[2,2,2048]{2,1,0:T(2,128)S(1)}, u32[]{:S(2)}, u32[]{:S(2)}) collective-permute-start(f32[2,2,2048]{2,1,0:T(2,128)S(1)} %copy.57), channel_id=1, source_target_pairs={{4,0},{8,4},{12,8},{16,12},{20,16},{24,20},{28,24},{5,1},{9,5},{13... | collective-permute-start | bytes 98312 | tf_op jit(solution)/shard_map/ppermute | solution.py:17
  175.2 0.7 broadcast_in_dim.7
  175.9 1.1 bitcast_dynamic-update-slice_fusion.1
  177.0 0.0 copy-start.3
  177.1 2.7 copy-done.3
  179.7 0.0 collective-permute-done.4
  179.7 0.6 copy.58
  180.4 4.5 %pad_maximum_fusion = f32[514,2,2048]{0,2,1:T(8,128)S(1)} fusion(f32[2,2,2048]{0,2,1:T(8,128)S(1)} %copy.58, f32[512,1,2048]{0,2,1:T(8,128)} %copy-done.1, f32[512,1,2048]{0,2,1:T(8,128)} %copy-done), kind=kLoop, calls=%fused_computation | loop fusion | flops 4210688 | bytes 16842752 | tf_op jit(solution)/shard_map/concatenate | solution.py:116
  184.9 10.2 %fusion.3 = bf16[512,2,2048]{0,2,1:T(8,128)(2,1)} fusion(f32[512,1,2048]{0,2,1:T(8,128)} %copy-done.1, f32[512,1,2048]{0,2,1:T(8,128)} %copy-done, f32[514,2,2048]{0,2,1:T(8,128)S(1)} %pad_maximum_fusion, f32[2,2048]{1,0:T(2,128)S(1)} %get-tuple-element.25, f32[2,2048]{1,0:T(2,128)S(1)} %get-tuple-element.26, f32[2,2048]{1,0:T(2,128)S(1)} %bitcast.71), kind=kLoop, calls=%fused_computation.7 | loop fusion | flops 14680064 | bytes 29409280 | tf_op jit(solution)/shard_map/convert_element_type | solution.py:120
  195.1 6.9 %reshape.62 = bf16[4,128,2,2048]{1,0,3,2:T(4,128)(2,1)} reshape(bf16[512,2,2048]{0,2,1:T(8,128)(2,1)} %fusion.3) | data formatting | bytes 8388608 | tf_op jit(solution)/shard_map/reshape | solution.py:93
  202.0 15.1 %constant_dynamic-slice_fusion = (bf16[1,128,2,2048]{1,0,3,2:T(2,128)(2,1)}, bf16[1,128,2,2048]{1,0,3,2:T(2,128)(2,1)}, bf16[1,128,2,2048]{1,0,3,2:T(2,128)(2,1)}, bf16[1,128,2,2048]{1,0,3,2:T(2,128)(2,1)S(1)}) fusion(bf16[4,128,2,2048]{1,0,3,2:T(4,128)(2,1)} %reshape.62, s32[]{:T(128)S(6)} %select_n.76, s32[]{:T(128)S(6)} %select_n.74, s32[]{:T(128)S(6)} %select_n.70, ...), kind=kLoop, calls=%fused_computation.36 | loop fusion | bytes 8388624 | tf_op jit(solution)/shard_map/jit(dynamic_index_in_dim)/dynamic_slice | solution.py:96
  217.1 5.9 %copy.60 = bf16[1,128,2,2048]{3,1,2,0:T(8,128)(2,1)} copy(bf16[1,128,2,2048]{1,0,3,2:T(2,128)(2,1)} %get-tuple-element.9) | data formatting | bytes 2097152 | tf_op jit(solution)/shard_map/jit(dynamic_index_in_dim)/dynamic_slice | solution.py:96
  222.9 0.3 collective-permute-start.5
  223.2 1.9 constant_dynamic-update-slice_fusion.4
  225.1 5.8 %copy.61 = bf16[1,128,2,2048]{3,1,2,0:T(8,128)(2,1)} copy(bf16[1,128,2,2048]{1,0,3,2:T(2,128)(2,1)} %get-tuple-element.8) | data formatting | bytes 2097152 | tf_op jit(solution)/shard_map/jit(dynamic_index_in_dim)/dynamic_slice | solution.py:96
  230.9 0.8 collective-permute-start.6
  231.8 1.9 constant_dynamic-update-slice_fusion.3
  233.6 5.8 %copy.62 = bf16[1,128,2,2048]{3,1,2,0:T(8,128)(2,1)} copy(bf16[1,128,2,2048]{1,0,3,2:T(2,128)(2,1)} %get-tuple-element.7) | data formatting | bytes 2097152 | tf_op jit(solution)/shard_map/jit(dynamic_index_in_dim)/dynamic_slice | solution.py:96
  239.5 1.4 collective-permute-start.7
  240.9 1.9 constant_dynamic-update-slice_fusion.2
  242.8 1.3 copy.59
  244.1 1.0 bitcast_dynamic-update-slice_fusion
  245.1 4.2 %collective-permute-done.5 = bf16[128,2,2048]{2,0,1:T(8,128)(2,1)} collective-permute-done((bf16[128,2,2048]{2,0,1:T(8,128)(2,1)}, bf16[128,2,2048]{2,0,1:T(8,128)(2,1)}, u32[]{:S(2)}, u32[]{:S(2)}) %collective-permute-start.5) | collective-permute-done | bytes 1048608 | tf_op jit(solution)/shard_map/ppermute | solution.py:98
  249.3 2.3 constant_dynamic-update-slice_fusion.1
  251.6 26.4 %collective-permute-done.6 = bf16[128,2,2048]{2,0,1:T(8,128)(2,1)} collective-permute-done((bf16[128,2,2048]{2,0,1:T(8,128)(2,1)}, bf16[128,2,2048]{2,0,1:T(8,128)(2,1)}, u32[]{:S(2)}, u32[]{:S(2)}) %collective-permute-start.6) | collective-permute-done | bytes 1048608 | tf_op jit(solution)/shard_map/ppermute | solution.py:98
  277.9 2.3 constant_dynamic-update-slice_fusion
  280.3 2.3 constant_dynamic-update-slice_fusion.5
  (15 shorter events, 0.1 us)
Async XLA Ops:
  1.7 15.5 %all-to-all-start.1 = ((bf16[512,8,16]{0,2,1:T(8,128)(2,1)}), bf16[512,8,16]{0,2,1:T(8,128)(2,1)S(1)}, u32[]{:S(2)}, u32[]{:S(2)}) async-start(bf16[512,8,16]{0,2,1:T(8,128)(2,1)} %bitcast.18), calls=%async_computation.1 | async-start | bytes 262144 | tf_op jit(solution)/shard_map/all_to_all | solution.py:72
  17.2 50.9 %all-to-all-start = ((bf16[512,8,256]{0,2,1:T(8,128)(2,1)}), bf16[512,8,256]{0,2,1:T(8,128)(2,1)S(1)}, u32[]{:S(2)}, u32[]{:S(2)}) async-start(bf16[512,8,256]{0,2,1:T(8,128)(2,1)} %bitcast.14), calls=%async_computation | async-start | bytes 4194304 | tf_op jit(solution)/shard_map/all_to_all | solution.py:71
  96.8 13.5 %copy-start.4 = (f32[3,3,2048]{2,1,0:T(4,128)S(1)}, f32[3,3,2048]{2,1,0:T(4,128)}, u32[]{:S(2)}) copy-start(f32[3,3,2048]{2,1,0:T(4,128)} %param.9) | copy-start | bytes 221188
  100.5 64.0 %all-to-all-start.2 = ((bf16[8,512,256]{1,2,0:T(8,128)(2,1)}), bf16[8,512,256]{1,2,0:T(8,128)(2,1)S(1)}, u32[]{:S(2)}, u32[]{:S(2)}) async-start(bf16[8,512,256]{1,2,0:T(8,128)(2,1)} %copy.54), calls=%async_computation.2 | async-start | bytes 4194304 | tf_op jit(solution)/shard_map/all_to_all | solution.py:78
  108.2 45.0 %collective-permute-start = (f32[2,1,2048]{2,0,1:T(2,128)S(1)}, f32[2,1,2048]{2,0,1:T(2,128)S(1)}, u32[]{:S(2)}, u32[]{:S(2)}) collective-permute-start(f32[2,1,2048]{2,0,1:T(2,128)S(1)} %slice_bitcast_fusion), channel_id=1, source_target_pairs={{4,0},{8,4},{12,8},{16,12},{20,16},{24,20},{28,24},{5,1},{9,5},{13... | collective-permute-start | bytes 49160 | tf_op jit(solution)/shard_map/ppermute | solution.py:17
  158.9 3.2 %copy-start.2 = (bf16[512,1,2048]{2,0,1:T(8,128)(2,1)}, bf16[512,1,2048]{2,0,1:T(8,128)(2,1)S(1)}, u32[]{:S(2)}) copy-start(bf16[512,1,2048]{2,0,1:T(8,128)(2,1)S(1)} %fusion.8) | copy-start | bytes 6291460
  160.1 80.8 %collective-permute-start.3 = (bf16[128,1,2048]{2,0,1:T(8,128)(2,1)S(1)}, bf16[128,1,2048]{2,0,1:T(8,128)(2,1)}, u32[]{:S(2)}, u32[]{:S(2)}) collective-permute-start(bf16[128,1,2048]{2,0,1:T(8,128)(2,1)S(1)} %get-tuple-element.16), channel_id=1, source_target_pairs={{0,3},{1,0},{2,1},{3,2},{4,7},{5,4},{6,5},{7,6},{8,11},{9,8},{10,9... | collective-permute-start | bytes 1572872 | tf_op jit(solution)/shard_map/ppermute | solution.py:98
  160.6 71.1 %collective-permute-start.2 = (bf16[128,1,2048]{2,0,1:T(8,128)(2,1)S(1)}, bf16[128,1,2048]{2,0,1:T(8,128)(2,1)}, u32[]{:S(2)}, u32[]{:S(2)}) collective-permute-start(bf16[128,1,2048]{2,0,1:T(8,128)(2,1)S(1)} %get-tuple-element.17), channel_id=1, source_target_pairs={{0,2},{1,3},{2,0},{3,1},{4,6},{5,7},{6,4},{7,5},{8,10},{9,11},{10,... | collective-permute-start | bytes 1572872 | tf_op jit(solution)/shard_map/ppermute | solution.py:98
  162.2 61.1 %collective-permute-start.1 = (bf16[128,1,2048]{2,0,1:T(8,128)(2,1)}, bf16[128,1,2048]{2,0,1:T(8,128)(2,1)}, u32[]{:S(2)}, u32[]{:S(2)}) collective-permute-start(bf16[128,1,2048]{2,0,1:T(8,128)(2,1)} %get-tuple-element.18), channel_id=1, source_target_pairs={{0,1},{1,2},{2,3},{3,0},{4,5},{5,6},{6,7},{7,4},{8,9},{9,10},{10,1... | collective-permute-start | bytes 1572872 | tf_op jit(solution)/shard_map/ppermute | solution.py:98
  168.1 2.0 copy-start
  168.1 3.2 %copy-start.1 = (f32[512,1,2048]{0,2,1:T(8,128)}, f32[512,1,2048]{0,2,1:T(8,128)S(1)}, u32[]{:S(2)}) copy-start(f32[512,1,2048]{0,2,1:T(8,128)S(1)} %get-tuple-element.14) | copy-start | bytes 12582916
  172.2 7.5 %collective-permute-start.4 = (f32[2,2,2048]{2,1,0:T(2,128)S(1)}, f32[2,2,2048]{2,1,0:T(2,128)S(1)}, u32[]{:S(2)}, u32[]{:S(2)}) collective-permute-start(f32[2,2,2048]{2,1,0:T(2,128)S(1)} %copy.57), channel_id=1, source_target_pairs={{4,0},{8,4},{12,8},{16,12},{20,16},{24,20},{28,24},{5,1},{9,5},{13... | collective-permute-start | bytes 98312 | tf_op jit(solution)/shard_map/ppermute | solution.py:17
  177.0 2.7 copy-start.3
  222.9 26.3 %collective-permute-start.5 = (bf16[128,2,2048]{2,0,1:T(8,128)(2,1)}, bf16[128,2,2048]{2,0,1:T(8,128)(2,1)}, u32[]{:S(2)}, u32[]{:S(2)}) collective-permute-start(bf16[128,2,2048]{2,0,1:T(8,128)(2,1)} %bitcast.27), channel_id=1, source_target_pairs={{0,1},{1,2},{2,3},{3,0},{4,5},{5,6},{6,7},{7,4},{8,9},{9,10},{10,1... | collective-permute-start | bytes 3145736 | tf_op jit(solution)/shard_map/ppermute | solution.py:98
  230.9 47.0 %collective-permute-start.6 = (bf16[128,2,2048]{2,0,1:T(8,128)(2,1)}, bf16[128,2,2048]{2,0,1:T(8,128)(2,1)}, u32[]{:S(2)}, u32[]{:S(2)}) collective-permute-start(bf16[128,2,2048]{2,0,1:T(8,128)(2,1)} %bitcast.28), channel_id=1, source_target_pairs={{0,2},{1,3},{2,0},{3,1},{4,6},{5,7},{6,4},{7,5},{8,10},{9,11},{10,... | collective-permute-start | bytes 3145736 | tf_op jit(solution)/shard_map/ppermute | solution.py:98
  239.5 40.8 %collective-permute-start.7 = (bf16[128,2,2048]{2,0,1:T(8,128)(2,1)}, bf16[128,2,2048]{2,0,1:T(8,128)(2,1)}, u32[]{:S(2)}, u32[]{:S(2)}) collective-permute-start(bf16[128,2,2048]{2,0,1:T(8,128)(2,1)} %bitcast.29), channel_id=1, source_target_pairs={{0,3},{1,0},{2,1},{3,2},{4,7},{5,4},{6,5},{7,6},{8,11},{9,8},{10,9... | collective-permute-start | bytes 3145736 | tf_op jit(solution)/shard_map/ppermute | solution.py:98

commit v7 on v1

--- a/solution.py
+++ b/solution.py
@@ -61,7 +61,7 @@
 
 
 def on_device(grad_out, qkv_saved, conv_saved, long_taps, short_taps):
-    block_rows = grad_out.shape[0]
+    block_rows, channels = grad_out.shape
     out_wide = grad_out.astype(jnp.float32)
     query = qkv_saved[:, 0, :]
     key_part = qkv_saved[:, 1, :]
@@ -70,22 +70,79 @@
     grad_mixed = (out_wide * query.astype(jnp.float32)).astype(jnp.bfloat16)
     mixed_cols = lax.all_to_all(grad_mixed, "seq", split_axis=1, concat_axis=0, tiled=True)
     taps_cols = lax.all_to_all(long_taps, "seq", split_axis=1, concat_axis=0, tiled=True)
+    query_rows = spread_rows(short_filter(grad_query, short_taps[0]), "chan")
     z_cols = correlate(mixed_cols, taps_cols)
-    grad_z = lax.all_to_all(z_cols, "seq", split_axis=0, concat_axis=1, tiled=True)
-    grad_key = grad_z * value_part.astype(jnp.float32)
-    grad_value = grad_z * key_part.astype(jnp.float32)
-    stacked = jnp.stack([grad_query, grad_key, grad_value], 1)
-    short_len = short_taps.shape[1]
-    borrowed = shifted(stacked[: short_len - 1], "seq", -1)
-    extended = jnp.concatenate([stacked, borrowed], 0)
-    result = jnp.zeros_like(stacked)
+    shards = lax.axis_size("seq")
+    z_narrow = z_cols.astype(jnp.bfloat16).reshape(shards, block_rows, -1)
+    z_split = lax.all_to_all(z_narrow, "seq", split_axis=0, concat_axis=0, tiled=True)
+    z_split = z_split.astype(jnp.float32)
+    width = z_split.shape[2]
+    value_split = value_part.reshape(block_rows, shards, width).transpose(1, 0, 2)
+    key_split = key_part.reshape(block_rows, shards, width).transpose(1, 0, 2)
+    grad_key = z_split * value_split.astype(jnp.float32)
+    grad_value = z_split * key_split.astype(jnp.float32)
+    key_rows = spread_split(split_filter(grad_key, short_taps[1]), "chan")
+    value_rows = spread_split(split_filter(grad_value, short_taps[2]), "chan")
+    count = lax.axis_size("chan")
+    planes = [query_rows, key_rows, value_rows]
+    out = jnp.zeros((block_rows // count, len(planes), count * channels), jnp.bfloat16)
+    for plane, pieces in enumerate(planes):
+        for source, piece in pieces:
+            out = lax.dynamic_update_slice(out, piece[:, None, :], (0, plane, source * channels))
+    return out
+
+
+def spread_rows(value, axis):
+    count = lax.axis_size(axis)
+    me = lax.axis_index(axis)
+    rows, channels = value.shape
+    chunks = value.reshape(count, rows // count, channels)
+    pieces = [(me, lax.dynamic_index_in_dim(chunks, me, 0, keepdims=False))]
+    for step in range(1, count):
+        outgoing = lax.dynamic_index_in_dim(chunks, (me + step) % count, 0, keepdims=False)
+        pairs = [(source, (source + step) % count) for source in range(count)]
+        pieces.append(((me + count - step) % count, lax.ppermute(outgoing, axis, pairs)))
+    return pieces
+
+
+def split_filter(rows, taps):
+    shards, block_rows, width = rows.shape
+    short_len = taps.shape[0]
+    taps = taps.reshape(short_len, shards, 1, width)
+    borrowed = shifted(rows[:, : short_len - 1], "seq", -1)
+    extended = jnp.concatenate([rows, borrowed], 1)
+    result = jnp.zeros_like(rows)
     for lag_index in range(short_len):
-        result = (
-            result
-            + short_taps[:, lag_index, :][None] * extended[lag_index : lag_index + block_rows]
-        )
-    mixed = result.astype(jnp.bfloat16)
-    return lax.all_to_all(mixed, "chan", split_axis=0, concat_axis=2, tiled=True)
+        result = result + taps[lag_index] * extended[:, lag_index : lag_index + block_rows]
+    return result.astype(jnp.bfloat16)
+
+
+def spread_split(value, axis):
+    count = lax.axis_size(axis)
+    me = lax.axis_index(axis)
+    shards, rows, width = value.shape
+    chunks = value.reshape(shards, count, rows // count, width)
+
+    def flat(piece):
+        return piece.transpose(1, 0, 2).reshape(rows // count, shards * width)
+
+    pieces = [(me, flat(lax.dynamic_index_in_dim(chunks, me, 1, keepdims=False)))]
+    for step in range(1, count):
+        outgoing = lax.dynamic_index_in_dim(chunks, (me + step) % count, 1, keepdims=False)
+        pairs = [(source, (source + step) % count) for source in range(count)]
+        pieces.append(((me + count - step) % count, flat(lax.ppermute(outgoing, axis, pairs))))
+    return pieces
+
+
+def short_filter(rows, taps):
+    block_rows = rows.shape[0]
+    short_len = taps.shape[0]
+    borrowed = shifted(rows[: short_len - 1], "seq", -1)
+    extended = jnp.concatenate([rows, borrowed], 0)
+    result = jnp.zeros_like(rows)
+    for lag_index in range(short_len):
+        result = result + taps[lag_index][None] * extended[lag_index : lag_index + block_rows]
+    return result.astype(jnp.bfloat16)
 
 
 def solution(mesh):

time: 402 us -> 296 us (0.74); the launches traced: 395 us -> 294 us
  blocking collectives: 99.7 us -> 0 us
  waiting for transfers between devices: 128 us -> 93.5 us
  local copies, waits for them, and re-layouts: 97.6 us -> 113 us
  starting transfers between devices: 20 us -> 34.4 us
    all_to_all x1 -> x0, blocking collectives: 99.7 us -> none  [on_device(): lax.all_to_all(mixed, 'chan', split_axis=0, concat_axis=2, tiled=True)]
    all_to_all x1, waiting for transfers between devices: 84 us -> 0.01 us  [on_device(): lax.all_to_all(z_narrow, 'seq', split_axis=0, concat_axis=0, tiled=True)]
    all_to_all x4 -> x0, local copies, waits for them, and re-layouts: 34.8 us -> none  [the longest x2 23.1 us: on_device(): lax.all_to_all(mixed, 'chan', split_axis=0, concat_axis=2, tiled=True)]
    ppermute x1 -> x3, waiting for transfers between devices: 1.67 us -> 29.7 us  [shifted(): lax.ppermute(value, axis, [(source, source + steps) for source in range(l...]
    ppermute x0 -> x9, waiting for transfers between devices: none -> 21.3 us  [the longest x6 21.3 us: spread_split(): lax.ppermute(outgoing, axis, pairs)]
    convert_element_type x1 -> x5, other arithmetic: 13.3 us -> 31.4 us  [the longest x2 17.1 us: split_filter(): return result.astype(jnp.bfloat16)]
    dynamic_slice x0 -> x1, local copies, waits for them, and re-layouts: none -> 14.6 us  [spread_split(): lax.dynamic_index_in_dim(chunks, (me + step) % count, 1, keepdims=False)]
    dynamic_update_slice x0 -> x12, local copies, waits for them, and re-layouts: none -> 14.1 us  [on_device(): lax.dynamic_update_slice(out, piece[:, None, :], (0, plane, source * chan...]
  transfers between devices with their start and end apart: 4 -> 15, of which waited for: 3 -> 5; matrix products, arithmetic and copies ran while one was open for 8% -> 41% of each run, Pallas kernels for 0% -> 0%
where the time goes in v7:
time: 296 us; the launch traced here: 294 us
  local copies, waits for them, and re-layouts  113 us (38%)
  waiting for transfers between devices  93.5 us (32%)
  other arithmetic  36.9 us (12%)
  starting transfers between devices  34.4 us (12%)
  Pallas kernels  15.7 us (5%)
    all_to_all x1, waiting for transfers between devices, on_device(): lax.all_to_all(grad_mixed, 'seq', split_axis=1, concat_axis=0, tiled=True)  42.5 us
    unnamed x21, local copies, waits for them, and re-layouts  30.8 us
    ppermute x3, waiting for transfers between devices, shifted(): lax.ppermute(value, axis, [(source, source + steps) for source in range(l...  29.7 us
    ppermute x6, waiting for transfers between devices, spread_split(): lax.ppermute(outgoing, axis, pairs)  21.3 us
    convert_element_type x2, other arithmetic, split_filter(): return result.astype(jnp.bfloat16)  17.1 us
    pallas_call x1, Pallas kernels, correlate(): pl.pallas_call(correlate_kernel, out_shape=jax.ShapeDtypeStruct((groups,...  15.7 us
    dynamic_slice x1, local copies, waits for them, and re-layouts, spread_split(): lax.dynamic_index_in_dim(chunks, (me + step) % count, 1, keepdims=False)  14.6 us
    dynamic_update_slice x12, local copies, waits for them, and re-layouts, on_device(): lax.dynamic_update_slice(out, piece[:, None, :], (0, plane, source * chan...  14.1 us
  transfers between devices with their start and end apart: 15, of which 5 were waited for; matrix products, arithmetic and copies ran while one was open for 41% of the time, Pallas kernels for 0%

profile of v7, /device:TPU:18, one launch (start us, length us, event | category | flops | bytes accessed | tf_op | source)
XLA Modules:
  0.0 294.1 jit_solution(12393315629575389698)
XLA Ops:
  0.0 1.7 copy.83
  1.7 5.2 %all-to-all-start.1 = ((bf16[512,8,16]{0,2,1:T(8,128)(2,1)}), bf16[512,8,16]{0,2,1:T(8,128)(2,1)S(1)}, u32[]{:S(2)}, u32[]{:S(2)}) async-start(bf16[512,8,16]{0,2,1:T(8,128)(2,1)} %bitcast.16), calls=%async_computation.1 | async-start | bytes 262144 | tf_op jit(solution)/shard_map/all_to_all | solution.py:72
  6.9 6.3 %fusion.15 = (bf16[512,2048]{1,0:T(8,128)(2,1)S(1)}, f32[512,2048]{1,0:T(8,128)}) fusion(bf16[512,2048]{1,0:T(8,128)(2,1)} %param.5, bf16[512,3,2048]{2,0,1:T(8,128)(2,1)} %param.6, bf16[512,2048]{1,0:T(8,128)(2,1)} %param.7), kind=kLoop, calls=%fused_computation.25 | loop fusion | flops 6291456 | bytes 12582912 | tf_op jit(solution)/shard_map/convert_element_type | solution.py:70
  13.1 2.5 copy.80
  15.6 5.1 %all-to-all-start = ((bf16[512,8,256]{0,2,1:T(8,128)(2,1)}), bf16[512,8,256]{0,2,1:T(8,128)(2,1)S(1)}, u32[]{:S(2)}, u32[]{:S(2)}) async-start(bf16[512,8,256]{0,2,1:T(8,128)(2,1)} %bitcast.12), calls=%async_computation | async-start | bytes 4194304 | tf_op jit(solution)/shard_map/all_to_all | solution.py:71
  20.8 2.3 rev.3
  23.1 0.9 reshape.67.h_ref
  24.0 42.5 %all-to-all-done = bf16[512,8,256]{0,2,1:T(8,128)(2,1)S(1)} async-done(((bf16[512,8,256]{0,2,1:T(8,128)(2,1)}), bf16[512,8,256]{0,2,1:T(8,128)(2,1)S(1)}, u32[]{:S(2)}, u32[]{:S(2)}) %all-to-all-start) | async-done | bytes 2097184 | tf_op jit(solution)/shard_map/all_to_all | solution.py:71
  66.5 2.5 copy.81
  69.0 2.7 reshape.65
  71.7 2.2 copy.82
  73.9 15.7 %shard_map.55 = f32[16,256,256]{2,1,0:T(8,128)} custom-call(bf16[16,256,256]{2,1,0:T(8,128)(2,1)} %bitcast.98, f32[16,1,4352]{2,1,0:T(1,128)} %reshape.67.h_ref), custom_call_target="tpu_custom_call" | custom-call | flops 4563402752 | bytes 6569984 | tf_op jit(solution)/shard_map/pallas_call | solution.py:46
  89.5 2.4 convert_element_type.73
  92.0 0.9 copy.131
  92.9 2.2 convert_element_type.76
  95.0 3.6 %copy.86 = bf16[8,512,256]{1,2,0:T(8,128)(2,1)} copy(bf16[8,512,256]{1,0,2:T(8,128)(2,1)} %convert_element_type.76) | data formatting | bytes 4194304 | tf_op jit(solution)/shard_map/convert_element_type | solution.py:76
  98.6 6.8 %all-to-all-start.2 = ((bf16[8,512,256]{1,2,0:T(8,128)(2,1)}), bf16[8,512,256]{1,2,0:T(8,128)(2,1)S(1)}, u32[]{:S(2)}, u32[]{:S(2)}) async-start(bf16[8,512,256]{1,2,0:T(8,128)(2,1)} %copy.86), calls=%async_computation.2 | async-start | bytes 4194304 | tf_op jit(solution)/shard_map/all_to_all | solution.py:77
  105.4 0.8 slice.105
  106.3 2.3 collective-permute-start
  108.6 4.8 %fusion.19 = (bf16[512,1,2048]{2,0,1:T(8,128)(2,1)}, bf16[512,1,2048]{2,0,1:T(8,128)(2,1)}) fusion(bf16[512,3,2048]{2,0,1:T(8,128)(2,1)} %param.6), kind=kLoop, calls=%fused_computation.65 | loop fusion | bytes 8388608 | tf_op jit(solution)/shard_map/slice | solution.py:67
  113.6 3.9 %copy.122 = bf16[512,1,2048]{0,2,1:T(8,128)(2,1)} copy(bf16[512,1,2048]{2,0,1:T(8,128)(2,1)} %get-tuple-element.11) | data formatting | bytes 4194304
  117.5 4.0 %copy.117 = bf16[512,1,2048]{0,2,1:T(8,128)(2,1)} copy(bf16[512,1,2048]{2,0,1:T(8,128)(2,1)} %get-tuple-element.12) | data formatting | bytes 4194304
  121.6 29.7 %collective-permute-done = f32[2,2048]{1,0:T(2,128)S(1)} collective-permute-done((f32[2,2048]{1,0:T(2,128)S(1)}, f32[2,2048]{1,0:T(2,128)S(1)}, u32[]{:S(2)}, u32[]{:S(2)}) %collective-permute-start) | collective-permute-done | bytes 16416 | tf_op jit(solution)/shard_map/ppermute | solution.py:17
  151.3 5.7 %fusion.4 = bf16[512,2048]{1,0:T(8,128)(2,1)S(1)} fusion(f32[512,2048]{1,0:T(8,128)} %get-tuple-element.24, f32[2,2048]{1,0:T(2,128)S(1)} %collective-permute-done, f32[2048]{0:T(1024)S(1)} %bitcast.113, f32[2048]{0:T(1024)S(1)} %bitcast.111, f32[2048]{0:T(1024)S(1)} %bitcast.112), kind=kLoop, calls=%fused_computation.14 | loop fusion | flops 8388608 | bytes 6332416 | tf_op jit(solution)/shard_map/convert_element_type | solution.py:145
  157.0 1.3 dynamic-slice_bitcast_fusion
  158.2 1.5 collective-permute-start.1
  160.2 1.6 collective-permute-start.3
  161.8 5.4 %convert_multiply_fusion = (f32[8,512,256]{1,2,0:T(8,128)S(1)}, f32[8,512,256]{1,2,0:T(8,128)}) fusion(bf16[8,512,256]{1,2,0:T(8,128)(2,1)S(1)} %all-to-all-done.2, bf16[512,8,256]{0,2,1:T(8,128)(2,1)} %bitcast.88, bf16[512,8,256]{0,2,1:T(8,128)(2,1)} %bitcast.89), kind=kLoop, calls=%fused_computation | loop fusion | flops 5242880 | bytes 14680064 | tf_op jit(solution)/shard_map/mul | solution.py:83
  167.2 2.0 copy-done
  169.6 3.2 %collective-permute-start.8 = (f32[8,2,256]{2,0,1:T(8,128)S(1)}, f32[8,2,256]{2,0,1:T(8,128)S(1)}, u32[]{:S(2)}, u32[]{:S(2)}) collective-permute-start(f32[8,2,256]{2,0,1:T(8,128)S(1)} %copy.103), channel_id=1, source_target_pairs={{4,0},{8,4},{12,8},{16,12},{20,16},{24,20},{28,24},{5,1},{9,5},{13... | collective-permute-start | bytes 49160 | tf_op jit(solution)/shard_map/ppermute | solution.py:17
  172.8 3.4 %broadcast_in_dim.16 = bf16[128,3,8192]{2,0,1:T(8,128)(2,1)} broadcast(bf16[]{:T(256)} %constant.99.clone.1), dimensions={} | broadcast | bytes 6291458 | tf_op jit(solution)/shard_map/broadcast_in_dim | solution.py:88
  176.2 1.9 bitcast_dynamic-update-slice_fusion.3
  178.1 1.3 slice.108
  179.7 1.9 collective-permute-start.4
  182.0 8.5 %fusion.9 = bf16[8,512,256]{1,2,0:T(8,128)(2,1)} fusion(f32[8,512,256]{1,2,0:T(8,128)} %copy-done, f32[8,2,256]{1,2,0:T(8,128)S(1)} %copy.104, f32[8,256]{1,0:T(8,128)S(1)} %mul.154, f32[8,256]{1,0:T(8,128)S(1)} %mul.151, f32[8,256]{1,0:T(8,128)S(1)} %mul.147), kind=kLoop, calls=%fused_computation.19 | loop fusion | flops 8388608 | bytes 6332416 | tf_op jit(solution)/shard_map/convert_element_type | solution.py:117
  190.5 2.5 reshape.69
  193.5 8.6 %fusion.14 = bf16[8,512,256]{1,2,0:T(8,128)(2,1)} fusion(f32[8,512,256]{1,2,0:T(8,128)} %get-tuple-element.18, f32[8,2,256]{1,2,0:T(8,128)S(1)} %copy.89, f32[8,256]{1,0:T(8,128)S(1)} %mul.144, f32[8,256]{1,0:T(8,128)S(1)} %mul.141, f32[8,256]{1,0:T(8,128)S(1)} %mul.136), kind=kLoop, calls=%fused_computation.24 | loop fusion | flops 8388608 | bytes 6332416 | tf_op jit(solution)/shard_map/convert_element_type | solution.py:117
  202.0 4.0 %reshape.68 = bf16[8,4,128,256]{2,1,3,0:T(4,128)(2,1)} reshape(bf16[8,512,256]{1,2,0:T(8,128)(2,1)} %fusion.14) | data formatting | bytes 4194304 | tf_op jit(solution)/shard_map/reshape | solution.py:124
  206.0 14.6 %constant_dynamic-slice_fusion = (bf16[8,1,128,256]{2,1,3,0:T(2,128)(2,1)}, bf16[8,1,128,256]{2,1,3,0:T(2,128)(2,1)}, bf16[8,1,128,256]{2,1,3,0:T(2,128)(2,1)}, ...) fusion(bf16[8,4,128,256]{2,1,3,0:T(4,128)(2,1)S(1)} %reshape.69, ...), kind=kLoop, calls=%fused_computation.49 | loop fusion | bytes 8388624 | tf_op jit(solution)/shard_map/jit(dynamic_index_in_dim)/dynamic_slice | solution.py:131
  220.6 3.5 %copy.119 = bf16[8,1,128,256]{3,2,0,1:T(8,128)(2,1)} copy(bf16[8,1,128,256]{2,1,3,0:T(2,128)(2,1)} %get-tuple-element.32) | data formatting | bytes 1048576
  224.1 1.4 collective-permute-start.5
  225.5 1.9 bitcast_dynamic-update-slice_fusion.2
  227.4 1.9 bitcast_dynamic-update-slice_fusion.1
  229.3 3.6 %copy.120 = bf16[8,1,128,256]{3,2,0,1:T(8,128)(2,1)} copy(bf16[8,1,128,256]{2,1,3,0:T(2,128)(2,1)} %get-tuple-element.33) | data formatting | bytes 1048576
  232.8 1.5 collective-permute-start.6
  234.4 3.5 %copy.121 = bf16[8,1,128,256]{3,2,0,1:T(8,128)(2,1)} copy(bf16[8,1,128,256]{2,1,3,0:T(2,128)(2,1)} %get-tuple-element.34) | data formatting | bytes 1048576
  237.9 3.5 %copy.124 = bf16[8,1,128,256]{3,2,0,1:T(8,128)(2,1)} copy(bf16[8,1,128,256]{2,1,3,0:T(2,128)(2,1)} %get-tuple-element.15) | data formatting | bytes 1048576
  241.3 2.9 collective-permute-start.9
  244.3 3.5 %copy.125 = bf16[8,1,128,256]{3,2,0,1:T(8,128)(2,1)} copy(bf16[8,1,128,256]{2,1,3,0:T(2,128)(2,1)} %get-tuple-element.14) | data formatting | bytes 1048576
  247.7 1.8 copy.126
  250.1 1.9 bitcast_dynamic-update-slice_fusion
  252.6 0.8 constant_dynamic-update-slice_fusion.6
  253.4 1.3 copy.94
  255.0 4.2 %collective-permute-done.6 = bf16[8,128,256]{2,1,0:T(8,128)(2,1)} collective-permute-done((bf16[8,128,256]{2,1,0:T(8,128)(2,1)}, bf16[8,128,256]{2,1,0:T(8,128)(2,1)}, u32[]{:S(2)}, u32[]{:S(2)}) %collective-permute-start.6) | collective-permute-done | bytes 524320 | tf_op jit(solution)/shard_map/ppermute | solution.py:133
  259.2 1.3 copy.97
  260.7 1.3 copy.100
  262.3 1.9 collective-permute-done.9
  264.1 1.3 copy.109
  265.7 15.2 %collective-permute-done.10 = bf16[8,128,256]{2,1,0:T(8,128)(2,1)} collective-permute-done((bf16[8,128,256]{2,1,0:T(8,128)(2,1)}, bf16[8,128,256]{2,1,0:T(8,128)(2,1)}, u32[]{:S(2)}, u32[]{:S(2)}) %collective-permute-start.10) | collective-permute-done | bytes 524320 | tf_op jit(solution)/shard_map/ppermute | solution.py:133
  280.9 2.0 copy.112
  283.0 1.2 copy.113
  284.2 2.1 copy.115
  286.3 2.0 copy.116
  293.3 0.8 constant_dynamic-update-slice_fusion.7
  (54 shorter events, 9.3 us)
Async XLA Ops:
  1.7 14.0 %all-to-all-start.1 = ((bf16[512,8,16]{0,2,1:T(8,128)(2,1)}), bf16[512,8,16]{0,2,1:T(8,128)(2,1)S(1)}, u32[]{:S(2)}, u32[]{:S(2)}) async-start(bf16[512,8,16]{0,2,1:T(8,128)(2,1)} %bitcast.16), calls=%async_computation.1 | async-start | bytes 262144 | tf_op jit(solution)/shard_map/all_to_all | solution.py:72
  15.6 50.9 %all-to-all-start = ((bf16[512,8,256]{0,2,1:T(8,128)(2,1)}), bf16[512,8,256]{0,2,1:T(8,128)(2,1)S(1)}, u32[]{:S(2)}, u32[]{:S(2)}) async-start(bf16[512,8,256]{0,2,1:T(8,128)(2,1)} %bitcast.12), calls=%async_computation | async-start | bytes 4194304 | tf_op jit(solution)/shard_map/all_to_all | solution.py:71
  98.6 63.1 %all-to-all-start.2 = ((bf16[8,512,256]{1,2,0:T(8,128)(2,1)}), bf16[8,512,256]{1,2,0:T(8,128)(2,1)S(1)}, u32[]{:S(2)}, u32[]{:S(2)}) async-start(bf16[8,512,256]{1,2,0:T(8,128)(2,1)} %copy.86), calls=%async_computation.2 | async-start | bytes 4194304 | tf_op jit(solution)/shard_map/all_to_all | solution.py:77
  106.3 7.1 %copy-start.5 = (f32[3,3,2048]{2,1,0:T(4,128)S(1)}, f32[3,3,2048]{2,1,0:T(4,128)}, u32[]{:S(2)}) copy-start(f32[3,3,2048]{2,1,0:T(4,128)} %param.9) | copy-start | bytes 221188
  106.3 45.0 %collective-permute-start = (f32[2,2048]{1,0:T(2,128)S(1)}, f32[2,2048]{1,0:T(2,128)S(1)}, u32[]{:S(2)}, u32[]{:S(2)}) collective-permute-start(f32[2,2048]{1,0:T(2,128)S(1)} %slice.105), channel_id=1, source_target_pairs={{4,0},{8,4},{12,8},{16,12},{20,16},{24,20},{28,24},{5,1},{9,5},{13... | collective-permute-start | bytes 49160 | tf_op jit(solution)/shard_map/ppermute | solution.py:17
  156.9 3.3 %copy-start.1 = (bf16[512,2048]{1,0:T(8,128)(2,1)}, bf16[512,2048]{1,0:T(8,128)(2,1)S(1)}, u32[]{:S(2)}) copy-start(bf16[512,2048]{1,0:T(8,128)(2,1)S(1)} %fusion.4) | copy-start | bytes 6291460
  158.2 67.3 %collective-permute-start.1 = (bf16[128,2048]{1,0:T(8,128)(2,1)}, bf16[128,2048]{1,0:T(8,128)(2,1)}, u32[]{:S(2)}, u32[]{:S(2)}) collective-permute-start(bf16[128,2048]{1,0:T(8,128)(2,1)} %get-tuple-element.27), channel_id=1, source_target_pairs={{0,1},{1,2},{2,3},{3,0},{4,5},{5,6},{6,7},{7,4},{8,9},{9,10},{10,1... | collective-permute-start | bytes 1572872 | tf_op jit(solution)/shard_map/ppermute | solution.py:104
  159.7 67.7 %collective-permute-start.2 = (bf16[128,2048]{1,0:T(8,128)(2,1)}, bf16[128,2048]{1,0:T(8,128)(2,1)}, u32[]{:S(2)}, u32[]{:S(2)}) collective-permute-start(bf16[128,2048]{1,0:T(8,128)(2,1)} %get-tuple-element.26), channel_id=1, source_target_pairs={{0,2},{1,3},{2,0},{3,1},{4,6},{5,7},{6,4},{7,5},{8,10},{9,11},{10,... | collective-permute-start | bytes 1572872 | tf_op jit(solution)/shard_map/ppermute | solution.py:104
  160.2 89.3 %collective-permute-start.3 = (bf16[128,2048]{1,0:T(8,128)(2,1)}, bf16[128,2048]{1,0:T(8,128)(2,1)}, u32[]{:S(2)}, u32[]{:S(2)}) collective-permute-start(bf16[128,2048]{1,0:T(8,128)(2,1)} %get-tuple-element.25), channel_id=1, source_target_pairs={{0,3},{1,0},{2,1},{3,2},{4,7},{5,4},{6,5},{7,6},{8,11},{9,8},{10,9... | collective-permute-start | bytes 1572872 | tf_op jit(solution)/shard_map/ppermute | solution.py:104
  167.2 2.0 copy-start
  169.6 12.1 %collective-permute-start.8 = (f32[8,2,256]{2,0,1:T(8,128)S(1)}, f32[8,2,256]{2,0,1:T(8,128)S(1)}, u32[]{:S(2)}, u32[]{:S(2)}) collective-permute-start(f32[8,2,256]{2,0,1:T(8,128)S(1)} %copy.103), channel_id=1, source_target_pairs={{4,0},{8,4},{12,8},{16,12},{20,16},{24,20},{28,24},{5,1},{9,5},{13... | collective-permute-start | bytes 49160 | tf_op jit(solution)/shard_map/ppermute | solution.py:17
  179.7 13.3 %collective-permute-start.4 = (f32[8,2,256]{2,0,1:T(8,128)S(1)}, f32[8,2,256]{2,0,1:T(8,128)S(1)}, u32[]{:S(2)}, u32[]{:S(2)}) collective-permute-start(f32[8,2,256]{2,0,1:T(8,128)S(1)} %copy.88), channel_id=1, source_target_pairs={{4,0},{8,4},{12,8},{16,12},{20,16},{24,20},{28,24},{5,1},{9,5},{13... | collective-permute-start | bytes 49160 | tf_op jit(solution)/shard_map/ppermute | solution.py:17
  224.1 23.6 %copy-start.3 = (bf16[8,1,128,256]{2,1,3,0:T(2,128)(2,1)S(1)}, bf16[8,1,128,256]{2,1,3,0:T(2,128)(2,1)}, u32[]{:S(2)}) copy-start(bf16[8,1,128,256]{2,1,3,0:T(2,128)(2,1)} %get-tuple-element.13) | copy-start | bytes 1572868
  224.1 25.9 %collective-permute-start.5 = (bf16[8,128,256]{2,1,0:T(8,128)(2,1)}, bf16[8,128,256]{2,1,0:T(8,128)(2,1)}, u32[]{:S(2)}, u32[]{:S(2)}) collective-permute-start(bf16[8,128,256]{2,1,0:T(8,128)(2,1)} %bitcast.26), channel_id=1, source_target_pairs={{0,1},{1,2},{2,3},{3,0},{4,5},{5,6},{6,7},{7,4},{8,9},{9,10},{10,1... | collective-permute-start | bytes 1572872 | tf_op jit(solution)/shard_map/ppermute | solution.py:133
  229.3 22.7 %copy-start.2 = (bf16[8,1,128,256]{2,1,3,0:T(2,128)(2,1)S(1)}, bf16[8,1,128,256]{2,1,3,0:T(2,128)(2,1)}, u32[]{:S(2)}) copy-start(bf16[8,1,128,256]{2,1,3,0:T(2,128)(2,1)} %get-tuple-element.31) | copy-start | bytes 1572868
  232.8 26.3 %collective-permute-start.6 = (bf16[8,128,256]{2,1,0:T(8,128)(2,1)}, bf16[8,128,256]{2,1,0:T(8,128)(2,1)}, u32[]{:S(2)}, u32[]{:S(2)}) collective-permute-start(bf16[8,128,256]{2,1,0:T(8,128)(2,1)} %bitcast.110), channel_id=1, source_target_pairs={{0,2},{1,3},{2,0},{3,1},{4,6},{5,7},{6,4},{7,5},{8,10},{9,11},{10,... | collective-permute-start | bytes 1572872 | tf_op jit(solution)/shard_map/ppermute | solution.py:133
  237.8 22.9 %collective-permute-start.7 = (bf16[8,128,256]{2,1,0:T(8,128)(2,1)}, bf16[8,128,256]{2,1,0:T(8,128)(2,1)}, u32[]{:S(2)}, u32[]{:S(2)}) collective-permute-start(bf16[8,128,256]{2,1,0:T(8,128)(2,1)} %bitcast.109), channel_id=1, source_target_pairs={{0,3},{1,0},{2,1},{3,2},{4,7},{5,4},{6,5},{7,6},{8,11},{9,8},{10,9... | collective-permute-start | bytes 1572872 | tf_op jit(solution)/shard_map/ppermute | solution.py:133
  241.3 22.8 %collective-permute-start.9 = (bf16[8,128,256]{2,1,0:T(8,128)(2,1)}, bf16[8,128,256]{2,1,0:T(8,128)(2,1)}, u32[]{:S(2)}, u32[]{:S(2)}) collective-permute-start(bf16[8,128,256]{2,1,0:T(8,128)(2,1)} %bitcast.108), channel_id=1, source_target_pairs={{0,1},{1,2},{2,3},{3,0},{4,5},{5,6},{6,7},{7,4},{8,9},{9,10},{10,1... | collective-permute-start | bytes 1572872 | tf_op jit(solution)/shard_map/ppermute | solution.py:133
  249.5 31.4 %collective-permute-start.10 = (bf16[8,128,256]{2,1,0:T(8,128)(2,1)}, bf16[8,128,256]{2,1,0:T(8,128)(2,1)}, u32[]{:S(2)}, u32[]{:S(2)}) collective-permute-start(bf16[8,128,256]{2,1,0:T(8,128)(2,1)} %bitcast.107), channel_id=1, source_target_pairs={{0,2},{1,3},{2,0},{3,1},{4,6},{5,7},{6,4},{7,5},{8,10},{9,11},{10,... | collective-permute-start | bytes 1572872 | tf_op jit(solution)/shard_map/ppermute | solution.py:133
  250.0 34.2 %collective-permute-start.11 = (bf16[8,128,256]{2,1,0:T(8,128)(2,1)}, bf16[8,128,256]{2,1,0:T(8,128)(2,1)}, u32[]{:S(2)}, u32[]{:S(2)}) collective-permute-start(bf16[8,128,256]{2,1,0:T(8,128)(2,1)} %bitcast.106), channel_id=1, source_target_pairs={{0,3},{1,0},{2,1},{3,2},{4,7},{5,4},{6,5},{7,6},{8,11},{9,8},{10,9... | collective-permute-start | bytes 1572872 | tf_op jit(solution)/shard_map/ppermute | solution.py:133
  288.3 5.0 %copy-start.4 = (bf16[128,1,2048]{2,0,1:T(8,128)(2,1)S(1)}, bf16[128,1,2048]{2,0,1:T(8,128)(2,1)}, u32[]{:S(2)}) copy-start(bf16[128,1,2048]{2,0,1:T(8,128)(2,1)} %copy.116) | copy-start | bytes 1572868

commit v8 on v6

--- a/solution.py
+++ b/solution.py
@@ -17,11 +17,11 @@
     return lax.ppermute(value, axis, [(source, source + steps) for source in range(leading, last)])
 
 
-def correlate_kernel(x_ref, h_ref, o_ref):
+def correlate_kernel(x_ref, h_ref, o_ref, acc_ref):
     rows_all = x_ref.shape[1]
     blocks = rows_all // per_group
     tokens = blocks * block
-    o_ref[...] = jnp.zeros(o_ref.shape, o_ref.dtype)
+    acc_ref[...] = jnp.zeros(acc_ref.shape, acc_ref.dtype)
     for lag_block in range(blocks):
         start = tokens - block * (lag_block + 1)
         window = h_ref[0, :, start : start + 2 * block]
@@ -30,7 +30,10 @@
         band = rolled[:, :block].astype(jnp.bfloat16)
         rows = per_group * (blocks - lag_block)
         source = x_ref[0, per_group * lag_block :, :]
-        o_ref[0, :rows, :] += jnp.dot(source, band, preferred_element_type=jnp.float32)
+        acc_ref[:rows, :] += jnp.dot(source, band, preferred_element_type=jnp.float32)
+    for index in range(blocks):
+        slab = acc_ref[per_group * index : per_group * (index + 1), :]
+        o_ref[:, block * index : block * (index + 1)] = slab.astype(o_ref.dtype)
 
 
 def correlate(grads, taps):
@@ -43,25 +46,24 @@
     padded = jnp.concatenate([reversed_taps, jnp.zeros((groups, block), jnp.float32)], 1)
     padded = padded.reshape(groups, 1, tokens + block)
     flops = 2 * groups * per_group * block * block * blocks * (blocks + 1) // 2
-    out = pl.pallas_call(
+    return pl.pallas_call(
         correlate_kernel,
-        out_shape=jax.ShapeDtypeStruct((groups, blocks * per_group, block), jnp.float32),
+        out_shape=jax.ShapeDtypeStruct((channels, tokens), jnp.bfloat16),
         grid=(groups,),
         in_specs=[
             pl.BlockSpec((1, blocks * per_group, block), lambda g: (g, 0, 0)),
             pl.BlockSpec((1, 1, tokens + block), lambda g: (g, 0, 0)),
         ],
-        out_specs=pl.BlockSpec((1, blocks * per_group, block), lambda g: (g, 0, 0)),
+        out_specs=pl.BlockSpec((per_group, tokens), lambda g: (g, 0)),
+        scratch_shapes=[pltpu.VMEM((blocks * per_group, block), jnp.float32)],
         cost_estimate=pl.CostEstimate(
-            flops=flops, bytes_accessed=grads.size * 6 + padded.size * 4, transcendentals=0
+            flops=flops, bytes_accessed=grads.size * 4 + padded.size * 4, transcendentals=0
         ),
     )(shaped, padded)
-    out = out.reshape(groups, blocks, per_group, block).transpose(1, 3, 0, 2)
-    return out.reshape(tokens, channels)
 
 
 def on_device(grad_out, qkv_saved, conv_saved, long_taps, short_taps):
-    block_rows = grad_out.shape[0]
+    block_rows, channels = grad_out.shape
     out_wide = grad_out.astype(jnp.float32)
     query = qkv_saved[:, 0, :]
     key_part = qkv_saved[:, 1, :]
@@ -73,17 +75,47 @@
     short_len = short_taps.shape[1]
     query_proj = short_filter(grad_query[:, None], short_taps[:1], block_rows)
     query_rows = spread_rows(query_proj, "chan")
-    z_cols = correlate(mixed_cols, taps_cols)
-    z_narrow = z_cols.astype(jnp.bfloat16)
-    grad_z = lax.all_to_all(z_narrow, "seq", split_axis=0, concat_axis=1, tiled=True)
-    grad_z = grad_z.astype(jnp.float32)
-    grad_key = grad_z * value_part.astype(jnp.float32)
-    grad_value = grad_z * key_part.astype(jnp.float32)
-    stacked = jnp.stack([grad_key, grad_value], 1)
-    pair_proj = short_filter(stacked, short_taps[1:], block_rows)
-    pair_rows = spread_rows(pair_proj, "chan")
+    z_lanes = correlate(mixed_cols, taps_cols)
+    z_rows = lax.all_to_all(z_lanes, "seq", split_axis=1, concat_axis=0, tiled=True)
+    z_wide = z_rows.astype(jnp.float32)
+    grad_key = z_wide * value_part.T.astype(jnp.float32)
+    grad_value = z_wide * key_part.T.astype(jnp.float32)
     count = lax.axis_size("chan")
-    return place_rows([query_rows, pair_rows], count, block_rows // count, grad_out.shape[1])
+    out = jnp.zeros((block_rows // count, 3, count * channels), jnp.bfloat16)
+    for source, piece in query_rows:
+        out = lax.dynamic_update_slice(out, piece, (0, 0, source * channels))
+    for plane, lanes in ((1, grad_key), (2, grad_value)):
+        filtered = lane_filter(lanes, short_taps[plane])
+        for source, piece in spread_lanes(filtered, "chan"):
+            out = lax.dynamic_update_slice(out, piece.T[:, None, :], (0, plane, source * channels))
+    return out
+
+
+def lane_filter(lanes, taps):
+    block_rows = lanes.shape[1]
+    short_len = taps.shape[0]
+    borrowed = shifted(lanes[:, : short_len - 1], "seq", -1)
+    extended = jnp.concatenate([lanes, borrowed], 1)
+    result = jnp.zeros_like(lanes)
+    for lag_index in range(short_len):
+        result = result + taps[lag_index][:, None] * extended[:, lag_index : lag_index + block_rows]
+    return result.astype(jnp.bfloat16)
+
+
+def spread_lanes(value, axis):
+    count = lax.axis_size(axis)
+    me = lax.axis_index(axis)
+    width = value.shape[1] // count
+
+    def lanes_for(index):
+        return lax.dynamic_slice_in_dim(value, pl.multiple_of(index * width, width), width, 1)
+
+    pieces = [(me, lanes_for(me))]
+    for step in range(1, count):
+        pairs = [(source, (source + step) % count) for source in range(count)]
+        outgoing = lanes_for((me + step) % count)
+        pieces.append(((me + count - step) % count, lax.ppermute(outgoing, axis, pairs)))
+    return pieces
 
 
 def spread_rows(value, axis):

time: 285 us -> 246 us (0.86)
  local copies, waits for them, and re-layouts: 99.9 us -> 44.5 us
  waiting for transfers between devices: 103 us -> 127 us
  other arithmetic: 34.6 us -> 24 us
  starting transfers between devices: 29.2 us -> 34.2 us
    ppermute x0 -> x6, waiting for transfers between devices: none -> 34.8 us  [spread_lanes(): lax.ppermute(outgoing, axis, pairs)]
    dynamic_slice x5 -> x2, local copies, waits for them, and re-layouts: 33.9 us -> 0.23 us  [lanes_for(): lax.dynamic_slice_in_dim(value, pl.multiple_of(index * width, width), wid...]
    ppermute x6 -> x3, waiting for transfers between devices: 30.5 us -> 6.65 us  [spread_rows(): lax.ppermute(outgoing, axis, pairs)]
    ppermute x2 -> x3, waiting for transfers between devices: 29.8 us -> 42.7 us  [shifted(): lax.ppermute(value, axis, [(source, source + steps) for source in range(l...]
    unnamed x15 -> x5, local copies, waits for them, and re-layouts: 15.6 us -> 2.99 us
    convert_element_type x2 -> x1, other arithmetic: 16 us -> 5.63 us  [short_filter(): return result.astype(jnp.bfloat16)]
    ppermute x0 -> x6, starting transfers between devices: none -> 7.59 us  [spread_lanes(): lax.ppermute(outgoing, axis, pairs)]
    reshape x1 -> x0, local copies, waits for them, and re-layouts: 6.9 us -> none  [spread_rows(): chunks = value.reshape(count, rows // count, planes, channels)]
  transfers between devices with their start and end apart: 11 -> 15, of which waited for: 4 -> 8; matrix products, arithmetic and copies ran while one was open for 38% -> 22% of each run, Pallas kernels for 0% -> 0%
where the time goes in v8:
time: 246 us; the launch traced here: 245 us
  waiting for transfers between devices  127 us (52%)
  local copies, waits for them, and re-layouts  44.5 us (18%)
  starting transfers between devices  34.2 us (14%)
  other arithmetic  24 us (10%)
  Pallas kernels  15.3 us (6%)
    ppermute x3, waiting for transfers between devices, shifted(): lax.ppermute(value, axis, [(source, source + steps) for source in range(l...  42.7 us
    all_to_all x1, waiting for transfers between devices, on_device(): lax.all_to_all(grad_mixed, 'seq', split_axis=1, concat_axis=0, tiled=True)  42.4 us
    ppermute x6, waiting for transfers between devices, spread_lanes(): lax.ppermute(outgoing, axis, pairs)  34.8 us
    pallas_call x1, Pallas kernels, correlate(): pl.pallas_call(correlate_kernel, out_shape=jax.ShapeDtypeStruct((channels...  15.3 us
    mul x1, other arithmetic, on_device(): grad_query = out_wide * conv_saved.astype(jnp.float32)  7.94 us
    ppermute x6, starting transfers between devices, spread_lanes(): lax.ppermute(outgoing, axis, pairs)  7.59 us
    dynamic_update_slice x4, local copies, waits for them, and re-layouts, on_device(): out = lax.dynamic_update_slice(out, piece, (0, 0, source * channels))  7.53 us
    all_to_all x1, starting transfers between devices, on_device(): lax.all_to_all(z_lanes, 'seq', split_axis=1, concat_axis=0, tiled=True)  6.8 us
  transfers between devices with their start and end apart: 15, of which 8 were waited for; matrix products, arithmetic and copies ran while one was open for 22% of the time, Pallas kernels for 0%

profile of v8, /device:TPU:18, one launch (start us, length us, event | category | flops | bytes accessed | tf_op | source)
XLA Modules:
  0.0 244.8 jit_solution(438697949409356157)
XLA Ops:
  0.0 1.7 copy.28
  1.7 5.2 %all-to-all-start.1 = ((bf16[512,8,16]{0,2,1:T(8,128)(2,1)}), bf16[512,8,16]{0,2,1:T(8,128)(2,1)S(1)}, u32[]{:S(2)}, u32[]{:S(2)}) async-start(bf16[512,8,16]{0,2,1:T(8,128)(2,1)} %bitcast.19), calls=%async_computation.1 | async-start | bytes 262144 | tf_op jit(solution)/shard_map/all_to_all | solution.py:74
  6.9 7.9 %convert_multiply_fusion.1 = (f32[512,2048]{1,0:T(8,128)}, f32[512,1,2048]{2,0,1:T(8,128)}, bf16[512,2048]{1,0:T(8,128)(2,1)S(1)}) fusion(bf16[512,2048]{1,0:T(8,128)(2,1)} %param.5, bf16[512,2048]{1,0:T(8,128)(2,1)} %param.7, bf16[512,3,2048]{2,0,1:T(8,128)(2,1)} %param.6), kind=kLoop, calls=%fused_computation.1 | loop fusion | flops 6291456 | bytes 16777216 | tf_op jit(solution)/shard_map/mul | solution.py:71
  14.8 2.5 %copy.25 = bf16[512,2048]{0,1:T(8,128)(2,1)} copy(bf16[512,2048]{1,0:T(8,128)(2,1)S(1)} %get-tuple-element.15) | data formatting | bytes 4194304 | tf_op jit(solution)/shard_map/convert_element_type | solution.py:72
  17.3 0.0 all-to-all-done.1
  17.3 5.1 %all-to-all-start = ((bf16[512,8,256]{0,2,1:T(8,128)(2,1)}), bf16[512,8,256]{0,2,1:T(8,128)(2,1)S(1)}, u32[]{:S(2)}, u32[]{:S(2)}) async-start(bf16[512,8,256]{0,2,1:T(8,128)(2,1)} %bitcast.15), calls=%async_computation | async-start | bytes 4194304 | tf_op jit(solution)/shard_map/all_to_all | solution.py:73
  22.5 2.3 rev.3
  24.8 0.1 concatenate.13
  24.8 0.9 reshape.61.h_ref
  25.7 42.4 %all-to-all-done = bf16[512,8,256]{0,2,1:T(8,128)(2,1)S(1)} async-done(((bf16[512,8,256]{0,2,1:T(8,128)(2,1)}), bf16[512,8,256]{0,2,1:T(8,128)(2,1)S(1)}, u32[]{:S(2)}, u32[]{:S(2)}) %all-to-all-start) | async-done | bytes 2097184 | tf_op jit(solution)/shard_map/all_to_all | solution.py:73
  68.2 2.5 %copy.26 = bf16[8,512,256]{1,0,2:T(8,128)(2,1)} copy(bf16[8,512,256]{1,2,0:T(8,128)(2,1)S(1)} %bitcast.99) | data formatting | bytes 4194304 | tf_op jit(solution)/shard_map/all_to_all | solution.py:73
  70.7 2.7 %reshape.59 = bf16[16,256,16,16]{1,0,3,2:T(8,128)(2,1)S(1)} reshape(bf16[8,512,256]{1,0,2:T(8,128)(2,1)} %copy.26) | data formatting | bytes 4194304 | tf_op jit(solution)/shard_map/reshape | solution.py:43
  73.4 2.2 copy.27
  75.6 15.3 %shard_map.55 = bf16[256,4096]{1,0:T(8,128)(2,1)} custom-call(bf16[16,256,256]{2,1,0:T(8,128)(2,1)} %bitcast.101, f32[16,1,4352]{2,1,0:T(1,128)} %reshape.61.h_ref), custom_call_target="tpu_custom_call" | custom-call | flops 4563402752 | bytes 4472832 | tf_op jit(solution)/shard_map/pallas_call | solution.py:49
  90.9 3.2 %copy.36 = bf16[32,8,8,512]{3,2,0,1:T(8,128)(2,1)} copy(bf16[32,8,8,512]{3,2,1,0:T(8,128)(2,1)} %bitcast.102) | data formatting | bytes 4194304 | tf_op jit(solution)/shard_map/all_to_all | solution.py:79
  94.1 6.8 %all-to-all-start.2 = ((bf16[256,8,512]{2,0,1:T(8,128)(2,1)}), bf16[256,8,512]{2,0,1:T(8,128)(2,1)S(1)}, u32[]{:S(2)}, u32[]{:S(2)}) async-start(bf16[256,8,512]{2,0,1:T(8,128)(2,1)} %bitcast.96), calls=%async_computation.2 | async-start | bytes 4194304 | tf_op jit(solution)/shard_map/all_to_all | solution.py:79
  100.9 0.8 slice_bitcast_fusion
  101.7 2.2 collective-permute-start
  103.9 0.1 fusion.22
  104.0 42.7 %collective-permute-done = f32[2,1,2048]{2,0,1:T(2,128)S(1)} collective-permute-done((f32[2,1,2048]{2,0,1:T(2,128)S(1)}, f32[2,1,2048]{2,0,1:T(2,128)S(1)}, u32[]{:S(2)}, u32[]{:S(2)}) %collective-permute-start) | collective-permute-done | bytes 16416 | tf_op jit(solution)/shard_map/ppermute | solution.py:17
  146.7 5.6 %fusion.14 = bf16[512,1,2048]{2,0,1:T(8,128)(2,1)S(1)} fusion(f32[512,1,2048]{2,0,1:T(8,128)} %get-tuple-element.8, f32[2,1,2048]{2,0,1:T(2,128)S(1)} %collective-permute-done, f32[2048]{0:T(1024)S(1)} %bitcast.110, f32[2048]{0:T(1024)S(1)} %bitcast.111, f32[2048]{0:T(1024)S(1)} %bitcast.112, bf16[512,2048]{1,0:T(8,128)(2,1)} %param.7, ...), kind=kLoop, calls=%fused_computation.22 | loop fusion | flops 11534336 | bytes 10526720 | tf_op jit(solution)/shard_map/convert_element_type | solution.py:152
  152.4 1.3 copy-done
  153.7 0.9 dynamic-slice_bitcast_fusion
  154.7 1.5 collective-permute-start.1
  156.1 0.5 collective-permute-start.2
  156.7 1.5 collective-permute-start.3
  158.2 3.4 %broadcast_in_dim.31 = bf16[128,3,8192]{2,0,1:T(8,128)(2,1)} broadcast(bf16[]{:T(256)} %constant.83.clone.1), dimensions={} | broadcast | bytes 6291458 | tf_op jit(solution)/shard_map/broadcast_in_dim | solution.py:84
  161.6 1.9 bitcast_dynamic-update-slice_fusion.8
  163.5 1.8 collective-permute-done.1
  165.3 1.9 constant_dynamic-update-slice_fusion.2
  167.2 4.9 %collective-permute-done.2 = bf16[128,1,2048]{2,0,1:T(8,128)(2,1)} collective-permute-done((bf16[128,1,2048]{2,0,1:T(8,128)(2,1)S(1)}, bf16[128,1,2048]{2,0,1:T(8,128)(2,1)}, u32[]{:S(2)}, u32[]{:S(2)}) %collective-permute-start.2) | collective-permute-done | bytes 524320 | tf_op jit(solution)/shard_map/ppermute | solution.py:130
  172.1 1.9 constant_dynamic-update-slice_fusion.1
  173.9 0.0 all-to-all-done.2
  173.9 2.5 %convert_element_type.81 = f32[256,8,512]{2,0,1:T(8,128)} convert(bf16[256,8,512]{2,0,1:T(8,128)(2,1)S(1)} %all-to-all-done.2) | non-fusion elementwise | flops 1048576 | bytes 6291456 | tf_op jit(solution)/shard_map/convert_element_type | solution.py:80
  176.5 5.4 %copy.31 = f32[2048,512]{0,1:T(8,128)} copy(f32[2048,512]{1,0:T(8,128)} %bitcast.95) | data formatting | bytes 8388608 | tf_op jit(solution)/shard_map/convert_element_type | solution.py:80
  181.9 4.7 %fusion.19 = (f32[2048,512]{0,1:T(8,128)S(1)}, f32[2048,512]{0,1:T(8,128)S(1)}) fusion(f32[2048,512]{0,1:T(8,128)} %copy.31, bf16[512,3,2048]{2,0,1:T(8,128)(2,1)} %param.6), kind=kLoop, calls=%fused_computation.31 | loop fusion | flops 4194304 | bytes 16777216 | tf_op jit(solution)/shard_map/mul | solution.py:82
  186.6 1.9 collective-permute-start.4
  188.5 0.0 collective-permute-done.3
  188.5 1.9 constant_dynamic-update-slice_fusion
  190.4 1.9 collective-permute-start.8
  192.3 0.0 collective-permute-done.4
  192.4 1.6 fusion.9
  194.0 0.1 constant_dynamic-slice_fusion.2
  194.1 1.3 collective-permute-start.5
  195.4 0.5 collective-permute-start.6
  195.9 0.8 collective-permute-start.7
  196.7 1.6 fusion.4
  198.3 0.1 constant_dynamic-slice_fusion.5
  198.4 2.2 collective-permute-start.9
  200.7 1.5 collective-permute-start.10
  202.2 0.8 bitcast_dynamic-update-slice_fusion.7
  203.0 5.9 %collective-permute-done.5 = bf16[2048,128]{0,1:T(8,128)(2,1)S(1)} collective-permute-done((bf16[2048,128]{0,1:T(8,128)(2,1)S(1)}, bf16[2048,128]{0,1:T(8,128)(2,1)S(1)}, u32[]{:S(2)}, u32[]{:S(2)}) %collective-permute-start.5) | collective-permute-done | bytes 524320 | tf_op jit(solution)/shard_map/ppermute | solution.py:117
  209.0 1.3 collective-permute-start.11
  210.2 0.8 bitcast_dynamic-update-slice_fusion.6
  211.0 10.4 %collective-permute-done.6 = bf16[2048,128]{0,1:T(8,128)(2,1)S(1)} collective-permute-done((bf16[2048,128]{0,1:T(8,128)(2,1)S(1)}, bf16[2048,128]{0,1:T(8,128)(2,1)S(1)}, u32[]{:S(2)}, u32[]{:S(2)}) %collective-permute-start.6) | collective-permute-done | bytes 524320 | tf_op jit(solution)/shard_map/ppermute | solution.py:117
  221.5 0.8 bitcast_dynamic-update-slice_fusion.5
  222.3 0.0 collective-permute-done.7
  222.3 0.8 bitcast_dynamic-update-slice_fusion.4
  223.1 0.8 bitcast_dynamic-update-slice_fusion.3
  224.0 7.5 %collective-permute-done.9 = bf16[2048,128]{0,1:T(8,128)(2,1)S(1)} collective-permute-done((bf16[2048,128]{0,1:T(8,128)(2,1)S(1)}, bf16[2048,128]{0,1:T(8,128)(2,1)S(1)}, u32[]{:S(2)}, u32[]{:S(2)}) %collective-permute-start.9) | collective-permute-done | bytes 524320 | tf_op jit(solution)/shard_map/ppermute | solution.py:117
  231.5 0.8 bitcast_dynamic-update-slice_fusion.2
  232.3 10.9 %collective-permute-done.10 = bf16[2048,128]{0,1:T(8,128)(2,1)S(1)} collective-permute-done((bf16[2048,128]{0,1:T(8,128)(2,1)S(1)}, bf16[2048,128]{0,1:T(8,128)(2,1)S(1)}, u32[]{:S(2)}, u32[]{:S(2)}) %collective-permute-start.10) | collective-permute-done | bytes 524320 | tf_op jit(solution)/shard_map/ppermute | solution.py:117
  243.2 0.8 bitcast_dynamic-update-slice_fusion.1
  244.0 0.8 bitcast_dynamic-update-slice_fusion
  (9 shorter events, 0.1 us)
Async XLA Ops:
  1.7 15.7 %all-to-all-start.1 = ((bf16[512,8,16]{0,2,1:T(8,128)(2,1)}), bf16[512,8,16]{0,2,1:T(8,128)(2,1)S(1)}, u32[]{:S(2)}, u32[]{:S(2)}) async-start(bf16[512,8,16]{0,2,1:T(8,128)(2,1)} %bitcast.19), calls=%async_computation.1 | async-start | bytes 262144 | tf_op jit(solution)/shard_map/all_to_all | solution.py:74
  17.3 50.9 %all-to-all-start = ((bf16[512,8,256]{0,2,1:T(8,128)(2,1)}), bf16[512,8,256]{0,2,1:T(8,128)(2,1)S(1)}, u32[]{:S(2)}, u32[]{:S(2)}) async-start(bf16[512,8,256]{0,2,1:T(8,128)(2,1)} %bitcast.15), calls=%async_computation | async-start | bytes 4194304 | tf_op jit(solution)/shard_map/all_to_all | solution.py:73
  90.9 13.0 %copy-start.1 = (f32[3,3,2048]{2,1,0:T(4,128)S(1)}, f32[3,3,2048]{2,1,0:T(4,128)}, u32[]{:S(2)}) copy-start(f32[3,3,2048]{2,1,0:T(4,128)} %param.9) | copy-start | bytes 221188
  94.1 79.8 %all-to-all-start.2 = ((bf16[256,8,512]{2,0,1:T(8,128)(2,1)}), bf16[256,8,512]{2,0,1:T(8,128)(2,1)S(1)}, u32[]{:S(2)}, u32[]{:S(2)}) async-start(bf16[256,8,512]{2,0,1:T(8,128)(2,1)} %bitcast.96), calls=%async_computation.2 | async-start | bytes 4194304 | tf_op jit(solution)/shard_map/all_to_all | solution.py:79
  101.7 45.0 %collective-permute-start = (f32[2,1,2048]{2,0,1:T(2,128)S(1)}, f32[2,1,2048]{2,0,1:T(2,128)S(1)}, u32[]{:S(2)}, u32[]{:S(2)}) collective-permute-start(f32[2,1,2048]{2,0,1:T(2,128)S(1)} %slice_bitcast_fusion), channel_id=1, source_target_pairs={{4,0},{8,4},{12,8},{16,12},{20,16},{24,20},{28,24},{5,1},{9,5},{13... | collective-permute-start | bytes 49160 | tf_op jit(solution)/shard_map/ppermute | solution.py:17
  152.4 1.3 copy-start
  154.7 10.7 %collective-permute-start.1 = (bf16[128,1,2048]{2,0,1:T(8,128)(2,1)}, bf16[128,1,2048]{2,0,1:T(8,128)(2,1)}, u32[]{:S(2)}, u32[]{:S(2)}) collective-permute-start(bf16[128,1,2048]{2,0,1:T(8,128)(2,1)} %get-tuple-element.18), channel_id=1, source_target_pairs={{0,1},{1,2},{2,3},{3,0},{4,5},{5,6},{6,7},{7,4},{8,9},{9,10},{10,1... | collective-permute-start | bytes 1572872 | tf_op jit(solution)/shard_map/ppermute | solution.py:130
  156.1 15.9 %collective-permute-start.2 = (bf16[128,1,2048]{2,0,1:T(8,128)(2,1)S(1)}, bf16[128,1,2048]{2,0,1:T(8,128)(2,1)}, u32[]{:S(2)}, u32[]{:S(2)}) collective-permute-start(bf16[128,1,2048]{2,0,1:T(8,128)(2,1)S(1)} %get-tuple-element.17), channel_id=1, source_target_pairs={{0,2},{1,3},{2,0},{3,1},{4,6},{5,7},{6,4},{7,5},{8,10},{9,11},{10,... | collective-permute-start | bytes 1572872 | tf_op jit(solution)/shard_map/ppermute | solution.py:130
  156.7 31.9 %collective-permute-start.3 = (bf16[128,1,2048]{2,0,1:T(8,128)(2,1)S(1)}, bf16[128,1,2048]{2,0,1:T(8,128)(2,1)}, u32[]{:S(2)}, u32[]{:S(2)}) collective-permute-start(bf16[128,1,2048]{2,0,1:T(8,128)(2,1)S(1)} %get-tuple-element.16), channel_id=1, source_target_pairs={{0,3},{1,0},{2,1},{3,2},{4,7},{5,4},{6,5},{7,6},{8,11},{9,8},{10,9... | collective-permute-start | bytes 1572872 | tf_op jit(solution)/shard_map/ppermute | solution.py:130
  186.6 5.8 %collective-permute-start.4 = (f32[2048,2]{0,1:T(2,128)S(1)}, f32[2048,2]{0,1:T(2,128)S(1)}, u32[]{:S(2)}, u32[]{:S(2)}) collective-permute-start(f32[2048,2]{0,1:T(2,128)S(1)} %slice.109), channel_id=1, source_target_pairs={{4,0},{8,4},{12,8},{16,12},{20,16},{24,20},{28,24},{5,1},{9,5},{13... | collective-permute-start | bytes 49160 | tf_op jit(solution)/shard_map/ppermute | solution.py:17
  190.4 6.3 %collective-permute-start.8 = (f32[2048,2]{0,1:T(2,128)S(1)}, f32[2048,2]{0,1:T(2,128)S(1)}, u32[]{:S(2)}, u32[]{:S(2)}) collective-permute-start(f32[2048,2]{0,1:T(2,128)S(1)} %slice.112), channel_id=1, source_target_pairs={{4,0},{8,4},{12,8},{16,12},{20,16},{24,20},{28,24},{5,1},{9,5},{13... | collective-permute-start | bytes 49160 | tf_op jit(solution)/shard_map/ppermute | solution.py:17
  194.1 14.9 %collective-permute-start.5 = (bf16[2048,128]{0,1:T(8,128)(2,1)S(1)}, bf16[2048,128]{0,1:T(8,128)(2,1)S(1)}, u32[]{:S(2)}, u32[]{:S(2)}) collective-permute-start(bf16[2048,128]{0,1:T(8,128)(2,1)S(1)} %get-tuple-element.14), channel_id=1, source_target_pairs={{0,1},{1,2},{2,3},{3,0},{4,5},{5,6},{6,7},{7,4},{8,9},{9,10},{10,1... | collective-permute-start | bytes 1572872 | tf_op jit(solution)/shard_map/ppermute | solution.py:117
  195.4 26.0 %collective-permute-start.6 = (bf16[2048,128]{0,1:T(8,128)(2,1)S(1)}, bf16[2048,128]{0,1:T(8,128)(2,1)S(1)}, u32[]{:S(2)}, u32[]{:S(2)}) collective-permute-start(bf16[2048,128]{0,1:T(8,128)(2,1)S(1)} %get-tuple-element.13), channel_id=1, source_target_pairs={{0,2},{1,3},{2,0},{3,1},{4,6},{5,7},{6,4},{7,5},{8,10},{9,11},{10,... | collective-permute-start | bytes 1572872 | tf_op jit(solution)/shard_map/ppermute | solution.py:117
  195.9 26.4 %collective-permute-start.7 = (bf16[2048,128]{0,1:T(8,128)(2,1)S(1)}, bf16[2048,128]{0,1:T(8,128)(2,1)S(1)}, u32[]{:S(2)}, u32[]{:S(2)}) collective-permute-start(bf16[2048,128]{0,1:T(8,128)(2,1)S(1)} %get-tuple-element.12), channel_id=1, source_target_pairs={{0,3},{1,0},{2,1},{3,2},{4,7},{5,4},{6,5},{7,6},{8,11},{9,8},{10,9... | collective-permute-start | bytes 1572872 | tf_op jit(solution)/shard_map/ppermute | solution.py:117
  198.4 33.0 %collective-permute-start.9 = (bf16[2048,128]{0,1:T(8,128)(2,1)S(1)}, bf16[2048,128]{0,1:T(8,128)(2,1)S(1)}, u32[]{:S(2)}, u32[]{:S(2)}) collective-permute-start(bf16[2048,128]{0,1:T(8,128)(2,1)S(1)} %get-tuple-element.11), channel_id=1, source_target_pairs={{0,1},{1,2},{2,3},{3,0},{4,5},{5,6},{6,7},{7,4},{8,9},{9,10},{10,1... | collective-permute-start | bytes 1572872 | tf_op jit(solution)/shard_map/ppermute | solution.py:117
  200.7 42.5 %collective-permute-start.10 = (bf16[2048,128]{0,1:T(8,128)(2,1)S(1)}, bf16[2048,128]{0,1:T(8,128)(2,1)S(1)}, u32[]{:S(2)}, u32[]{:S(2)}) collective-permute-start(bf16[2048,128]{0,1:T(8,128)(2,1)S(1)} %get-tuple-element.10), channel_id=1, source_target_pairs={{0,2},{1,3},{2,0},{3,1},{4,6},{5,7},{6,4},{7,5},{8,10},{9,11},{10,... | collective-permute-start | bytes 1572872 | tf_op jit(solution)/shard_map/ppermute | solution.py:117
  209.0 35.1 %collective-permute-start.11 = (bf16[2048,128]{0,1:T(8,128)(2,1)S(1)}, bf16[2048,128]{0,1:T(8,128)(2,1)S(1)}, u32[]{:S(2)}, u32[]{:S(2)}) collective-permute-start(bf16[2048,128]{0,1:T(8,128)(2,1)S(1)} %get-tuple-element.9), channel_id=1, source_target_pairs={{0,3},{1,0},{2,1},{3,2},{4,7},{5,4},{6,5},{7,6},{8,11},{9,8},{10,9... | collective-permute-start | bytes 1572872 | tf_op jit(solution)/shard_map/ppermute | solution.py:117

commit v9 on v8

--- a/solution.py
+++ b/solution.py
@@ -76,6 +76,7 @@
     query_proj = short_filter(grad_query[:, None], short_taps[:1], block_rows)
     query_rows = spread_rows(query_proj, "chan")
     z_lanes = correlate(mixed_cols, taps_cols)
+    z_lanes, query_rows = lax.optimization_barrier((z_lanes, query_rows))
     z_rows = lax.all_to_all(z_lanes, "seq", split_axis=1, concat_axis=0, tiled=True)
     z_wide = z_rows.astype(jnp.float32)
     grad_key = z_wide * value_part.T.astype(jnp.float32)

time: 246 us -> 234 us (0.951); the launches traced: 245 us -> 229 us
  waiting for transfers between devices: 127 us -> 114 us
    all_to_all x1, waiting for transfers between devices: 42.4 us -> 0.01 us  [on_device(): lax.all_to_all(grad_mixed, 'seq', split_axis=1, concat_axis=0, tiled=True)]
    all_to_all x1, waiting for transfers between devices: 0.01 us -> 37.7 us  [on_device(): lax.all_to_all(z_lanes, 'seq', split_axis=1, concat_axis=0, tiled=True)]
    ppermute x3, waiting for transfers between devices: 6.65 us -> 0.01 us  [spread_rows(): lax.ppermute(outgoing, axis, pairs)]
    all_to_all x1, starting transfers between devices: 6.8 us -> 4.2 us  [on_device(): lax.all_to_all(z_lanes, 'seq', split_axis=1, concat_axis=0, tiled=True)]
  transfers between devices with their start and end apart: 15 -> 15, of which waited for: 8 -> 6; matrix products, arithmetic and copies ran while one was open for 22% -> 21% of each run, Pallas kernels for 0% -> 7%
where the time goes in v9:
time: 234 us; the launch traced here: 229 us
  waiting for transfers between devices  114 us (49%)
  local copies, waits for them, and re-layouts  42.4 us (18%)
  starting transfers between devices  33.4 us (14%)
  other arithmetic  23.9 us (10%)
  Pallas kernels  15.3 us (7%)
    ppermute x3, waiting for transfers between devices, shifted(): lax.ppermute(value, axis, [(source, source + steps) for source in range(l...  42.7 us
    all_to_all x1, waiting for transfers between devices, on_device(): lax.all_to_all(z_lanes, 'seq', split_axis=1, concat_axis=0, tiled=True)  37.7 us
    ppermute x6, waiting for transfers between devices, spread_lanes(): lax.ppermute(outgoing, axis, pairs)  33.2 us
    pallas_call x1, Pallas kernels, correlate(): pl.pallas_call(correlate_kernel, out_shape=jax.ShapeDtypeStruct((channels...  15.3 us
    ppermute x6, starting transfers between devices, spread_lanes(): lax.ppermute(outgoing, axis, pairs)  8.81 us
    mul x1, other arithmetic, on_device(): grad_query = out_wide * conv_saved.astype(jnp.float32)  7.83 us
    dynamic_update_slice x8, local copies, waits for them, and re-layouts, on_device(): lax.dynamic_update_slice(out, piece.T[:, None, :], (0, plane, source * ch...  6.62 us
    ppermute x3, starting transfers between devices, shifted(): lax.ppermute(value, axis, [(source, source + steps) for source in range(l...  6.49 us
  transfers between devices with their start and end apart: 15, of which 6 were waited for; matrix products, arithmetic and copies ran while one was open for 21% of the time, Pallas kernels for 7%

profile of v9, /device:TPU:18, one launch (start us, length us, event | category | flops | bytes accessed | tf_op | source)
XLA Modules:
  0.0 228.9 jit_solution(14899014078181918849)
XLA Ops:
  0.0 1.7 copy.24
  1.7 5.2 %all-to-all-start.1 = ((bf16[512,8,16]{0,2,1:T(8,128)(2,1)}), bf16[512,8,16]{0,2,1:T(8,128)(2,1)S(1)}, u32[]{:S(2)}, u32[]{:S(2)}) async-start(bf16[512,8,16]{0,2,1:T(8,128)(2,1)} %bitcast.5), calls=%async_computation.1 | async-start | bytes 262144 | tf_op jit(solution)/shard_map/all_to_all | solution.py:74
  6.9 7.8 %convert_multiply_fusion = (f32[512,2048]{1,0:T(8,128)}, f32[512,1,2048]{2,0,1:T(8,128)}, bf16[512,2048]{1,0:T(8,128)(2,1)S(1)}) fusion(bf16[512,2048]{1,0:T(8,128)(2,1)} %param.5, bf16[512,2048]{1,0:T(8,128)(2,1)} %param.7, bf16[512,3,2048]{2,0,1:T(8,128)(2,1)} %param.6), kind=kLoop, calls=%fused_computation | loop fusion | flops 6291456 | bytes 16777216 | tf_op jit(solution)/shard_map/mul | solution.py:71
  14.7 2.5 %copy.21 = bf16[512,2048]{0,1:T(8,128)(2,1)} copy(bf16[512,2048]{1,0:T(8,128)(2,1)S(1)} %get-tuple-element.37) | data formatting | bytes 4194304 | tf_op jit(solution)/shard_map/convert_element_type | solution.py:72
  17.2 0.0 all-to-all-done.1
  17.2 5.1 %all-to-all-start = ((bf16[512,8,256]{0,2,1:T(8,128)(2,1)}), bf16[512,8,256]{0,2,1:T(8,128)(2,1)S(1)}, u32[]{:S(2)}, u32[]{:S(2)}) async-start(bf16[512,8,256]{0,2,1:T(8,128)(2,1)} %bitcast.1), calls=%async_computation | async-start | bytes 4194304 | tf_op jit(solution)/shard_map/all_to_all | solution.py:73
  22.3 0.8 slice_bitcast_fusion
  23.2 2.2 collective-permute-start
  25.4 0.1 fusion.22
  25.5 42.7 %collective-permute-done = f32[2,1,2048]{2,0,1:T(2,128)S(1)} collective-permute-done((f32[2,1,2048]{2,0,1:T(2,128)S(1)}, f32[2,1,2048]{2,0,1:T(2,128)S(1)}, u32[]{:S(2)}, u32[]{:S(2)}) %collective-permute-start) | collective-permute-done | bytes 16416 | tf_op jit(solution)/shard_map/ppermute | solution.py:17
  68.2 5.6 %fusion.14 = bf16[512,1,2048]{2,0,1:T(8,128)(2,1)S(1)} fusion(f32[512,1,2048]{2,0,1:T(8,128)} %get-tuple-element.26, f32[2,1,2048]{2,0,1:T(2,128)S(1)} %collective-permute-done, f32[2048]{0:T(1024)S(1)} %bitcast.109, f32[2048]{0:T(1024)S(1)} %bitcast.110, f32[2048]{0:T(1024)S(1)} %bitcast.111, bf16[512,2048]{1,0:T(8,128)(2,1)} %param.7, ...), kind=kLoop, calls=%fused_computation.22 | loop fusion | flops 11534336 | bytes 10526720 | tf_op jit(solution)/shard_map/convert_element_type | solution.py:153
  73.8 1.3 dynamic-slice_bitcast_fusion
  75.1 1.5 collective-permute-start.1
  76.6 0.5 collective-permute-start.2
  77.1 1.5 collective-permute-start.3
  78.7 2.3 rev.3
  81.0 0.1 concatenate.12
  81.1 0.9 reshape.60.h_ref
  82.0 0.0 all-to-all-done
  82.0 2.5 %copy.22 = bf16[8,512,256]{1,0,2:T(8,128)(2,1)} copy(bf16[8,512,256]{1,2,0:T(8,128)(2,1)S(1)} %bitcast.96) | data formatting | bytes 4194304 | tf_op jit(solution)/shard_map/all_to_all | solution.py:73
  84.5 2.7 %reshape.58 = bf16[16,256,16,16]{1,0,3,2:T(8,128)(2,1)S(1)} reshape(bf16[8,512,256]{1,0,2:T(8,128)(2,1)} %copy.22) | data formatting | bytes 4194304 | tf_op jit(solution)/shard_map/reshape | solution.py:43
  87.1 2.2 copy.23
  89.3 15.3 %shard_map.55 = bf16[256,4096]{1,0:T(8,128)(2,1)} custom-call(bf16[16,256,256]{2,1,0:T(8,128)(2,1)} %bitcast.101, f32[16,1,4352]{2,1,0:T(1,128)} %reshape.60.h_ref), custom_call_target="tpu_custom_call" | custom-call | flops 4563402752 | bytes 4472832 | tf_op jit(solution)/shard_map/pallas_call | solution.py:49
  104.6 0.0 collective-permute-done.1
  104.6 0.0 collective-permute-done.2
  104.7 3.1 %copy.36 = bf16[32,8,8,512]{3,2,0,1:T(8,128)(2,1)} copy(bf16[32,8,8,512]{3,2,1,0:T(8,128)(2,1)} %bitcast.100) | data formatting | bytes 4194304 | tf_op jit(solution)/shard_map/all_to_all | solution.py:80
  107.8 4.2 %all-to-all-start.2 = ((bf16[256,8,512]{2,0,1:T(8,128)(2,1)}), bf16[256,8,512]{2,0,1:T(8,128)(2,1)S(1)}, u32[]{:S(2)}, u32[]{:S(2)}) async-start(bf16[256,8,512]{2,0,1:T(8,128)(2,1)} %bitcast.97), calls=%async_computation.2 | async-start | bytes 4194304 | tf_op jit(solution)/shard_map/all_to_all | solution.py:80
  112.0 3.4 %broadcast_in_dim.31 = bf16[128,3,8192]{2,0,1:T(8,128)(2,1)} broadcast(bf16[]{:T(256)} %constant.83.clone.1), dimensions={} | broadcast | bytes 6291458 | tf_op jit(solution)/shard_map/broadcast_in_dim | solution.py:85
  115.4 0.8 constant_dynamic-update-slice_fusion.3
  116.2 1.9 constant_dynamic-update-slice_fusion.2
  118.1 1.9 constant_dynamic-update-slice_fusion.1
  120.0 37.7 %all-to-all-done.2 = bf16[256,8,512]{2,0,1:T(8,128)(2,1)S(1)} async-done(((bf16[256,8,512]{2,0,1:T(8,128)(2,1)}), bf16[256,8,512]{2,0,1:T(8,128)(2,1)S(1)}, u32[]{:S(2)}, u32[]{:S(2)}) %all-to-all-start.2) | async-done | bytes 2097184 | tf_op jit(solution)/shard_map/all_to_all | solution.py:80
  157.7 2.5 %convert_element_type.81 = f32[256,8,512]{2,0,1:T(8,128)} convert(bf16[256,8,512]{2,0,1:T(8,128)(2,1)S(1)} %all-to-all-done.2) | non-fusion elementwise | flops 1048576 | bytes 6291456 | tf_op jit(solution)/shard_map/convert_element_type | solution.py:81
  160.2 5.5 %copy.31 = f32[2048,512]{0,1:T(8,128)} copy(f32[2048,512]{1,0:T(8,128)} %bitcast.95) | data formatting | bytes 8388608 | tf_op jit(solution)/shard_map/convert_element_type | solution.py:81
  165.7 4.7 %fusion.19 = (f32[2048,512]{0,1:T(8,128)S(1)}, f32[2048,512]{0,1:T(8,128)S(1)}) fusion(f32[2048,512]{0,1:T(8,128)} %copy.31, bf16[512,3,2048]{2,0,1:T(8,128)(2,1)} %param.6), kind=kLoop, calls=%fused_computation.31 | loop fusion | flops 4194304 | bytes 16777216 | tf_op jit(solution)/shard_map/mul | solution.py:83
  170.4 2.0 collective-permute-start.4
  172.4 1.9 constant_dynamic-update-slice_fusion
  174.3 2.3 %collective-permute-start.8 = (f32[2048,2]{0,1:T(2,128)S(1)}, f32[2048,2]{0,1:T(2,128)S(1)}, u32[]{:S(2)}, u32[]{:S(2)}) collective-permute-start(f32[2048,2]{0,1:T(2,128)S(1)} %slice.112), channel_id=1, source_target_pairs={{4,0},{8,4},{12,8},{16,12},{20,16},{24,20},{28,24},{5,1},{9,5},{13... | collective-permute-start | bytes 49160 | tf_op jit(solution)/shard_map/ppermute | solution.py:17
  176.7 0.0 collective-permute-done.4
  176.7 1.6 fusion.9
  178.3 0.2 constant_dynamic-slice_fusion.2
  178.5 1.4 collective-permute-start.5
  179.9 1.5 collective-permute-start.6
  181.4 0.0 collective-permute-start.7
  181.4 0.0 collective-permute-done.8
  181.4 1.6 fusion.4
  183.1 0.1 constant_dynamic-slice_fusion.5
  183.2 3.0 %collective-permute-start.9 = (bf16[2048,128]{0,1:T(8,128)(2,1)S(1)}, bf16[2048,128]{0,1:T(8,128)(2,1)S(1)}, u32[]{:S(2)}, u32[]{:S(2)}) collective-permute-start(bf16[2048,128]{0,1:T(8,128)(2,1)S(1)} %get-tuple-element.29), channel_id=1, source_target_pairs={{0,1},{1,2},{2,3},{3,0},{4,5},{5,6},{6,7},{7,4},{8,9},{9,10},{10,1... | collective-permute-start | bytes 1572872 | tf_op jit(solution)/shard_map/ppermute | solution.py:118
  186.2 0.5 collective-permute-start.10
  186.7 0.8 bitcast_dynamic-update-slice_fusion.7
  187.5 5.8 %collective-permute-done.5 = bf16[2048,128]{0,1:T(8,128)(2,1)S(1)} collective-permute-done((bf16[2048,128]{0,1:T(8,128)(2,1)S(1)}, bf16[2048,128]{0,1:T(8,128)(2,1)S(1)}, u32[]{:S(2)}, u32[]{:S(2)}) %collective-permute-start.5) | collective-permute-done | bytes 524320 | tf_op jit(solution)/shard_map/ppermute | solution.py:118
  193.3 2.4 %collective-permute-start.11 = (bf16[2048,128]{0,1:T(8,128)(2,1)S(1)}, bf16[2048,128]{0,1:T(8,128)(2,1)S(1)}, u32[]{:S(2)}, u32[]{:S(2)}) collective-permute-start(bf16[2048,128]{0,1:T(8,128)(2,1)S(1)} %get-tuple-element.27), channel_id=1, source_target_pairs={{0,3},{1,0},{2,1},{3,2},{4,7},{5,4},{6,5},{7,6},{8,11},{9,8},{10,9... | collective-permute-start | bytes 1572872 | tf_op jit(solution)/shard_map/ppermute | solution.py:118
  195.7 0.8 bitcast_dynamic-update-slice_fusion.6
  196.5 9.4 %collective-permute-done.6 = bf16[2048,128]{0,1:T(8,128)(2,1)S(1)} collective-permute-done((bf16[2048,128]{0,1:T(8,128)(2,1)S(1)}, bf16[2048,128]{0,1:T(8,128)(2,1)S(1)}, u32[]{:S(2)}, u32[]{:S(2)}) %collective-permute-start.6) | collective-permute-done | bytes 524320 | tf_op jit(solution)/shard_map/ppermute | solution.py:118
  206.0 0.8 bitcast_dynamic-update-slice_fusion.5
  206.8 0.0 collective-permute-done.7
  206.8 0.8 bitcast_dynamic-update-slice_fusion.4
  207.6 0.8 bitcast_dynamic-update-slice_fusion.3
  208.4 7.4 %collective-permute-done.9 = bf16[2048,128]{0,1:T(8,128)(2,1)S(1)} collective-permute-done((bf16[2048,128]{0,1:T(8,128)(2,1)S(1)}, bf16[2048,128]{0,1:T(8,128)(2,1)S(1)}, u32[]{:S(2)}, u32[]{:S(2)}) %collective-permute-start.9) | collective-permute-done | bytes 524320 | tf_op jit(solution)/shard_map/ppermute | solution.py:118
  215.9 0.8 bitcast_dynamic-update-slice_fusion.2
  216.7 10.6 %collective-permute-done.10 = bf16[2048,128]{0,1:T(8,128)(2,1)S(1)} collective-permute-done((bf16[2048,128]{0,1:T(8,128)(2,1)S(1)}, bf16[2048,128]{0,1:T(8,128)(2,1)S(1)}, u32[]{:S(2)}, u32[]{:S(2)}) %collective-permute-start.10) | collective-permute-done | bytes 524320 | tf_op jit(solution)/shard_map/ppermute | solution.py:118
  227.2 0.8 bitcast_dynamic-update-slice_fusion.1
  228.1 0.0 collective-permute-done.11
  228.1 0.8 bitcast_dynamic-update-slice_fusion
  (7 shorter events, 0.1 us)
Async XLA Ops:
  1.7 15.6 %all-to-all-start.1 = ((bf16[512,8,16]{0,2,1:T(8,128)(2,1)}), bf16[512,8,16]{0,2,1:T(8,128)(2,1)S(1)}, u32[]{:S(2)}, u32[]{:S(2)}) async-start(bf16[512,8,16]{0,2,1:T(8,128)(2,1)} %bitcast.5), calls=%async_computation.1 | async-start | bytes 262144 | tf_op jit(solution)/shard_map/all_to_all | solution.py:74
  14.7 10.6 %copy-start = (f32[3,3,2048]{2,1,0:T(4,128)S(1)}, f32[3,3,2048]{2,1,0:T(4,128)}, u32[]{:S(2)}) copy-start(f32[3,3,2048]{2,1,0:T(4,128)} %param.9) | copy-start | bytes 221188
  17.2 64.8 %all-to-all-start = ((bf16[512,8,256]{0,2,1:T(8,128)(2,1)}), bf16[512,8,256]{0,2,1:T(8,128)(2,1)S(1)}, u32[]{:S(2)}, u32[]{:S(2)}) async-start(bf16[512,8,256]{0,2,1:T(8,128)(2,1)} %bitcast.1), calls=%async_computation | async-start | bytes 4194304 | tf_op jit(solution)/shard_map/all_to_all | solution.py:73
  23.2 45.0 %collective-permute-start = (f32[2,1,2048]{2,0,1:T(2,128)S(1)}, f32[2,1,2048]{2,0,1:T(2,128)S(1)}, u32[]{:S(2)}, u32[]{:S(2)}) collective-permute-start(f32[2,1,2048]{2,0,1:T(2,128)S(1)} %slice_bitcast_fusion), channel_id=1, source_target_pairs={{4,0},{8,4},{12,8},{16,12},{20,16},{24,20},{28,24},{5,1},{9,5},{13... | collective-permute-start | bytes 49160 | tf_op jit(solution)/shard_map/ppermute | solution.py:17
  75.1 29.5 %collective-permute-start.1 = (bf16[128,1,2048]{2,0,1:T(8,128)(2,1)}, bf16[128,1,2048]{2,0,1:T(8,128)(2,1)}, u32[]{:S(2)}, u32[]{:S(2)}) collective-permute-start(bf16[128,1,2048]{2,0,1:T(8,128)(2,1)} %get-tuple-element.35), channel_id=1, source_target_pairs={{0,1},{1,2},{2,3},{3,0},{4,5},{5,6},{6,7},{7,4},{8,9},{9,10},{10,1... | collective-permute-start | bytes 1572872 | tf_op jit(solution)/shard_map/ppermute | solution.py:131
  76.6 28.0 %collective-permute-start.2 = (bf16[128,1,2048]{2,0,1:T(8,128)(2,1)}, bf16[128,1,2048]{2,0,1:T(8,128)(2,1)}, u32[]{:S(2)}, u32[]{:S(2)}) collective-permute-start(bf16[128,1,2048]{2,0,1:T(8,128)(2,1)} %get-tuple-element.34), channel_id=1, source_target_pairs={{0,2},{1,3},{2,0},{3,1},{4,6},{5,7},{6,4},{7,5},{8,10},{9,11},{10,... | collective-permute-start | bytes 1572872 | tf_op jit(solution)/shard_map/ppermute | solution.py:131
  77.1 27.5 %collective-permute-start.3 = (bf16[128,1,2048]{2,0,1:T(8,128)(2,1)}, bf16[128,1,2048]{2,0,1:T(8,128)(2,1)}, u32[]{:S(2)}, u32[]{:S(2)}) collective-permute-start(bf16[128,1,2048]{2,0,1:T(8,128)(2,1)} %get-tuple-element.33), channel_id=1, source_target_pairs={{0,3},{1,0},{2,1},{3,2},{4,7},{5,4},{6,5},{7,6},{8,11},{9,8},{10,9... | collective-permute-start | bytes 1572872 | tf_op jit(solution)/shard_map/ppermute | solution.py:131
  107.8 50.0 %all-to-all-start.2 = ((bf16[256,8,512]{2,0,1:T(8,128)(2,1)}), bf16[256,8,512]{2,0,1:T(8,128)(2,1)S(1)}, u32[]{:S(2)}, u32[]{:S(2)}) async-start(bf16[256,8,512]{2,0,1:T(8,128)(2,1)} %bitcast.97), calls=%async_computation.2 | async-start | bytes 4194304 | tf_op jit(solution)/shard_map/all_to_all | solution.py:80
  170.4 6.2 %collective-permute-start.4 = (f32[2048,2]{0,1:T(2,128)S(1)}, f32[2048,2]{0,1:T(2,128)S(1)}, u32[]{:S(2)}, u32[]{:S(2)}) collective-permute-start(f32[2048,2]{0,1:T(2,128)S(1)} %slice.109), channel_id=1, source_target_pairs={{4,0},{8,4},{12,8},{16,12},{20,16},{24,20},{28,24},{5,1},{9,5},{13... | collective-permute-start | bytes 49160 | tf_op jit(solution)/shard_map/ppermute | solution.py:17
  174.3 7.1 %collective-permute-start.8 = (f32[2048,2]{0,1:T(2,128)S(1)}, f32[2048,2]{0,1:T(2,128)S(1)}, u32[]{:S(2)}, u32[]{:S(2)}) collective-permute-start(f32[2048,2]{0,1:T(2,128)S(1)} %slice.112), channel_id=1, source_target_pairs={{4,0},{8,4},{12,8},{16,12},{20,16},{24,20},{28,24},{5,1},{9,5},{13... | collective-permute-start | bytes 49160 | tf_op jit(solution)/shard_map/ppermute | solution.py:17
  178.5 14.8 %collective-permute-start.5 = (bf16[2048,128]{0,1:T(8,128)(2,1)S(1)}, bf16[2048,128]{0,1:T(8,128)(2,1)S(1)}, u32[]{:S(2)}, u32[]{:S(2)}) collective-permute-start(bf16[2048,128]{0,1:T(8,128)(2,1)S(1)} %get-tuple-element.32), channel_id=1, source_target_pairs={{0,1},{1,2},{2,3},{3,0},{4,5},{5,6},{6,7},{7,4},{8,9},{9,10},{10,1... | collective-permute-start | bytes 1572872 | tf_op jit(solution)/shard_map/ppermute | solution.py:118
  179.9 26.0 %collective-permute-start.6 = (bf16[2048,128]{0,1:T(8,128)(2,1)S(1)}, bf16[2048,128]{0,1:T(8,128)(2,1)S(1)}, u32[]{:S(2)}, u32[]{:S(2)}) collective-permute-start(bf16[2048,128]{0,1:T(8,128)(2,1)S(1)} %get-tuple-element.31), channel_id=1, source_target_pairs={{0,2},{1,3},{2,0},{3,1},{4,6},{5,7},{6,4},{7,5},{8,10},{9,11},{10,... | collective-permute-start | bytes 1572872 | tf_op jit(solution)/shard_map/ppermute | solution.py:118
  181.4 25.3 %collective-permute-start.7 = (bf16[2048,128]{0,1:T(8,128)(2,1)S(1)}, bf16[2048,128]{0,1:T(8,128)(2,1)S(1)}, u32[]{:S(2)}, u32[]{:S(2)}) collective-permute-start(bf16[2048,128]{0,1:T(8,128)(2,1)S(1)} %get-tuple-element.30), channel_id=1, source_target_pairs={{0,3},{1,0},{2,1},{3,2},{4,7},{5,4},{6,5},{7,6},{8,11},{9,8},{10,9... | collective-permute-start | bytes 1572872 | tf_op jit(solution)/shard_map/ppermute | solution.py:118
  183.2 32.7 %collective-permute-start.9 = (bf16[2048,128]{0,1:T(8,128)(2,1)S(1)}, bf16[2048,128]{0,1:T(8,128)(2,1)S(1)}, u32[]{:S(2)}, u32[]{:S(2)}) collective-permute-start(bf16[2048,128]{0,1:T(8,128)(2,1)S(1)} %get-tuple-element.29), channel_id=1, source_target_pairs={{0,1},{1,2},{2,3},{3,0},{4,5},{5,6},{6,7},{7,4},{8,9},{9,10},{10,1... | collective-permute-start | bytes 1572872 | tf_op jit(solution)/shard_map/ppermute | solution.py:118
  186.2 41.1 %collective-permute-start.10 = (bf16[2048,128]{0,1:T(8,128)(2,1)S(1)}, bf16[2048,128]{0,1:T(8,128)(2,1)S(1)}, u32[]{:S(2)}, u32[]{:S(2)}) collective-permute-start(bf16[2048,128]{0,1:T(8,128)(2,1)S(1)} %get-tuple-element.28), channel_id=1, source_target_pairs={{0,2},{1,3},{2,0},{3,1},{4,6},{5,7},{6,4},{7,5},{8,10},{9,11},{10,... | collective-permute-start | bytes 1572872 | tf_op jit(solution)/shard_map/ppermute | solution.py:118
  193.3 34.7 %collective-permute-start.11 = (bf16[2048,128]{0,1:T(8,128)(2,1)S(1)}, bf16[2048,128]{0,1:T(8,128)(2,1)S(1)}, u32[]{:S(2)}, u32[]{:S(2)}) collective-permute-start(bf16[2048,128]{0,1:T(8,128)(2,1)S(1)} %get-tuple-element.27), channel_id=1, source_target_pairs={{0,3},{1,0},{2,1},{3,2},{4,7},{5,4},{6,5},{7,6},{8,11},{9,8},{10,9... | collective-permute-start | bytes 1572872 | tf_op jit(solution)/shard_map/ppermute | solution.py:118

commit v10 on v9

--- a/solution.py
+++ b/solution.py
@@ -70,10 +70,13 @@
     value_part = qkv_saved[:, 2, :]
     grad_query = out_wide * conv_saved.astype(jnp.float32)
     grad_mixed = (out_wide * query.astype(jnp.float32)).astype(jnp.bfloat16)
+    short_len = short_taps.shape[1]
+    query_next = shifted(grad_query[: short_len - 1, None], "seq", -1)
+    grad_mixed, query_next = lax.optimization_barrier((grad_mixed, query_next))
     mixed_cols = lax.all_to_all(grad_mixed, "seq", split_axis=1, concat_axis=0, tiled=True)
     taps_cols = lax.all_to_all(long_taps, "seq", split_axis=1, concat_axis=0, tiled=True)
     short_len = short_taps.shape[1]
-    query_proj = short_filter(grad_query[:, None], short_taps[:1], block_rows)
+    query_proj = short_filter(grad_query[:, None], short_taps[:1], block_rows, query_next)
     query_rows = spread_rows(query_proj, "chan")
     z_lanes = correlate(mixed_cols, taps_cols)
     z_lanes, query_rows = lax.optimization_barrier((z_lanes, query_rows))
@@ -143,9 +146,8 @@
     return out
 
 
-def short_filter(stacked, taps, block_rows):
+def short_filter(stacked, taps, block_rows, borrowed):
     short_len = taps.shape[1]
-    borrowed = shifted(stacked[: short_len - 1], "seq", -1)
     extended = jnp.concatenate([stacked, borrowed], 0)
     result = jnp.zeros_like(stacked)
     for lag_index in range(short_len):

time: 234 us -> 224 us (0.957)
  waiting for transfers between devices: 114 us -> 105 us
    ppermute x3, waiting for transfers between devices: 42.7 us -> 1.43 us  [shifted(): lax.ppermute(value, axis, [(source, source + steps) for source in range(l...]
    all_to_all x1, waiting for transfers between devices: 0.01 us -> 32 us  [on_device(): lax.all_to_all(grad_mixed, 'seq', split_axis=1, concat_axis=0, tiled=True)]
    mul x1 -> x0, other arithmetic: 7.83 us -> none  [on_device(): grad_query = out_wide * conv_saved.astype(jnp.float32)]
    broadcast_in_dim x0 -> x1, other arithmetic: none -> 6.34 us  [on_device(): grad_query[:, None]]
    all_to_all x1, starting transfers between devices: 4.2 us -> 6.8 us  [on_device(): lax.all_to_all(z_lanes, 'seq', split_axis=1, concat_axis=0, tiled=True)]
    convert_element_type x1 -> x0, local copies, waits for them, and re-layouts: 2.51 us -> none  [on_device(): grad_mixed = (out_wide * query.astype(jnp.float32)).astype(jnp.bfloat16)]
    optimization_barrier x0 -> x1, local copies, waits for them, and re-layouts: none -> 2.5 us  [on_device(): grad_mixed, query_next = lax.optimization_barrier((grad_mixed, query_next))]
  transfers between devices with their start and end apart: 15 -> 15, of which waited for: 6 -> 7; matrix products, arithmetic and copies ran while one was open for 21% -> 21% of each run, Pallas kernels for 7% -> 7%
where the time goes in v10:
time: 224 us; the launch traced here: 220 us
  waiting for transfers between devices  105 us (47%)
  local copies, waits for them, and re-layouts  41.4 us (18%)
  starting transfers between devices  35.4 us (16%)
  other arithmetic  22.4 us (10%)
  Pallas kernels  15.3 us (7%)
    all_to_all x1, waiting for transfers between devices, on_device(): lax.all_to_all(z_lanes, 'seq', split_axis=1, concat_axis=0, tiled=True)  37.7 us
    ppermute x6, waiting for transfers between devices, spread_lanes(): lax.ppermute(outgoing, axis, pairs)  34.1 us
    all_to_all x1, waiting for transfers between devices, on_device(): lax.all_to_all(grad_mixed, 'seq', split_axis=1, concat_axis=0, tiled=True)  32 us
    pallas_call x1, Pallas kernels, correlate(): pl.pallas_call(correlate_kernel, out_shape=jax.ShapeDtypeStruct((channels...  15.3 us
    ppermute x6, starting transfers between devices, spread_lanes(): lax.ppermute(outgoing, axis, pairs)  8.02 us
    all_to_all x1, starting transfers between devices, on_device(): lax.all_to_all(z_lanes, 'seq', split_axis=1, concat_axis=0, tiled=True)  6.8 us
    dynamic_update_slice x8, local copies, waits for them, and re-layouts, on_device(): lax.dynamic_update_slice(out, piece.T[:, None, :], (0, plane, source * ch...  6.62 us
    dynamic_update_slice x4, local copies, waits for them, and re-layouts, on_device(): out = lax.dynamic_update_slice(out, piece, (0, 0, source * channels))  6.47 us
  transfers between devices with their start and end apart: 15, of which 7 were waited for; matrix products, arithmetic and copies ran while one was open for 21% of the time, Pallas kernels for 7%

profile of v10, /device:TPU:18, one launch (start us, length us, event | category | flops | bytes accessed | tf_op | source)
XLA Modules:
  0.0 220.1 jit_solution(9448758208031211178)
XLA Ops:
  0.0 1.7 copy.24
  1.7 5.2 %all-to-all-start.1 = ((bf16[512,8,16]{0,2,1:T(8,128)(2,1)}), bf16[512,8,16]{0,2,1:T(8,128)(2,1)S(1)}, u32[]{:S(2)}, u32[]{:S(2)}) async-start(bf16[512,8,16]{0,2,1:T(8,128)(2,1)} %bitcast.6), calls=%async_computation.1 | async-start | bytes 262144 | tf_op jit(solution)/shard_map/all_to_all | solution.py:77
  6.9 6.3 %fusion.21 = (f32[512,1,2048]{2,0,1:T(8,128)}, f32[512,2048]{1,0:T(8,128)S(1)}, bf16[512,2048]{1,0:T(8,128)(2,1)S(1)}) fusion(bf16[512,2048]{1,0:T(8,128)(2,1)} %param.7, bf16[512,2048]{1,0:T(8,128)(2,1)} %param.5, bf16[512,3,2048]{2,0,1:T(8,128)(2,1)} %param.6), kind=kLoop, calls=%fused_computation.59 | loop fusion | flops 6291456 | bytes 16777216 | tf_op jit(solution)/shard_map/broadcast_in_dim | solution.py:79
  13.2 2.2 collective-permute-start
  15.4 1.4 collective-permute-done
  16.8 2.5 %copy.21 = bf16[512,2048]{0,1:T(8,128)(2,1)} copy(bf16[512,2048]{1,0:T(8,128)(2,1)S(1)} %get-tuple-element.16) | data formatting | bytes 4194304 | tf_op jit(solution)/shard_map/optimization_barrier | solution.py:75
  19.3 0.0 all-to-all-done.1
  19.3 5.4 %all-to-all-start = ((bf16[512,8,256]{0,2,1:T(8,128)(2,1)}), bf16[512,8,256]{0,2,1:T(8,128)(2,1)S(1)}, u32[]{:S(2)}, u32[]{:S(2)}) async-start(bf16[512,8,256]{0,2,1:T(8,128)(2,1)} %bitcast.2), calls=%async_computation | async-start | bytes 4194304 | tf_op jit(solution)/shard_map/all_to_all | solution.py:76
  24.7 0.1 fusion.22
  24.8 5.6 %fusion.14 = bf16[512,1,2048]{2,0,1:T(8,128)(2,1)S(1)} fusion(f32[512,1,2048]{2,0,1:T(8,128)} %get-tuple-element.29, f32[2,1,2048]{2,0,1:T(2,128)S(1)} %collective-permute-done, f32[2048]{0:T(1024)S(1)} %bitcast.109, f32[2048]{0:T(1024)S(1)} %bitcast.110, f32[2048]{0:T(1024)S(1)} %bitcast.111, bf16[512,2048]{1,0:T(8,128)(2,1)} %param.7, ...), kind=kLoop, calls=%fused_computation.22 | loop fusion | flops 11534336 | bytes 10526720 | tf_op jit(solution)/shard_map/convert_element_type | solution.py:155
  30.4 1.2 dynamic-slice_bitcast_fusion
  31.6 1.5 collective-permute-start.1
  33.1 0.5 collective-permute-start.2
  33.6 1.5 collective-permute-start.3
  35.2 2.3 %rev.3 = f32[16,4096]{1,0:T(8,128)S(1)} reverse(f32[16,4096]{1,0:T(8,128)S(1)} %bitcast.102), dimensions={1} | reverse | bytes 524288 | tf_op jit(solution)/shard_map/rev | solution.py:45
  37.5 0.1 concatenate.12
  37.5 0.9 reshape.59.h_ref
  38.4 32.0 %all-to-all-done = bf16[512,8,256]{0,2,1:T(8,128)(2,1)S(1)} async-done(((bf16[512,8,256]{0,2,1:T(8,128)(2,1)}), bf16[512,8,256]{0,2,1:T(8,128)(2,1)S(1)}, u32[]{:S(2)}, u32[]{:S(2)}) %all-to-all-start) | async-done | bytes 2097184 | tf_op jit(solution)/shard_map/all_to_all | solution.py:76
  70.5 2.5 %copy.22 = bf16[8,512,256]{1,0,2:T(8,128)(2,1)} copy(bf16[8,512,256]{1,2,0:T(8,128)(2,1)S(1)} %bitcast.96) | data formatting | bytes 4194304 | tf_op jit(solution)/shard_map/all_to_all | solution.py:76
  72.9 2.7 %reshape.57 = bf16[16,256,16,16]{1,0,3,2:T(8,128)(2,1)S(1)} reshape(bf16[8,512,256]{1,0,2:T(8,128)(2,1)} %copy.22) | data formatting | bytes 4194304 | tf_op jit(solution)/shard_map/reshape | solution.py:43
  75.6 2.2 copy.23
  77.8 15.3 %shard_map.55 = bf16[256,4096]{1,0:T(8,128)(2,1)} custom-call(bf16[16,256,256]{2,1,0:T(8,128)(2,1)} %bitcast.101, f32[16,1,4352]{2,1,0:T(1,128)} %reshape.59.h_ref), custom_call_target="tpu_custom_call" | custom-call | flops 4563402752 | bytes 4472832 | tf_op jit(solution)/shard_map/pallas_call | solution.py:49
  93.1 0.0 collective-permute-done.1
  93.1 0.0 collective-permute-done.2
  93.1 0.0 collective-permute-done.3
  93.1 3.1 %copy.36 = bf16[32,8,8,512]{3,2,0,1:T(8,128)(2,1)} copy(bf16[32,8,8,512]{3,2,1,0:T(8,128)(2,1)} %bitcast.100) | data formatting | bytes 4194304 | tf_op jit(solution)/shard_map/all_to_all | solution.py:83
  96.2 6.8 %all-to-all-start.2 = ((bf16[256,8,512]{2,0,1:T(8,128)(2,1)}), bf16[256,8,512]{2,0,1:T(8,128)(2,1)S(1)}, u32[]{:S(2)}, u32[]{:S(2)}) async-start(bf16[256,8,512]{2,0,1:T(8,128)(2,1)} %bitcast.97), calls=%async_computation.2 | async-start | bytes 4194304 | tf_op jit(solution)/shard_map/all_to_all | solution.py:83
  103.0 3.4 %broadcast_in_dim.34 = bf16[128,3,8192]{2,0,1:T(8,128)(2,1)} broadcast(bf16[]{:T(256)} %constant.83.clone.1), dimensions={} | broadcast | bytes 6291458 | tf_op jit(solution)/shard_map/broadcast_in_dim | solution.py:88
  106.5 0.8 constant_dynamic-update-slice_fusion.3
  107.3 1.9 constant_dynamic-update-slice_fusion.2
  109.2 1.9 constant_dynamic-update-slice_fusion.1
  111.1 37.7 %all-to-all-done.2 = bf16[256,8,512]{2,0,1:T(8,128)(2,1)S(1)} async-done(((bf16[256,8,512]{2,0,1:T(8,128)(2,1)}), bf16[256,8,512]{2,0,1:T(8,128)(2,1)S(1)}, u32[]{:S(2)}, u32[]{:S(2)}) %all-to-all-start.2) | async-done | bytes 2097184 | tf_op jit(solution)/shard_map/all_to_all | solution.py:83
  148.8 2.5 %convert_element_type.81 = f32[256,8,512]{2,0,1:T(8,128)} convert(bf16[256,8,512]{2,0,1:T(8,128)(2,1)S(1)} %all-to-all-done.2) | non-fusion elementwise | flops 1048576 | bytes 6291456 | tf_op jit(solution)/shard_map/convert_element_type | solution.py:84
  151.3 5.5 %copy.31 = f32[2048,512]{0,1:T(8,128)} copy(f32[2048,512]{1,0:T(8,128)} %bitcast.95) | data formatting | bytes 8388608 | tf_op jit(solution)/shard_map/convert_element_type | solution.py:84
  156.8 4.7 %fusion.19 = (f32[2048,512]{0,1:T(8,128)S(1)}, f32[2048,512]{0,1:T(8,128)S(1)}) fusion(f32[2048,512]{0,1:T(8,128)} %copy.31, bf16[512,3,2048]{2,0,1:T(8,128)(2,1)} %param.6), kind=kLoop, calls=%fused_computation.31 | loop fusion | flops 4194304 | bytes 16777216 | tf_op jit(solution)/shard_map/mul | solution.py:86
  161.5 1.9 collective-permute-start.4
  163.5 1.9 constant_dynamic-update-slice_fusion
  165.4 2.3 %collective-permute-start.8 = (f32[2048,2]{0,1:T(2,128)S(1)}, f32[2048,2]{0,1:T(2,128)S(1)}, u32[]{:S(2)}, u32[]{:S(2)}) collective-permute-start(f32[2048,2]{0,1:T(2,128)S(1)} %slice.108), channel_id=1, source_target_pairs={{4,0},{8,4},{12,8},{16,12},{20,16},{24,20},{28,24},{5,1},{9,5},{13... | collective-permute-start | bytes 49160 | tf_op jit(solution)/shard_map/ppermute | solution.py:17
  167.7 0.0 collective-permute-done.4
  167.7 1.6 fusion.9
  169.4 0.2 constant_dynamic-slice_fusion.2
  169.6 1.5 collective-permute-start.5
  171.1 0.5 collective-permute-start.6
  171.6 1.5 collective-permute-start.7
  173.2 0.0 collective-permute-done.8
  173.2 1.6 fusion.4
  174.8 0.1 constant_dynamic-slice_fusion.5
  174.9 1.4 collective-permute-start.9
  176.3 1.5 collective-permute-start.10
  177.8 0.8 bitcast_dynamic-update-slice_fusion.7
  178.7 5.7 %collective-permute-done.5 = bf16[2048,128]{0,1:T(8,128)(2,1)S(1)} collective-permute-done((bf16[2048,128]{0,1:T(8,128)(2,1)S(1)}, bf16[2048,128]{0,1:T(8,128)(2,1)S(1)}, u32[]{:S(2)}, u32[]{:S(2)}) %collective-permute-start.5) | collective-permute-done | bytes 524320 | tf_op jit(solution)/shard_map/ppermute | solution.py:121
  184.4 1.5 collective-permute-start.11
  185.9 0.8 bitcast_dynamic-update-slice_fusion.6
  186.7 10.4 %collective-permute-done.6 = bf16[2048,128]{0,1:T(8,128)(2,1)S(1)} collective-permute-done((bf16[2048,128]{0,1:T(8,128)(2,1)S(1)}, bf16[2048,128]{0,1:T(8,128)(2,1)S(1)}, u32[]{:S(2)}, u32[]{:S(2)}) %collective-permute-start.6) | collective-permute-done | bytes 524320 | tf_op jit(solution)/shard_map/ppermute | solution.py:121
  197.1 0.8 bitcast_dynamic-update-slice_fusion.5
  198.0 0.0 collective-permute-done.7
  198.0 0.8 bitcast_dynamic-update-slice_fusion.4
  198.8 0.8 bitcast_dynamic-update-slice_fusion.3
  199.6 7.3 %collective-permute-done.9 = bf16[2048,128]{0,1:T(8,128)(2,1)S(1)} collective-permute-done((bf16[2048,128]{0,1:T(8,128)(2,1)S(1)}, bf16[2048,128]{0,1:T(8,128)(2,1)S(1)}, u32[]{:S(2)}, u32[]{:S(2)}) %collective-permute-start.9) | collective-permute-done | bytes 524320 | tf_op jit(solution)/shard_map/ppermute | solution.py:121
  206.9 0.8 bitcast_dynamic-update-slice_fusion.2
  207.8 10.7 %collective-permute-done.10 = bf16[2048,128]{0,1:T(8,128)(2,1)S(1)} collective-permute-done((bf16[2048,128]{0,1:T(8,128)(2,1)S(1)}, bf16[2048,128]{0,1:T(8,128)(2,1)S(1)}, u32[]{:S(2)}, u32[]{:S(2)}) %collective-permute-start.10) | collective-permute-done | bytes 524320 | tf_op jit(solution)/shard_map/ppermute | solution.py:121
  218.4 0.8 bitcast_dynamic-update-slice_fusion.1
  219.2 0.0 collective-permute-done.11
  219.2 0.8 bitcast_dynamic-update-slice_fusion
  (7 shorter events, 0.1 us)
Async XLA Ops:
  1.7 17.7 %all-to-all-start.1 = ((bf16[512,8,16]{0,2,1:T(8,128)(2,1)}), bf16[512,8,16]{0,2,1:T(8,128)(2,1)S(1)}, u32[]{:S(2)}, u32[]{:S(2)}) async-start(bf16[512,8,16]{0,2,1:T(8,128)(2,1)} %bitcast.6), calls=%async_computation.1 | async-start | bytes 262144 | tf_op jit(solution)/shard_map/all_to_all | solution.py:77
  13.2 3.6 %collective-permute-start = (f32[2,1,2048]{2,0,1:T(2,128)S(1)}, f32[2,1,2048]{2,0,1:T(2,128)S(1)}, u32[]{:S(2)}, u32[]{:S(2)}) collective-permute-start(f32[2,1,2048]{2,0,1:T(2,128)S(1)} %slice_bitcast_fusion), channel_id=1, source_target_pairs={{4,0},{8,4},{12,8},{16,12},{20,16},{24,20},{28,24},{5,1},{9,5},{13... | collective-permute-start | bytes 49160 | tf_op jit(solution)/shard_map/ppermute | solution.py:17
  16.8 7.9 %copy-start = (f32[3,3,2048]{2,1,0:T(4,128)S(1)}, f32[3,3,2048]{2,1,0:T(4,128)}, u32[]{:S(2)}) copy-start(f32[3,3,2048]{2,1,0:T(4,128)} %param.9) | copy-start | bytes 221188
  19.3 51.1 %all-to-all-start = ((bf16[512,8,256]{0,2,1:T(8,128)(2,1)}), bf16[512,8,256]{0,2,1:T(8,128)(2,1)S(1)}, u32[]{:S(2)}, u32[]{:S(2)}) async-start(bf16[512,8,256]{0,2,1:T(8,128)(2,1)} %bitcast.2), calls=%async_computation | async-start | bytes 4194304 | tf_op jit(solution)/shard_map/all_to_all | solution.py:76
  31.6 61.5 %collective-permute-start.1 = (bf16[128,1,2048]{2,0,1:T(8,128)(2,1)}, bf16[128,1,2048]{2,0,1:T(8,128)(2,1)}, u32[]{:S(2)}, u32[]{:S(2)}) collective-permute-start(bf16[128,1,2048]{2,0,1:T(8,128)(2,1)} %get-tuple-element.39), channel_id=1, source_target_pairs={{0,1},{1,2},{2,3},{3,0},{4,5},{5,6},{6,7},{7,4},{8,9},{9,10},{10,1... | collective-permute-start | bytes 1572872 | tf_op jit(solution)/shard_map/ppermute | solution.py:134
  33.1 60.0 %collective-permute-start.2 = (bf16[128,1,2048]{2,0,1:T(8,128)(2,1)}, bf16[128,1,2048]{2,0,1:T(8,128)(2,1)}, u32[]{:S(2)}, u32[]{:S(2)}) collective-permute-start(bf16[128,1,2048]{2,0,1:T(8,128)(2,1)} %get-tuple-element.38), channel_id=1, source_target_pairs={{0,2},{1,3},{2,0},{3,1},{4,6},{5,7},{6,4},{7,5},{8,10},{9,11},{10,... | collective-permute-start | bytes 1572872 | tf_op jit(solution)/shard_map/ppermute | solution.py:134
  33.6 59.5 %collective-permute-start.3 = (bf16[128,1,2048]{2,0,1:T(8,128)(2,1)}, bf16[128,1,2048]{2,0,1:T(8,128)(2,1)}, u32[]{:S(2)}, u32[]{:S(2)}) collective-permute-start(bf16[128,1,2048]{2,0,1:T(8,128)(2,1)} %get-tuple-element.37), channel_id=1, source_target_pairs={{0,3},{1,0},{2,1},{3,2},{4,7},{5,4},{6,5},{7,6},{8,11},{9,8},{10,9... | collective-permute-start | bytes 1572872 | tf_op jit(solution)/shard_map/ppermute | solution.py:134
  96.2 52.6 %all-to-all-start.2 = ((bf16[256,8,512]{2,0,1:T(8,128)(2,1)}), bf16[256,8,512]{2,0,1:T(8,128)(2,1)S(1)}, u32[]{:S(2)}, u32[]{:S(2)}) async-start(bf16[256,8,512]{2,0,1:T(8,128)(2,1)} %bitcast.97), calls=%async_computation.2 | async-start | bytes 4194304 | tf_op jit(solution)/shard_map/all_to_all | solution.py:83
  161.5 6.2 %collective-permute-start.4 = (f32[2048,2]{0,1:T(2,128)S(1)}, f32[2048,2]{0,1:T(2,128)S(1)}, u32[]{:S(2)}, u32[]{:S(2)}) collective-permute-start(f32[2048,2]{0,1:T(2,128)S(1)} %slice.105), channel_id=1, source_target_pairs={{4,0},{8,4},{12,8},{16,12},{20,16},{24,20},{28,24},{5,1},{9,5},{13... | collective-permute-start | bytes 49160 | tf_op jit(solution)/shard_map/ppermute | solution.py:17
  165.4 7.8 %collective-permute-start.8 = (f32[2048,2]{0,1:T(2,128)S(1)}, f32[2048,2]{0,1:T(2,128)S(1)}, u32[]{:S(2)}, u32[]{:S(2)}) collective-permute-start(f32[2048,2]{0,1:T(2,128)S(1)} %slice.108), channel_id=1, source_target_pairs={{4,0},{8,4},{12,8},{16,12},{20,16},{24,20},{28,24},{5,1},{9,5},{13... | collective-permute-start | bytes 49160 | tf_op jit(solution)/shard_map/ppermute | solution.py:17
  169.6 14.8 %collective-permute-start.5 = (bf16[2048,128]{0,1:T(8,128)(2,1)S(1)}, bf16[2048,128]{0,1:T(8,128)(2,1)S(1)}, u32[]{:S(2)}, u32[]{:S(2)}) collective-permute-start(bf16[2048,128]{0,1:T(8,128)(2,1)S(1)} %get-tuple-element.36), channel_id=1, source_target_pairs={{0,1},{1,2},{2,3},{3,0},{4,5},{5,6},{6,7},{7,4},{8,9},{9,10},{10,1... | collective-permute-start | bytes 1572872 | tf_op jit(solution)/shard_map/ppermute | solution.py:121
  171.1 26.0 %collective-permute-start.6 = (bf16[2048,128]{0,1:T(8,128)(2,1)S(1)}, bf16[2048,128]{0,1:T(8,128)(2,1)S(1)}, u32[]{:S(2)}, u32[]{:S(2)}) collective-permute-start(bf16[2048,128]{0,1:T(8,128)(2,1)S(1)} %get-tuple-element.35), channel_id=1, source_target_pairs={{0,2},{1,3},{2,0},{3,1},{4,6},{5,7},{6,4},{7,5},{8,10},{9,11},{10,... | collective-permute-start | bytes 1572872 | tf_op jit(solution)/shard_map/ppermute | solution.py:121
  171.6 26.4 %collective-permute-start.7 = (bf16[2048,128]{0,1:T(8,128)(2,1)S(1)}, bf16[2048,128]{0,1:T(8,128)(2,1)S(1)}, u32[]{:S(2)}, u32[]{:S(2)}) collective-permute-start(bf16[2048,128]{0,1:T(8,128)(2,1)S(1)} %get-tuple-element.34), channel_id=1, source_target_pairs={{0,3},{1,0},{2,1},{3,2},{4,7},{5,4},{6,5},{7,6},{8,11},{9,8},{10,9... | collective-permute-start | bytes 1572872 | tf_op jit(solution)/shard_map/ppermute | solution.py:121
  174.9 32.0 %collective-permute-start.9 = (bf16[2048,128]{0,1:T(8,128)(2,1)S(1)}, bf16[2048,128]{0,1:T(8,128)(2,1)S(1)}, u32[]{:S(2)}, u32[]{:S(2)}) collective-permute-start(bf16[2048,128]{0,1:T(8,128)(2,1)S(1)} %get-tuple-element.33), channel_id=1, source_target_pairs={{0,1},{1,2},{2,3},{3,0},{4,5},{5,6},{6,7},{7,4},{8,9},{9,10},{10,1... | collective-permute-start | bytes 1572872 | tf_op jit(solution)/shard_map/ppermute | solution.py:121
  176.3 42.1 %collective-permute-start.10 = (bf16[2048,128]{0,1:T(8,128)(2,1)S(1)}, bf16[2048,128]{0,1:T(8,128)(2,1)S(1)}, u32[]{:S(2)}, u32[]{:S(2)}) collective-permute-start(bf16[2048,128]{0,1:T(8,128)(2,1)S(1)} %get-tuple-element.32), channel_id=1, source_target_pairs={{0,2},{1,3},{2,0},{3,1},{4,6},{5,7},{6,4},{7,5},{8,10},{9,11},{10,... | collective-permute-start | bytes 1572872 | tf_op jit(solution)/shard_map/ppermute | solution.py:121
  184.4 34.8 %collective-permute-start.11 = (bf16[2048,128]{0,1:T(8,128)(2,1)S(1)}, bf16[2048,128]{0,1:T(8,128)(2,1)S(1)}, u32[]{:S(2)}, u32[]{:S(2)}) collective-permute-start(bf16[2048,128]{0,1:T(8,128)(2,1)S(1)} %get-tuple-element.31), channel_id=1, source_target_pairs={{0,3},{1,0},{2,1},{3,2},{4,7},{5,4},{6,5},{7,6},{8,11},{9,8},{10,9... | collective-permute-start | bytes 1572872 | tf_op jit(solution)/shard_map/ppermute | solution.py:121

commit v11 on v10

--- a/solution.py
+++ b/solution.py
@@ -17,10 +17,11 @@
     return lax.ppermute(value, axis, [(source, source + steps) for source in range(leading, last)])
 
 
-def correlate_kernel(x_ref, h_ref, o_ref, acc_ref):
-    rows_all = x_ref.shape[1]
-    blocks = rows_all // per_group
-    tokens = blocks * block
+def correlate_kernel(x_ref, h_ref, o_ref, acc_ref, rows_ref):
+    tokens = x_ref.shape[1]
+    blocks = tokens // block
+    for index in range(blocks):
+        rows_ref[per_group * index : per_group * (index + 1), :] = x_ref[:, block * index : block * (index + 1)]
     acc_ref[...] = jnp.zeros(acc_ref.shape, acc_ref.dtype)
     for lag_block in range(blocks):
         start = tokens - block * (lag_block + 1)
@@ -29,7 +30,7 @@
         rolled = pltpu.roll(spread, block + 1, 1, stride=1, stride_axis=0)
         band = rolled[:, :block].astype(jnp.bfloat16)
         rows = per_group * (blocks - lag_block)
-        source = x_ref[0, per_group * lag_block :, :]
+        source = rows_ref[per_group * lag_block :, :]
         acc_ref[:rows, :] += jnp.dot(source, band, preferred_element_type=jnp.float32)
     for index in range(blocks):
         slab = acc_ref[per_group * index : per_group * (index + 1), :]
@@ -37,11 +38,9 @@
 
 
 def correlate(grads, taps):
-    tokens, channels = grads.shape
+    channels, tokens = grads.shape
     groups = taps.shape[1]
     blocks = tokens // block
-    shaped = grads.reshape(blocks, block, groups, per_group).transpose(2, 0, 3, 1)
-    shaped = shaped.reshape(groups, blocks * per_group, block)
     reversed_taps = taps.astype(jnp.float32).T[:, ::-1]
     padded = jnp.concatenate([reversed_taps, jnp.zeros((groups, block), jnp.float32)], 1)
     padded = padded.reshape(groups, 1, tokens + block)
@@ -51,15 +50,18 @@
         out_shape=jax.ShapeDtypeStruct((channels, tokens), jnp.bfloat16),
         grid=(groups,),
         in_specs=[
-            pl.BlockSpec((1, blocks * per_group, block), lambda g: (g, 0, 0)),
+            pl.BlockSpec((per_group, tokens), lambda g: (g, 0)),
             pl.BlockSpec((1, 1, tokens + block), lambda g: (g, 0, 0)),
         ],
         out_specs=pl.BlockSpec((per_group, tokens), lambda g: (g, 0)),
-        scratch_shapes=[pltpu.VMEM((blocks * per_group, block), jnp.float32)],
+        scratch_shapes=[
+            pltpu.VMEM((blocks * per_group, block), jnp.float32),
+            pltpu.VMEM((blocks * per_group, block), jnp.bfloat16),
+        ],
         cost_estimate=pl.CostEstimate(
             flops=flops, bytes_accessed=grads.size * 4 + padded.size * 4, transcendentals=0
         ),
-    )(shaped, padded)
+    )(grads, padded)
 
 
 def on_device(grad_out, qkv_saved, conv_saved, long_taps, short_taps):
@@ -73,7 +75,7 @@
     short_len = short_taps.shape[1]
     query_next = shifted(grad_query[: short_len - 1, None], "seq", -1)
     grad_mixed, query_next = lax.optimization_barrier((grad_mixed, query_next))
-    mixed_cols = lax.all_to_all(grad_mixed, "seq", split_axis=1, concat_axis=0, tiled=True)
+    mixed_cols = lax.all_to_all(grad_mixed.T, "seq", split_axis=0, concat_axis=1, tiled=True)
     taps_cols = lax.all_to_all(long_taps, "seq", split_axis=1, concat_axis=0, tiled=True)
     short_len = short_taps.shape[1]
     query_proj = short_filter(grad_query[:, None], short_taps[:1], block_rows, query_next)

time: 224 us -> 219 us (0.978)
  local copies, waits for them, and re-layouts: 41.4 us -> 35.7 us
    reshape x1 -> x0, local copies, waits for them, and re-layouts: 2.67 us -> none  [correlate(): grads.reshape(blocks, block, groups, per_group).transpose(2, 0, 3, 1)]
    optimization_barrier x1 -> x0, local copies, waits for them, and re-layouts: 2.5 us -> none  [on_device(): grad_mixed, query_next = lax.optimization_barrier((grad_mixed, query_next))]
  transfers between devices with their start and end apart: 15 -> 15, of which waited for: 7 -> 7; matrix products, arithmetic and copies ran while one was open for 21% -> 19% of each run, Pallas kernels for 7% -> 7%
where the time goes in v11:
time: 219 us; the launch traced here: 214 us
  waiting for transfers between devices  105 us (48%)
  local copies, waits for them, and re-layouts  35.7 us (16%)
  starting transfers between devices  35.4 us (16%)
  other arithmetic  22.4 us (10%)
  Pallas kernels  15.3 us (7%)
    all_to_all x1, waiting for transfers between devices, on_device(): lax.all_to_all(z_lanes, 'seq', split_axis=1, concat_axis=0, tiled=True)  37.7 us
    ppermute x6, waiting for transfers between devices, spread_lanes(): lax.ppermute(outgoing, axis, pairs)  34.1 us
    all_to_all x1, waiting for transfers between devices, on_device(): lax.all_to_all(grad_mixed.T, 'seq', split_axis=0, concat_axis=1, tiled=True)  32 us
    pallas_call x1, Pallas kernels, correlate(): pl.pallas_call(correlate_kernel, out_shape=jax.ShapeDtypeStruct((channels...  15.3 us
    ppermute x6, starting transfers between devices, spread_lanes(): lax.ppermute(outgoing, axis, pairs)  8.02 us
    all_to_all x1, starting transfers between devices, on_device(): lax.all_to_all(z_lanes, 'seq', split_axis=1, concat_axis=0, tiled=True)  6.8 us
    dynamic_update_slice x8, local copies, waits for them, and re-layouts, on_device(): lax.dynamic_update_slice(out, piece.T[:, None, :], (0, plane, source * ch...  6.62 us
    dynamic_update_slice x4, local copies, waits for them, and re-layouts, on_device(): out = lax.dynamic_update_slice(out, piece, (0, 0, source * channels))  6.47 us
  transfers between devices with their start and end apart: 15, of which 7 were waited for; matrix products, arithmetic and copies ran while one was open for 19% of the time, Pallas kernels for 7%

profile of v11, /device:TPU:18, one launch (start us, length us, event | category | flops | bytes accessed | tf_op | source)
XLA Modules:
  0.0 214.3 jit_solution(4636379547605671136)
XLA Ops:
  0.0 1.7 copy.23
  1.7 5.2 %all-to-all-start.1 = ((bf16[512,8,16]{0,2,1:T(8,128)(2,1)}), bf16[512,8,16]{0,2,1:T(8,128)(2,1)S(1)}, u32[]{:S(2)}, u32[]{:S(2)}) async-start(bf16[512,8,16]{0,2,1:T(8,128)(2,1)} %bitcast.5), calls=%async_computation.1 | async-start | bytes 262144 | tf_op jit(solution)/shard_map/all_to_all | solution.py:79
  6.9 6.3 %fusion.21 = (f32[512,1,2048]{2,0,1:T(8,128)}, f32[512,2048]{1,0:T(8,128)S(1)}, bf16[512,2048]{1,0:T(8,128)(2,1)S(1)}) fusion(bf16[512,2048]{1,0:T(8,128)(2,1)} %param.7, bf16[512,2048]{1,0:T(8,128)(2,1)} %param.5, bf16[512,3,2048]{2,0,1:T(8,128)(2,1)} %param.6), kind=kLoop, calls=%fused_computation.59 | loop fusion | flops 6291456 | bytes 16777216 | tf_op jit(solution)/shard_map/broadcast_in_dim | solution.py:81
  13.2 2.2 %collective-permute-start = (f32[2,1,2048]{2,0,1:T(2,128)S(1)}, f32[2,1,2048]{2,0,1:T(2,128)S(1)}, u32[]{:S(2)}, u32[]{:S(2)}) collective-permute-start(f32[2,1,2048]{2,0,1:T(2,128)S(1)} %slice_bitcast_fusion), channel_id=1, source_target_pairs={{4,0},{8,4},{12,8},{16,12},{20,16},{24,20},{28,24},{5,1},{9,5},{13... | collective-permute-start | bytes 49160 | tf_op jit(solution)/shard_map/ppermute | solution.py:17
  15.4 1.4 collective-permute-done
  16.8 0.0 copy-start
  16.8 2.5 %copy.21 = bf16[2048,512]{1,0:T(8,128)(2,1)} copy(bf16[2048,512]{0,1:T(8,128)(2,1)S(1)} %bitcast.98) | data formatting | bytes 4194304 | tf_op jit(solution)/shard_map/transpose | solution.py:78
  19.3 0.0 all-to-all-done.1
  19.3 5.4 %all-to-all-start = ((bf16[8,256,512]{2,1,0:T(8,128)(2,1)}), bf16[8,256,512]{2,1,0:T(8,128)(2,1)S(1)}, u32[]{:S(2)}, u32[]{:S(2)}) async-start(bf16[8,256,512]{2,1,0:T(8,128)(2,1)} %bitcast.3), calls=%async_computation | async-start | bytes 4194304 | tf_op jit(solution)/shard_map/all_to_all | solution.py:78
  24.7 0.0 copy-done
  24.7 0.1 fusion.22
  24.8 5.6 %fusion.14 = bf16[512,1,2048]{2,0,1:T(8,128)(2,1)S(1)} fusion(f32[512,1,2048]{2,0,1:T(8,128)} %get-tuple-element.29, f32[2,1,2048]{2,0,1:T(2,128)S(1)} %collective-permute-done, f32[2048]{0:T(1024)S(1)} %bitcast.108, f32[2048]{0:T(1024)S(1)} %bitcast.109, f32[2048]{0:T(1024)S(1)} %bitcast.110, bf16[512,2048]{1,0:T(8,128)(2,1)} %param.7, ...), kind=kLoop, calls=%fused_computation.22 | loop fusion | flops 11534336 | bytes 10526720 | tf_op jit(solution)/shard_map/convert_element_type | solution.py:157
  30.4 1.2 dynamic-slice_bitcast_fusion
  31.6 1.5 collective-permute-start.1
  33.1 0.5 collective-permute-start.2
  33.6 1.5 collective-permute-start.3
  35.2 2.3 %rev.3 = f32[16,4096]{1,0:T(8,128)S(1)} reverse(f32[16,4096]{1,0:T(8,128)S(1)} %bitcast.101), dimensions={1} | reverse | bytes 524288 | tf_op jit(solution)/shard_map/rev | solution.py:44
  37.5 0.1 concatenate.12
  37.5 0.9 reshape.50.h_ref
  38.4 32.0 %all-to-all-done = bf16[8,256,512]{2,1,0:T(8,128)(2,1)S(1)} async-done(((bf16[8,256,512]{2,1,0:T(8,128)(2,1)}), bf16[8,256,512]{2,1,0:T(8,128)(2,1)S(1)}, u32[]{:S(2)}, u32[]{:S(2)}) %all-to-all-start) | async-done | bytes 2097184 | tf_op jit(solution)/shard_map/all_to_all | solution.py:78
  70.5 1.6 copy.33
  72.1 15.3 %shard_map.55 = bf16[256,4096]{1,0:T(8,128)(2,1)} custom-call(bf16[256,4096]{1,0:T(8,128)(2,1)} %bitcast.100, f32[16,1,4352]{2,1,0:T(1,128)} %reshape.50.h_ref), custom_call_target="tpu_custom_call" | custom-call | flops 4563402752 | bytes 4472832 | tf_op jit(solution)/shard_map/pallas_call | solution.py:48
  87.4 0.0 collective-permute-done.1
  87.4 0.0 collective-permute-done.2
  87.4 0.0 collective-permute-done.3
  87.4 3.1 %copy.36 = bf16[32,8,8,512]{3,2,0,1:T(8,128)(2,1)} copy(bf16[32,8,8,512]{3,2,1,0:T(8,128)(2,1)} %bitcast.99) | data formatting | bytes 4194304 | tf_op jit(solution)/shard_map/all_to_all | solution.py:85
  90.5 6.8 %all-to-all-start.2 = ((bf16[256,8,512]{2,0,1:T(8,128)(2,1)}), bf16[256,8,512]{2,0,1:T(8,128)(2,1)S(1)}, u32[]{:S(2)}, u32[]{:S(2)}) async-start(bf16[256,8,512]{2,0,1:T(8,128)(2,1)} %bitcast.96), calls=%async_computation.2 | async-start | bytes 4194304 | tf_op jit(solution)/shard_map/all_to_all | solution.py:85
  97.3 3.4 %broadcast_in_dim.34 = bf16[128,3,8192]{2,0,1:T(8,128)(2,1)} broadcast(bf16[]{:T(256)} %constant.83.clone.1), dimensions={} | broadcast | bytes 6291458 | tf_op jit(solution)/shard_map/broadcast_in_dim | solution.py:90
  100.7 0.8 constant_dynamic-update-slice_fusion.3
  101.6 1.9 constant_dynamic-update-slice_fusion.2
  103.4 1.9 constant_dynamic-update-slice_fusion.1
  105.3 37.7 %all-to-all-done.2 = bf16[256,8,512]{2,0,1:T(8,128)(2,1)S(1)} async-done(((bf16[256,8,512]{2,0,1:T(8,128)(2,1)}), bf16[256,8,512]{2,0,1:T(8,128)(2,1)S(1)}, u32[]{:S(2)}, u32[]{:S(2)}) %all-to-all-start.2) | async-done | bytes 2097184 | tf_op jit(solution)/shard_map/all_to_all | solution.py:85
  143.1 2.5 %convert_element_type.81 = f32[256,8,512]{2,0,1:T(8,128)} convert(bf16[256,8,512]{2,0,1:T(8,128)(2,1)S(1)} %all-to-all-done.2) | non-fusion elementwise | flops 1048576 | bytes 6291456 | tf_op jit(solution)/shard_map/convert_element_type | solution.py:86
  145.6 5.5 %copy.30 = f32[2048,512]{0,1:T(8,128)} copy(f32[2048,512]{1,0:T(8,128)} %bitcast.94) | data formatting | bytes 8388608 | tf_op jit(solution)/shard_map/convert_element_type | solution.py:86
  151.1 4.7 %fusion.19 = (f32[2048,512]{0,1:T(8,128)S(1)}, f32[2048,512]{0,1:T(8,128)S(1)}) fusion(f32[2048,512]{0,1:T(8,128)} %copy.30, bf16[512,3,2048]{2,0,1:T(8,128)(2,1)} %param.6), kind=kLoop, calls=%fused_computation.31 | loop fusion | flops 4194304 | bytes 16777216 | tf_op jit(solution)/shard_map/mul | solution.py:88
  155.8 1.9 collective-permute-start.4
  157.7 1.9 constant_dynamic-update-slice_fusion
  159.6 2.3 %collective-permute-start.8 = (f32[2048,2]{0,1:T(2,128)S(1)}, f32[2048,2]{0,1:T(2,128)S(1)}, u32[]{:S(2)}, u32[]{:S(2)}) collective-permute-start(f32[2048,2]{0,1:T(2,128)S(1)} %slice.108), channel_id=1, source_target_pairs={{4,0},{8,4},{12,8},{16,12},{20,16},{24,20},{28,24},{5,1},{9,5},{13... | collective-permute-start | bytes 49160 | tf_op jit(solution)/shard_map/ppermute | solution.py:17
  162.0 0.0 collective-permute-done.4
  162.0 1.6 fusion.9
  163.6 0.2 constant_dynamic-slice_fusion.2
  163.8 1.5 collective-permute-start.5
  165.3 0.5 collective-permute-start.6
  165.8 1.5 collective-permute-start.7
  167.4 0.0 collective-permute-done.8
  167.4 1.6 fusion.4
  169.0 0.1 constant_dynamic-slice_fusion.5
  169.1 1.4 collective-permute-start.9
  170.6 1.5 collective-permute-start.10
  172.1 0.8 bitcast_dynamic-update-slice_fusion.7
  172.9 5.7 %collective-permute-done.5 = bf16[2048,128]{0,1:T(8,128)(2,1)S(1)} collective-permute-done((bf16[2048,128]{0,1:T(8,128)(2,1)S(1)}, bf16[2048,128]{0,1:T(8,128)(2,1)S(1)}, u32[]{:S(2)}, u32[]{:S(2)}) %collective-permute-start.5) | collective-permute-done | bytes 524320 | tf_op jit(solution)/shard_map/ppermute | solution.py:123
  178.6 1.5 collective-permute-start.11
  180.1 0.8 bitcast_dynamic-update-slice_fusion.6
  180.9 10.4 %collective-permute-done.6 = bf16[2048,128]{0,1:T(8,128)(2,1)S(1)} collective-permute-done((bf16[2048,128]{0,1:T(8,128)(2,1)S(1)}, bf16[2048,128]{0,1:T(8,128)(2,1)S(1)}, u32[]{:S(2)}, u32[]{:S(2)}) %collective-permute-start.6) | collective-permute-done | bytes 524320 | tf_op jit(solution)/shard_map/ppermute | solution.py:123
  191.4 0.8 bitcast_dynamic-update-slice_fusion.5
  192.2 0.0 collective-permute-done.7
  192.2 0.8 bitcast_dynamic-update-slice_fusion.4
  193.0 0.8 bitcast_dynamic-update-slice_fusion.3
  193.9 7.3 %collective-permute-done.9 = bf16[2048,128]{0,1:T(8,128)(2,1)S(1)} collective-permute-done((bf16[2048,128]{0,1:T(8,128)(2,1)S(1)}, bf16[2048,128]{0,1:T(8,128)(2,1)S(1)}, u32[]{:S(2)}, u32[]{:S(2)}) %collective-permute-start.9) | collective-permute-done | bytes 524320 | tf_op jit(solution)/shard_map/ppermute | solution.py:123
  201.2 0.8 bitcast_dynamic-update-slice_fusion.2
  202.0 10.7 %collective-permute-done.10 = bf16[2048,128]{0,1:T(8,128)(2,1)S(1)} collective-permute-done((bf16[2048,128]{0,1:T(8,128)(2,1)S(1)}, bf16[2048,128]{0,1:T(8,128)(2,1)S(1)}, u32[]{:S(2)}, u32[]{:S(2)}) %collective-permute-start.10) | collective-permute-done | bytes 524320 | tf_op jit(solution)/shard_map/ppermute | solution.py:123
  212.7 0.8 bitcast_dynamic-update-slice_fusion.1
  213.5 0.0 collective-permute-done.11
  213.5 0.8 bitcast_dynamic-update-slice_fusion
  (5 shorter events, 0.1 us)
Async XLA Ops:
  1.7 17.7 %all-to-all-start.1 = ((bf16[512,8,16]{0,2,1:T(8,128)(2,1)}), bf16[512,8,16]{0,2,1:T(8,128)(2,1)S(1)}, u32[]{:S(2)}, u32[]{:S(2)}) async-start(bf16[512,8,16]{0,2,1:T(8,128)(2,1)} %bitcast.5), calls=%async_computation.1 | async-start | bytes 262144 | tf_op jit(solution)/shard_map/all_to_all | solution.py:79
  13.2 3.6 %collective-permute-start = (f32[2,1,2048]{2,0,1:T(2,128)S(1)}, f32[2,1,2048]{2,0,1:T(2,128)S(1)}, u32[]{:S(2)}, u32[]{:S(2)}) collective-permute-start(f32[2,1,2048]{2,0,1:T(2,128)S(1)} %slice_bitcast_fusion), channel_id=1, source_target_pairs={{4,0},{8,4},{12,8},{16,12},{20,16},{24,20},{28,24},{5,1},{9,5},{13... | collective-permute-start | bytes 49160 | tf_op jit(solution)/shard_map/ppermute | solution.py:17
  16.8 7.9 %copy-start = (f32[3,3,2048]{2,1,0:T(4,128)S(1)}, f32[3,3,2048]{2,1,0:T(4,128)}, u32[]{:S(2)}) copy-start(f32[3,3,2048]{2,1,0:T(4,128)} %param.9) | copy-start | bytes 221188
  19.3 51.1 %all-to-all-start = ((bf16[8,256,512]{2,1,0:T(8,128)(2,1)}), bf16[8,256,512]{2,1,0:T(8,128)(2,1)S(1)}, u32[]{:S(2)}, u32[]{:S(2)}) async-start(bf16[8,256,512]{2,1,0:T(8,128)(2,1)} %bitcast.3), calls=%async_computation | async-start | bytes 4194304 | tf_op jit(solution)/shard_map/all_to_all | solution.py:78
  31.6 55.8 %collective-permute-start.1 = (bf16[128,1,2048]{2,0,1:T(8,128)(2,1)}, bf16[128,1,2048]{2,0,1:T(8,128)(2,1)}, u32[]{:S(2)}, u32[]{:S(2)}) collective-permute-start(bf16[128,1,2048]{2,0,1:T(8,128)(2,1)} %get-tuple-element.39), channel_id=1, source_target_pairs={{0,1},{1,2},{2,3},{3,0},{4,5},{5,6},{6,7},{7,4},{8,9},{9,10},{10,1... | collective-permute-start | bytes 1572872 | tf_op jit(solution)/shard_map/ppermute | solution.py:136
  33.1 54.3 %collective-permute-start.2 = (bf16[128,1,2048]{2,0,1:T(8,128)(2,1)}, bf16[128,1,2048]{2,0,1:T(8,128)(2,1)}, u32[]{:S(2)}, u32[]{:S(2)}) collective-permute-start(bf16[128,1,2048]{2,0,1:T(8,128)(2,1)} %get-tuple-element.38), channel_id=1, source_target_pairs={{0,2},{1,3},{2,0},{3,1},{4,6},{5,7},{6,4},{7,5},{8,10},{9,11},{10,... | collective-permute-start | bytes 1572872 | tf_op jit(solution)/shard_map/ppermute | solution.py:136
  33.6 53.8 %collective-permute-start.3 = (bf16[128,1,2048]{2,0,1:T(8,128)(2,1)}, bf16[128,1,2048]{2,0,1:T(8,128)(2,1)}, u32[]{:S(2)}, u32[]{:S(2)}) collective-permute-start(bf16[128,1,2048]{2,0,1:T(8,128)(2,1)} %get-tuple-element.37), channel_id=1, source_target_pairs={{0,3},{1,0},{2,1},{3,2},{4,7},{5,4},{6,5},{7,6},{8,11},{9,8},{10,9... | collective-permute-start | bytes 1572872 | tf_op jit(solution)/shard_map/ppermute | solution.py:136
  90.5 52.6 %all-to-all-start.2 = ((bf16[256,8,512]{2,0,1:T(8,128)(2,1)}), bf16[256,8,512]{2,0,1:T(8,128)(2,1)S(1)}, u32[]{:S(2)}, u32[]{:S(2)}) async-start(bf16[256,8,512]{2,0,1:T(8,128)(2,1)} %bitcast.96), calls=%async_computation.2 | async-start | bytes 4194304 | tf_op jit(solution)/shard_map/all_to_all | solution.py:85
  155.8 6.2 %collective-permute-start.4 = (f32[2048,2]{0,1:T(2,128)S(1)}, f32[2048,2]{0,1:T(2,128)S(1)}, u32[]{:S(2)}, u32[]{:S(2)}) collective-permute-start(f32[2048,2]{0,1:T(2,128)S(1)} %slice.105), channel_id=1, source_target_pairs={{4,0},{8,4},{12,8},{16,12},{20,16},{24,20},{28,24},{5,1},{9,5},{13... | collective-permute-start | bytes 49160 | tf_op jit(solution)/shard_map/ppermute | solution.py:17
  159.6 7.8 %collective-permute-start.8 = (f32[2048,2]{0,1:T(2,128)S(1)}, f32[2048,2]{0,1:T(2,128)S(1)}, u32[]{:S(2)}, u32[]{:S(2)}) collective-permute-start(f32[2048,2]{0,1:T(2,128)S(1)} %slice.108), channel_id=1, source_target_pairs={{4,0},{8,4},{12,8},{16,12},{20,16},{24,20},{28,24},{5,1},{9,5},{13... | collective-permute-start | bytes 49160 | tf_op jit(solution)/shard_map/ppermute | solution.py:17
  163.8 14.8 %collective-permute-start.5 = (bf16[2048,128]{0,1:T(8,128)(2,1)S(1)}, bf16[2048,128]{0,1:T(8,128)(2,1)S(1)}, u32[]{:S(2)}, u32[]{:S(2)}) collective-permute-start(bf16[2048,128]{0,1:T(8,128)(2,1)S(1)} %get-tuple-element.36), channel_id=1, source_target_pairs={{0,1},{1,2},{2,3},{3,0},{4,5},{5,6},{6,7},{7,4},{8,9},{9,10},{10,1... | collective-permute-start | bytes 1572872 | tf_op jit(solution)/shard_map/ppermute | solution.py:123
  165.3 26.0 %collective-permute-start.6 = (bf16[2048,128]{0,1:T(8,128)(2,1)S(1)}, bf16[2048,128]{0,1:T(8,128)(2,1)S(1)}, u32[]{:S(2)}, u32[]{:S(2)}) collective-permute-start(bf16[2048,128]{0,1:T(8,128)(2,1)S(1)} %get-tuple-element.35), channel_id=1, source_target_pairs={{0,2},{1,3},{2,0},{3,1},{4,6},{5,7},{6,4},{7,5},{8,10},{9,11},{10,... | collective-permute-start | bytes 1572872 | tf_op jit(solution)/shard_map/ppermute | solution.py:123
  165.8 26.4 %collective-permute-start.7 = (bf16[2048,128]{0,1:T(8,128)(2,1)S(1)}, bf16[2048,128]{0,1:T(8,128)(2,1)S(1)}, u32[]{:S(2)}, u32[]{:S(2)}) collective-permute-start(bf16[2048,128]{0,1:T(8,128)(2,1)S(1)} %get-tuple-element.34), channel_id=1, source_target_pairs={{0,3},{1,0},{2,1},{3,2},{4,7},{5,4},{6,5},{7,6},{8,11},{9,8},{10,9... | collective-permute-start | bytes 1572872 | tf_op jit(solution)/shard_map/ppermute | solution.py:123
  169.1 32.0 %collective-permute-start.9 = (bf16[2048,128]{0,1:T(8,128)(2,1)S(1)}, bf16[2048,128]{0,1:T(8,128)(2,1)S(1)}, u32[]{:S(2)}, u32[]{:S(2)}) collective-permute-start(bf16[2048,128]{0,1:T(8,128)(2,1)S(1)} %get-tuple-element.33), channel_id=1, source_target_pairs={{0,1},{1,2},{2,3},{3,0},{4,5},{5,6},{6,7},{7,4},{8,9},{9,10},{10,1... | collective-permute-start | bytes 1572872 | tf_op jit(solution)/shard_map/ppermute | solution.py:123
  170.6 42.1 %collective-permute-start.10 = (bf16[2048,128]{0,1:T(8,128)(2,1)S(1)}, bf16[2048,128]{0,1:T(8,128)(2,1)S(1)}, u32[]{:S(2)}, u32[]{:S(2)}) collective-permute-start(bf16[2048,128]{0,1:T(8,128)(2,1)S(1)} %get-tuple-element.32), channel_id=1, source_target_pairs={{0,2},{1,3},{2,0},{3,1},{4,6},{5,7},{6,4},{7,5},{8,10},{9,11},{10,... | collective-permute-start | bytes 1572872 | tf_op jit(solution)/shard_map/ppermute | solution.py:123
  178.6 34.8 %collective-permute-start.11 = (bf16[2048,128]{0,1:T(8,128)(2,1)S(1)}, bf16[2048,128]{0,1:T(8,128)(2,1)S(1)}, u32[]{:S(2)}, u32[]{:S(2)}) collective-permute-start(bf16[2048,128]{0,1:T(8,128)(2,1)S(1)} %get-tuple-element.31), channel_id=1, source_target_pairs={{0,3},{1,0},{2,1},{3,2},{4,7},{5,4},{6,5},{7,6},{8,11},{9,8},{10,9... | collective-permute-start | bytes 1572872 | tf_op jit(solution)/shard_map/ppermute | solution.py:123

commit v12 on v11

--- a/solution.py
+++ b/solution.py
@@ -80,9 +80,21 @@
     short_len = short_taps.shape[1]
     query_proj = short_filter(grad_query[:, None], short_taps[:1], block_rows, query_next)
     query_rows = spread_rows(query_proj, "chan")
-    z_lanes = correlate(mixed_cols, taps_cols)
-    z_lanes, query_rows = lax.optimization_barrier((z_lanes, query_rows))
-    z_rows = lax.all_to_all(z_lanes, "seq", split_axis=1, concat_axis=0, tiled=True)
+    halves = 2
+    part = mixed_cols.shape[0] // halves
+    group_part = taps_cols.shape[1] // halves
+    returned = []
+    for half in range(halves):
+        z_lanes = correlate(
+            mixed_cols[half * part : (half + 1) * part],
+            taps_cols[:, half * group_part : (half + 1) * group_part],
+        )
+        if half == 0:
+            z_lanes, query_rows = lax.optimization_barrier((z_lanes, query_rows))
+        returned.append(lax.all_to_all(z_lanes, "seq", split_axis=1, concat_axis=0, tiled=True))
+    shards = lax.axis_size("seq")
+    z_rows = jnp.stack([piece.reshape(shards, part, -1) for piece in returned], 1)
+    z_rows = z_rows.reshape(shards * halves * part, -1)
     z_wide = z_rows.astype(jnp.float32)
     grad_key = z_wide * value_part.T.astype(jnp.float32)
     grad_value = z_wide * key_part.T.astype(jnp.float32)

time: 219 us -> 234 us (1.068)
  waiting for transfers between devices: 105 us -> 74.9 us
  local copies, waits for them, and re-layouts: 35.7 us -> 60.5 us
  other arithmetic: 22.4 us -> 35.8 us
  starting transfers between devices: 35.4 us -> 41.4 us
    all_to_all x1 -> x2, waiting for transfers between devices: 37.7 us -> 16 us  [on_device(): lax.all_to_all(z_lanes, 'seq', split_axis=1, concat_axis=0, tiled=True)]
    convert_element_type x2, other arithmetic: 3.23 us -> 18.7 us  [lane_filter(): return result.astype(jnp.bfloat16)]
    unnamed x3 -> x20, local copies, waits for them, and re-layouts: 1.68 us -> 12 us
    ppermute x6, waiting for transfers between devices: 34.1 us -> 25.7 us  [spread_lanes(): lax.ppermute(outgoing, axis, pairs)]
    all_to_all x1 -> x2, starting transfers between devices: 6.8 us -> 14.2 us  [on_device(): lax.all_to_all(z_lanes, 'seq', split_axis=1, concat_axis=0, tiled=True)]
    slice x0 -> x3, local copies, waits for them, and re-layouts: none -> 6.99 us  [the longest x1 4.84 us: on_device(): key_part = qkv_saved[:, 1, :]]
    broadcast_in_dim x0 -> x8, local copies, waits for them, and re-layouts: none -> 5.6 us  [on_device(): piece.T[:, None, :]]
    convert_element_type x1 -> x0, local copies, waits for them, and re-layouts: 5.48 us -> none  [on_device(): z_wide = z_rows.astype(jnp.float32)]
  transfers between devices with their start and end apart: 15 -> 16, of which waited for: 7 -> 8; matrix products, arithmetic and copies ran while one was open for 19% -> 33% of each run, Pallas kernels for 7% -> 7%
where the time goes in v12:
time: 234 us; the launch traced here: 229 us
  waiting for transfers between devices  74.9 us (32%)
  local copies, waits for them, and re-layouts  60.5 us (26%)
  starting transfers between devices  41.4 us (18%)
  other arithmetic  35.8 us (15%)
  Pallas kernels  16.7 us (7%)
    all_to_all x1, waiting for transfers between devices, on_device(): lax.all_to_all(grad_mixed.T, 'seq', split_axis=0, concat_axis=1, tiled=True)  31.8 us
    ppermute x6, waiting for transfers between devices, spread_lanes(): lax.ppermute(outgoing, axis, pairs)  25.7 us
    convert_element_type x2, other arithmetic, lane_filter(): return result.astype(jnp.bfloat16)  18.7 us
    pallas_call x2, Pallas kernels, correlate(): pl.pallas_call(correlate_kernel, out_shape=jax.ShapeDtypeStruct((channels...  16.7 us
    all_to_all x2, waiting for transfers between devices, on_device(): lax.all_to_all(z_lanes, 'seq', split_axis=1, concat_axis=0, tiled=True)  16 us
    all_to_all x2, starting transfers between devices, on_device(): lax.all_to_all(z_lanes, 'seq', split_axis=1, concat_axis=0, tiled=True)  14.2 us
    unnamed x20, local copies, waits for them, and re-layouts  12 us
    ppermute x3, starting transfers between devices, shifted(): lax.ppermute(value, axis, [(source, source + steps) for source in range(l...  6.66 us
  transfers between devices with their start and end apart: 16, of which 8 were waited for; matrix products, arithmetic and copies ran while one was open for 33% of the time, Pallas kernels for 7%

profile of v12, /device:TPU:18, one launch (start us, length us, event | category | flops | bytes accessed | tf_op | source)
XLA Modules:
  0.0 229.4 jit_solution(10498400435786827070)
XLA Ops:
  0.0 1.7 copy.59
  1.7 5.2 %all-to-all-start.1 = ((bf16[512,8,16]{0,2,1:T(8,128)(2,1)}), bf16[512,8,16]{0,2,1:T(8,128)(2,1)S(1)}, u32[]{:S(2)}, u32[]{:S(2)}) async-start(bf16[512,8,16]{0,2,1:T(8,128)(2,1)} %bitcast.5), calls=%async_computation.1 | async-start | bytes 262144 | tf_op jit(solution)/shard_map/all_to_all | solution.py:79
  6.9 6.3 %fusion.19 = (f32[512,1,2048]{2,0,1:T(8,128)}, f32[512,2048]{1,0:T(8,128)S(1)}, bf16[512,2048]{1,0:T(8,128)(2,1)S(1)}) fusion(bf16[512,2048]{1,0:T(8,128)(2,1)} %param.7, bf16[512,2048]{1,0:T(8,128)(2,1)} %param.5, bf16[512,3,2048]{2,0,1:T(8,128)(2,1)} %param.6), kind=kLoop, calls=%fused_computation.67 | loop fusion | flops 6291456 | bytes 16777216 | tf_op jit(solution)/shard_map/broadcast_in_dim | solution.py:81
  13.2 2.2 collective-permute-start
  15.4 1.4 collective-permute-done
  16.8 2.5 %copy.57 = bf16[2048,512]{1,0:T(8,128)(2,1)} copy(bf16[2048,512]{0,1:T(8,128)(2,1)S(1)} %bitcast.109) | data formatting | bytes 4194304 | tf_op jit(solution)/shard_map/transpose | solution.py:78
  19.3 5.4 %all-to-all-start = ((bf16[8,256,512]{2,1,0:T(8,128)(2,1)}), bf16[8,256,512]{2,1,0:T(8,128)(2,1)S(1)}, u32[]{:S(2)}, u32[]{:S(2)}) async-start(bf16[8,256,512]{2,1,0:T(8,128)(2,1)} %bitcast.107), calls=%async_computation | async-start | bytes 4194304 | tf_op jit(solution)/shard_map/all_to_all | solution.py:78
  24.7 5.8 %fusion.4 = bf16[512,1,2048]{2,0,1:T(8,128)(2,1)S(1)} fusion(f32[512,1,2048]{2,0,1:T(8,128)} %get-tuple-element.29, f32[2,1,2048]{2,0,1:T(2,128)S(1)} %collective-permute-done, f32[2048]{0:T(1024)S(1)} %bitcast.126, f32[2048]{0:T(1024)S(1)} %bitcast.127, f32[2048]{0:T(1024)S(1)} %bitcast.128, bf16[512,2048]{1,0:T(8,128)(2,1)} %param.7, ...), kind=kLoop, calls=%fused_computation.14 | loop fusion | flops 11534336 | bytes 10526720 | tf_op jit(solution)/shard_map/convert_element_type | solution.py:169
  30.6 1.4 dynamic-slice_bitcast_fusion.2
  32.0 1.5 collective-permute-start.1
  34.0 1.5 collective-permute-start.3
  35.6 2.2 rev.6
  37.8 0.8 copy.61.h_ref
  38.6 31.8 %all-to-all-done = bf16[8,256,512]{2,1,0:T(8,128)(2,1)S(1)} async-done(((bf16[8,256,512]{2,1,0:T(8,128)(2,1)}), bf16[8,256,512]{2,1,0:T(8,128)(2,1)S(1)}, u32[]{:S(2)}, u32[]{:S(2)}) %all-to-all-start) | async-done | bytes 2097184 | tf_op jit(solution)/shard_map/all_to_all | solution.py:78
  70.5 1.2 slice_bitcast_fusion
  71.6 1.1 copy.87
  72.7 8.3 %shard_map.55 = bf16[128,4096]{1,0:T(8,128)(2,1)} custom-call(bf16[128,4096]{1,0:T(8,128)(2,1)} %bitcast.112, f32[8,1,4352]{2,1,0:T(1,128)} %copy.61.h_ref), custom_call_target="tpu_custom_call" | custom-call | flops 2281701376 | bytes 2236416 | tf_op jit(solution)/shard_map/pallas_call | solution.py:48
  81.1 2.5 %copy.93 = bf16[16,8,8,512]{3,2,0,1:T(8,128)(2,1)} copy(bf16[16,8,8,512]{3,2,1,0:T(8,128)(2,1)} %bitcast.111) | data formatting | bytes 2097152 | tf_op jit(solution)/shard_map/all_to_all | solution.py:94
  83.6 6.8 %all-to-all-start.2 = ((bf16[128,8,512]{2,0,1:T(8,128)(2,1)}), bf16[128,8,512]{2,0,1:T(8,128)(2,1)S(1)}, u32[]{:S(2)}, u32[]{:S(2)}) async-start(bf16[128,8,512]{2,0,1:T(8,128)(2,1)} %bitcast.105), calls=%async_computation.2 | async-start | bytes 2097152 | tf_op jit(solution)/shard_map/all_to_all | solution.py:94
  90.3 2.2 rev.7
  92.6 0.8 reshape.61.h_ref
  93.3 1.1 copy.89
  94.4 8.3 %shard_map.56 = bf16[128,4096]{1,0:T(8,128)(2,1)} custom-call(bf16[128,4096]{1,0:T(8,128)(2,1)} %bitcast.113, f32[8,1,4352]{2,1,0:T(1,128)} %reshape.61.h_ref), custom_call_target="tpu_custom_call" | custom-call | flops 2281701376 | bytes 2236416 | tf_op jit(solution)/shard_map/pallas_call | solution.py:48
  102.7 2.3 %copy.92 = bf16[16,8,8,512]{3,2,0,1:T(8,128)(2,1)} copy(bf16[16,8,8,512]{3,2,1,0:T(8,128)(2,1)} %bitcast.114) | data formatting | bytes 2097152 | tf_op jit(solution)/shard_map/all_to_all | solution.py:94
  105.0 8.6 %all-to-all-done.2 = bf16[128,8,512]{2,0,1:T(8,128)(2,1)S(1)} async-done(((bf16[128,8,512]{2,0,1:T(8,128)(2,1)}), bf16[128,8,512]{2,0,1:T(8,128)(2,1)S(1)}, u32[]{:S(2)}, u32[]{:S(2)}) %all-to-all-start.2) | async-done | bytes 1048608 | tf_op jit(solution)/shard_map/all_to_all | solution.py:94
  113.6 7.4 %all-to-all-start.3 = ((bf16[128,8,512]{2,0,1:T(8,128)(2,1)}), bf16[128,8,512]{2,0,1:T(8,128)(2,1)}, u32[]{:S(2)}, u32[]{:S(2)}) async-start(bf16[128,8,512]{2,0,1:T(8,128)(2,1)} %bitcast.104), calls=%async_computation.3 | async-start | bytes 2097152 | tf_op jit(solution)/shard_map/all_to_all | solution.py:94
  121.0 4.8 %fusion.20 = (bf16[512,1,2048]{2,0,1:T(8,128)(2,1)}, bf16[512,1,2048]{2,0,1:T(8,128)(2,1)}) fusion(bf16[512,3,2048]{2,0,1:T(8,128)(2,1)} %param.6), kind=kLoop, calls=%fused_computation.68 | loop fusion | bytes 8388608 | tf_op jit(solution)/shard_map/slice | solution.py:71
  125.9 2.9 %copy.83 = bf16[512,1,2048]{0,2,1:T(8,128)(2,1)S(1)} copy(bf16[512,1,2048]{2,0,1:T(8,128)(2,1)} %get-tuple-element.28) | data formatting | bytes 4194304
  128.7 3.9 %copy.84 = bf16[512,1,2048]{0,2,1:T(8,128)(2,1)} copy(bf16[512,1,2048]{2,0,1:T(8,128)(2,1)} %get-tuple-element.27) | data formatting | bytes 4194304
  132.7 3.4 %broadcast_in_dim.33 = bf16[128,3,8192]{2,0,1:T(8,128)(2,1)} broadcast(bf16[]{:T(256)} %constant.83.clone.1), dimensions={} | broadcast | bytes 6291458 | tf_op jit(solution)/shard_map/broadcast_in_dim | solution.py:102
  136.1 0.8 constant_dynamic-update-slice_fusion.11
  136.9 7.4 %all-to-all-done.3 = bf16[128,8,512]{2,0,1:T(8,128)(2,1)} async-done(((bf16[128,8,512]{2,0,1:T(8,128)(2,1)}), bf16[128,8,512]{2,0,1:T(8,128)(2,1)}, u32[]{:S(2)}, u32[]{:S(2)}) %all-to-all-start.3) | async-done | bytes 1048608 | tf_op jit(solution)/shard_map/all_to_all | solution.py:94
  144.3 1.6 pad_maximum_fusion.3
  146.2 3.3 %convert_multiply_fusion = (f32[2048,512]{1,0:T(8,128)}, f32[2048,512]{1,0:T(8,128)S(1)}) fusion(bf16[512,1,2048]{0,2,1:T(8,128)(2,1)S(1)} %copy-done.1, bf16[8,2,128,512]{3,2,1,0:T(8,128)(2,1)S(1)} %pad_maximum_fusion.3, bf16[512,1,2048]{0,2,1:T(8,128)(2,1)S(1)} %copy.83), kind=kLoop, calls=%fused_computation | loop fusion | flops 5242880 | bytes 14680064 | tf_op jit(solution)/shard_map/mul | solution.py:100
  149.6 2.0 copy-done
  152.0 1.9 collective-permute-start.4
  154.0 1.9 constant_dynamic-update-slice_fusion.10
  155.9 1.3 slice.136
  157.5 2.5 %collective-permute-start.8 = (f32[2048,2]{0,1:T(2,128)S(1)}, f32[2048,2]{0,1:T(2,128)S(1)}, u32[]{:S(2)}, u32[]{:S(2)}) collective-permute-start(f32[2048,2]{0,1:T(2,128)S(1)} %copy.77), channel_id=1, source_target_pairs={{4,0},{8,4},{12,8},{16,12},{20,16},{24,20},{28,24},{5,1},{9,5},{13... | collective-permute-start | bytes 49160 | tf_op jit(solution)/shard_map/ppermute | solution.py:17
  160.4 9.4 %fusion.14 = bf16[2048,512]{1,0:T(8,128)(2,1)S(1)} fusion(f32[2048,512]{1,0:T(8,128)} %copy-done, f32[2048,2]{1,0:T(8,128)S(1)} %copy.71, f32[2048]{0:T(1024)S(1)} %bitcast.123, f32[2048]{0:T(1024)S(1)} %bitcast.124, f32[2048]{0:T(1024)S(1)} %bitcast.125), kind=kLoop, calls=%fused_computation.24 | loop fusion | flops 8388608 | bytes 6332416 | tf_op jit(solution)/shard_map/convert_element_type | solution.py:120
  169.8 1.4 constant_dynamic-slice_fusion.3
  171.2 1.5 collective-permute-start.5
  173.2 1.5 collective-permute-start.7
  175.1 9.3 %fusion.9 = bf16[2048,512]{1,0:T(8,128)(2,1)S(1)} fusion(f32[2048,512]{1,0:T(8,128)} %get-tuple-element.35, f32[2048,2]{1,0:T(8,128)S(1)} %copy.78, f32[2048]{0:T(1024)S(1)} %bitcast.121, f32[2048]{0:T(1024)S(1)} %bitcast.122, f32[2048]{0:T(1024)S(1)} %bitcast.120), kind=kLoop, calls=%fused_computation.19 | loop fusion | flops 8388608 | bytes 6332416 | tf_op jit(solution)/shard_map/convert_element_type | solution.py:120
  184.5 1.4 constant_dynamic-slice_fusion
  185.9 1.4 collective-permute-start.9
  187.3 1.5 collective-permute-start.10
  188.8 1.9 constant_dynamic-update-slice_fusion.9
  190.7 0.8 constant_dynamic-update-slice_fusion.8
  191.9 0.8 constant_dynamic-update-slice_fusion.7
  193.0 4.4 %collective-permute-done.6 = bf16[2048,128]{1,0:T(8,128)(2,1)S(1)} collective-permute-done((bf16[2048,128]{1,0:T(8,128)(2,1)}, bf16[2048,128]{1,0:T(8,128)(2,1)S(1)}, u32[]{:S(2)}, u32[]{:S(2)}) %collective-permute-start.6) | collective-permute-done | bytes 524320 | tf_op jit(solution)/shard_map/ppermute | solution.py:135
  197.6 0.9 collective-permute-done.7
  198.7 10.2 %collective-permute-done.9 = bf16[2048,128]{1,0:T(8,128)(2,1)} collective-permute-done((bf16[2048,128]{1,0:T(8,128)(2,1)}, bf16[2048,128]{1,0:T(8,128)(2,1)}, u32[]{:S(2)}, u32[]{:S(2)}) %collective-permute-start.9) | collective-permute-done | bytes 524320 | tf_op jit(solution)/shard_map/ppermute | solution.py:135
  208.8 1.2 copy.80
  210.1 10.2 %collective-permute-done.10 = bf16[2048,128]{1,0:T(8,128)(2,1)} collective-permute-done((bf16[2048,128]{1,0:T(8,128)(2,1)}, bf16[2048,128]{1,0:T(8,128)(2,1)}, u32[]{:S(2)}, u32[]{:S(2)}) %collective-permute-start.10) | collective-permute-done | bytes 524320 | tf_op jit(solution)/shard_map/ppermute | solution.py:135
  220.3 1.2 copy.81
  221.6 2.0 copy.82
  223.6 0.8 constant_dynamic-update-slice_fusion.6
  224.5 0.8 constant_dynamic-update-slice_fusion.5
  225.3 0.8 constant_dynamic-update-slice_fusion.4
  226.1 0.8 constant_dynamic-update-slice_fusion.3
  227.0 0.8 constant_dynamic-update-slice_fusion.2
  227.8 0.8 constant_dynamic-update-slice_fusion.1
  228.6 0.8 constant_dynamic-update-slice_fusion
  (42 shorter events, 4.1 us)
Async XLA Ops:
  1.7 17.7 %all-to-all-start.1 = ((bf16[512,8,16]{0,2,1:T(8,128)(2,1)}), bf16[512,8,16]{0,2,1:T(8,128)(2,1)S(1)}, u32[]{:S(2)}, u32[]{:S(2)}) async-start(bf16[512,8,16]{0,2,1:T(8,128)(2,1)} %bitcast.5), calls=%async_computation.1 | async-start | bytes 262144 | tf_op jit(solution)/shard_map/all_to_all | solution.py:79
  13.2 3.6 %collective-permute-start = (f32[2,1,2048]{2,0,1:T(2,128)S(1)}, f32[2,1,2048]{2,0,1:T(2,128)S(1)}, u32[]{:S(2)}, u32[]{:S(2)}) collective-permute-start(f32[2,1,2048]{2,0,1:T(2,128)S(1)} %slice_bitcast_fusion.2), channel_id=1, source_target_pairs={{4,0},{8,4},{12,8},{16,12},{20,16},{24,20},{28,24},{5,1},{9,5},{13... | collective-permute-start | bytes 49160 | tf_op jit(solution)/shard_map/ppermute | solution.py:17
  16.8 7.9 %copy-start.7 = (f32[3,3,2048]{2,1,0:T(4,128)S(1)}, f32[3,3,2048]{2,1,0:T(4,128)}, u32[]{:S(2)}) copy-start(f32[3,3,2048]{2,1,0:T(4,128)} %param.9) | copy-start | bytes 221188
  19.3 51.1 %all-to-all-start = ((bf16[8,256,512]{2,1,0:T(8,128)(2,1)}), bf16[8,256,512]{2,1,0:T(8,128)(2,1)S(1)}, u32[]{:S(2)}, u32[]{:S(2)}) async-start(bf16[8,256,512]{2,1,0:T(8,128)(2,1)} %bitcast.107), calls=%async_computation | async-start | bytes 4194304 | tf_op jit(solution)/shard_map/all_to_all | solution.py:78
  32.0 49.1 %collective-permute-start.1 = (bf16[128,1,2048]{2,0,1:T(8,128)(2,1)}, bf16[128,1,2048]{2,0,1:T(8,128)(2,1)}, u32[]{:S(2)}, u32[]{:S(2)}) collective-permute-start(bf16[128,1,2048]{2,0,1:T(8,128)(2,1)} %get-tuple-element.45), channel_id=1, source_target_pairs={{0,1},{1,2},{2,3},{3,0},{4,5},{5,6},{6,7},{7,4},{8,9},{9,10},{10,1... | collective-permute-start | bytes 1572872 | tf_op jit(solution)/shard_map/ppermute | solution.py:148
  33.5 47.6 %collective-permute-start.2 = (bf16[128,1,2048]{2,0,1:T(8,128)(2,1)}, bf16[128,1,2048]{2,0,1:T(8,128)(2,1)}, u32[]{:S(2)}, u32[]{:S(2)}) collective-permute-start(bf16[128,1,2048]{2,0,1:T(8,128)(2,1)} %get-tuple-element.44), channel_id=1, source_target_pairs={{0,2},{1,3},{2,0},{3,1},{4,6},{5,7},{6,4},{7,5},{8,10},{9,11},{10,... | collective-permute-start | bytes 1572872 | tf_op jit(solution)/shard_map/ppermute | solution.py:148
  34.0 47.1 %collective-permute-start.3 = (bf16[128,1,2048]{2,0,1:T(8,128)(2,1)}, bf16[128,1,2048]{2,0,1:T(8,128)(2,1)S(1)}, u32[]{:S(2)}, u32[]{:S(2)}) collective-permute-start(bf16[128,1,2048]{2,0,1:T(8,128)(2,1)} %get-tuple-element.43), channel_id=1, source_target_pairs={{0,3},{1,0},{2,1},{3,2},{4,7},{5,4},{6,5},{7,6},{8,11},{9,8},{10,9... | collective-permute-start | bytes 1572872 | tf_op jit(solution)/shard_map/ppermute | solution.py:148
  81.0 12.3 %copy-start.2 = (bf16[8,16,8,512]{3,2,1,0:T(8,128)(2,1)S(1)}, bf16[8,16,8,512]{3,2,1,0:T(8,128)(2,1)}, u32[]{:S(2)}) copy-start(bf16[8,16,8,512]{3,2,1,0:T(8,128)(2,1)} %get-tuple-element.41) | copy-start | bytes 3145732
  81.0 2.5 %copy-start.5 = (bf16[128,1,2048]{2,0,1:T(8,128)(2,1)}, bf16[128,1,2048]{2,0,1:T(8,128)(2,1)S(1)}, u32[]{:S(2)}) copy-start(bf16[128,1,2048]{2,0,1:T(8,128)(2,1)S(1)} %collective-permute-done.3) | copy-start | bytes 1572868
  83.6 30.1 %all-to-all-start.2 = ((bf16[128,8,512]{2,0,1:T(8,128)(2,1)}), bf16[128,8,512]{2,0,1:T(8,128)(2,1)S(1)}, u32[]{:S(2)}, u32[]{:S(2)}) async-start(bf16[128,8,512]{2,0,1:T(8,128)(2,1)} %bitcast.105), calls=%async_computation.2 | async-start | bytes 2097152 | tf_op jit(solution)/shard_map/all_to_all | solution.py:94
  113.6 30.7 %all-to-all-start.3 = ((bf16[128,8,512]{2,0,1:T(8,128)(2,1)}), bf16[128,8,512]{2,0,1:T(8,128)(2,1)}, u32[]{:S(2)}, u32[]{:S(2)}) async-start(bf16[128,8,512]{2,0,1:T(8,128)(2,1)} %bitcast.104), calls=%async_computation.3 | async-start | bytes 2097152 | tf_op jit(solution)/shard_map/all_to_all | solution.py:94
  132.7 3.5 %copy-start.4 = (bf16[128,1,2048]{2,0,1:T(8,128)(2,1)S(1)}, bf16[128,1,2048]{2,0,1:T(8,128)(2,1)}, u32[]{:S(2)}) copy-start(bf16[128,1,2048]{2,0,1:T(8,128)(2,1)} %get-tuple-element.18) | copy-start | bytes 1572868
  144.3 1.9 copy-start.1
  149.6 2.0 copy-start
  152.0 8.0 %collective-permute-start.4 = (f32[2048,2]{0,1:T(2,128)S(1)}, f32[2048,2]{0,1:T(2,128)S(1)}, u32[]{:S(2)}, u32[]{:S(2)}) collective-permute-start(f32[2048,2]{0,1:T(2,128)S(1)} %copy.70), channel_id=1, source_target_pairs={{4,0},{8,4},{12,8},{16,12},{20,16},{24,20},{28,24},{5,1},{9,5},{13... | collective-permute-start | bytes 49160 | tf_op jit(solution)/shard_map/ppermute | solution.py:17
  157.5 17.3 %collective-permute-start.8 = (f32[2048,2]{0,1:T(2,128)S(1)}, f32[2048,2]{0,1:T(2,128)S(1)}, u32[]{:S(2)}, u32[]{:S(2)}) collective-permute-start(f32[2048,2]{0,1:T(2,128)S(1)} %copy.77), channel_id=1, source_target_pairs={{4,0},{8,4},{12,8},{16,12},{20,16},{24,20},{28,24},{5,1},{9,5},{13... | collective-permute-start | bytes 49160 | tf_op jit(solution)/shard_map/ppermute | solution.py:17
  171.2 17.6 %collective-permute-start.5 = (bf16[2048,128]{1,0:T(8,128)(2,1)}, bf16[2048,128]{1,0:T(8,128)(2,1)S(1)}, u32[]{:S(2)}, u32[]{:S(2)}) collective-permute-start(bf16[2048,128]{1,0:T(8,128)(2,1)} %get-tuple-element.39), channel_id=1, source_target_pairs={{0,1},{1,2},{2,3},{3,0},{4,5},{5,6},{6,7},{7,4},{8,9},{9,10},{10,1... | collective-permute-start | bytes 1572872 | tf_op jit(solution)/shard_map/ppermute | solution.py:135
  172.7 24.7 %collective-permute-start.6 = (bf16[2048,128]{1,0:T(8,128)(2,1)}, bf16[2048,128]{1,0:T(8,128)(2,1)S(1)}, u32[]{:S(2)}, u32[]{:S(2)}) collective-permute-start(bf16[2048,128]{1,0:T(8,128)(2,1)} %get-tuple-element.38), channel_id=1, source_target_pairs={{0,2},{1,3},{2,0},{3,1},{4,6},{5,7},{6,4},{7,5},{8,10},{9,11},{10,... | collective-permute-start | bytes 1572872 | tf_op jit(solution)/shard_map/ppermute | solution.py:135
  173.2 25.2 %collective-permute-start.7 = (bf16[2048,128]{1,0:T(8,128)(2,1)}, bf16[2048,128]{1,0:T(8,128)(2,1)S(1)}, u32[]{:S(2)}, u32[]{:S(2)}) collective-permute-start(bf16[2048,128]{1,0:T(8,128)(2,1)} %get-tuple-element.37), channel_id=1, source_target_pairs={{0,3},{1,0},{2,1},{3,2},{4,7},{5,4},{6,5},{7,6},{8,11},{9,8},{10,9... | collective-permute-start | bytes 1572872 | tf_op jit(solution)/shard_map/ppermute | solution.py:135
  184.5 6.2 %copy-start.6 = (bf16[128,1,2048]{2,0,1:T(8,128)(2,1)S(1)}, bf16[128,1,2048]{2,0,1:T(8,128)(2,1)}, u32[]{:S(2)}) copy-start(bf16[128,1,2048]{2,0,1:T(8,128)(2,1)} %copy-done.5) | copy-start | bytes 1572868
  185.9 23.0 %collective-permute-start.9 = (bf16[2048,128]{1,0:T(8,128)(2,1)}, bf16[2048,128]{1,0:T(8,128)(2,1)}, u32[]{:S(2)}, u32[]{:S(2)}) collective-permute-start(bf16[2048,128]{1,0:T(8,128)(2,1)} %get-tuple-element.33), channel_id=1, source_target_pairs={{0,1},{1,2},{2,3},{3,0},{4,5},{5,6},{6,7},{7,4},{8,9},{9,10},{10,1... | collective-permute-start | bytes 1572872 | tf_op jit(solution)/shard_map/ppermute | solution.py:135
  187.3 33.1 %collective-permute-start.10 = (bf16[2048,128]{1,0:T(8,128)(2,1)}, bf16[2048,128]{1,0:T(8,128)(2,1)}, u32[]{:S(2)}, u32[]{:S(2)}) collective-permute-start(bf16[2048,128]{1,0:T(8,128)(2,1)} %get-tuple-element.32), channel_id=1, source_target_pairs={{0,2},{1,3},{2,0},{3,1},{4,6},{5,7},{6,4},{7,5},{8,10},{9,11},{10,... | collective-permute-start | bytes 1572872 | tf_op jit(solution)/shard_map/ppermute | solution.py:135
  188.8 32.8 %collective-permute-start.11 = (bf16[2048,128]{1,0:T(8,128)(2,1)}, bf16[2048,128]{1,0:T(8,128)(2,1)}, u32[]{:S(2)}, u32[]{:S(2)}) collective-permute-start(bf16[2048,128]{1,0:T(8,128)(2,1)} %get-tuple-element.31), channel_id=1, source_target_pairs={{0,3},{1,0},{2,1},{3,2},{4,7},{5,4},{6,5},{7,6},{8,11},{9,8},{10,9... | collective-permute-start | bytes 1572872 | tf_op jit(solution)/shard_map/ppermute | solution.py:135
  223.6 5.0 %copy-start.3 = (bf16[128,1,2048]{2,0,1:T(8,128)(2,1)S(1)}, bf16[128,1,2048]{2,0,1:T(8,128)(2,1)}, u32[]{:S(2)}) copy-start(bf16[128,1,2048]{2,0,1:T(8,128)(2,1)} %copy.82) | copy-start | bytes 1572868

commit v13 on v11

--- a/solution.py
+++ b/solution.py
@@ -39,9 +39,9 @@
 
 def correlate(grads, taps):
     channels, tokens = grads.shape
-    groups = taps.shape[1]
+    groups = taps.shape[0]
     blocks = tokens // block
-    reversed_taps = taps.astype(jnp.float32).T[:, ::-1]
+    reversed_taps = taps.astype(jnp.float32)[:, ::-1]
     padded = jnp.concatenate([reversed_taps, jnp.zeros((groups, block), jnp.float32)], 1)
     padded = padded.reshape(groups, 1, tokens + block)
     flops = 2 * groups * per_group * block * block * blocks * (blocks + 1) // 2
@@ -75,8 +75,14 @@
     short_len = short_taps.shape[1]
     query_next = shifted(grad_query[: short_len - 1, None], "seq", -1)
     grad_mixed, query_next = lax.optimization_barrier((grad_mixed, query_next))
-    mixed_cols = lax.all_to_all(grad_mixed.T, "seq", split_axis=0, concat_axis=1, tiled=True)
-    taps_cols = lax.all_to_all(long_taps, "seq", split_axis=1, concat_axis=0, tiled=True)
+    shards = lax.axis_size("seq")
+    mixed_parts = grad_mixed.T.reshape(shards, -1, block_rows)
+    taps_parts = long_taps.T.reshape(shards, -1, block_rows)
+    width = mixed_parts.shape[1]
+    joined = jnp.concatenate([mixed_parts, taps_parts], 1)
+    joined = lax.all_to_all(joined, "seq", split_axis=0, concat_axis=0, tiled=True)
+    mixed_cols = joined[:, :width].transpose(1, 0, 2).reshape(width, shards * block_rows)
+    taps_cols = joined[:, width:].transpose(1, 0, 2).reshape(-1, shards * block_rows)
     short_len = short_taps.shape[1]
     query_proj = short_filter(grad_query[:, None], short_taps[:1], block_rows, query_next)
     query_rows = spread_rows(query_proj, "chan")

time: 219 us -> 219 us (level)
  waiting for transfers between devices: 105 us -> 112 us
  starting transfers between devices: 35.4 us -> 30 us
  other arithmetic: 22.4 us -> 24.9 us
    all_to_all x2 -> x1, waiting for transfers between devices: 32 us -> 38.1 us  [on_device(): lax.all_to_all(joined, 'seq', split_axis=0, concat_axis=0, tiled=True)]
    all_to_all x2 -> x1, starting transfers between devices: 10.6 us -> 5.47 us  [on_device(): lax.all_to_all(joined, 'seq', split_axis=0, concat_axis=0, tiled=True)]
  transfers between devices with their start and end apart: 15 -> 14, of which waited for: 7 -> 7; matrix products, arithmetic and copies ran while one was open for 19% -> 14% of each run, Pallas kernels for 7% -> 7%
where the time goes in v13:
time: 219 us; the launch traced here: 216 us
  waiting for transfers between devices  112 us (51%)
  local copies, waits for them, and re-layouts  33.6 us (15%)
  starting transfers between devices  30 us (14%)
  other arithmetic  24.9 us (11%)
  Pallas kernels  15.3 us (7%)
    all_to_all x1, waiting for transfers between devices, on_device(): lax.all_to_all(joined, 'seq', split_axis=0, concat_axis=0, tiled=True)  38.1 us
    all_to_all x1, waiting for transfers between devices, on_device(): lax.all_to_all(z_lanes, 'seq', split_axis=1, concat_axis=0, tiled=True)  37.7 us
    ppermute x6, waiting for transfers between devices, spread_lanes(): lax.ppermute(outgoing, axis, pairs)  34.5 us
    pallas_call x1, Pallas kernels, correlate(): pl.pallas_call(correlate_kernel, out_shape=jax.ShapeDtypeStruct((channels...  15.3 us
    ppermute x6, starting transfers between devices, spread_lanes(): lax.ppermute(outgoing, axis, pairs)  8.02 us
    broadcast_in_dim x1, other arithmetic, on_device(): grad_query[:, None]  7.23 us
    all_to_all x1, starting transfers between devices, on_device(): lax.all_to_all(z_lanes, 'seq', split_axis=1, concat_axis=0, tiled=True)  6.8 us
    dynamic_update_slice x8, local copies, waits for them, and re-layouts, on_device(): lax.dynamic_update_slice(out, piece.T[:, None, :], (0, plane, source * ch...  6.62 us
  transfers between devices with their start and end apart: 14, of which 7 were waited for; matrix products, arithmetic and copies ran while one was open for 14% of the time, Pallas kernels for 7%

profile of v13, /device:TPU:18, one launch (start us, length us, event | category | flops | bytes accessed | tf_op | source)
XLA Modules:
  0.0 215.7 jit_solution(8908109063543822289)
XLA Ops:
  0.0 7.2 %fusion.21 = (f32[512,1,2048]{2,0,1:T(8,128)}, f32[512,2048]{1,0:T(8,128)S(1)}, bf16[512,2048]{1,0:T(8,128)(2,1)}) fusion(bf16[512,2048]{1,0:T(8,128)(2,1)} %param.7, bf16[512,2048]{1,0:T(8,128)(2,1)} %param.5, bf16[512,3,2048]{2,0,1:T(8,128)(2,1)} %param.6), kind=kLoop, calls=%fused_computation.61 | loop fusion | flops 6291456 | bytes 16777216 | tf_op jit(solution)/shard_map/broadcast_in_dim | solution.py:87
  7.2 1.9 collective-permute-start
  9.2 0.0 copy-done
  9.2 0.1 copy.22
  9.3 1.3 collective-permute-done
  10.6 2.9 %copy.21 = bf16[2048,512]{1,0:T(8,128)(2,1)S(1)} copy(bf16[2048,512]{0,1:T(8,128)(2,1)} %bitcast.99) | data formatting | bytes 4194304 | tf_op jit(solution)/shard_map/transpose | solution.py:79
  13.4 0.0 copy-start.1
  13.5 1.6 pad_maximum_fusion.3
  15.1 5.5 %all-to-all-start = ((bf16[8,272,512]{2,1,0:T(8,128)(2,1)}), bf16[8,272,512]{2,1,0:T(8,128)(2,1)S(1)}, u32[]{:S(2)}, u32[]{:S(2)}) async-start(bf16[8,272,512]{2,1,0:T(8,128)(2,1)} %pad_maximum_fusion.3), calls=%async_computation | async-start | bytes 4456448 | tf_op jit(solution)/shard_map/all_to_all | solution.py:83
  20.5 0.1 fusion.22
  20.6 5.6 %fusion.14 = bf16[512,1,2048]{2,0,1:T(8,128)(2,1)S(1)} fusion(f32[512,1,2048]{2,0,1:T(8,128)} %get-tuple-element.29, f32[2,1,2048]{2,0,1:T(2,128)S(1)} %collective-permute-done, f32[2048]{0:T(1024)S(1)} %bitcast.110, f32[2048]{0:T(1024)S(1)} %bitcast.111, f32[2048]{0:T(1024)S(1)} %bitcast.112, bf16[512,2048]{1,0:T(8,128)(2,1)} %param.7, ...), kind=kLoop, calls=%fused_computation.22 | loop fusion | flops 11534336 | bytes 10526720 | tf_op jit(solution)/shard_map/convert_element_type | solution.py:163
  26.2 1.2 dynamic-slice_bitcast_fusion
  27.4 1.5 collective-permute-start.1
  28.9 0.5 collective-permute-start.2
  29.4 1.5 collective-permute-start.3
  31.0 38.1 %all-to-all-done = bf16[8,272,512]{2,1,0:T(8,128)(2,1)S(1)} async-done(((bf16[8,272,512]{2,1,0:T(8,128)(2,1)}), bf16[8,272,512]{2,1,0:T(8,128)(2,1)S(1)}, u32[]{:S(2)}, u32[]{:S(2)}) %all-to-all-start) | async-done | bytes 2228256 | tf_op jit(solution)/shard_map/all_to_all | solution.py:83
  69.1 0.2 slice_bitcast_fusion
  69.3 1.6 copy.33
  70.9 2.3 %rev.3 = f32[16,4096]{1,0:T(8,128)S(1)} reverse(f32[16,4096]{1,0:T(8,128)S(1)} %bitcast.102), dimensions={1} | reverse | bytes 524288 | tf_op jit(solution)/shard_map/rev | solution.py:44
  73.2 0.1 concatenate.16
  73.3 0.9 reshape.57.h_ref
  74.2 15.3 %shard_map.55 = bf16[256,4096]{1,0:T(8,128)(2,1)} custom-call(bf16[256,4096]{1,0:T(8,128)(2,1)} %bitcast.101, f32[16,1,4352]{2,1,0:T(1,128)} %reshape.57.h_ref), custom_call_target="tpu_custom_call" | custom-call | flops 4563402752 | bytes 4472832 | tf_op jit(solution)/shard_map/pallas_call | solution.py:48
  89.5 0.0 collective-permute-done.1
  89.5 0.0 collective-permute-done.2
  89.5 0.0 collective-permute-done.3
  89.5 3.1 %copy.36 = bf16[32,8,8,512]{3,2,0,1:T(8,128)(2,1)} copy(bf16[32,8,8,512]{3,2,1,0:T(8,128)(2,1)} %bitcast.100) | data formatting | bytes 4194304 | tf_op jit(solution)/shard_map/all_to_all | solution.py:91
  92.6 6.8 %all-to-all-start.1 = ((bf16[256,8,512]{2,0,1:T(8,128)(2,1)}), bf16[256,8,512]{2,0,1:T(8,128)(2,1)S(1)}, u32[]{:S(2)}, u32[]{:S(2)}) async-start(bf16[256,8,512]{2,0,1:T(8,128)(2,1)} %bitcast.96), calls=%async_computation.1 | async-start | bytes 4194304 | tf_op jit(solution)/shard_map/all_to_all | solution.py:91
  99.4 3.4 %broadcast_in_dim.34 = bf16[128,3,8192]{2,0,1:T(8,128)(2,1)} broadcast(bf16[]{:T(256)} %constant.83.clone.1), dimensions={} | broadcast | bytes 6291458 | tf_op jit(solution)/shard_map/broadcast_in_dim | solution.py:96
  102.8 0.8 constant_dynamic-update-slice_fusion.3
  103.7 1.9 constant_dynamic-update-slice_fusion.2
  105.5 1.9 constant_dynamic-update-slice_fusion.1
  107.4 37.7 %all-to-all-done.1 = bf16[256,8,512]{2,0,1:T(8,128)(2,1)S(1)} async-done(((bf16[256,8,512]{2,0,1:T(8,128)(2,1)}), bf16[256,8,512]{2,0,1:T(8,128)(2,1)S(1)}, u32[]{:S(2)}, u32[]{:S(2)}) %all-to-all-start.1) | async-done | bytes 2097184 | tf_op jit(solution)/shard_map/all_to_all | solution.py:91
  145.2 2.5 %convert_element_type.86 = f32[256,8,512]{2,0,1:T(8,128)} convert(bf16[256,8,512]{2,0,1:T(8,128)(2,1)S(1)} %all-to-all-done.1) | non-fusion elementwise | flops 1048576 | bytes 6291456 | tf_op jit(solution)/shard_map/convert_element_type | solution.py:92
  147.7 5.5 %copy.30 = f32[2048,512]{0,1:T(8,128)} copy(f32[2048,512]{1,0:T(8,128)} %bitcast.95) | data formatting | bytes 8388608 | tf_op jit(solution)/shard_map/convert_element_type | solution.py:92
  153.1 4.7 %fusion.19 = (f32[2048,512]{0,1:T(8,128)S(1)}, f32[2048,512]{0,1:T(8,128)S(1)}) fusion(f32[2048,512]{0,1:T(8,128)} %copy.30, bf16[512,3,2048]{2,0,1:T(8,128)(2,1)} %param.6), kind=kLoop, calls=%fused_computation.31 | loop fusion | flops 4194304 | bytes 16777216 | tf_op jit(solution)/shard_map/mul | solution.py:94
  157.9 1.9 collective-permute-start.4
  159.8 0.8 constant_dynamic-update-slice_fusion
  160.7 2.3 %collective-permute-start.8 = (f32[2048,2]{0,1:T(2,128)S(1)}, f32[2048,2]{0,1:T(2,128)S(1)}, u32[]{:S(2)}, u32[]{:S(2)}) collective-permute-start(f32[2048,2]{0,1:T(2,128)S(1)} %slice.118), channel_id=1, source_target_pairs={{4,0},{8,4},{12,8},{16,12},{20,16},{24,20},{28,24},{5,1},{9,5},{13... | collective-permute-start | bytes 49160 | tf_op jit(solution)/shard_map/ppermute | solution.py:17
  163.0 0.0 collective-permute-done.4
  163.0 1.6 fusion.9
  164.6 0.2 constant_dynamic-slice_fusion.2
  164.8 1.5 collective-permute-start.5
  166.4 0.5 collective-permute-start.6
  166.9 1.5 collective-permute-start.7
  168.4 0.0 collective-permute-done.8
  168.4 1.6 fusion.4
  170.0 0.1 constant_dynamic-slice_fusion.5
  170.2 1.4 collective-permute-start.9
  171.6 1.5 collective-permute-start.10
  173.1 0.8 bitcast_dynamic-update-slice_fusion.7
  173.9 5.7 %collective-permute-done.5 = bf16[2048,128]{0,1:T(8,128)(2,1)S(1)} collective-permute-done((bf16[2048,128]{0,1:T(8,128)(2,1)S(1)}, bf16[2048,128]{0,1:T(8,128)(2,1)S(1)}, u32[]{:S(2)}, u32[]{:S(2)}) %collective-permute-start.5) | collective-permute-done | bytes 524320 | tf_op jit(solution)/shard_map/ppermute | solution.py:129
  179.7 1.5 collective-permute-start.11
  181.2 0.8 bitcast_dynamic-update-slice_fusion.6
  182.0 10.4 %collective-permute-done.6 = bf16[2048,128]{0,1:T(8,128)(2,1)S(1)} collective-permute-done((bf16[2048,128]{0,1:T(8,128)(2,1)S(1)}, bf16[2048,128]{0,1:T(8,128)(2,1)S(1)}, u32[]{:S(2)}, u32[]{:S(2)}) %collective-permute-start.6) | collective-permute-done | bytes 524320 | tf_op jit(solution)/shard_map/ppermute | solution.py:129
  192.4 0.8 bitcast_dynamic-update-slice_fusion.5
  193.2 0.0 collective-permute-done.7
  193.2 0.8 bitcast_dynamic-update-slice_fusion.4
  194.1 0.8 bitcast_dynamic-update-slice_fusion.3
  194.9 7.3 %collective-permute-done.9 = bf16[2048,128]{0,1:T(8,128)(2,1)S(1)} collective-permute-done((bf16[2048,128]{0,1:T(8,128)(2,1)S(1)}, bf16[2048,128]{0,1:T(8,128)(2,1)S(1)}, u32[]{:S(2)}, u32[]{:S(2)}) %collective-permute-start.9) | collective-permute-done | bytes 524320 | tf_op jit(solution)/shard_map/ppermute | solution.py:129
  202.2 0.8 bitcast_dynamic-update-slice_fusion.2
  203.0 11.1 %collective-permute-done.10 = bf16[2048,128]{0,1:T(8,128)(2,1)S(1)} collective-permute-done((bf16[2048,128]{0,1:T(8,128)(2,1)S(1)}, bf16[2048,128]{0,1:T(8,128)(2,1)S(1)}, u32[]{:S(2)}, u32[]{:S(2)}) %collective-permute-start.10) | collective-permute-done | bytes 524320 | tf_op jit(solution)/shard_map/ppermute | solution.py:129
  214.1 0.8 bitcast_dynamic-update-slice_fusion.1
  214.9 0.0 collective-permute-done.11
  214.9 0.8 bitcast_dynamic-update-slice_fusion
  (7 shorter events, 0.1 us)
Async XLA Ops:
  0.0 9.2 %copy-start = (bf16[512,128]{1,0:T(8,128)(2,1)S(1)}, bf16[512,128]{1,0:T(8,128)(2,1)}, u32[]{:S(2)}) copy-start(bf16[512,128]{1,0:T(8,128)(2,1)} %param.8) | copy-start | bytes 393220
  7.2 3.3 %collective-permute-start = (f32[2,1,2048]{2,0,1:T(2,128)S(1)}, f32[2,1,2048]{2,0,1:T(2,128)S(1)}, u32[]{:S(2)}, u32[]{:S(2)}) collective-permute-start(f32[2,1,2048]{2,0,1:T(2,128)S(1)} %slice_bitcast_fusion.1), channel_id=1, source_target_pairs={{4,0},{8,4},{12,8},{16,12},{20,16},{24,20},{28,24},{5,1},{9,5},{13... | collective-permute-start | bytes 49160 | tf_op jit(solution)/shard_map/ppermute | solution.py:17
  13.4 7.1 %copy-start.1 = (f32[3,3,2048]{2,1,0:T(4,128)S(1)}, f32[3,3,2048]{2,1,0:T(4,128)}, u32[]{:S(2)}) copy-start(f32[3,3,2048]{2,1,0:T(4,128)} %param.9) | copy-start | bytes 221188
  15.1 54.0 %all-to-all-start = ((bf16[8,272,512]{2,1,0:T(8,128)(2,1)}), bf16[8,272,512]{2,1,0:T(8,128)(2,1)S(1)}, u32[]{:S(2)}, u32[]{:S(2)}) async-start(bf16[8,272,512]{2,1,0:T(8,128)(2,1)} %pad_maximum_fusion.3), calls=%async_computation | async-start | bytes 4456448 | tf_op jit(solution)/shard_map/all_to_all | solution.py:83
  27.4 62.1 %collective-permute-start.1 = (bf16[128,1,2048]{2,0,1:T(8,128)(2,1)}, bf16[128,1,2048]{2,0,1:T(8,128)(2,1)}, u32[]{:S(2)}, u32[]{:S(2)}) collective-permute-start(bf16[128,1,2048]{2,0,1:T(8,128)(2,1)} %get-tuple-element.39), channel_id=1, source_target_pairs={{0,1},{1,2},{2,3},{3,0},{4,5},{5,6},{6,7},{7,4},{8,9},{9,10},{10,1... | collective-permute-start | bytes 1572872 | tf_op jit(solution)/shard_map/ppermute | solution.py:142
  28.9 60.6 %collective-permute-start.2 = (bf16[128,1,2048]{2,0,1:T(8,128)(2,1)}, bf16[128,1,2048]{2,0,1:T(8,128)(2,1)}, u32[]{:S(2)}, u32[]{:S(2)}) collective-permute-start(bf16[128,1,2048]{2,0,1:T(8,128)(2,1)} %get-tuple-element.38), channel_id=1, source_target_pairs={{0,2},{1,3},{2,0},{3,1},{4,6},{5,7},{6,4},{7,5},{8,10},{9,11},{10,... | collective-permute-start | bytes 1572872 | tf_op jit(solution)/shard_map/ppermute | solution.py:142
  29.4 60.1 %collective-permute-start.3 = (bf16[128,1,2048]{2,0,1:T(8,128)(2,1)}, bf16[128,1,2048]{2,0,1:T(8,128)(2,1)S(1)}, u32[]{:S(2)}, u32[]{:S(2)}) collective-permute-start(bf16[128,1,2048]{2,0,1:T(8,128)(2,1)} %get-tuple-element.37), channel_id=1, source_target_pairs={{0,3},{1,0},{2,1},{3,2},{4,7},{5,4},{6,5},{7,6},{8,11},{9,8},{10,9... | collective-permute-start | bytes 1572872 | tf_op jit(solution)/shard_map/ppermute | solution.py:142
  92.6 52.6 %all-to-all-start.1 = ((bf16[256,8,512]{2,0,1:T(8,128)(2,1)}), bf16[256,8,512]{2,0,1:T(8,128)(2,1)S(1)}, u32[]{:S(2)}, u32[]{:S(2)}) async-start(bf16[256,8,512]{2,0,1:T(8,128)(2,1)} %bitcast.96), calls=%async_computation.1 | async-start | bytes 4194304 | tf_op jit(solution)/shard_map/all_to_all | solution.py:91
  157.9 5.1 %collective-permute-start.4 = (f32[2048,2]{0,1:T(2,128)S(1)}, f32[2048,2]{0,1:T(2,128)S(1)}, u32[]{:S(2)}, u32[]{:S(2)}) collective-permute-start(f32[2048,2]{0,1:T(2,128)S(1)} %slice.115), channel_id=1, source_target_pairs={{4,0},{8,4},{12,8},{16,12},{20,16},{24,20},{28,24},{5,1},{9,5},{13... | collective-permute-start | bytes 49160 | tf_op jit(solution)/shard_map/ppermute | solution.py:17
  160.7 7.8 %collective-permute-start.8 = (f32[2048,2]{0,1:T(2,128)S(1)}, f32[2048,2]{0,1:T(2,128)S(1)}, u32[]{:S(2)}, u32[]{:S(2)}) collective-permute-start(f32[2048,2]{0,1:T(2,128)S(1)} %slice.118), channel_id=1, source_target_pairs={{4,0},{8,4},{12,8},{16,12},{20,16},{24,20},{28,24},{5,1},{9,5},{13... | collective-permute-start | bytes 49160 | tf_op jit(solution)/shard_map/ppermute | solution.py:17
  164.8 14.9 %collective-permute-start.5 = (bf16[2048,128]{0,1:T(8,128)(2,1)S(1)}, bf16[2048,128]{0,1:T(8,128)(2,1)S(1)}, u32[]{:S(2)}, u32[]{:S(2)}) collective-permute-start(bf16[2048,128]{0,1:T(8,128)(2,1)S(1)} %get-tuple-element.36), channel_id=1, source_target_pairs={{0,1},{1,2},{2,3},{3,0},{4,5},{5,6},{6,7},{7,4},{8,9},{9,10},{10,1... | collective-permute-start | bytes 1572872 | tf_op jit(solution)/shard_map/ppermute | solution.py:129
  166.4 26.0 %collective-permute-start.6 = (bf16[2048,128]{0,1:T(8,128)(2,1)S(1)}, bf16[2048,128]{0,1:T(8,128)(2,1)S(1)}, u32[]{:S(2)}, u32[]{:S(2)}) collective-permute-start(bf16[2048,128]{0,1:T(8,128)(2,1)S(1)} %get-tuple-element.35), channel_id=1, source_target_pairs={{0,2},{1,3},{2,0},{3,1},{4,6},{5,7},{6,4},{7,5},{8,10},{9,11},{10,... | collective-permute-start | bytes 1572872 | tf_op jit(solution)/shard_map/ppermute | solution.py:129
  166.9 26.4 %collective-permute-start.7 = (bf16[2048,128]{0,1:T(8,128)(2,1)S(1)}, bf16[2048,128]{0,1:T(8,128)(2,1)S(1)}, u32[]{:S(2)}, u32[]{:S(2)}) collective-permute-start(bf16[2048,128]{0,1:T(8,128)(2,1)S(1)} %get-tuple-element.34), channel_id=1, source_target_pairs={{0,3},{1,0},{2,1},{3,2},{4,7},{5,4},{6,5},{7,6},{8,11},{9,8},{10,9... | collective-permute-start | bytes 1572872 | tf_op jit(solution)/shard_map/ppermute | solution.py:129
  170.2 32.0 %collective-permute-start.9 = (bf16[2048,128]{0,1:T(8,128)(2,1)S(1)}, bf16[2048,128]{0,1:T(8,128)(2,1)S(1)}, u32[]{:S(2)}, u32[]{:S(2)}) collective-permute-start(bf16[2048,128]{0,1:T(8,128)(2,1)S(1)} %get-tuple-element.33), channel_id=1, source_target_pairs={{0,1},{1,2},{2,3},{3,0},{4,5},{5,6},{6,7},{7,4},{8,9},{9,10},{10,1... | collective-permute-start | bytes 1572872 | tf_op jit(solution)/shard_map/ppermute | solution.py:129
  171.6 42.5 %collective-permute-start.10 = (bf16[2048,128]{0,1:T(8,128)(2,1)S(1)}, bf16[2048,128]{0,1:T(8,128)(2,1)S(1)}, u32[]{:S(2)}, u32[]{:S(2)}) collective-permute-start(bf16[2048,128]{0,1:T(8,128)(2,1)S(1)} %get-tuple-element.32), channel_id=1, source_target_pairs={{0,2},{1,3},{2,0},{3,1},{4,6},{5,7},{6,4},{7,5},{8,10},{9,11},{10,... | collective-permute-start | bytes 1572872 | tf_op jit(solution)/shard_map/ppermute | solution.py:129
  179.7 35.2 %collective-permute-start.11 = (bf16[2048,128]{0,1:T(8,128)(2,1)S(1)}, bf16[2048,128]{0,1:T(8,128)(2,1)S(1)}, u32[]{:S(2)}, u32[]{:S(2)}) collective-permute-start(bf16[2048,128]{0,1:T(8,128)(2,1)S(1)} %get-tuple-element.31), channel_id=1, source_target_pairs={{0,3},{1,0},{2,1},{3,2},{4,7},{5,4},{6,5},{7,6},{8,11},{9,8},{10,9... | collective-permute-start | bytes 1572872 | tf_op jit(solution)/shard_map/ppermute | solution.py:129

commit v14 on v11

--- a/solution.py
+++ b/solution.py
@@ -23,15 +23,20 @@
     for index in range(blocks):
         rows_ref[per_group * index : per_group * (index + 1), :] = x_ref[:, block * index : block * (index + 1)]
     acc_ref[...] = jnp.zeros(acc_ref.shape, acc_ref.dtype)
-    for lag_block in range(blocks):
-        start = tokens - block * (lag_block + 1)
-        window = h_ref[0, :, start : start + 2 * block]
-        spread = jnp.broadcast_to(window, (block, 2 * block))
-        rolled = pltpu.roll(spread, block + 1, 1, stride=1, stride_axis=0)
-        band = rolled[:, :block].astype(jnp.bfloat16)
-        rows = per_group * (blocks - lag_block)
-        source = rows_ref[per_group * lag_block :, :]
-        acc_ref[:rows, :] += jnp.dot(source, band, preferred_element_type=jnp.float32)
+    lag_block = 0
+    while lag_block < blocks:
+        paired = 2 if lag_block + 1 < blocks else 1
+        start = tokens - block * (lag_block + paired)
+        window = h_ref[0, :, start : start + (paired + 1) * block]
+        spread = jnp.broadcast_to(window, (block, (paired + 1) * block))
+        rolled = pltpu.roll(spread, paired * block + 1, 1, stride=1, stride_axis=0)
+        for offset in range(paired):
+            band = rolled[:, (paired - 1 - offset) * block : (paired - offset) * block]
+            band = band.astype(jnp.bfloat16)
+            rows = per_group * (blocks - lag_block - offset)
+            source = rows_ref[per_group * (lag_block + offset) :, :]
+            acc_ref[:rows, :] += jnp.dot(source, band, preferred_element_type=jnp.float32)
+        lag_block += paired
     for index in range(blocks):
         slab = acc_ref[per_group * index : per_group * (index + 1), :]
         o_ref[:, block * index : block * (index + 1)] = slab.astype(o_ref.dtype)

time: 219 us -> 218 us (level)
  no operation moved by 1% of the time
where the time goes in v14:
time: 218 us; the launch traced here: 214 us
  waiting for transfers between devices  105 us (48%)
  local copies, waits for them, and re-layouts  35.7 us (16%)
  starting transfers between devices  35.4 us (16%)
  other arithmetic  22.4 us (10%)
  Pallas kernels  15 us (7%)
    all_to_all x1, waiting for transfers between devices, on_device(): lax.all_to_all(z_lanes, 'seq', split_axis=1, concat_axis=0, tiled=True)  37.7 us
    ppermute x6, waiting for transfers between devices, spread_lanes(): lax.ppermute(outgoing, axis, pairs)  34.1 us
    all_to_all x1, waiting for transfers between devices, on_device(): lax.all_to_all(grad_mixed.T, 'seq', split_axis=0, concat_axis=1, tiled=True)  32 us
    pallas_call x1, Pallas kernels, correlate(): pl.pallas_call(correlate_kernel, out_shape=jax.ShapeDtypeStruct((channels...  15 us
    ppermute x6, starting transfers between devices, spread_lanes(): lax.ppermute(outgoing, axis, pairs)  8.02 us
    all_to_all x1, starting transfers between devices, on_device(): lax.all_to_all(z_lanes, 'seq', split_axis=1, concat_axis=0, tiled=True)  6.8 us
    dynamic_update_slice x8, local copies, waits for them, and re-layouts, on_device(): lax.dynamic_update_slice(out, piece.T[:, None, :], (0, plane, source * ch...  6.62 us
    dynamic_update_slice x4, local copies, waits for them, and re-layouts, on_device(): out = lax.dynamic_update_slice(out, piece, (0, 0, source * channels))  6.47 us
  transfers between devices with their start and end apart: 15, of which 7 were waited for; matrix products, arithmetic and copies ran while one was open for 19% of the time, Pallas kernels for 7%

profile of v14, /device:TPU:18, one launch (start us, length us, event | category | flops | bytes accessed | tf_op | source)
XLA Modules:
  0.0 214.0 jit_solution(3256706267647897204)
XLA Ops:
  0.0 1.7 copy.23
  1.7 5.2 %all-to-all-start.1 = ((bf16[512,8,16]{0,2,1:T(8,128)(2,1)}), bf16[512,8,16]{0,2,1:T(8,128)(2,1)S(1)}, u32[]{:S(2)}, u32[]{:S(2)}) async-start(bf16[512,8,16]{0,2,1:T(8,128)(2,1)} %bitcast.5), calls=%async_computation.1 | async-start | bytes 262144 | tf_op jit(solution)/shard_map/all_to_all | solution.py:84
  6.9 6.3 %fusion.21 = (f32[512,1,2048]{2,0,1:T(8,128)}, f32[512,2048]{1,0:T(8,128)S(1)}, bf16[512,2048]{1,0:T(8,128)(2,1)S(1)}) fusion(bf16[512,2048]{1,0:T(8,128)(2,1)} %param.7, bf16[512,2048]{1,0:T(8,128)(2,1)} %param.5, bf16[512,3,2048]{2,0,1:T(8,128)(2,1)} %param.6), kind=kLoop, calls=%fused_computation.59 | loop fusion | flops 6291456 | bytes 16777216 | tf_op jit(solution)/shard_map/broadcast_in_dim | solution.py:86
  13.2 2.2 %collective-permute-start = (f32[2,1,2048]{2,0,1:T(2,128)S(1)}, f32[2,1,2048]{2,0,1:T(2,128)S(1)}, u32[]{:S(2)}, u32[]{:S(2)}) collective-permute-start(f32[2,1,2048]{2,0,1:T(2,128)S(1)} %slice_bitcast_fusion), channel_id=1, source_target_pairs={{4,0},{8,4},{12,8},{16,12},{20,16},{24,20},{28,24},{5,1},{9,5},{13... | collective-permute-start | bytes 49160 | tf_op jit(solution)/shard_map/ppermute | solution.py:17
  15.4 1.4 collective-permute-done
  16.8 0.0 copy-start
  16.8 2.5 %copy.21 = bf16[2048,512]{1,0:T(8,128)(2,1)} copy(bf16[2048,512]{0,1:T(8,128)(2,1)S(1)} %bitcast.98) | data formatting | bytes 4194304 | tf_op jit(solution)/shard_map/transpose | solution.py:83
  19.3 0.0 all-to-all-done.1
  19.3 5.4 %all-to-all-start = ((bf16[8,256,512]{2,1,0:T(8,128)(2,1)}), bf16[8,256,512]{2,1,0:T(8,128)(2,1)S(1)}, u32[]{:S(2)}, u32[]{:S(2)}) async-start(bf16[8,256,512]{2,1,0:T(8,128)(2,1)} %bitcast.3), calls=%async_computation | async-start | bytes 4194304 | tf_op jit(solution)/shard_map/all_to_all | solution.py:83
  24.7 0.0 copy-done
  24.7 0.1 fusion.22
  24.8 5.6 %fusion.14 = bf16[512,1,2048]{2,0,1:T(8,128)(2,1)S(1)} fusion(f32[512,1,2048]{2,0,1:T(8,128)} %get-tuple-element.29, f32[2,1,2048]{2,0,1:T(2,128)S(1)} %collective-permute-done, f32[2048]{0:T(1024)S(1)} %bitcast.108, f32[2048]{0:T(1024)S(1)} %bitcast.109, f32[2048]{0:T(1024)S(1)} %bitcast.110, bf16[512,2048]{1,0:T(8,128)(2,1)} %param.7, ...), kind=kLoop, calls=%fused_computation.22 | loop fusion | flops 11534336 | bytes 10526720 | tf_op jit(solution)/shard_map/convert_element_type | solution.py:162
  30.4 1.2 dynamic-slice_bitcast_fusion
  31.6 1.5 collective-permute-start.1
  33.1 0.5 collective-permute-start.2
  33.6 1.5 collective-permute-start.3
  35.2 2.3 %rev.3 = f32[16,4096]{1,0:T(8,128)S(1)} reverse(f32[16,4096]{1,0:T(8,128)S(1)} %bitcast.101), dimensions={1} | reverse | bytes 524288 | tf_op jit(solution)/shard_map/rev | solution.py:49
  37.5 0.1 concatenate.12
  37.5 0.9 reshape.50.h_ref
  38.4 32.0 %all-to-all-done = bf16[8,256,512]{2,1,0:T(8,128)(2,1)S(1)} async-done(((bf16[8,256,512]{2,1,0:T(8,128)(2,1)}), bf16[8,256,512]{2,1,0:T(8,128)(2,1)S(1)}, u32[]{:S(2)}, u32[]{:S(2)}) %all-to-all-start) | async-done | bytes 2097184 | tf_op jit(solution)/shard_map/all_to_all | solution.py:83
  70.5 1.6 copy.33
  72.1 15.0 %shard_map.55 = bf16[256,4096]{1,0:T(8,128)(2,1)} custom-call(bf16[256,4096]{1,0:T(8,128)(2,1)} %bitcast.100, f32[16,1,4352]{2,1,0:T(1,128)} %reshape.50.h_ref), custom_call_target="tpu_custom_call" | custom-call | flops 4563402752 | bytes 4472832 | tf_op jit(solution)/shard_map/pallas_call | solution.py:53
  87.1 0.0 collective-permute-done.1
  87.1 0.0 collective-permute-done.2
  87.1 0.0 collective-permute-done.3
  87.1 3.1 %copy.36 = bf16[32,8,8,512]{3,2,0,1:T(8,128)(2,1)} copy(bf16[32,8,8,512]{3,2,1,0:T(8,128)(2,1)} %bitcast.99) | data formatting | bytes 4194304 | tf_op jit(solution)/shard_map/all_to_all | solution.py:90
  90.2 6.8 %all-to-all-start.2 = ((bf16[256,8,512]{2,0,1:T(8,128)(2,1)}), bf16[256,8,512]{2,0,1:T(8,128)(2,1)S(1)}, u32[]{:S(2)}, u32[]{:S(2)}) async-start(bf16[256,8,512]{2,0,1:T(8,128)(2,1)} %bitcast.96), calls=%async_computation.2 | async-start | bytes 4194304 | tf_op jit(solution)/shard_map/all_to_all | solution.py:90
  97.0 3.4 %broadcast_in_dim.34 = bf16[128,3,8192]{2,0,1:T(8,128)(2,1)} broadcast(bf16[]{:T(256)} %constant.83.clone.1), dimensions={} | broadcast | bytes 6291458 | tf_op jit(solution)/shard_map/broadcast_in_dim | solution.py:95
  100.4 0.8 constant_dynamic-update-slice_fusion.3
  101.3 1.9 constant_dynamic-update-slice_fusion.2
  103.2 1.9 constant_dynamic-update-slice_fusion.1
  105.0 37.7 %all-to-all-done.2 = bf16[256,8,512]{2,0,1:T(8,128)(2,1)S(1)} async-done(((bf16[256,8,512]{2,0,1:T(8,128)(2,1)}), bf16[256,8,512]{2,0,1:T(8,128)(2,1)S(1)}, u32[]{:S(2)}, u32[]{:S(2)}) %all-to-all-start.2) | async-done | bytes 2097184 | tf_op jit(solution)/shard_map/all_to_all | solution.py:90
  142.8 2.5 %convert_element_type.81 = f32[256,8,512]{2,0,1:T(8,128)} convert(bf16[256,8,512]{2,0,1:T(8,128)(2,1)S(1)} %all-to-all-done.2) | non-fusion elementwise | flops 1048576 | bytes 6291456 | tf_op jit(solution)/shard_map/convert_element_type | solution.py:91
  145.3 5.5 %copy.30 = f32[2048,512]{0,1:T(8,128)} copy(f32[2048,512]{1,0:T(8,128)} %bitcast.94) | data formatting | bytes 8388608 | tf_op jit(solution)/shard_map/convert_element_type | solution.py:91
  150.8 4.7 %fusion.19 = (f32[2048,512]{0,1:T(8,128)S(1)}, f32[2048,512]{0,1:T(8,128)S(1)}) fusion(f32[2048,512]{0,1:T(8,128)} %copy.30, bf16[512,3,2048]{2,0,1:T(8,128)(2,1)} %param.6), kind=kLoop, calls=%fused_computation.31 | loop fusion | flops 4194304 | bytes 16777216 | tf_op jit(solution)/shard_map/mul | solution.py:93
  155.5 1.9 collective-permute-start.4
  157.4 1.9 constant_dynamic-update-slice_fusion
  159.3 2.3 %collective-permute-start.8 = (f32[2048,2]{0,1:T(2,128)S(1)}, f32[2048,2]{0,1:T(2,128)S(1)}, u32[]{:S(2)}, u32[]{:S(2)}) collective-permute-start(f32[2048,2]{0,1:T(2,128)S(1)} %slice.108), channel_id=1, source_target_pairs={{4,0},{8,4},{12,8},{16,12},{20,16},{24,20},{28,24},{5,1},{9,5},{13... | collective-permute-start | bytes 49160 | tf_op jit(solution)/shard_map/ppermute | solution.py:17
  161.7 0.0 collective-permute-done.4
  161.7 1.6 fusion.9
  163.3 0.2 constant_dynamic-slice_fusion.2
  163.5 1.5 collective-permute-start.5
  165.1 0.5 collective-permute-start.6
  165.6 1.5 collective-permute-start.7
  167.1 0.0 collective-permute-done.8
  167.1 1.6 fusion.4
  168.7 0.1 constant_dynamic-slice_fusion.5
  168.8 1.4 collective-permute-start.9
  170.3 1.5 collective-permute-start.10
  171.8 0.8 bitcast_dynamic-update-slice_fusion.7
  172.6 5.7 %collective-permute-done.5 = bf16[2048,128]{0,1:T(8,128)(2,1)S(1)} collective-permute-done((bf16[2048,128]{0,1:T(8,128)(2,1)S(1)}, bf16[2048,128]{0,1:T(8,128)(2,1)S(1)}, u32[]{:S(2)}, u32[]{:S(2)}) %collective-permute-start.5) | collective-permute-done | bytes 524320 | tf_op jit(solution)/shard_map/ppermute | solution.py:128
  178.4 1.5 collective-permute-start.11
  179.8 0.8 bitcast_dynamic-update-slice_fusion.6
  180.7 10.4 %collective-permute-done.6 = bf16[2048,128]{0,1:T(8,128)(2,1)S(1)} collective-permute-done((bf16[2048,128]{0,1:T(8,128)(2,1)S(1)}, bf16[2048,128]{0,1:T(8,128)(2,1)S(1)}, u32[]{:S(2)}, u32[]{:S(2)}) %collective-permute-start.6) | collective-permute-done | bytes 524320 | tf_op jit(solution)/shard_map/ppermute | solution.py:128
  191.1 0.8 bitcast_dynamic-update-slice_fusion.5
  191.9 0.0 collective-permute-done.7
  191.9 0.8 bitcast_dynamic-update-slice_fusion.4
  192.7 0.8 bitcast_dynamic-update-slice_fusion.3
  193.6 7.3 %collective-permute-done.9 = bf16[2048,128]{0,1:T(8,128)(2,1)S(1)} collective-permute-done((bf16[2048,128]{0,1:T(8,128)(2,1)S(1)}, bf16[2048,128]{0,1:T(8,128)(2,1)S(1)}, u32[]{:S(2)}, u32[]{:S(2)}) %collective-permute-start.9) | collective-permute-done | bytes 524320 | tf_op jit(solution)/shard_map/ppermute | solution.py:128
  200.9 0.8 bitcast_dynamic-update-slice_fusion.2
  201.7 10.7 %collective-permute-done.10 = bf16[2048,128]{0,1:T(8,128)(2,1)S(1)} collective-permute-done((bf16[2048,128]{0,1:T(8,128)(2,1)S(1)}, bf16[2048,128]{0,1:T(8,128)(2,1)S(1)}, u32[]{:S(2)}, u32[]{:S(2)}) %collective-permute-start.10) | collective-permute-done | bytes 524320 | tf_op jit(solution)/shard_map/ppermute | solution.py:128
  212.4 0.8 bitcast_dynamic-update-slice_fusion.1
  213.2 0.0 collective-permute-done.11
  213.2 0.8 bitcast_dynamic-update-slice_fusion
  (5 shorter events, 0.1 us)
Async XLA Ops:
  1.7 17.7 %all-to-all-start.1 = ((bf16[512,8,16]{0,2,1:T(8,128)(2,1)}), bf16[512,8,16]{0,2,1:T(8,128)(2,1)S(1)}, u32[]{:S(2)}, u32[]{:S(2)}) async-start(bf16[512,8,16]{0,2,1:T(8,128)(2,1)} %bitcast.5), calls=%async_computation.1 | async-start | bytes 262144 | tf_op jit(solution)/shard_map/all_to_all | solution.py:84
  13.2 3.6 %collective-permute-start = (f32[2,1,2048]{2,0,1:T(2,128)S(1)}, f32[2,1,2048]{2,0,1:T(2,128)S(1)}, u32[]{:S(2)}, u32[]{:S(2)}) collective-permute-start(f32[2,1,2048]{2,0,1:T(2,128)S(1)} %slice_bitcast_fusion), channel_id=1, source_target_pairs={{4,0},{8,4},{12,8},{16,12},{20,16},{24,20},{28,24},{5,1},{9,5},{13... | collective-permute-start | bytes 49160 | tf_op jit(solution)/shard_map/ppermute | solution.py:17
  16.8 7.9 %copy-start = (f32[3,3,2048]{2,1,0:T(4,128)S(1)}, f32[3,3,2048]{2,1,0:T(4,128)}, u32[]{:S(2)}) copy-start(f32[3,3,2048]{2,1,0:T(4,128)} %param.9) | copy-start | bytes 221188
  19.3 51.1 %all-to-all-start = ((bf16[8,256,512]{2,1,0:T(8,128)(2,1)}), bf16[8,256,512]{2,1,0:T(8,128)(2,1)S(1)}, u32[]{:S(2)}, u32[]{:S(2)}) async-start(bf16[8,256,512]{2,1,0:T(8,128)(2,1)} %bitcast.3), calls=%async_computation | async-start | bytes 4194304 | tf_op jit(solution)/shard_map/all_to_all | solution.py:83
  31.6 55.5 %collective-permute-start.1 = (bf16[128,1,2048]{2,0,1:T(8,128)(2,1)}, bf16[128,1,2048]{2,0,1:T(8,128)(2,1)}, u32[]{:S(2)}, u32[]{:S(2)}) collective-permute-start(bf16[128,1,2048]{2,0,1:T(8,128)(2,1)} %get-tuple-element.39), channel_id=1, source_target_pairs={{0,1},{1,2},{2,3},{3,0},{4,5},{5,6},{6,7},{7,4},{8,9},{9,10},{10,1... | collective-permute-start | bytes 1572872 | tf_op jit(solution)/shard_map/ppermute | solution.py:141
  33.1 54.0 %collective-permute-start.2 = (bf16[128,1,2048]{2,0,1:T(8,128)(2,1)}, bf16[128,1,2048]{2,0,1:T(8,128)(2,1)}, u32[]{:S(2)}, u32[]{:S(2)}) collective-permute-start(bf16[128,1,2048]{2,0,1:T(8,128)(2,1)} %get-tuple-element.38), channel_id=1, source_target_pairs={{0,2},{1,3},{2,0},{3,1},{4,6},{5,7},{6,4},{7,5},{8,10},{9,11},{10,... | collective-permute-start | bytes 1572872 | tf_op jit(solution)/shard_map/ppermute | solution.py:141
  33.6 53.5 %collective-permute-start.3 = (bf16[128,1,2048]{2,0,1:T(8,128)(2,1)}, bf16[128,1,2048]{2,0,1:T(8,128)(2,1)}, u32[]{:S(2)}, u32[]{:S(2)}) collective-permute-start(bf16[128,1,2048]{2,0,1:T(8,128)(2,1)} %get-tuple-element.37), channel_id=1, source_target_pairs={{0,3},{1,0},{2,1},{3,2},{4,7},{5,4},{6,5},{7,6},{8,11},{9,8},{10,9... | collective-permute-start | bytes 1572872 | tf_op jit(solution)/shard_map/ppermute | solution.py:141
  90.2 52.6 %all-to-all-start.2 = ((bf16[256,8,512]{2,0,1:T(8,128)(2,1)}), bf16[256,8,512]{2,0,1:T(8,128)(2,1)S(1)}, u32[]{:S(2)}, u32[]{:S(2)}) async-start(bf16[256,8,512]{2,0,1:T(8,128)(2,1)} %bitcast.96), calls=%async_computation.2 | async-start | bytes 4194304 | tf_op jit(solution)/shard_map/all_to_all | solution.py:90
  155.5 6.2 %collective-permute-start.4 = (f32[2048,2]{0,1:T(2,128)S(1)}, f32[2048,2]{0,1:T(2,128)S(1)}, u32[]{:S(2)}, u32[]{:S(2)}) collective-permute-start(f32[2048,2]{0,1:T(2,128)S(1)} %slice.105), channel_id=1, source_target_pairs={{4,0},{8,4},{12,8},{16,12},{20,16},{24,20},{28,24},{5,1},{9,5},{13... | collective-permute-start | bytes 49160 | tf_op jit(solution)/shard_map/ppermute | solution.py:17
  159.3 7.8 %collective-permute-start.8 = (f32[2048,2]{0,1:T(2,128)S(1)}, f32[2048,2]{0,1:T(2,128)S(1)}, u32[]{:S(2)}, u32[]{:S(2)}) collective-permute-start(f32[2048,2]{0,1:T(2,128)S(1)} %slice.108), channel_id=1, source_target_pairs={{4,0},{8,4},{12,8},{16,12},{20,16},{24,20},{28,24},{5,1},{9,5},{13... | collective-permute-start | bytes 49160 | tf_op jit(solution)/shard_map/ppermute | solution.py:17
  163.5 14.8 %collective-permute-start.5 = (bf16[2048,128]{0,1:T(8,128)(2,1)S(1)}, bf16[2048,128]{0,1:T(8,128)(2,1)S(1)}, u32[]{:S(2)}, u32[]{:S(2)}) collective-permute-start(bf16[2048,128]{0,1:T(8,128)(2,1)S(1)} %get-tuple-element.36), channel_id=1, source_target_pairs={{0,1},{1,2},{2,3},{3,0},{4,5},{5,6},{6,7},{7,4},{8,9},{9,10},{10,1... | collective-permute-start | bytes 1572872 | tf_op jit(solution)/shard_map/ppermute | solution.py:128
  165.1 26.0 %collective-permute-start.6 = (bf16[2048,128]{0,1:T(8,128)(2,1)S(1)}, bf16[2048,128]{0,1:T(8,128)(2,1)S(1)}, u32[]{:S(2)}, u32[]{:S(2)}) collective-permute-start(bf16[2048,128]{0,1:T(8,128)(2,1)S(1)} %get-tuple-element.35), channel_id=1, source_target_pairs={{0,2},{1,3},{2,0},{3,1},{4,6},{5,7},{6,4},{7,5},{8,10},{9,11},{10,... | collective-permute-start | bytes 1572872 | tf_op jit(solution)/shard_map/ppermute | solution.py:128
  165.6 26.4 %collective-permute-start.7 = (bf16[2048,128]{0,1:T(8,128)(2,1)S(1)}, bf16[2048,128]{0,1:T(8,128)(2,1)S(1)}, u32[]{:S(2)}, u32[]{:S(2)}) collective-permute-start(bf16[2048,128]{0,1:T(8,128)(2,1)S(1)} %get-tuple-element.34), channel_id=1, source_target_pairs={{0,3},{1,0},{2,1},{3,2},{4,7},{5,4},{6,5},{7,6},{8,11},{9,8},{10,9... | collective-permute-start | bytes 1572872 | tf_op jit(solution)/shard_map/ppermute | solution.py:128
  168.8 32.0 %collective-permute-start.9 = (bf16[2048,128]{0,1:T(8,128)(2,1)S(1)}, bf16[2048,128]{0,1:T(8,128)(2,1)S(1)}, u32[]{:S(2)}, u32[]{:S(2)}) collective-permute-start(bf16[2048,128]{0,1:T(8,128)(2,1)S(1)} %get-tuple-element.33), channel_id=1, source_target_pairs={{0,1},{1,2},{2,3},{3,0},{4,5},{5,6},{6,7},{7,4},{8,9},{9,10},{10,1... | collective-permute-start | bytes 1572872 | tf_op jit(solution)/shard_map/ppermute | solution.py:128
  170.3 42.1 %collective-permute-start.10 = (bf16[2048,128]{0,1:T(8,128)(2,1)S(1)}, bf16[2048,128]{0,1:T(8,128)(2,1)S(1)}, u32[]{:S(2)}, u32[]{:S(2)}) collective-permute-start(bf16[2048,128]{0,1:T(8,128)(2,1)S(1)} %get-tuple-element.32), channel_id=1, source_target_pairs={{0,2},{1,3},{2,0},{3,1},{4,6},{5,7},{6,4},{7,5},{8,10},{9,11},{10,... | collective-permute-start | bytes 1572872 | tf_op jit(solution)/shard_map/ppermute | solution.py:128
  178.4 34.8 %collective-permute-start.11 = (bf16[2048,128]{0,1:T(8,128)(2,1)S(1)}, bf16[2048,128]{0,1:T(8,128)(2,1)S(1)}, u32[]{:S(2)}, u32[]{:S(2)}) collective-permute-start(bf16[2048,128]{0,1:T(8,128)(2,1)S(1)} %get-tuple-element.31), channel_id=1, source_target_pairs={{0,3},{1,0},{2,1},{3,2},{4,7},{5,4},{6,5},{7,6},{8,11},{9,8},{10,9... | collective-permute-start | bytes 1572872 | tf_op jit(solution)/shard_map/ppermute | solution.py:128

commit v15 on v11

--- a/solution.py
+++ b/solution.py
@@ -84,8 +84,8 @@
     z_lanes, query_rows = lax.optimization_barrier((z_lanes, query_rows))
     z_rows = lax.all_to_all(z_lanes, "seq", split_axis=1, concat_axis=0, tiled=True)
     z_wide = z_rows.astype(jnp.float32)
-    grad_key = z_wide * value_part.T.astype(jnp.float32)
-    grad_value = z_wide * key_part.T.astype(jnp.float32)
+    grad_key = z_wide * lanes_first(value_part)
+    grad_value = z_wide * lanes_first(key_part)
     count = lax.axis_size("chan")
     out = jnp.zeros((block_rows // count, 3, count * channels), jnp.bfloat16)
     for source, piece in query_rows:
@@ -95,6 +95,21 @@
         for source, piece in spread_lanes(filtered, "chan"):
             out = lax.dynamic_update_slice(out, piece.T[:, None, :], (0, plane, source * channels))
     return out
+
+
+def transpose_kernel(x_ref, o_ref):
+    o_ref[...] = x_ref[...].astype(jnp.float32).T
+
+
+def lanes_first(rows):
+    count, width = rows.shape
+    return pl.pallas_call(
+        transpose_kernel,
+        out_shape=jax.ShapeDtypeStruct((width, count), jnp.float32),
+        grid=(width // block,),
+        in_specs=[pl.BlockSpec((count, block), lambda j: (0, j))],
+        out_specs=pl.BlockSpec((block, count), lambda j: (j, 0)),
+    )(rows)
 
 
 def lane_filter(lanes, taps):

time: 219 us -> 234 us (1.068)
  waiting for transfers between devices: 105 us -> 81.8 us
  other arithmetic: 22.4 us -> 37.5 us
  Pallas kernels: 15.3 us -> 28.1 us
  local copies, waits for them, and re-layouts: 35.7 us -> 47.9 us
    convert_element_type x2, other arithmetic: 3.23 us -> 18.6 us  [lane_filter(): return result.astype(jnp.bfloat16)]
    all_to_all x1, waiting for transfers between devices: 37.7 us -> 23.8 us  [on_device(): lax.all_to_all(z_lanes, 'seq', split_axis=1, concat_axis=0, tiled=True)]
    pallas_call x0 -> x2, Pallas kernels: none -> 12.8 us  [lanes_first(): pl.pallas_call(transpose_kernel, out_shape=jax.ShapeDtypeStruct((width, c...]
    ppermute x6, waiting for transfers between devices: 34.1 us -> 24.7 us  [spread_lanes(): lax.ppermute(outgoing, axis, pairs)]
    broadcast_in_dim x0 -> x8, local copies, waits for them, and re-layouts: none -> 5.61 us  [on_device(): piece.T[:, None, :]]
    convert_element_type x1 -> x0, local copies, waits for them, and re-layouts: 5.48 us -> none  [on_device(): z_wide = z_rows.astype(jnp.float32)]
    squeeze x0 -> x1, local copies, waits for them, and re-layouts: none -> 4.85 us  [on_device(): key_part = qkv_saved[:, 1, :]]
    convert_element_type x1 -> x0, other arithmetic: 2.53 us -> none  [on_device(): z_wide = z_rows.astype(jnp.float32)]
  transfers between devices with their start and end apart: 15 -> 15, of which waited for: 7 -> 7; matrix products, arithmetic and copies ran while one was open for 19% -> 28% of each run, Pallas kernels for 7% -> 12%
where the time goes in v15:
time: 234 us; the launch traced here: 229 us
  waiting for transfers between devices  81.8 us (35%)
  local copies, waits for them, and re-layouts  47.9 us (20%)
  other arithmetic  37.5 us (16%)
  starting transfers between devices  33.8 us (14%)
  Pallas kernels  28.1 us (12%)
    all_to_all x1, waiting for transfers between devices, on_device(): lax.all_to_all(grad_mixed.T, 'seq', split_axis=0, concat_axis=1, tiled=True)  31.9 us
    ppermute x6, waiting for transfers between devices, spread_lanes(): lax.ppermute(outgoing, axis, pairs)  24.7 us
    all_to_all x1, waiting for transfers between devices, on_device(): lax.all_to_all(z_lanes, 'seq', split_axis=1, concat_axis=0, tiled=True)  23.8 us
    convert_element_type x2, other arithmetic, lane_filter(): return result.astype(jnp.bfloat16)  18.6 us
    pallas_call x1, Pallas kernels, correlate(): pl.pallas_call(correlate_kernel, out_shape=jax.ShapeDtypeStruct((channels...  15.3 us
    pallas_call x2, Pallas kernels, lanes_first(): pl.pallas_call(transpose_kernel, out_shape=jax.ShapeDtypeStruct((width, c...  12.8 us
    all_to_all x1, starting transfers between devices, on_device(): lax.all_to_all(z_lanes, 'seq', split_axis=1, concat_axis=0, tiled=True)  6.8 us
    mul x1, other arithmetic, on_device(): grad_value = z_wide * lanes_first(key_part)  6.66 us
  transfers between devices with their start and end apart: 15, of which 7 were waited for; matrix products, arithmetic and copies ran while one was open for 28% of the time, Pallas kernels for 12%

profile of v15, /device:TPU:18, one launch (start us, length us, event | category | flops | bytes accessed | tf_op | source)
XLA Modules:
  0.0 229.3 jit_solution(13105433735934047407)
XLA Ops:
  0.0 1.6 copy.39
  1.6 5.2 %all-to-all-start.1 = ((bf16[512,8,16]{0,2,1:T(8,128)(2,1)}), bf16[512,8,16]{0,2,1:T(8,128)(2,1)S(1)}, u32[]{:S(2)}, u32[]{:S(2)}) async-start(bf16[512,8,16]{0,2,1:T(8,128)(2,1)} %bitcast.5), calls=%async_computation.1 | async-start | bytes 262144 | tf_op jit(solution)/shard_map/all_to_all | solution.py:79
  6.9 6.3 %fusion.19 = (f32[512,1,2048]{2,0,1:T(8,128)}, f32[512,2048]{1,0:T(8,128)S(1)}, bf16[512,2048]{1,0:T(8,128)(2,1)S(1)}) fusion(bf16[512,2048]{1,0:T(8,128)(2,1)} %param.7, bf16[512,2048]{1,0:T(8,128)(2,1)} %param.5, bf16[512,3,2048]{2,0,1:T(8,128)(2,1)} %param.6), kind=kLoop, calls=%fused_computation.61 | loop fusion | flops 6291456 | bytes 16777216 | tf_op jit(solution)/shard_map/broadcast_in_dim | solution.py:81
  13.2 2.2 collective-permute-start
  15.4 1.4 collective-permute-done
  16.8 2.5 %copy.37 = bf16[2048,512]{1,0:T(8,128)(2,1)} copy(bf16[2048,512]{0,1:T(8,128)(2,1)S(1)} %bitcast.83) | data formatting | bytes 4194304 | tf_op jit(solution)/shard_map/transpose | solution.py:78
  19.3 5.4 %all-to-all-start = ((bf16[8,256,512]{2,1,0:T(8,128)(2,1)}), bf16[8,256,512]{2,1,0:T(8,128)(2,1)S(1)}, u32[]{:S(2)}, u32[]{:S(2)}) async-start(bf16[8,256,512]{2,1,0:T(8,128)(2,1)} %bitcast.3), calls=%async_computation | async-start | bytes 4194304 | tf_op jit(solution)/shard_map/all_to_all | solution.py:78
  24.7 5.8 %fusion.4 = bf16[512,1,2048]{2,0,1:T(8,128)(2,1)S(1)} fusion(f32[512,1,2048]{2,0,1:T(8,128)} %get-tuple-element.29, f32[2,1,2048]{2,0,1:T(2,128)S(1)} %collective-permute-done, f32[2048]{0:T(1024)S(1)} %bitcast.96, f32[2048]{0:T(1024)S(1)} %bitcast.97, f32[2048]{0:T(1024)S(1)} %bitcast.98, bf16[512,2048]{1,0:T(8,128)(2,1)} %param.7, bf16[512,2048]{1,0:T(8,128)(2,1)} %param.5), kind=kLoop, calls=%fused_computation.12 | loop fusion | flops 11534336 | bytes 10526720 | tf_op jit(solution)/shard_map/convert_element_type | solution.py:172
  30.6 1.2 dynamic-slice_bitcast_fusion.2
  31.7 1.5 collective-permute-start.1
  33.2 0.5 collective-permute-start.2
  33.7 1.5 collective-permute-start.3
  35.3 2.3 rev.3
  37.7 0.9 reshape.46.h_ref
  38.6 31.9 %all-to-all-done = bf16[8,256,512]{2,1,0:T(8,128)(2,1)S(1)} async-done(((bf16[8,256,512]{2,1,0:T(8,128)(2,1)}), bf16[8,256,512]{2,1,0:T(8,128)(2,1)S(1)}, u32[]{:S(2)}, u32[]{:S(2)}) %all-to-all-start) | async-done | bytes 2097184 | tf_op jit(solution)/shard_map/all_to_all | solution.py:78
  70.4 1.6 copy.59
  72.0 15.3 %shard_map.55 = bf16[256,4096]{1,0:T(8,128)(2,1)} custom-call(bf16[256,4096]{1,0:T(8,128)(2,1)} %bitcast.85, f32[16,1,4352]{2,1,0:T(1,128)} %reshape.46.h_ref), custom_call_target="tpu_custom_call" | custom-call | flops 4563402752 | bytes 4472832 | tf_op jit(solution)/shard_map/pallas_call | solution.py:48
  87.3 3.2 %copy.62 = bf16[32,8,8,512]{3,2,0,1:T(8,128)(2,1)} copy(bf16[32,8,8,512]{3,2,1,0:T(8,128)(2,1)} %bitcast.84) | data formatting | bytes 4194304 | tf_op jit(solution)/shard_map/all_to_all | solution.py:85
  90.5 6.8 %all-to-all-start.2 = ((bf16[256,8,512]{2,0,1:T(8,128)(2,1)}), bf16[256,8,512]{2,0,1:T(8,128)(2,1)S(1)}, u32[]{:S(2)}, u32[]{:S(2)}) async-start(bf16[256,8,512]{2,0,1:T(8,128)(2,1)} %bitcast.81), calls=%async_computation.2 | async-start | bytes 4194304 | tf_op jit(solution)/shard_map/all_to_all | solution.py:85
  97.3 4.9 %slice_bitcast_fusion = (bf16[512,2048]{1,0:T(8,128)(2,1)}, bf16[512,2048]{1,0:T(8,128)(2,1)}) fusion(bf16[512,3,2048]{2,0,1:T(8,128)(2,1)} %param.6), kind=kLoop, calls=%fused_computation.33 | loop fusion | bytes 8388608 | tf_op jit(solution)/shard_map/squeeze | solution.py:71
  102.2 6.4 %shard_map.56 = f32[2048,512]{1,0:T(8,128)} custom-call(bf16[512,2048]{1,0:T(8,128)(2,1)} %get-tuple-element.28.x_ref), custom_call_target="tpu_custom_call" | custom-call | tf_op jit(solution)/shard_map/pallas_call | solution.py:106
  108.6 6.4 %shard_map.57 = f32[2048,512]{1,0:T(8,128)} custom-call(bf16[512,2048]{1,0:T(8,128)(2,1)} %get-tuple-element.27.x_ref), custom_call_target="tpu_custom_call" | custom-call | tf_op jit(solution)/shard_map/pallas_call | solution.py:106
  115.0 3.4 %broadcast_in_dim.34 = bf16[128,3,8192]{2,0,1:T(8,128)(2,1)} broadcast(bf16[]{:T(256)} %constant.83.clone.1), dimensions={} | broadcast | bytes 6291458 | tf_op jit(solution)/shard_map/broadcast_in_dim | solution.py:90
  118.5 0.8 constant_dynamic-update-slice_fusion.11
  119.3 23.8 %all-to-all-done.2 = bf16[256,8,512]{2,0,1:T(8,128)(2,1)S(1)} async-done(((bf16[256,8,512]{2,0,1:T(8,128)(2,1)}), bf16[256,8,512]{2,0,1:T(8,128)(2,1)S(1)}, u32[]{:S(2)}, u32[]{:S(2)}) %all-to-all-start.2) | async-done | bytes 2097184 | tf_op jit(solution)/shard_map/all_to_all | solution.py:85
  143.1 6.7 %bitcast_multiply_fusion = (f32[2048,512]{1,0:T(8,128)}, f32[2048,512]{1,0:T(8,128)S(1)}) fusion(f32[2048,512]{1,0:T(8,128)} %shard_map.57, bf16[256,8,512]{2,0,1:T(8,128)(2,1)S(1)} %all-to-all-done.2, f32[2048,512]{1,0:T(8,128)} %shard_map.56), kind=kLoop, calls=%fused_computation.30 | loop fusion | flops 3145728 | bytes 18874368 | tf_op jit(solution)/shard_map/mul | solution.py:88
  149.7 1.9 copy-done
  151.8 0.3 copy.46
  152.2 1.9 collective-permute-start.4
  154.1 1.9 constant_dynamic-update-slice_fusion.10
  156.0 1.3 slice.108
  157.3 0.3 copy.52
  157.6 2.4 %collective-permute-start.8 = (f32[2048,2]{0,1:T(2,128)S(1)}, f32[2048,2]{0,1:T(2,128)S(1)}, u32[]{:S(2)}, u32[]{:S(2)}) collective-permute-start(f32[2048,2]{0,1:T(2,128)S(1)} %copy.52), channel_id=1, source_target_pairs={{4,0},{8,4},{12,8},{16,12},{20,16},{24,20},{28,24},{5,1},{9,5},{13... | collective-permute-start | bytes 49160 | tf_op jit(solution)/shard_map/ppermute | solution.py:17
  160.0 0.4 copy.47
  160.4 9.3 %fusion.14 = bf16[2048,512]{1,0:T(8,128)(2,1)S(1)} fusion(f32[2048,512]{1,0:T(8,128)} %copy-done, f32[2048,2]{1,0:T(8,128)S(1)} %copy.47, f32[2048]{0:T(1024)S(1)} %bitcast.93, f32[2048]{0:T(1024)S(1)} %bitcast.94, f32[2048]{0:T(1024)S(1)} %bitcast.95), kind=kLoop, calls=%fused_computation.22 | loop fusion | flops 8388608 | bytes 6332416 | tf_op jit(solution)/shard_map/convert_element_type | solution.py:123
  169.7 1.4 constant_dynamic-slice_fusion.3
  171.1 1.5 collective-permute-start.5
  172.6 0.5 collective-permute-start.6
  173.1 1.5 collective-permute-start.7
  174.6 0.4 copy.53
  175.0 9.3 %fusion.9 = bf16[2048,512]{1,0:T(8,128)(2,1)S(1)} fusion(f32[2048,512]{1,0:T(8,128)} %get-tuple-element.35, f32[2048,2]{1,0:T(8,128)S(1)} %copy.53, f32[2048]{0:T(1024)S(1)} %bitcast.91, f32[2048]{0:T(1024)S(1)} %bitcast.92, f32[2048]{0:T(1024)S(1)} %bitcast.90), kind=kLoop, calls=%fused_computation.17 | loop fusion | flops 8388608 | bytes 6332416 | tf_op jit(solution)/shard_map/convert_element_type | solution.py:123
  184.3 1.4 constant_dynamic-slice_fusion
  185.7 1.4 collective-permute-start.9
  187.0 1.5 collective-permute-start.10
  188.6 1.9 constant_dynamic-update-slice_fusion.9
  190.5 1.9 constant_dynamic-update-slice_fusion.8
  192.3 0.2 copy.54
  192.6 0.2 copy.48
  192.8 0.8 constant_dynamic-update-slice_fusion.7
  193.8 3.4 %collective-permute-done.6 = bf16[2048,128]{1,0:T(8,128)(2,1)S(1)} collective-permute-done((bf16[2048,128]{1,0:T(8,128)(2,1)}, bf16[2048,128]{1,0:T(8,128)(2,1)S(1)}, u32[]{:S(2)}, u32[]{:S(2)}) %collective-permute-start.6) | collective-permute-done | bytes 524320 | tf_op jit(solution)/shard_map/ppermute | solution.py:138
  197.2 0.2 copy.50
  197.5 0.9 collective-permute-done.7
  198.5 10.2 %collective-permute-done.9 = bf16[2048,128]{1,0:T(8,128)(2,1)} collective-permute-done((bf16[2048,128]{1,0:T(8,128)(2,1)}, bf16[2048,128]{1,0:T(8,128)(2,1)}, u32[]{:S(2)}, u32[]{:S(2)}) %collective-permute-start.9) | collective-permute-done | bytes 524320 | tf_op jit(solution)/shard_map/ppermute | solution.py:138
  208.7 1.2 copy.55
  210.0 10.2 %collective-permute-done.10 = bf16[2048,128]{1,0:T(8,128)(2,1)} collective-permute-done((bf16[2048,128]{1,0:T(8,128)(2,1)}, bf16[2048,128]{1,0:T(8,128)(2,1)}, u32[]{:S(2)}, u32[]{:S(2)}) %collective-permute-start.10) | collective-permute-done | bytes 524320 | tf_op jit(solution)/shard_map/ppermute | solution.py:138
  220.2 1.2 copy.56
  221.5 2.1 copy.57
  223.5 0.8 constant_dynamic-update-slice_fusion.6
  224.4 0.8 constant_dynamic-update-slice_fusion.5
  225.2 0.8 constant_dynamic-update-slice_fusion.4
  226.0 0.8 constant_dynamic-update-slice_fusion.3
  226.8 0.8 constant_dynamic-update-slice_fusion.2
  227.7 0.8 constant_dynamic-update-slice_fusion.1
  228.5 0.8 constant_dynamic-update-slice_fusion
  (22 shorter events, 0.8 us)
Async XLA Ops:
  1.6 17.7 %all-to-all-start.1 = ((bf16[512,8,16]{0,2,1:T(8,128)(2,1)}), bf16[512,8,16]{0,2,1:T(8,128)(2,1)S(1)}, u32[]{:S(2)}, u32[]{:S(2)}) async-start(bf16[512,8,16]{0,2,1:T(8,128)(2,1)} %bitcast.5), calls=%async_computation.1 | async-start | bytes 262144 | tf_op jit(solution)/shard_map/all_to_all | solution.py:79
  13.2 3.6 %collective-permute-start = (f32[2,1,2048]{2,0,1:T(2,128)S(1)}, f32[2,1,2048]{2,0,1:T(2,128)S(1)}, u32[]{:S(2)}, u32[]{:S(2)}) collective-permute-start(f32[2,1,2048]{2,0,1:T(2,128)S(1)} %slice_bitcast_fusion.2), channel_id=1, source_target_pairs={{4,0},{8,4},{12,8},{16,12},{20,16},{24,20},{28,24},{5,1},{9,5},{13... | collective-permute-start | bytes 49160 | tf_op jit(solution)/shard_map/ppermute | solution.py:17
  16.8 7.9 %copy-start.2 = (f32[3,3,2048]{2,1,0:T(4,128)S(1)}, f32[3,3,2048]{2,1,0:T(4,128)}, u32[]{:S(2)}) copy-start(f32[3,3,2048]{2,1,0:T(4,128)} %param.9) | copy-start | bytes 221188
  19.3 51.1 %all-to-all-start = ((bf16[8,256,512]{2,1,0:T(8,128)(2,1)}), bf16[8,256,512]{2,1,0:T(8,128)(2,1)S(1)}, u32[]{:S(2)}, u32[]{:S(2)}) async-start(bf16[8,256,512]{2,1,0:T(8,128)(2,1)} %bitcast.3), calls=%async_computation | async-start | bytes 4194304 | tf_op jit(solution)/shard_map/all_to_all | solution.py:78
  31.7 55.6 %collective-permute-start.1 = (bf16[128,1,2048]{2,0,1:T(8,128)(2,1)}, bf16[128,1,2048]{2,0,1:T(8,128)(2,1)}, u32[]{:S(2)}, u32[]{:S(2)}) collective-permute-start(bf16[128,1,2048]{2,0,1:T(8,128)(2,1)} %get-tuple-element.43), channel_id=1, source_target_pairs={{0,1},{1,2},{2,3},{3,0},{4,5},{5,6},{6,7},{7,4},{8,9},{9,10},{10,1... | collective-permute-start | bytes 1572872 | tf_op jit(solution)/shard_map/ppermute | solution.py:151
  33.2 54.1 %collective-permute-start.2 = (bf16[128,1,2048]{2,0,1:T(8,128)(2,1)}, bf16[128,1,2048]{2,0,1:T(8,128)(2,1)}, u32[]{:S(2)}, u32[]{:S(2)}) collective-permute-start(bf16[128,1,2048]{2,0,1:T(8,128)(2,1)} %get-tuple-element.42), channel_id=1, source_target_pairs={{0,2},{1,3},{2,0},{3,1},{4,6},{5,7},{6,4},{7,5},{8,10},{9,11},{10,... | collective-permute-start | bytes 1572872 | tf_op jit(solution)/shard_map/ppermute | solution.py:151
  33.7 53.6 %collective-permute-start.3 = (bf16[128,1,2048]{2,0,1:T(8,128)(2,1)}, bf16[128,1,2048]{2,0,1:T(8,128)(2,1)}, u32[]{:S(2)}, u32[]{:S(2)}) collective-permute-start(bf16[128,1,2048]{2,0,1:T(8,128)(2,1)} %get-tuple-element.41), channel_id=1, source_target_pairs={{0,3},{1,0},{2,1},{3,2},{4,7},{5,4},{6,5},{7,6},{8,11},{9,8},{10,9... | collective-permute-start | bytes 1572872 | tf_op jit(solution)/shard_map/ppermute | solution.py:151
  90.5 52.6 %all-to-all-start.2 = ((bf16[256,8,512]{2,0,1:T(8,128)(2,1)}), bf16[256,8,512]{2,0,1:T(8,128)(2,1)S(1)}, u32[]{:S(2)}, u32[]{:S(2)}) async-start(bf16[256,8,512]{2,0,1:T(8,128)(2,1)} %bitcast.81), calls=%async_computation.2 | async-start | bytes 4194304 | tf_op jit(solution)/shard_map/all_to_all | solution.py:85
  149.7 1.9 copy-start
  152.2 7.8 %collective-permute-start.4 = (f32[2048,2]{0,1:T(2,128)S(1)}, f32[2048,2]{0,1:T(2,128)S(1)}, u32[]{:S(2)}, u32[]{:S(2)}) collective-permute-start(f32[2048,2]{0,1:T(2,128)S(1)} %copy.46), channel_id=1, source_target_pairs={{4,0},{8,4},{12,8},{16,12},{20,16},{24,20},{28,24},{5,1},{9,5},{13... | collective-permute-start | bytes 49160 | tf_op jit(solution)/shard_map/ppermute | solution.py:17
  157.6 17.0 %collective-permute-start.8 = (f32[2048,2]{0,1:T(2,128)S(1)}, f32[2048,2]{0,1:T(2,128)S(1)}, u32[]{:S(2)}, u32[]{:S(2)}) collective-permute-start(f32[2048,2]{0,1:T(2,128)S(1)} %copy.52), channel_id=1, source_target_pairs={{4,0},{8,4},{12,8},{16,12},{20,16},{24,20},{28,24},{5,1},{9,5},{13... | collective-permute-start | bytes 49160 | tf_op jit(solution)/shard_map/ppermute | solution.py:17
  171.1 17.5 %collective-permute-start.5 = (bf16[2048,128]{1,0:T(8,128)(2,1)}, bf16[2048,128]{1,0:T(8,128)(2,1)S(1)}, u32[]{:S(2)}, u32[]{:S(2)}) collective-permute-start(bf16[2048,128]{1,0:T(8,128)(2,1)} %get-tuple-element.39), channel_id=1, source_target_pairs={{0,1},{1,2},{2,3},{3,0},{4,5},{5,6},{6,7},{7,4},{8,9},{9,10},{10,1... | collective-permute-start | bytes 1572872 | tf_op jit(solution)/shard_map/ppermute | solution.py:138
  172.6 24.7 %collective-permute-start.6 = (bf16[2048,128]{1,0:T(8,128)(2,1)}, bf16[2048,128]{1,0:T(8,128)(2,1)S(1)}, u32[]{:S(2)}, u32[]{:S(2)}) collective-permute-start(bf16[2048,128]{1,0:T(8,128)(2,1)} %get-tuple-element.38), channel_id=1, source_target_pairs={{0,2},{1,3},{2,0},{3,1},{4,6},{5,7},{6,4},{7,5},{8,10},{9,11},{10,... | collective-permute-start | bytes 1572872 | tf_op jit(solution)/shard_map/ppermute | solution.py:138
  173.1 25.2 %collective-permute-start.7 = (bf16[2048,128]{1,0:T(8,128)(2,1)}, bf16[2048,128]{1,0:T(8,128)(2,1)S(1)}, u32[]{:S(2)}, u32[]{:S(2)}) collective-permute-start(bf16[2048,128]{1,0:T(8,128)(2,1)} %get-tuple-element.37), channel_id=1, source_target_pairs={{0,3},{1,0},{2,1},{3,2},{4,7},{5,4},{6,5},{7,6},{8,11},{9,8},{10,9... | collective-permute-start | bytes 1572872 | tf_op jit(solution)/shard_map/ppermute | solution.py:138
  185.7 23.0 %collective-permute-start.9 = (bf16[2048,128]{1,0:T(8,128)(2,1)}, bf16[2048,128]{1,0:T(8,128)(2,1)}, u32[]{:S(2)}, u32[]{:S(2)}) collective-permute-start(bf16[2048,128]{1,0:T(8,128)(2,1)} %get-tuple-element.33), channel_id=1, source_target_pairs={{0,1},{1,2},{2,3},{3,0},{4,5},{5,6},{6,7},{7,4},{8,9},{9,10},{10,1... | collective-permute-start | bytes 1572872 | tf_op jit(solution)/shard_map/ppermute | solution.py:138
  187.0 33.2 %collective-permute-start.10 = (bf16[2048,128]{1,0:T(8,128)(2,1)}, bf16[2048,128]{1,0:T(8,128)(2,1)}, u32[]{:S(2)}, u32[]{:S(2)}) collective-permute-start(bf16[2048,128]{1,0:T(8,128)(2,1)} %get-tuple-element.32), channel_id=1, source_target_pairs={{0,2},{1,3},{2,0},{3,1},{4,6},{5,7},{6,4},{7,5},{8,10},{9,11},{10,... | collective-permute-start | bytes 1572872 | tf_op jit(solution)/shard_map/ppermute | solution.py:138
  188.6 32.9 %collective-permute-start.11 = (bf16[2048,128]{1,0:T(8,128)(2,1)}, bf16[2048,128]{1,0:T(8,128)(2,1)}, u32[]{:S(2)}, u32[]{:S(2)}) collective-permute-start(bf16[2048,128]{1,0:T(8,128)(2,1)} %get-tuple-element.31), channel_id=1, source_target_pairs={{0,3},{1,0},{2,1},{3,2},{4,7},{5,4},{6,5},{7,6},{8,11},{9,8},{10,9... | collective-permute-start | bytes 1572872 | tf_op jit(solution)/shard_map/ppermute | solution.py:138
  223.5 5.0 %copy-start.1 = (bf16[128,1,2048]{2,0,1:T(8,128)(2,1)S(1)}, bf16[128,1,2048]{2,0,1:T(8,128)(2,1)}, u32[]{:S(2)}) copy-start(bf16[128,1,2048]{2,0,1:T(8,128)(2,1)} %copy.57) | copy-start | bytes 1572868

commit v16 on v11

--- a/solution.py
+++ b/solution.py
@@ -34,10 +34,11 @@
         acc_ref[:rows, :] += jnp.dot(source, band, preferred_element_type=jnp.float32)
     for index in range(blocks):
         slab = acc_ref[per_group * index : per_group * (index + 1), :]
-        o_ref[:, block * index : block * (index + 1)] = slab.astype(o_ref.dtype)
+        first = block * index
+        o_ref[first // o_ref.shape[2], :, pl.ds(first % o_ref.shape[2], block)] = slab.astype(o_ref.dtype)
 
 
-def correlate(grads, taps):
+def correlate(grads, taps, span):
     channels, tokens = grads.shape
     groups = taps.shape[1]
     blocks = tokens // block
@@ -47,13 +48,13 @@
     flops = 2 * groups * per_group * block * block * blocks * (blocks + 1) // 2
     return pl.pallas_call(
         correlate_kernel,
-        out_shape=jax.ShapeDtypeStruct((channels, tokens), jnp.bfloat16),
+        out_shape=jax.ShapeDtypeStruct((tokens // span, channels, span), jnp.bfloat16),
         grid=(groups,),
         in_specs=[
             pl.BlockSpec((per_group, tokens), lambda g: (g, 0)),
             pl.BlockSpec((1, 1, tokens + block), lambda g: (g, 0, 0)),
         ],
-        out_specs=pl.BlockSpec((per_group, tokens), lambda g: (g, 0)),
+        out_specs=pl.BlockSpec((tokens // span, per_group, span), lambda g: (0, g, 0)),
         scratch_shapes=[
             pltpu.VMEM((blocks * per_group, block), jnp.float32),
             pltpu.VMEM((blocks * per_group, block), jnp.bfloat16),
@@ -80,9 +81,10 @@
     short_len = short_taps.shape[1]
     query_proj = short_filter(grad_query[:, None], short_taps[:1], block_rows, query_next)
     query_rows = spread_rows(query_proj, "chan")
-    z_lanes = correlate(mixed_cols, taps_cols)
+    z_lanes = correlate(mixed_cols, taps_cols, block_rows)
     z_lanes, query_rows = lax.optimization_barrier((z_lanes, query_rows))
-    z_rows = lax.all_to_all(z_lanes, "seq", split_axis=1, concat_axis=0, tiled=True)
+    z_rows = lax.all_to_all(z_lanes, "seq", split_axis=0, concat_axis=0, tiled=True)
+    z_rows = z_rows.reshape(-1, block_rows)
     z_wide = z_rows.astype(jnp.float32)
     grad_key = z_wide * value_part.T.astype(jnp.float32)
     grad_value = z_wide * key_part.T.astype(jnp.float32)

time: 219 us -> 216 us (0.986)
  local copies, waits for them, and re-layouts: 35.7 us -> 32.6 us
    all_to_all x1 -> x0, local copies, waits for them, and re-layouts: 3.1 us -> none  [on_device(): lax.all_to_all(z_lanes, 'seq', split_axis=1, concat_axis=0, tiled=True)]
where the time goes in v16:
time: 216 us; the launch traced here: 211 us
  waiting for transfers between devices  105 us (49%)
  starting transfers between devices  35.4 us (16%)
  local copies, waits for them, and re-layouts  32.6 us (15%)
  other arithmetic  22.6 us (10%)
  Pallas kernels  15.3 us (7%)
    all_to_all x1, waiting for transfers between devices, on_device(): lax.all_to_all(z_lanes, 'seq', split_axis=0, concat_axis=0, tiled=True)  37.7 us
    ppermute x6, waiting for transfers between devices, spread_lanes(): lax.ppermute(outgoing, axis, pairs)  34.1 us
    all_to_all x1, waiting for transfers between devices, on_device(): lax.all_to_all(grad_mixed.T, 'seq', split_axis=0, concat_axis=1, tiled=True)  32 us
    pallas_call x1, Pallas kernels, correlate(): pl.pallas_call(correlate_kernel, out_shape=jax.ShapeDtypeStruct((tokens /...  15.3 us
    ppermute x6, starting transfers between devices, spread_lanes(): lax.ppermute(outgoing, axis, pairs)  8.03 us
    all_to_all x1, starting transfers between devices, on_device(): lax.all_to_all(z_lanes, 'seq', split_axis=0, concat_axis=0, tiled=True)  6.81 us
    dynamic_update_slice x8, local copies, waits for them, and re-layouts, on_device(): lax.dynamic_update_slice(out, piece.T[:, None, :], (0, plane, source * ch...  6.62 us
    dynamic_update_slice x4, local copies, waits for them, and re-layouts, on_device(): out = lax.dynamic_update_slice(out, piece, (0, 0, source * channels))  6.47 us
  transfers between devices with their start and end apart: 15, of which 7 were waited for; matrix products, arithmetic and copies ran while one was open for 19% of the time, Pallas kernels for 7%

profile of v16, /device:TPU:18, one launch (start us, length us, event | category | flops | bytes accessed | tf_op | source)
XLA Modules:
  0.0 211.4 jit_solution(7331475369485578715)
XLA Ops:
  0.0 1.7 copy.25
  1.7 5.2 %all-to-all-start.1 = ((bf16[512,8,16]{0,2,1:T(8,128)(2,1)}), bf16[512,8,16]{0,2,1:T(8,128)(2,1)S(1)}, u32[]{:S(2)}, u32[]{:S(2)}) async-start(bf16[512,8,16]{0,2,1:T(8,128)(2,1)} %bitcast.5), calls=%async_computation.1 | async-start | bytes 262144 | tf_op jit(solution)/shard_map/all_to_all | solution.py:80
  6.9 6.3 %fusion.21 = (f32[512,1,2048]{2,0,1:T(8,128)}, f32[512,2048]{1,0:T(8,128)S(1)}, bf16[512,2048]{1,0:T(8,128)(2,1)S(1)}) fusion(bf16[512,2048]{1,0:T(8,128)(2,1)} %param.7, bf16[512,2048]{1,0:T(8,128)(2,1)} %param.5, bf16[512,3,2048]{2,0,1:T(8,128)(2,1)} %param.6), kind=kLoop, calls=%fused_computation.59 | loop fusion | flops 6291456 | bytes 16777216 | tf_op jit(solution)/shard_map/broadcast_in_dim | solution.py:82
  13.2 2.2 %collective-permute-start = (f32[2,1,2048]{2,0,1:T(2,128)S(1)}, f32[2,1,2048]{2,0,1:T(2,128)S(1)}, u32[]{:S(2)}, u32[]{:S(2)}) collective-permute-start(f32[2,1,2048]{2,0,1:T(2,128)S(1)} %slice_bitcast_fusion), channel_id=1, source_target_pairs={{4,0},{8,4},{12,8},{16,12},{20,16},{24,20},{28,24},{5,1},{9,5},{13... | collective-permute-start | bytes 49160 | tf_op jit(solution)/shard_map/ppermute | solution.py:17
  15.4 1.4 collective-permute-done
  16.8 0.0 copy-start
  16.8 2.5 %copy.23 = bf16[2048,512]{1,0:T(8,128)(2,1)} copy(bf16[2048,512]{0,1:T(8,128)(2,1)S(1)} %bitcast.92) | data formatting | bytes 4194304 | tf_op jit(solution)/shard_map/transpose | solution.py:79
  19.3 0.0 all-to-all-done.1
  19.3 5.4 %all-to-all-start = ((bf16[8,256,512]{2,1,0:T(8,128)(2,1)}), bf16[8,256,512]{2,1,0:T(8,128)(2,1)S(1)}, u32[]{:S(2)}, u32[]{:S(2)}) async-start(bf16[8,256,512]{2,1,0:T(8,128)(2,1)} %bitcast.3), calls=%async_computation | async-start | bytes 4194304 | tf_op jit(solution)/shard_map/all_to_all | solution.py:79
  24.7 0.0 copy-done
  24.7 0.1 fusion.22
  24.8 5.6 %fusion.14 = bf16[512,1,2048]{2,0,1:T(8,128)(2,1)S(1)} fusion(f32[512,1,2048]{2,0,1:T(8,128)} %get-tuple-element.29, f32[2,1,2048]{2,0,1:T(2,128)S(1)} %collective-permute-done, f32[2048]{0:T(1024)S(1)} %bitcast.101, f32[2048]{0:T(1024)S(1)} %bitcast.102, f32[2048]{0:T(1024)S(1)} %bitcast.103, bf16[512,2048]{1,0:T(8,128)(2,1)} %param.7, ...), kind=kLoop, calls=%fused_computation.22 | loop fusion | flops 11534336 | bytes 10526720 | tf_op jit(solution)/shard_map/convert_element_type | solution.py:159
  30.4 1.2 dynamic-slice_bitcast_fusion
  31.6 1.5 collective-permute-start.1
  33.1 0.5 collective-permute-start.2
  33.6 1.5 collective-permute-start.3
  35.2 2.3 %rev.3 = f32[16,4096]{1,0:T(8,128)S(1)} reverse(f32[16,4096]{1,0:T(8,128)S(1)} %bitcast.94), dimensions={1} | reverse | bytes 524288 | tf_op jit(solution)/shard_map/rev | solution.py:45
  37.5 0.1 concatenate.12
  37.5 0.9 reshape.48.h_ref
  38.4 32.0 %all-to-all-done = bf16[8,256,512]{2,1,0:T(8,128)(2,1)S(1)} async-done(((bf16[8,256,512]{2,1,0:T(8,128)(2,1)}), bf16[8,256,512]{2,1,0:T(8,128)(2,1)S(1)}, u32[]{:S(2)}, u32[]{:S(2)}) %all-to-all-start) | async-done | bytes 2097184 | tf_op jit(solution)/shard_map/all_to_all | solution.py:79
  70.5 1.6 copy.33
  72.1 15.3 %shard_map.55 = bf16[8,256,512]{2,1,0:T(8,128)(2,1)} custom-call(bf16[256,4096]{1,0:T(8,128)(2,1)} %bitcast.93, f32[16,1,4352]{2,1,0:T(1,128)} %reshape.48.h_ref), custom_call_target="tpu_custom_call" | custom-call | flops 4563402752 | bytes 4472832 | tf_op jit(solution)/shard_map/pallas_call | solution.py:49
  87.4 0.0 collective-permute-done.1
  87.4 0.0 collective-permute-done.2
  87.4 0.0 collective-permute-done.3
  87.4 6.8 %all-to-all-start.2 = ((bf16[8,256,512]{2,1,0:T(8,128)(2,1)}), bf16[8,256,512]{2,1,0:T(8,128)(2,1)S(1)}, u32[]{:S(2)}, u32[]{:S(2)}) async-start(bf16[8,256,512]{2,1,0:T(8,128)(2,1)} %shard_map.55), calls=%async_computation.2 | async-start | bytes 4194304 | tf_op jit(solution)/shard_map/all_to_all | solution.py:86
  94.2 3.4 %broadcast_in_dim.34 = bf16[128,3,8192]{2,0,1:T(8,128)(2,1)} broadcast(bf16[]{:T(256)} %constant.83.clone.1), dimensions={} | broadcast | bytes 6291458 | tf_op jit(solution)/shard_map/broadcast_in_dim | solution.py:92
  97.7 0.8 constant_dynamic-update-slice_fusion.3
  98.5 1.9 constant_dynamic-update-slice_fusion.2
  100.4 1.9 constant_dynamic-update-slice_fusion.1
  102.2 37.7 %all-to-all-done.2 = bf16[8,256,512]{2,1,0:T(8,128)(2,1)S(1)} async-done(((bf16[8,256,512]{2,1,0:T(8,128)(2,1)}), bf16[8,256,512]{2,1,0:T(8,128)(2,1)S(1)}, u32[]{:S(2)}, u32[]{:S(2)}) %all-to-all-start.2) | async-done | bytes 2097184 | tf_op jit(solution)/shard_map/all_to_all | solution.py:86
  140.0 2.7 %bitcast_convert_fusion = f32[2048,512]{1,0:T(8,128)} fusion(bf16[8,256,512]{2,1,0:T(8,128)(2,1)S(1)} %all-to-all-done.2), kind=kLoop, calls=%fused_computation.34 | loop fusion | flops 1048576 | bytes 6291456 | tf_op jit(solution)/shard_map/convert_element_type | solution.py:88
  142.6 5.5 %copy.31 = f32[2048,512]{0,1:T(8,128)} copy(f32[2048,512]{1,0:T(8,128)} %bitcast_convert_fusion) | data formatting | bytes 8388608 | tf_op jit(solution)/shard_map/convert_element_type | solution.py:88
  148.1 4.7 %fusion.19 = (f32[2048,512]{0,1:T(8,128)S(1)}, f32[2048,512]{0,1:T(8,128)S(1)}) fusion(f32[2048,512]{0,1:T(8,128)} %copy.31, bf16[512,3,2048]{2,0,1:T(8,128)(2,1)} %param.6), kind=kLoop, calls=%fused_computation.31 | loop fusion | flops 4194304 | bytes 16777216 | tf_op jit(solution)/shard_map/mul | solution.py:90
  152.8 1.9 collective-permute-start.4
  154.8 1.9 constant_dynamic-update-slice_fusion
  156.7 2.3 %collective-permute-start.8 = (f32[2048,2]{0,1:T(2,128)S(1)}, f32[2048,2]{0,1:T(2,128)S(1)}, u32[]{:S(2)}, u32[]{:S(2)}) collective-permute-start(f32[2048,2]{0,1:T(2,128)S(1)} %slice.108), channel_id=1, source_target_pairs={{4,0},{8,4},{12,8},{16,12},{20,16},{24,20},{28,24},{5,1},{9,5},{13... | collective-permute-start | bytes 49160 | tf_op jit(solution)/shard_map/ppermute | solution.py:17
  159.0 0.0 collective-permute-done.4
  159.1 1.6 fusion.9
  160.7 0.2 constant_dynamic-slice_fusion.2
  160.9 1.5 collective-permute-start.5
  162.4 0.5 collective-permute-start.6
  162.9 1.5 collective-permute-start.7
  164.5 0.0 collective-permute-done.8
  164.5 1.6 fusion.4
  166.1 0.1 constant_dynamic-slice_fusion.5
  166.2 1.4 collective-permute-start.9
  167.6 1.5 collective-permute-start.10
  169.2 0.8 bitcast_dynamic-update-slice_fusion.7
  170.0 5.7 %collective-permute-done.5 = bf16[2048,128]{0,1:T(8,128)(2,1)S(1)} collective-permute-done((bf16[2048,128]{0,1:T(8,128)(2,1)S(1)}, bf16[2048,128]{0,1:T(8,128)(2,1)S(1)}, u32[]{:S(2)}, u32[]{:S(2)}) %collective-permute-start.5) | collective-permute-done | bytes 524320 | tf_op jit(solution)/shard_map/ppermute | solution.py:125
  175.7 1.5 collective-permute-start.11
  177.2 0.8 bitcast_dynamic-update-slice_fusion.6
  178.0 10.4 %collective-permute-done.6 = bf16[2048,128]{0,1:T(8,128)(2,1)S(1)} collective-permute-done((bf16[2048,128]{0,1:T(8,128)(2,1)S(1)}, bf16[2048,128]{0,1:T(8,128)(2,1)S(1)}, u32[]{:S(2)}, u32[]{:S(2)}) %collective-permute-start.6) | collective-permute-done | bytes 524320 | tf_op jit(solution)/shard_map/ppermute | solution.py:125
  188.4 0.8 bitcast_dynamic-update-slice_fusion.5
  189.3 0.0 collective-permute-done.7
  189.3 0.8 bitcast_dynamic-update-slice_fusion.4
  190.1 0.8 bitcast_dynamic-update-slice_fusion.3
  190.9 7.3 %collective-permute-done.9 = bf16[2048,128]{0,1:T(8,128)(2,1)S(1)} collective-permute-done((bf16[2048,128]{0,1:T(8,128)(2,1)S(1)}, bf16[2048,128]{0,1:T(8,128)(2,1)S(1)}, u32[]{:S(2)}, u32[]{:S(2)}) %collective-permute-start.9) | collective-permute-done | bytes 524320 | tf_op jit(solution)/shard_map/ppermute | solution.py:125
  198.2 0.8 bitcast_dynamic-update-slice_fusion.2
  199.1 10.7 %collective-permute-done.10 = bf16[2048,128]{0,1:T(8,128)(2,1)S(1)} collective-permute-done((bf16[2048,128]{0,1:T(8,128)(2,1)S(1)}, bf16[2048,128]{0,1:T(8,128)(2,1)S(1)}, u32[]{:S(2)}, u32[]{:S(2)}) %collective-permute-start.10) | collective-permute-done | bytes 524320 | tf_op jit(solution)/shard_map/ppermute | solution.py:125
  209.7 0.8 bitcast_dynamic-update-slice_fusion.1
  210.6 0.0 collective-permute-done.11
  210.6 0.8 bitcast_dynamic-update-slice_fusion
  (5 shorter events, 0.1 us)
Async XLA Ops:
  1.7 17.7 %all-to-all-start.1 = ((bf16[512,8,16]{0,2,1:T(8,128)(2,1)}), bf16[512,8,16]{0,2,1:T(8,128)(2,1)S(1)}, u32[]{:S(2)}, u32[]{:S(2)}) async-start(bf16[512,8,16]{0,2,1:T(8,128)(2,1)} %bitcast.5), calls=%async_computation.1 | async-start | bytes 262144 | tf_op jit(solution)/shard_map/all_to_all | solution.py:80
  13.2 3.6 %collective-permute-start = (f32[2,1,2048]{2,0,1:T(2,128)S(1)}, f32[2,1,2048]{2,0,1:T(2,128)S(1)}, u32[]{:S(2)}, u32[]{:S(2)}) collective-permute-start(f32[2,1,2048]{2,0,1:T(2,128)S(1)} %slice_bitcast_fusion), channel_id=1, source_target_pairs={{4,0},{8,4},{12,8},{16,12},{20,16},{24,20},{28,24},{5,1},{9,5},{13... | collective-permute-start | bytes 49160 | tf_op jit(solution)/shard_map/ppermute | solution.py:17
  16.8 7.9 %copy-start = (f32[3,3,2048]{2,1,0:T(4,128)S(1)}, f32[3,3,2048]{2,1,0:T(4,128)}, u32[]{:S(2)}) copy-start(f32[3,3,2048]{2,1,0:T(4,128)} %param.9) | copy-start | bytes 221188
  19.3 51.1 %all-to-all-start = ((bf16[8,256,512]{2,1,0:T(8,128)(2,1)}), bf16[8,256,512]{2,1,0:T(8,128)(2,1)S(1)}, u32[]{:S(2)}, u32[]{:S(2)}) async-start(bf16[8,256,512]{2,1,0:T(8,128)(2,1)} %bitcast.3), calls=%async_computation | async-start | bytes 4194304 | tf_op jit(solution)/shard_map/all_to_all | solution.py:79
  31.6 55.8 %collective-permute-start.1 = (bf16[128,1,2048]{2,0,1:T(8,128)(2,1)}, bf16[128,1,2048]{2,0,1:T(8,128)(2,1)}, u32[]{:S(2)}, u32[]{:S(2)}) collective-permute-start(bf16[128,1,2048]{2,0,1:T(8,128)(2,1)} %get-tuple-element.39), channel_id=1, source_target_pairs={{0,1},{1,2},{2,3},{3,0},{4,5},{5,6},{6,7},{7,4},{8,9},{9,10},{10,1... | collective-permute-start | bytes 1572872 | tf_op jit(solution)/shard_map/ppermute | solution.py:138
  33.1 54.3 %collective-permute-start.2 = (bf16[128,1,2048]{2,0,1:T(8,128)(2,1)}, bf16[128,1,2048]{2,0,1:T(8,128)(2,1)}, u32[]{:S(2)}, u32[]{:S(2)}) collective-permute-start(bf16[128,1,2048]{2,0,1:T(8,128)(2,1)} %get-tuple-element.38), channel_id=1, source_target_pairs={{0,2},{1,3},{2,0},{3,1},{4,6},{5,7},{6,4},{7,5},{8,10},{9,11},{10,... | collective-permute-start | bytes 1572872 | tf_op jit(solution)/shard_map/ppermute | solution.py:138
  33.6 53.8 %collective-permute-start.3 = (bf16[128,1,2048]{2,0,1:T(8,128)(2,1)}, bf16[128,1,2048]{2,0,1:T(8,128)(2,1)}, u32[]{:S(2)}, u32[]{:S(2)}) collective-permute-start(bf16[128,1,2048]{2,0,1:T(8,128)(2,1)} %get-tuple-element.37), channel_id=1, source_target_pairs={{0,3},{1,0},{2,1},{3,2},{4,7},{5,4},{6,5},{7,6},{8,11},{9,8},{10,9... | collective-permute-start | bytes 1572872 | tf_op jit(solution)/shard_map/ppermute | solution.py:138
  87.4 52.6 %all-to-all-start.2 = ((bf16[8,256,512]{2,1,0:T(8,128)(2,1)}), bf16[8,256,512]{2,1,0:T(8,128)(2,1)S(1)}, u32[]{:S(2)}, u32[]{:S(2)}) async-start(bf16[8,256,512]{2,1,0:T(8,128)(2,1)} %shard_map.55), calls=%async_computation.2 | async-start | bytes 4194304 | tf_op jit(solution)/shard_map/all_to_all | solution.py:86
  152.8 6.2 %collective-permute-start.4 = (f32[2048,2]{0,1:T(2,128)S(1)}, f32[2048,2]{0,1:T(2,128)S(1)}, u32[]{:S(2)}, u32[]{:S(2)}) collective-permute-start(f32[2048,2]{0,1:T(2,128)S(1)} %slice.105), channel_id=1, source_target_pairs={{4,0},{8,4},{12,8},{16,12},{20,16},{24,20},{28,24},{5,1},{9,5},{13... | collective-permute-start | bytes 49160 | tf_op jit(solution)/shard_map/ppermute | solution.py:17
  156.7 7.8 %collective-permute-start.8 = (f32[2048,2]{0,1:T(2,128)S(1)}, f32[2048,2]{0,1:T(2,128)S(1)}, u32[]{:S(2)}, u32[]{:S(2)}) collective-permute-start(f32[2048,2]{0,1:T(2,128)S(1)} %slice.108), channel_id=1, source_target_pairs={{4,0},{8,4},{12,8},{16,12},{20,16},{24,20},{28,24},{5,1},{9,5},{13... | collective-permute-start | bytes 49160 | tf_op jit(solution)/shard_map/ppermute | solution.py:17
  160.9 14.8 %collective-permute-start.5 = (bf16[2048,128]{0,1:T(8,128)(2,1)S(1)}, bf16[2048,128]{0,1:T(8,128)(2,1)S(1)}, u32[]{:S(2)}, u32[]{:S(2)}) collective-permute-start(bf16[2048,128]{0,1:T(8,128)(2,1)S(1)} %get-tuple-element.36), channel_id=1, source_target_pairs={{0,1},{1,2},{2,3},{3,0},{4,5},{5,6},{6,7},{7,4},{8,9},{9,10},{10,1... | collective-permute-start | bytes 1572872 | tf_op jit(solution)/shard_map/ppermute | solution.py:125
  162.4 26.0 %collective-permute-start.6 = (bf16[2048,128]{0,1:T(8,128)(2,1)S(1)}, bf16[2048,128]{0,1:T(8,128)(2,1)S(1)}, u32[]{:S(2)}, u32[]{:S(2)}) collective-permute-start(bf16[2048,128]{0,1:T(8,128)(2,1)S(1)} %get-tuple-element.35), channel_id=1, source_target_pairs={{0,2},{1,3},{2,0},{3,1},{4,6},{5,7},{6,4},{7,5},{8,10},{9,11},{10,... | collective-permute-start | bytes 1572872 | tf_op jit(solution)/shard_map/ppermute | solution.py:125
  162.9 26.4 %collective-permute-start.7 = (bf16[2048,128]{0,1:T(8,128)(2,1)S(1)}, bf16[2048,128]{0,1:T(8,128)(2,1)S(1)}, u32[]{:S(2)}, u32[]{:S(2)}) collective-permute-start(bf16[2048,128]{0,1:T(8,128)(2,1)S(1)} %get-tuple-element.34), channel_id=1, source_target_pairs={{0,3},{1,0},{2,1},{3,2},{4,7},{5,4},{6,5},{7,6},{8,11},{9,8},{10,9... | collective-permute-start | bytes 1572872 | tf_op jit(solution)/shard_map/ppermute | solution.py:125
  166.2 32.0 %collective-permute-start.9 = (bf16[2048,128]{0,1:T(8,128)(2,1)S(1)}, bf16[2048,128]{0,1:T(8,128)(2,1)S(1)}, u32[]{:S(2)}, u32[]{:S(2)}) collective-permute-start(bf16[2048,128]{0,1:T(8,128)(2,1)S(1)} %get-tuple-element.33), channel_id=1, source_target_pairs={{0,1},{1,2},{2,3},{3,0},{4,5},{5,6},{6,7},{7,4},{8,9},{9,10},{10,1... | collective-permute-start | bytes 1572872 | tf_op jit(solution)/shard_map/ppermute | solution.py:125
  167.6 42.1 %collective-permute-start.10 = (bf16[2048,128]{0,1:T(8,128)(2,1)S(1)}, bf16[2048,128]{0,1:T(8,128)(2,1)S(1)}, u32[]{:S(2)}, u32[]{:S(2)}) collective-permute-start(bf16[2048,128]{0,1:T(8,128)(2,1)S(1)} %get-tuple-element.32), channel_id=1, source_target_pairs={{0,2},{1,3},{2,0},{3,1},{4,6},{5,7},{6,4},{7,5},{8,10},{9,11},{10,... | collective-permute-start | bytes 1572872 | tf_op jit(solution)/shard_map/ppermute | solution.py:125
  175.7 34.8 %collective-permute-start.11 = (bf16[2048,128]{0,1:T(8,128)(2,1)S(1)}, bf16[2048,128]{0,1:T(8,128)(2,1)S(1)}, u32[]{:S(2)}, u32[]{:S(2)}) collective-permute-start(bf16[2048,128]{0,1:T(8,128)(2,1)S(1)} %get-tuple-element.31), channel_id=1, source_target_pairs={{0,3},{1,0},{2,1},{3,2},{4,7},{5,4},{6,5},{7,6},{8,11},{9,8},{10,9... | collective-permute-start | bytes 1572872 | tf_op jit(solution)/shard_map/ppermute | solution.py:125
